TPU v7x, 256 devices: a whole 4x4x8 slice. The times are simulated.
256 devices in a mesh: prow: 64 (over x, z, core), pcol: 4 (over y).
Axes of the slice: x: 4, y: 4, z: 8, core: 2. Of those that a mesh axis runs over, the one named last changes fastest.
Arguments:
- right_side: float32 [512, 65536], P('pcol', 'prow'), may hold values from -6 to 6
- factor: float32 [65536, 2048], P('prow', 'pcol'), may hold values from -0.125 to 0.125
- inverses: float32 [2048, 512], replicated, as said below
Outputs:
- solved: float32 [512, 65536], P('pcol', 'prow')
Inputs may be any that keep to these rules, and one draw needn't show every extreme that they name: Each 512 x 512 block of inverses is lower triangular with a positive diagonal.
All inputs are finite; a program needn't handle non-finite values.
Results may differ from a plain program's by a relative error of at most 0.0001.
Values sent between devices are 32-bit elements; how exact they have to be, the bound alone decides.
No kernel may reach another device: no remote copies, remote signals or barrier semaphores. Data moves between devices by JAX's collectives and lax.ppermute only.
A program may use at most 64 MiB of HBM per device.

v0:
```python
import jax
import jax.numpy as jnp
from jax import lax
from jax.sharding import PartitionSpec as P


def spread(block, axis, source):
    block = jnp.where(lax.axis_index(axis) == source, block, jnp.zeros_like(block))
    return lax.psum(block, axis)


def contract(left, right):
    return lax.dot_general(
        left,
        right,
        (((1,), (1,)), ((), ())),
        precision=lax.Precision.HIGHEST,
        preferred_element_type=jnp.float32,
    )


def per_device(right_side, factor, inverses):
    block = factor.shape[1]
    rhs_width = right_side.shape[0]
    sections = lax.axis_size("pcol")
    all_samples = rhs_width * sections
    row_at = lax.axis_index("prow")
    col_at = lax.axis_index("pcol")
    top_block = factor[:block]
    panel_own = jnp.zeros((all_samples, block), jnp.float32)
    solved_head = jnp.zeros((rhs_width, block), jnp.float32)
    own_panels = []
    for section in range(sections):
        current = right_side[:, :block]
        if section > 0:
            current = current - lax.psum_scatter(
                contract(panel_own, top_block), "pcol", scatter_dimension=0, tiled=True
            )
        block_inverse = inverses[section * block : (section + 1) * block]
        solved_part = contract(current, block_inverse)
        solved_head = jnp.where(row_at == section, solved_part, solved_head)
        gathered = lax.all_gather(solved_part, "pcol", axis=0, tiled=True)
        panel_full = spread(gathered, "prow", section)
        panel_own = jnp.where(col_at == section, panel_full, panel_own)
        own_panels.append(lax.dynamic_slice_in_dim(panel_full, col_at * rhs_width, rhs_width, 0))
    updated = right_side - lax.psum_scatter(
        contract(panel_own, factor), "pcol", scatter_dimension=0, tiled=True
    )
    head_block = jnp.where(row_at < sections, solved_head, updated[:, :block])
    return jnp.concatenate([head_block, updated[:, block:]], axis=1)


def solution(mesh):
    return jax.shard_map(
        per_device,
        mesh=mesh,
        in_specs=(P("pcol", "prow"), P("prow", "pcol"), P()),
        out_specs=P("pcol", "prow"),
        check_vma=False,
    )
```

profile of v0, /device:TPU:7, one launch (start us, length us, event | category | flops | bytes accessed | tf_op | source)
XLA Modules:
  0.0 1011.0 jit_solution(16642700536585829825)
XLA Ops:
  6.5 3.2 fusion.8
  9.8 28.6 %all-gather.5.cloned.1.call-done = f32[512,512]{1,0:T(8,128)} async-done(((f32[128,512]{1,0:T(8,128)}), f32[512,512]{1,0:T(8,128)}) %all-gather.5.cloned.1.call-update) | async-done | bytes 1048592 | tf_op jit(solution)/shard_map/all_gather | solution.py:42
  39.6 186.7 %all-reduce.5.cloned.1.call-done = f32[512,512]{1,0:T(8,128)} async-done(((f32[512,512]{1,0:T(8,128)}), f32[512,512]{1,0:T(8,128)}) %all-reduce.5.cloned.1.call-update) | async-done | bytes 1048592 | tf_op jit(solution)/shard_map/psum | solution.py:9
  226.3 4.1 fusion.10
  230.4 23.2 %reduce-scatter.5.cloned.1.call-done = f32[128,512]{1,0:T(8,128)} async-done(((f32[512,512]{1,0:T(8,128)}), f32[128,512]{1,0:T(8,128)}) %reduce-scatter.5.cloned.1.call-update) | async-done | bytes 262160 | tf_op jit(solution)/shard_map/reduce_scatter | solution.py:36
  253.6 3.2 fusion.6
  256.9 26.8 %all-gather.7.cloned.1.call-done = f32[512,512]{1,0:T(8,128)} async-done(((f32[128,512]{1,0:T(8,128)}), f32[512,512]{1,0:T(8,128)}) %all-gather.7.cloned.1.call-update) | async-done | bytes 1048592 | tf_op jit(solution)/shard_map/all_gather | solution.py:42
  284.9 186.5 %all-reduce.7.cloned.1.call-done = f32[512,512]{1,0:T(8,128)} async-done(((f32[512,512]{1,0:T(8,128)}), f32[512,512]{1,0:T(8,128)}) %all-reduce.7.cloned.1.call-update) | async-done | bytes 1048592 | tf_op jit(solution)/shard_map/psum | solution.py:9
  471.4 1.4 select_select_fusion
  472.8 2.8 fusion.14
  475.8 23.2 %reduce-scatter.7.cloned.1.call-done = f32[128,512]{1,0:T(8,128)} async-done(((f32[512,512]{1,0:T(8,128)}), f32[128,512]{1,0:T(8,128)}) %reduce-scatter.7.cloned.1.call-update) | async-done | bytes 262160 | tf_op jit(solution)/shard_map/reduce_scatter | solution.py:36
  499.0 3.3 fusion.4
  502.3 26.9 %all-gather.9.cloned.1.call-done = f32[512,512]{1,0:T(8,128)} async-done(((f32[128,512]{1,0:T(8,128)}), f32[512,512]{1,0:T(8,128)}) %all-gather.9.cloned.1.call-update) | async-done | bytes 1048592 | tf_op jit(solution)/shard_map/all_gather | solution.py:42
  529.3 1.1 broadcast_select_fusion.1
  530.4 186.7 %all-reduce.9.cloned.1.call-done = f32[512,512]{1,0:T(8,128)} async-done(((f32[512,512]{1,0:T(8,128)}), f32[512,512]{1,0:T(8,128)}) %all-reduce.9.cloned.1.call-update) | async-done | bytes 1048592 | tf_op jit(solution)/shard_map/psum | solution.py:9
  717.1 2.8 fusion.12
  720.0 25.7 %reduce-scatter.9.cloned.1.call-done = f32[128,512]{1,0:T(8,128)} async-done(((f32[512,512]{1,0:T(8,128)}), f32[128,512]{1,0:T(8,128)}) %reduce-scatter.9.cloned.1.call-update) | async-done | bytes 262160 | tf_op jit(solution)/shard_map/reduce_scatter | solution.py:36
  745.7 3.3 fusion.2
  749.1 26.9 %all-gather.11.cloned.1.call-done = f32[512,512]{1,0:T(8,128)} async-done(((f32[128,512]{1,0:T(8,128)}), f32[512,512]{1,0:T(8,128)}) %all-gather.11.cloned.1.call-update) | async-done | bytes 1048592 | tf_op jit(solution)/shard_map/all_gather | solution.py:42
  775.9 1.1 broadcast_select_fusion
  777.3 186.5 %all-reduce.11.cloned.1.call-done = f32[512,512]{1,0:T(8,128)} async-done(((f32[512,512]{1,0:T(8,128)}), f32[512,512]{1,0:T(8,128)}) %all-reduce.11.cloned.1.call-update) | async-done | bytes 1048592 | tf_op jit(solution)/shard_map/psum | solution.py:9
  963.8 4.9 fusion
  968.7 33.3 %reduce-scatter.11.cloned.1.call-done = f32[128,1024]{1,0:T(8,128)} async-done(((f32[512,1024]{1,0:T(8,128)}), f32[128,1024]{1,0:T(8,128)}) %reduce-scatter.11.cloned.1.call-update) | async-done | bytes 524304 | tf_op jit(solution)/shard_map/reduce_scatter | solution.py:46
  1002.0 1.1 sub.15
  (44 shorter events, 4.0 us)
Async XLA Ops:
  6.5 31.9 %all-gather.5.cloned.1.call-start = ((), (), s32[]{:S(2)}) async-start(), calls=%async_computation.4 | async-start | bytes 1310720 | tf_op jit(solution)/shard_map/all_gather | solution.py:42
  9.7 216.5 %copy-start = (f32[1024,512]{1,0:T(8,128)S(1)}, f32[1024,512]{1,0:T(8,128)}, u32[]{:S(2)}) copy-start(f32[1024,512]{1,0:T(8,128)} %param.4) | copy-start | bytes 6291460
  9.7 216.5 %all-reduce.5.cloned.1.call-start = ((), (), s32[]{:S(2)}) async-start(), calls=%async_computation.5 | async-start | bytes 2097152 | tf_op jit(solution)/shard_map/psum | solution.py:9
  39.5 214.1 %reduce-scatter.5.cloned.1.call-start = ((), (), s32[]{:S(2)}) async-start(), calls=%async_computation.6 | async-start | bytes 1310720 | tf_op jit(solution)/shard_map/reduce_scatter | solution.py:36
  39.6 214.0 %copy-start.1 = (f32[128,1024]{1,0:T(8,128)S(1)}, f32[128,1024]{1,0:T(8,128)}, u32[]{:S(2)}) copy-start(f32[128,1024]{1,0:T(8,128)} %param.3) | copy-start | bytes 1572868
  230.3 53.4 %all-gather.7.cloned.1.call-start = ((), (), s32[]{:S(2)}) async-start(), calls=%async_computation.7 | async-start | bytes 1310720 | tf_op jit(solution)/shard_map/all_gather | solution.py:42
  256.8 214.6 %all-reduce.7.cloned.1.call-start = ((), (), s32[]{:S(2)}) async-start(), calls=%async_computation.8 | async-start | bytes 2097152 | tf_op jit(solution)/shard_map/psum | solution.py:9
  284.8 214.2 %reduce-scatter.7.cloned.1.call-start = ((), (), s32[]{:S(2)}) async-start(), calls=%async_computation.9 | async-start | bytes 1310720 | tf_op jit(solution)/shard_map/reduce_scatter | solution.py:36
  475.7 53.5 %all-gather.9.cloned.1.call-start = ((), (), s32[]{:S(2)}) async-start(), calls=%async_computation.10 | async-start | bytes 1310720 | tf_op jit(solution)/shard_map/all_gather | solution.py:42
  502.3 214.8 %all-reduce.9.cloned.1.call-start = ((), (), s32[]{:S(2)}) async-start(), calls=%async_computation.11 | async-start | bytes 2097152 | tf_op jit(solution)/shard_map/psum | solution.py:9
  530.4 215.3 %reduce-scatter.9.cloned.1.call-start = ((), (), s32[]{:S(2)}) async-start(), calls=%async_computation.12 | async-start | bytes 1310720 | tf_op jit(solution)/shard_map/reduce_scatter | solution.py:36
  719.9 56.0 %all-gather.11.cloned.1.call-start = ((), (), s32[]{:S(2)}) async-start(), calls=%async_computation.13 | async-start | bytes 1310720 | tf_op jit(solution)/shard_map/all_gather | solution.py:42
  749.0 214.8 %all-reduce.11.cloned.1.call-start = ((), (), s32[]{:S(2)}) async-start(), calls=%async_computation.14 | async-start | bytes 2097152 | tf_op jit(solution)/shard_map/psum | solution.py:9
  777.0 225.0 %reduce-scatter.11.cloned.1.call-start = ((), (), s32[]{:S(2)}) async-start(), calls=%async_computation.15 | async-start | bytes 2621440 | tf_op jit(solution)/shard_map/reduce_scatter | solution.py:46
  968.6 33.4 %copy-start.2 = (f32[128,1024]{1,0:T(8,128)S(1)}, f32[128,1024]{1,0:T(8,128)}, u32[]{:S(2)}) copy-start(f32[128,1024]{1,0:T(8,128)} %param.3) | copy-start | bytes 1572868
  968.6 34.5 %copy-start.3 = (f32[128,512]{1,0:T(8,128)S(1)}, f32[128,512]{1,0:T(8,128)}, u32[]{:S(2)}) copy-start(f32[128,512]{1,0:T(8,128)} %fusion.6) | copy-start | bytes 786436
  968.6 34.5 %copy-start.4 = (f32[128,512]{1,0:T(8,128)S(1)}, f32[128,512]{1,0:T(8,128)}, u32[]{:S(2)}) copy-start(f32[128,512]{1,0:T(8,128)} %fusion.4) | copy-start | bytes 786436
  968.6 34.5 %copy-start.5 = (f32[128,512]{1,0:T(8,128)S(1)}, f32[128,512]{1,0:T(8,128)}, u32[]{:S(2)}) copy-start(f32[128,512]{1,0:T(8,128)} %fusion.2) | copy-start | bytes 786436
  968.7 34.5 %copy-start.6 = (f32[128,512]{1,0:T(8,128)S(1)}, f32[128,512]{1,0:T(8,128)}, u32[]{:S(2)}) copy-start(f32[128,512]{1,0:T(8,128)} %fusion.8) | copy-start | bytes 786436
  1003.3 0.8 copy-start.7
Sparse Core Ops, SparseCore 0:
  9.9 28.5 all-gather.4
  41.9 184.3 all-reduce.4
  230.5 23.0 reduce-scatter.4
  257.0 26.7 all-gather.6
  287.0 184.3 all-reduce.6
  475.8 23.0 reduce-scatter.6
  502.4 26.8 all-gather.8
  532.7 184.3 all-reduce.8
  720.1 25.5 reduce-scatter.8
  749.1 26.7 all-gather.10
  779.4 184.3 all-reduce.10
  968.8 33.1 reduce-scatter.10
where the time goes:
time: 1010 us
  waiting for transfers between devices  961 us (95%)
  matrix products  27.6 us (3%)
  between operations  13.7 us (1%)
    psum x4, waiting for transfers between devices, spread(): return lax.psum(block, axis)  746 us
    all_gather x4, waiting for transfers between devices, per_device(): gathered = lax.all_gather(solved_part, 'pcol', axis=0, tiled=True)  109 us
    reduce_scatter x3, waiting for transfers between devices, per_device(): lax.psum_scatter(contract(panel_own, top_block), 'pcol', scatter_dimensio...  72.1 us
    reduce_scatter x1, waiting for transfers between devices, per_device(): lax.psum_scatter(contract(panel_own, factor), 'pcol', scatter_dimension=0...  33.3 us
    dot_general x8, matrix products, contract(): lax.dot_general(left, right, (((1,), (1,)), ((), ())), precision=lax.Prec...  27.6 us
  transfers between devices with their start and end apart: 12, of which 12 were waited for; matrix products, arithmetic and copies ran while one was open for 0% of the time, Pallas kernels for 0%

commit v1 on v0

v1 whole, which is shorter than its diff:
```python
import jax
import jax.numpy as jnp
from jax import lax
from jax.sharding import PartitionSpec as P


def contract(left, right):
    return lax.dot_general(
        left,
        right,
        (((1,), (1,)), ((), ())),
        precision=lax.Precision.HIGHEST,
        preferred_element_type=jnp.float32,
    )


AXES = ("prow", "pcol")


def per_device(right_side, factor, inverses):
    block = factor.shape[1]
    rhs_width = right_side.shape[0]
    n_col = lax.axis_size("pcol")
    n_row = lax.axis_size("prow")
    steps = n_col
    row_at = lax.axis_index("prow")
    col_at = lax.axis_index("pcol")

    def at(p, c):
        return p * n_col + c

    top_rhs = right_side[:, :block]
    top_block = factor[:block]

    fetched = [top_block]
    for shift in range(1, n_col):
        pairs = [
            (at(i, j), at(i, (j + shift) % n_col))
            for i in range(1, steps)
            for j in range(i)
        ]
        fetched.append(lax.ppermute(top_block, AXES, pairs))
    fetched = jnp.stack(fetched)

    acc = jnp.zeros((rhs_width, block), jnp.float32)
    own = jnp.zeros((rhs_width, block), jnp.float32)
    for k in range(steps):
        solved = contract(top_rhs - acc, inverses[k * block : (k + 1) * block])
        own = jnp.where(row_at == k, solved, own)
        if k == steps - 1:
            break
        arrived = jnp.zeros_like(solved)
        for i in range(k + 1, steps):
            pairs = [(at(k, c), at(i, c)) for c in range(n_col)]
            arrived = arrived + lax.ppermute(solved, AXES, pairs)
        lower = lax.dynamic_index_in_dim(fetched, (col_at - k) % n_col, 0, keepdims=False)
        acc = acc + contract(arrived, lower)

    pairs = [(at(j, c), at(c, j)) for j in range(steps) for c in range(n_col) if j != c]
    piece = lax.ppermute(own, AXES, pairs)
    piece = jnp.where(row_at == col_at, own, piece)

    span = n_row // 2
    while span >= steps:
        pairs = [(p, p + span) for p in range(n_row) if p % (2 * span) < steps]
        arrived = lax.ppermute(piece, "prow", pairs)
        rel = row_at % (2 * span)
        piece = jnp.where((rel >= span) & (rel < span + steps), arrived, piece)
        span //= 2
    b0 = row_at % 2
    b1 = (row_at // 2) % 2
    other = lax.ppermute(piece, "prow", [(p, p ^ 2) for p in range(n_row)])
    pair = jnp.where(b1 == 0, jnp.concatenate([piece, other]), jnp.concatenate([other, piece]))
    theirs = lax.ppermute(pair, "prow", [(p, p ^ 1) for p in range(n_row)])
    mine_first = jnp.concatenate([pair[:rhs_width], theirs[:rhs_width], pair[rhs_width:], theirs[rhs_width:]])
    theirs_first = jnp.concatenate([theirs[:rhs_width], pair[:rhs_width], theirs[rhs_width:], pair[rhs_width:]])
    panel = jnp.where(b0 == 0, mine_first, theirs_first)

    updated = right_side - lax.psum_scatter(
        contract(panel, factor), "pcol", scatter_dimension=0, tiled=True
    )
    head_block = jnp.where(row_at < steps, own, updated[:, :block])
    return jnp.concatenate([head_block, updated[:, block:]], axis=1)


def solution(mesh):
    return jax.shard_map(
        per_device,
        mesh=mesh,
        in_specs=(P("pcol", "prow"), P("prow", "pcol"), P()),
        out_specs=P("pcol", "prow"),
        check_vma=False,
    )
```

time: 1010 us -> 196 us (0.19)
  waiting for transfers between devices: 961 us -> 114 us
  starting transfers between devices: 0.64 us -> 34.5 us
    psum x4 -> x0, waiting for transfers between devices: 746 us -> none  [spread(): return lax.psum(block, axis)]
    all_gather x4 -> x0, waiting for transfers between devices: 109 us -> none  [per_device(): gathered = lax.all_gather(solved_part, 'pcol', axis=0, tiled=True)]
    ppermute x0 -> x16, waiting for transfers between devices: none -> 81.4 us  [the longest x4 75.7 us: per_device(): arrived = lax.ppermute(piece, 'prow', pairs)]
    reduce_scatter x4 -> x1, waiting for transfers between devices: 105 us -> 32.8 us  [per_device(): lax.psum_scatter(contract(panel, factor), 'pcol', scatter_dimension=0, ti...]
    ppermute x0 -> x16, starting transfers between devices: none -> 34.5 us  [the longest x1 17 us: per_device(): other = lax.ppermute(piece, 'prow', [(p, p ^ 2) for p in range(n_row)])]
  transfers between devices with their start and end apart: 12 -> 17, of which waited for: 12 -> 6; matrix products, arithmetic and copies ran while one was open for 0% -> 3% of each run, Pallas kernels for 0% -> 0%
where the time goes in v1:
time: 196 us; the launch traced here: 195 us
  waiting for transfers between devices  114 us (58%)
  starting transfers between devices  34.5 us (18%)
  matrix products  23 us (12%)
  between operations  13.8 us (7%)
  local copies, waits for them, and re-layouts  5.23 us (3%)
  other arithmetic  3.76 us (2%)
    ppermute x4, waiting for transfers between devices, per_device(): arrived = lax.ppermute(piece, 'prow', pairs)  75.7 us
    reduce_scatter x1, waiting for transfers between devices, per_device(): lax.psum_scatter(contract(panel, factor), 'pcol', scatter_dimension=0, ti...  32.8 us
    dot_general x8, matrix products, contract(): lax.dot_general(left, right, (((1,), (1,)), ((), ())), precision=lax.Prec...  23 us
    ppermute x1, starting transfers between devices, per_device(): other = lax.ppermute(piece, 'prow', [(p, p ^ 2) for p in range(n_row)])  17 us
    ppermute x6, starting transfers between devices, per_device(): arrived = arrived + lax.ppermute(solved, AXES, pairs)  4.77 us
    ppermute x4, starting transfers between devices, per_device(): arrived = lax.ppermute(piece, 'prow', pairs)  4.58 us
    ppermute x1, waiting for transfers between devices, per_device(): other = lax.ppermute(piece, 'prow', [(p, p ^ 2) for p in range(n_row)])  4.12 us
    ppermute x3, starting transfers between devices, per_device(): fetched.append(lax.ppermute(top_block, AXES, pairs))  4.02 us
  transfers between devices with their start and end apart: 17, of which 6 were waited for; matrix products, arithmetic and copies ran while one was open for 3% of the time, Pallas kernels for 0%

profile of v1, /device:TPU:7, one launch (start us, length us, event | category | flops | bytes accessed | tf_op | source)
XLA Modules:
  0.0 194.5 jit_solution(10623068641595624824)
XLA Ops:
  6.5 1.5 slice_bitcast_fusion
  8.8 1.6 collective-permute-start.4
  10.4 1.6 collective-permute-start.3
  12.0 2.5 %fusion.27 = f32[128,512]{1,0:T(8,128)S(1)} fusion(f32[2048,512]{1,0:T(8,128)} %param.5, f32[128,1024]{1,0:T(8,128)} %param.3), kind=kOutput, calls=%fused_computation.32 | convolution fusion | flops 402653184 | bytes 1572864 | tf_op jit(solution)/shard_map/dot_general | solution.py:8
  16.9 1.4 collective-permute-start.1
  18.3 2.4 %pad_maximum_fusion = f32[4,512,512]{2,1,0:T(8,128)S(1)} fusion(f32[1,512,512]{2,1,0:T(8,128)} %bitcast.17, f32[1,512,512]{2,1,0:T(8,128)} %bitcast.2, f32[1,512,512]{2,1,0:T(8,128)} %bitcast.1, f32[1,512,512]{2,1,0:T(8,128)S(1)} %get-tuple-element.5), kind=kLoop, calls=%fused_computation | loop fusion | flops 3145728 | bytes 8388608 | tf_op jit(solution)/shard_map/stack | solution.py:43
  20.7 1.9 copy-done
  22.6 2.1 %fusion.17 = f32[128,512]{1,0:T(8,128)S(1)} fusion(f32[4,512,512]{2,1,0:T(8,128)S(1)} %pad_maximum_fusion, s32[]{:T(128)S(6)} %select_n.134, f32[128,512]{1,0:T(8,128)S(1)} %collective-permute-done.2, f32[128,512]{1,0:T(8,128)S(1)} %collective-permute-done, f32[128,512]{1,0:T(8,128)} %collective-permute-done.1), kind=kOutput, calls=%fused_computation.22 | convolution fusion | flops 402784256 | bytes 2097156 | tf_op jit(solution)/shard_map/dot_general | solution.py:8
  24.7 2.4 %fusion.24 = f32[128,512]{1,0:T(8,128)S(1)} fusion(f32[2048,512]{1,0:T(8,128)} %param.5, f32[128,512]{1,0:T(8,128)S(1)} %fusion.17, f32[128,1024]{1,0:T(8,128)S(1)} %copy-done.1), kind=kOutput, calls=%fused_computation.29 | convolution fusion | flops 402718720 | bytes 1835008 | tf_op jit(solution)/shard_map/dot_general | solution.py:8
  28.5 2.4 %convolution_add_fusion.1 = f32[128,512]{1,0:T(8,128)S(1)} fusion(f32[128,512]{1,0:T(8,128)S(1)} %fusion.17, f32[4,512,512]{2,1,0:T(8,128)} %copy-done, s32[]{:T(128)S(6)} %select_n.136, f32[128,512]{1,0:T(8,128)S(1)} %collective-permute-done.6, f32[128,512]{1,0:T(8,128)S(1)} %collective-permute-done.7), kind=kOutput, calls=%fused_computation.4 | convolution fusion | flops 402784256 | bytes 2097156 | tf_op jit(solution)/shard_map/dot_general | solution.py:8
  30.9 2.4 %fusion.21 = f32[128,512]{1,0:T(8,128)S(1)} fusion(f32[2048,512]{1,0:T(8,128)} %param.5, f32[128,512]{1,0:T(8,128)S(1)} %convolution_add_fusion.1, f32[128,1024]{1,0:T(8,128)S(1)} %copy-done.1), kind=kOutput, calls=%fused_computation.26 | convolution fusion | flops 402718720 | bytes 1835008 | tf_op jit(solution)/shard_map/dot_general | solution.py:8
  34.0 2.4 %fusion = f32[128,512]{1,0:T(8,128)S(1)} fusion(f32[128,512]{1,0:T(8,128)S(1)} %convolution_add_fusion.1, f32[128,512]{1,0:T(8,128)S(1)} %collective-permute-done.8, f32[4,512,512]{2,1,0:T(8,128)} %copy-done, s32[]{:T(128)S(6)} %select_n.138, f32[128,1024]{1,0:T(8,128)S(1)} %copy-done.1), kind=kOutput, calls=%fused_computation.3 | convolution fusion | flops 402784256 | bytes 2097156 | tf_op jit(solution)/shard_map/dot_general | solution.py:8
  36.4 2.4 %convolution_select_fusion = f32[128,512]{1,0:T(8,128)S(1)} fusion(f32[128,512]{1,0:T(8,128)S(1)} %fusion, f32[2048,512]{1,0:T(8,128)} %param.5, f32[128,512]{1,0:T(8,128)S(1)} %fusion.21, f32[128,512]{1,0:T(8,128)S(1)} %fusion.24, f32[128,512]{1,0:T(8,128)S(1)} %fusion.27, pred[]{:T(512)S(6)} %eq.34, pred[]{:T(512)S(6)} %eq.33, pred[]{:T(512)S(6)} %eq.32, ...), kind=kOutput, calls=%fused_computation.1 | convolution fusion | flops 402915328 | bytes 2359300 | tf_op jit(solution)/shard_map/dot_general | solution.py:8
  41.6 69.2 %collective-permute-done.11 = f32[128,512]{1,0:T(8,128)S(1)} collective-permute-done((f32[128,512]{1,0:T(8,128)S(1)}, f32[128,512]{1,0:T(8,128)S(1)}, u32[]{:S(2)}, u32[]{:S(2)}) %collective-permute-start.11) | collective-permute-done | bytes 262176 | tf_op jit(solution)/shard_map/ppermute | solution.py:66
  110.9 1.3 collective-permute-start.12
  112.2 3.3 %collective-permute-done.12 = f32[128,512]{1,0:T(8,128)S(1)} collective-permute-done((f32[128,512]{1,0:T(8,128)S(1)}, f32[128,512]{1,0:T(8,128)S(1)}, u32[]{:S(2)}, u32[]{:S(2)}) %collective-permute-start.12) | collective-permute-done | bytes 262176 | tf_op jit(solution)/shard_map/ppermute | solution.py:66
  115.5 1.3 collective-permute-start.13
  116.8 3.3 %collective-permute-done.13 = f32[128,512]{1,0:T(8,128)S(1)} collective-permute-done((f32[128,512]{1,0:T(8,128)S(1)}, f32[128,512]{1,0:T(8,128)S(1)}, u32[]{:S(2)}, u32[]{:S(2)}) %collective-permute-start.13) | collective-permute-done | bytes 262176 | tf_op jit(solution)/shard_map/ppermute | solution.py:66
  120.1 17.0 %collective-permute-start.14 = (f32[128,512]{1,0:T(8,128)S(1)}, f32[128,512]{1,0:T(8,128)S(1)}, u32[]{:S(2)}, u32[]{:S(2)}) collective-permute-start(f32[128,512]{1,0:T(8,128)S(1)} %broadcast_select_fusion.4), channel_id=1, source_target_pairs={{0,8},{4,12},{8,0},{12,4},{16,24},{20,28},{24,16},{28,20},{32,40},... | collective-permute-start | bytes 786440 | tf_op jit(solution)/shard_map/ppermute | solution.py:72
  137.2 4.1 %collective-permute-done.14 = f32[128,512]{1,0:T(8,128)S(1)} collective-permute-done((f32[128,512]{1,0:T(8,128)S(1)}, f32[128,512]{1,0:T(8,128)S(1)}, u32[]{:S(2)}, u32[]{:S(2)}) %collective-permute-start.14) | collective-permute-done | bytes 262176 | tf_op jit(solution)/shard_map/ppermute | solution.py:72
  141.3 3.4 %collective-permute-start.15 = (f32[256,512]{1,0:T(8,128)S(1)}, f32[256,512]{1,0:T(8,128)S(1)}, u32[]{:S(2)}, u32[]{:S(2)}) collective-permute-start(f32[256,512]{1,0:T(8,128)S(1)} %maximum_select_fusion.2), channel_id=1, source_target_pairs={{0,4},{4,0},{8,12},{12,8},{16,20},{20,16},{24,28},{28,24},{32,36},... | collective-permute-start | bytes 1572872 | tf_op jit(solution)/shard_map/ppermute | solution.py:74
  144.8 1.5 collective-permute-done.15
  146.3 6.5 %fusion.1 = f32[512,1024]{1,0:T(8,128)} fusion(f32[1024,512]{1,0:T(8,128)} %param.4, f32[128,512]{1,0:T(8,128)S(1)} %get-tuple-element.12, f32[128,512]{1,0:T(8,128)S(1)} %get-tuple-element.10, f32[128,512]{1,0:T(8,128)S(1)} %get-tuple-element.11, f32[128,512]{1,0:T(8,128)S(1)} %get-tuple-element.9, pred[]{:T(512)S(6)} %eq.35), kind=kOutput, calls=%fused_computation.6 | convolution fusion | flops 3223060480 | bytes 5242881 | tf_op jit(solution)/shard_map/dot_general | solution.py:8
  152.9 32.8 %reduce-scatter.2.cloned.1.call-done = f32[128,1024]{1,0:T(8,128)} async-done(((f32[512,1024]{1,0:T(8,128)}), f32[128,1024]{1,0:T(8,128)}) %reduce-scatter.2.cloned.1.call-update) | async-done | bytes 524304 | tf_op jit(solution)/shard_map/reduce_scatter | solution.py:79
  (40 shorter events, 10.1 us)
Async XLA Ops:
  6.5 179.2 %reduce-scatter.2.cloned.1.call-start = ((), (), s32[]{:S(2)}) async-start(), calls=%async_computation.1 | async-start | bytes 2621440 | tf_op jit(solution)/shard_map/reduce_scatter | solution.py:79
  8.0 7.9 %collective-permute-start.5 = (f32[512,512]{1,0:T(8,128)S(1)}, f32[512,512]{1,0:T(8,128)S(1)}, u32[]{:S(2)}, u32[]{:S(2)}) collective-permute-start(f32[512,512]{1,0:T(8,128)S(1)} %get-tuple-element.6), channel_id=1, source_target_pairs={{4,7},{8,11},{9,8},{12,15},{13,12},{14,13}} | collective-permute-start | bytes 3145736 | tf_op jit(solution)/shard_map/ppermute | solution.py:42
  8.8 9.5 %collective-permute-start.4 = (f32[512,512]{1,0:T(8,128)S(1)}, f32[512,512]{1,0:T(8,128)}, u32[]{:S(2)}, u32[]{:S(2)}) collective-permute-start(f32[512,512]{1,0:T(8,128)S(1)} %get-tuple-element.6), channel_id=1, source_target_pairs={{4,6},{8,10},{9,11},{12,14},{13,15},{14,12}} | collective-permute-start | bytes 3145736 | tf_op jit(solution)/shard_map/ppermute | solution.py:42
  10.4 7.9 %collective-permute-start.3 = (f32[512,512]{1,0:T(8,128)S(1)}, f32[512,512]{1,0:T(8,128)}, u32[]{:S(2)}, u32[]{:S(2)}) collective-permute-start(f32[512,512]{1,0:T(8,128)S(1)} %get-tuple-element.6), channel_id=1, source_target_pairs={{4,5},{8,9},{9,10},{12,13},{13,14},{14,15}} | collective-permute-start | bytes 3145736 | tf_op jit(solution)/shard_map/ppermute | solution.py:42
  14.5 6.1 %collective-permute-start.2 = (f32[128,512]{1,0:T(8,128)S(1)}, f32[128,512]{1,0:T(8,128)S(1)}, u32[]{:S(2)}, u32[]{:S(2)}) collective-permute-start(f32[128,512]{1,0:T(8,128)S(1)} %fusion.27), channel_id=1, source_target_pairs={{0,12},{1,13},{2,14},{3,15}} | collective-permute-start | bytes 786440 | tf_op jit(solution)/shard_map/ppermute | solution.py:55
  15.2 5.5 %collective-permute-start = (f32[128,512]{1,0:T(8,128)S(1)}, f32[128,512]{1,0:T(8,128)S(1)}, u32[]{:S(2)}, u32[]{:S(2)}) collective-permute-start(f32[128,512]{1,0:T(8,128)S(1)} %fusion.27), channel_id=1, source_target_pairs={{0,4},{1,5},{2,6},{3,7}} | collective-permute-start | bytes 786440 | tf_op jit(solution)/shard_map/ppermute | solution.py:55
  15.9 1.0 copy-start.2
  16.9 3.8 %collective-permute-start.1 = (f32[128,512]{1,0:T(8,128)S(1)}, f32[128,512]{1,0:T(8,128)}, u32[]{:S(2)}, u32[]{:S(2)}) collective-permute-start(f32[128,512]{1,0:T(8,128)S(1)} %fusion.27), channel_id=1, source_target_pairs={{0,8},{1,9},{2,10},{3,11}} | collective-permute-start | bytes 786440 | tf_op jit(solution)/shard_map/ppermute | solution.py:55
  18.3 6.4 %copy-start.1 = (f32[128,1024]{1,0:T(8,128)S(1)}, f32[128,1024]{1,0:T(8,128)}, u32[]{:S(2)}) copy-start(f32[128,1024]{1,0:T(8,128)} %param.3) | copy-start | bytes 1572868
  20.6 1.9 %copy-start = (f32[4,512,512]{2,1,0:T(8,128)}, f32[4,512,512]{2,1,0:T(8,128)S(1)}, u32[]{:S(2)}) copy-start(f32[4,512,512]{2,1,0:T(8,128)S(1)} %pad_maximum_fusion) | copy-start | bytes 12582916
  27.1 1.4 collective-permute-start.6
  27.8 0.7 collective-permute-start.7
  33.3 0.7 collective-permute-start.8
  38.8 0.7 collective-permute-start.9
  39.6 0.7 collective-permute-start.10
  40.3 70.5 %collective-permute-start.11 = (f32[128,512]{1,0:T(8,128)S(1)}, f32[128,512]{1,0:T(8,128)S(1)}, u32[]{:S(2)}, u32[]{:S(2)}) collective-permute-start(f32[128,512]{1,0:T(8,128)S(1)} %broadcast_select_fusion.1), channel_id=1, source_target_pairs={{0,64},{4,68},{8,72},{12,76},{128,192},{132,196},{136,200},{140,20... | collective-permute-start | bytes 786440 | tf_op jit(solution)/shard_map/ppermute | solution.py:66
  110.9 4.6 %collective-permute-start.12 = (f32[128,512]{1,0:T(8,128)S(1)}, f32[128,512]{1,0:T(8,128)S(1)}, u32[]{:S(2)}, u32[]{:S(2)}) collective-permute-start(f32[128,512]{1,0:T(8,128)S(1)} %broadcast_select_fusion.2), channel_id=1, source_target_pairs={{0,32},{4,36},{8,40},{12,44},{64,96},{68,100},{72,104},{76,108},{1... | collective-permute-start | bytes 786440 | tf_op jit(solution)/shard_map/ppermute | solution.py:66
  115.5 4.6 %collective-permute-start.13 = (f32[128,512]{1,0:T(8,128)S(1)}, f32[128,512]{1,0:T(8,128)S(1)}, u32[]{:S(2)}, u32[]{:S(2)}) collective-permute-start(f32[128,512]{1,0:T(8,128)S(1)} %broadcast_select_fusion.3), channel_id=1, source_target_pairs={{0,16},{4,20},{8,24},{12,28},{32,48},{36,52},{40,56},{44,60},{64,8... | collective-permute-start | bytes 786440 | tf_op jit(solution)/shard_map/ppermute | solution.py:66
  120.1 21.1 %collective-permute-start.14 = (f32[128,512]{1,0:T(8,128)S(1)}, f32[128,512]{1,0:T(8,128)S(1)}, u32[]{:S(2)}, u32[]{:S(2)}) collective-permute-start(f32[128,512]{1,0:T(8,128)S(1)} %broadcast_select_fusion.4), channel_id=1, source_target_pairs={{0,8},{4,12},{8,0},{12,4},{16,24},{20,28},{24,16},{28,20},{32,40},... | collective-permute-start | bytes 786440 | tf_op jit(solution)/shard_map/ppermute | solution.py:72
  141.3 4.9 %collective-permute-start.15 = (f32[256,512]{1,0:T(8,128)S(1)}, f32[256,512]{1,0:T(8,128)S(1)}, u32[]{:S(2)}, u32[]{:S(2)}) collective-permute-start(f32[256,512]{1,0:T(8,128)S(1)} %maximum_select_fusion.2), channel_id=1, source_target_pairs={{0,4},{4,0},{8,12},{12,8},{16,20},{20,16},{24,28},{28,24},{32,36},... | collective-permute-start | bytes 1572872 | tf_op jit(solution)/shard_map/ppermute | solution.py:74
  186.9 0.8 copy-start.3
Sparse Core Ops, SparseCore 0:
  153.0 32.6 reduce-scatter.1

commit v2 on v1

v2 whole, which is shorter than its diff:
```python
import jax
import jax.numpy as jnp
from jax import lax
from jax.sharding import PartitionSpec as P


def contract(left, right):
    return lax.dot_general(
        left,
        right,
        (((1,), (1,)), ((), ())),
        precision=lax.Precision.HIGHEST,
        preferred_element_type=jnp.float32,
    )


AXES = ("prow", "pcol")


def per_device(right_side, factor, inverses):
    block = factor.shape[1]
    rhs_width = right_side.shape[0]
    n_col = lax.axis_size("pcol")
    n_row = lax.axis_size("prow")
    steps = n_col
    row_at = lax.axis_index("prow")
    col_at = lax.axis_index("pcol")

    def at(p, c):
        return p * n_col + c

    top_rhs = right_side[:, :block]
    top_block = factor[:block]

    fetched = [top_block]
    for shift in range(1, n_col):
        pairs = [
            (at(i, j), at(i, (j + shift) % n_col))
            for i in range(1, steps)
            for j in range(i)
        ]
        fetched.append(lax.ppermute(top_block, AXES, pairs))
    fetched = jnp.stack(fetched)

    b0 = row_at % 2
    b1 = (row_at // 2) % 2
    acc = jnp.zeros((rhs_width, block), jnp.float32)
    own = jnp.zeros((rhs_width, block), jnp.float32)
    panels = []
    for k in range(steps):
        solved = contract(top_rhs - acc, inverses[k * block : (k + 1) * block])
        own = jnp.where(row_at == k, solved, own)
        if k < steps - 1:
            arrived = jnp.zeros_like(solved)
            for i in range(k + 1, steps):
                pairs = [(at(k, c), at(i, c)) for c in range(n_col)]
                arrived = arrived + lax.ppermute(solved, AXES, pairs)
            lower = lax.dynamic_index_in_dim(fetched, (col_at - k) % n_col, 0, keepdims=False)
            acc = acc + contract(arrived, lower)

        pairs = [(at(k, c), at(c, k)) for c in range(n_col) if c != k]
        piece = lax.ppermute(solved, AXES, pairs)
        piece = jnp.where(row_at == k, solved, piece)
        span = n_row // 2
        while span >= steps:
            pairs = [(at(p, k), at(p + span, k)) for p in range(n_row) if p % (2 * span) < steps]
            arrived = lax.ppermute(piece, AXES, pairs)
            rel = row_at % (2 * span)
            piece = jnp.where((rel >= span) & (rel < span + steps), arrived, piece)
            span //= 2
        other = lax.ppermute(piece, AXES, [(at(p, k), at(p ^ 2, k)) for p in range(n_row)])
        pair = jnp.where(b1 == 0, jnp.concatenate([piece, other]), jnp.concatenate([other, piece]))
        theirs = lax.ppermute(pair, AXES, [(at(p, k), at(p ^ 1, k)) for p in range(n_row)])
        mine_first = jnp.concatenate([pair[:rhs_width], theirs[:rhs_width], pair[rhs_width:], theirs[rhs_width:]])
        theirs_first = jnp.concatenate([theirs[:rhs_width], pair[:rhs_width], theirs[rhs_width:], pair[rhs_width:]])
        panels.append(jnp.where(b0 == 0, mine_first, theirs_first))

    panel = panels[0]
    for k in range(1, steps):
        panel = jnp.where(col_at == k, panels[k], panel)

    partial = contract(panel, factor)
    total = lax.dynamic_slice_in_dim(partial, col_at * rhs_width, rhs_width, 0)
    for shift in range(1, n_col):
        chunk = lax.dynamic_slice_in_dim(partial, ((col_at + shift) % n_col) * rhs_width, rhs_width, 0)
        total = total + lax.ppermute(chunk, "pcol", [(c, (c + shift) % n_col) for c in range(n_col)])
    updated = right_side - total
    head_block = jnp.where(row_at < steps, own, updated[:, :block])
    return jnp.concatenate([head_block, updated[:, block:]], axis=1)


def solution(mesh):
    return jax.shard_map(
        per_device,
        mesh=mesh,
        in_specs=(P("pcol", "prow"), P("prow", "pcol"), P()),
        out_specs=P("pcol", "prow"),
        check_vma=False,
    )
```

time: 196 us -> 215 us (1.097)
  starting transfers between devices: 34.5 us -> 149 us
  waiting for transfers between devices: 114 us -> 33 us
  between operations: 13.8 us -> 1.1 us
  matrix products: 23 us -> 19.4 us
  other arithmetic: 3.76 us -> 5.97 us
    ppermute x7 -> x31, starting transfers between devices: 25.7 us -> 140 us  [the longest x4 71.4 us: per_device(): lax.ppermute(piece, AXES, [(at(p, k), at(p ^ 2, k)) for p in range(n_row)])]
    ppermute x7 -> x31, waiting for transfers between devices: 81.3 us -> 33 us  [the longest x16 18.4 us: per_device(): arrived = lax.ppermute(piece, AXES, pairs)]
    reduce_scatter x1 -> x0, waiting for transfers between devices: 32.8 us -> none  [per_device(): lax.psum_scatter(contract(panel, factor), 'pcol', scatter_dimension=0, ti...]
    dot_general x8, matrix products: 23 us -> 19.4 us  [contract(): lax.dot_general(left, right, (((1,), (1,)), ((), ())), precision=lax.Prec...]
  transfers between devices with their start and end apart: 17 -> 40, of which waited for: 6 -> 3; matrix products, arithmetic and copies ran while one was open for 3% -> 8% of each run, Pallas kernels for 0% -> 0%
where the time goes in v2:
time: 215 us; the launch traced here: 213 us
  starting transfers between devices  149 us (69%)
  waiting for transfers between devices  33 us (15%)
  matrix products  19.4 us (9%)
  other arithmetic  5.97 us (3%)
  local copies, waits for them, and re-layouts  5.23 us (2%)
    ppermute x4, starting transfers between devices, per_device(): lax.ppermute(piece, AXES, [(at(p, k), at(p ^ 2, k)) for p in range(n_row)])  71.4 us
    ppermute x3, starting transfers between devices, per_device(): lax.ppermute(chunk, 'pcol', [(c, (c + shift) % n_col) for c in range(n_co...  45.4 us
    dot_general x8, matrix products, contract(): lax.dot_general(left, right, (((1,), (1,)), ((), ())), precision=lax.Prec...  19.4 us
    ppermute x16, waiting for transfers between devices, per_device(): arrived = lax.ppermute(piece, AXES, pairs)  18.4 us
    ppermute x3, waiting for transfers between devices, per_device(): lax.ppermute(chunk, 'pcol', [(c, (c + shift) % n_col) for c in range(n_co...  14.6 us
    ppermute x16, starting transfers between devices, per_device(): arrived = lax.ppermute(piece, AXES, pairs)  13.4 us
    ppermute x4, starting transfers between devices, per_device(): lax.ppermute(pair, AXES, [(at(p, k), at(p ^ 1, k)) for p in range(n_row)])  6.72 us
    ppermute x3, starting transfers between devices, per_device(): fetched.append(lax.ppermute(top_block, AXES, pairs))  4.91 us
  transfers between devices with their start and end apart: 40, of which 3 were waited for; matrix products, arithmetic and copies ran while one was open for 8% of the time, Pallas kernels for 0%

profile of v2, /device:TPU:7, one launch (start us, length us, event | category | flops | bytes accessed | tf_op | source)
XLA Modules:
  0.0 213.3 jit_solution(15093845866911825295)
XLA Ops:
  0.0 2.5 %fusion.73 = f32[128,512]{1,0:T(8,128)S(1)} fusion(f32[2048,512]{1,0:T(8,128)} %param.5, f32[128,1024]{1,0:T(8,128)} %param.3), kind=kOutput, calls=%fused_computation.77 | convolution fusion | flops 402653184 | bytes 1572864 | tf_op jit(solution)/shard_map/dot_general | solution.py:8
  3.2 1.5 slice_bitcast_fusion
  4.7 1.7 collective-permute-start.5
  6.3 1.6 collective-permute-start.4
  7.9 1.6 collective-permute-start.3
  12.4 18.3 %collective-permute-done.32 = f32[128,512]{1,0:T(8,128)S(1)} collective-permute-done((f32[128,512]{1,0:T(8,128)S(1)}, f32[128,512]{1,0:T(8,128)S(1)}, u32[]{:S(2)}, u32[]{:S(2)}) %collective-permute-start.32) | collective-permute-done | bytes 262176 | tf_op jit(solution)/shard_map/ppermute | solution.py:67
  32.2 2.0 collective-permute-start.33
  34.2 2.4 %pad_maximum_fusion = f32[4,512,512]{2,1,0:T(8,128)S(1)} fusion(f32[1,512,512]{2,1,0:T(8,128)} %bitcast.3, f32[1,512,512]{2,1,0:T(8,128)} %bitcast.2, f32[1,512,512]{2,1,0:T(8,128)} %bitcast.1, f32[1,512,512]{2,1,0:T(8,128)S(1)} %get-tuple-element.8), kind=kLoop, calls=%fused_computation | loop fusion | flops 3145728 | bytes 8388608 | tf_op jit(solution)/shard_map/stack | solution.py:43
  36.6 1.9 copy-done
  39.7 2.4 %fusion.70 = f32[128,512]{1,0:T(8,128)S(1)} fusion(f32[2048,512]{1,0:T(8,128)} %param.5, f32[128,512]{1,0:T(8,128)S(1)} %fusion.62, f32[128,1024]{1,0:T(8,128)S(1)} %copy-done.1), kind=kOutput, calls=%fused_computation.74 | convolution fusion | flops 402718720 | bytes 1835008 | tf_op jit(solution)/shard_map/dot_general | solution.py:8
  45.7 2.4 %convolution_add_fusion.1 = f32[128,512]{1,0:T(8,128)S(1)} fusion(f32[128,512]{1,0:T(8,128)S(1)} %fusion.62, f32[4,512,512]{2,1,0:T(8,128)} %copy-done, s32[]{:T(128)S(6)} %select_n.284, f32[128,512]{1,0:T(8,128)S(1)} %collective-permute-done.6, f32[128,512]{1,0:T(8,128)S(1)} %collective-permute-done.7), kind=kOutput, calls=%fused_computation.3 | convolution fusion | flops 402784256 | bytes 2097156 | tf_op jit(solution)/shard_map/dot_general | solution.py:8
  48.1 2.4 %fusion.67 = f32[128,512]{1,0:T(8,128)S(1)} fusion(f32[2048,512]{1,0:T(8,128)} %param.5, f32[128,512]{1,0:T(8,128)S(1)} %convolution_add_fusion.1, f32[128,1024]{1,0:T(8,128)S(1)} %copy-done.1), kind=kOutput, calls=%fused_computation.71 | convolution fusion | flops 402718720 | bytes 1835008 | tf_op jit(solution)/shard_map/dot_general | solution.py:8
  52.7 4.3 %collective-permute-start.35 = (f32[128,512]{1,0:T(8,128)S(1)}, f32[128,512]{1,0:T(8,128)S(1)}, u32[]{:S(2)}, u32[]{:S(2)}) collective-permute-start(f32[128,512]{1,0:T(8,128)S(1)} %broadcast_select_fusion.12), channel_id=1, source_target_pairs={{0,8},{4,12},{8,0},{12,4},{16,24},{20,28},{24,16},{28,20},{32,40},... | collective-permute-start | bytes 786440 | tf_op jit(solution)/shard_map/ppermute | solution.py:71
  56.9 2.4 %fusion = f32[128,512]{1,0:T(8,128)S(1)} fusion(f32[128,512]{1,0:T(8,128)S(1)} %convolution_add_fusion.1, f32[128,512]{1,0:T(8,128)S(1)} %collective-permute-done.8, f32[4,512,512]{2,1,0:T(8,128)} %copy-done, s32[]{:T(128)S(6)} %select_n.286, f32[128,1024]{1,0:T(8,128)S(1)} %copy-done.1), kind=kOutput, calls=%fused_computation.2 | convolution fusion | flops 402784256 | bytes 2097156 | tf_op jit(solution)/shard_map/dot_general | solution.py:8
  59.3 2.4 %fusion.64 = f32[128,512]{1,0:T(8,128)S(1)} fusion(f32[128,512]{1,0:T(8,128)S(1)} %fusion, f32[2048,512]{1,0:T(8,128)} %param.5), kind=kOutput, calls=%fused_computation.68 | convolution fusion | flops 402653184 | bytes 1572864 | tf_op jit(solution)/shard_map/dot_general | solution.py:8
  61.8 4.5 %collective-permute-start.36 = (f32[256,512]{1,0:T(8,128)S(1)}, f32[256,512]{1,0:T(8,128)S(1)}, u32[]{:S(2)}, u32[]{:S(2)}) collective-permute-start(f32[256,512]{1,0:T(8,128)S(1)} %maximum_select_fusion.8), channel_id=1, source_target_pairs={{0,4},{4,0},{8,12},{12,8},{16,20},{20,16},{24,28},{28,24},{32,36},... | collective-permute-start | bytes 1572872 | tf_op jit(solution)/shard_map/ppermute | solution.py:73
  77.6 65.8 %collective-permute-start.14 = (f32[128,512]{1,0:T(8,128)S(1)}, f32[128,512]{1,0:T(8,128)S(1)}, u32[]{:S(2)}, u32[]{:S(2)}) collective-permute-start(f32[128,512]{1,0:T(8,128)S(1)} %broadcast_select_fusion.15), channel_id=1, source_target_pairs={{3,11},{7,15},{11,3},{15,7},{19,27},{23,31},{27,19},{31,23},{35,43... | collective-permute-start | bytes 786440 | tf_op jit(solution)/shard_map/ppermute | solution.py:71
  145.4 3.8 %fusion.2 = f32[512,1024]{1,0:T(8,128)S(1)} fusion(f32[1024,512]{1,0:T(8,128)S(1)} %copy-done.3, f32[128,512]{1,0:T(8,128)S(1)} %get-tuple-element.27, f32[128,512]{1,0:T(8,128)S(1)} %get-tuple-element.25, f32[128,512]{1,0:T(8,128)S(1)} %get-tuple-element.26, f32[128,512]{1,0:T(8,128)S(1)} %get-tuple-element.24, f32[128,512]{1,0:T(8,128)S(1)} %get-tuple-element.23, ...), kind=kOutput, calls=%fused_computation.6 | convolution fusion | flops 3229351936 | bytes 8388612 | tf_op jit(solution)/shard_map/dot_general | solution.py:8
  150.7 21.7 %collective-permute-start.39 = (f32[128,1024]{1,0:T(8,128)S(1)}, f32[128,1024]{1,0:T(8,128)}, u32[]{:S(2)}, u32[]{:S(2)}) collective-permute-start(f32[128,1024]{1,0:T(8,128)S(1)} %get-tuple-element.6), channel_id=1, source_target_pairs={{0,3},{1,0},{2,1},{3,2},{4,7},{5,4},{6,5},{7,6},{8,11},{9,8},{10,9... | collective-permute-start | bytes 1572872 | tf_op jit(solution)/shard_map/ppermute | solution.py:86
  172.4 11.8 %collective-permute-start.38 = (f32[128,1024]{1,0:T(8,128)S(1)}, f32[128,1024]{1,0:T(8,128)}, u32[]{:S(2)}, u32[]{:S(2)}) collective-permute-start(f32[128,1024]{1,0:T(8,128)S(1)} %get-tuple-element.7), channel_id=1, source_target_pairs={{0,2},{1,3},{2,0},{3,1},{4,6},{5,7},{6,4},{7,5},{8,10},{9,11},{10,... | collective-permute-start | bytes 1572872 | tf_op jit(solution)/shard_map/ppermute | solution.py:86
  184.2 11.8 %collective-permute-start.37 = (f32[128,1024]{1,0:T(8,128)S(1)}, f32[128,1024]{1,0:T(8,128)}, u32[]{:S(2)}, u32[]{:S(2)}) collective-permute-start(f32[128,1024]{1,0:T(8,128)S(1)} %get-tuple-element.5), channel_id=1, source_target_pairs={{0,1},{1,2},{2,3},{3,0},{4,5},{5,6},{6,7},{7,4},{8,9},{9,10},{10,1... | collective-permute-start | bytes 1572872 | tf_op jit(solution)/shard_map/ppermute | solution.py:86
  196.1 3.0 %collective-permute-done.38 = f32[128,1024]{1,0:T(8,128)} collective-permute-done((f32[128,1024]{1,0:T(8,128)S(1)}, f32[128,1024]{1,0:T(8,128)}, u32[]{:S(2)}, u32[]{:S(2)}) %collective-permute-start.38) | collective-permute-done | bytes 524320 | tf_op jit(solution)/shard_map/ppermute | solution.py:86
  199.1 11.6 %collective-permute-done.37 = f32[128,1024]{1,0:T(8,128)} collective-permute-done((f32[128,1024]{1,0:T(8,128)S(1)}, f32[128,1024]{1,0:T(8,128)}, u32[]{:S(2)}, u32[]{:S(2)}) %collective-permute-start.37) | collective-permute-done | bytes 524320 | tf_op jit(solution)/shard_map/ppermute | solution.py:86
  210.7 1.7 add_subtract_fusion
  (110 shorter events, 26.7 us)
Async XLA Ops:
  2.5 7.1 %collective-permute-start.30 = (f32[128,512]{1,0:T(8,128)S(1)}, f32[128,512]{1,0:T(8,128)S(1)}, u32[]{:S(2)}, u32[]{:S(2)}) collective-permute-start(f32[128,512]{1,0:T(8,128)S(1)} %fusion.73), channel_id=1, source_target_pairs={{1,4},{2,8},{3,12}} | collective-permute-start | bytes 786440 | tf_op jit(solution)/shard_map/ppermute | solution.py:62
  4.7 26.8 %collective-permute-start.5 = (f32[512,512]{1,0:T(8,128)S(1)}, f32[512,512]{1,0:T(8,128)}, u32[]{:S(2)}, u32[]{:S(2)}) collective-permute-start(f32[512,512]{1,0:T(8,128)S(1)} %get-tuple-element.9), channel_id=1, source_target_pairs={{4,7},{8,11},{9,8},{12,15},{13,12},{14,13}} | collective-permute-start | bytes 3145736 | tf_op jit(solution)/shard_map/ppermute | solution.py:42
  6.3 25.8 %collective-permute-start.4 = (f32[512,512]{1,0:T(8,128)S(1)}, f32[512,512]{1,0:T(8,128)}, u32[]{:S(2)}, u32[]{:S(2)}) collective-permute-start(f32[512,512]{1,0:T(8,128)S(1)} %get-tuple-element.9), channel_id=1, source_target_pairs={{4,6},{8,10},{9,11},{12,14},{13,15},{14,12}} | collective-permute-start | bytes 3145736 | tf_op jit(solution)/shard_map/ppermute | solution.py:42
  7.9 26.2 %collective-permute-start.3 = (f32[512,512]{1,0:T(8,128)S(1)}, f32[512,512]{1,0:T(8,128)}, u32[]{:S(2)}, u32[]{:S(2)}) collective-permute-start(f32[512,512]{1,0:T(8,128)S(1)} %get-tuple-element.9), channel_id=1, source_target_pairs={{4,5},{8,9},{9,10},{12,13},{13,14},{14,15}} | collective-permute-start | bytes 3145736 | tf_op jit(solution)/shard_map/ppermute | solution.py:42
  10.4 20.4 %collective-permute-start.32 = (f32[128,512]{1,0:T(8,128)S(1)}, f32[128,512]{1,0:T(8,128)S(1)}, u32[]{:S(2)}, u32[]{:S(2)}) collective-permute-start(f32[128,512]{1,0:T(8,128)S(1)} %broadcast_select_fusion), channel_id=1, source_target_pairs={{0,64},{4,68},{8,72},{12,76},{128,192},{132,196},{136,200},{140,204}} | collective-permute-start | bytes 786440 | tf_op jit(solution)/shard_map/ppermute | solution.py:67
  11.7 24.9 %collective-permute-start.2 = (f32[128,512]{1,0:T(8,128)S(1)}, f32[128,512]{1,0:T(8,128)S(1)}, u32[]{:S(2)}, u32[]{:S(2)}) collective-permute-start(f32[128,512]{1,0:T(8,128)S(1)} %fusion.73), channel_id=1, source_target_pairs={{0,12},{1,13},{2,14},{3,15}} | collective-permute-start | bytes 786440 | tf_op jit(solution)/shard_map/ppermute | solution.py:57
  30.7 5.8 %collective-permute-start = (f32[128,512]{1,0:T(8,128)S(1)}, f32[128,512]{1,0:T(8,128)S(1)}, u32[]{:S(2)}, u32[]{:S(2)}) collective-permute-start(f32[128,512]{1,0:T(8,128)S(1)} %fusion.73), channel_id=1, source_target_pairs={{0,4},{1,5},{2,6},{3,7}} | collective-permute-start | bytes 786440 | tf_op jit(solution)/shard_map/ppermute | solution.py:57
  31.4 5.2 %collective-permute-start.1 = (f32[128,512]{1,0:T(8,128)S(1)}, f32[128,512]{1,0:T(8,128)S(1)}, u32[]{:S(2)}, u32[]{:S(2)}) collective-permute-start(f32[128,512]{1,0:T(8,128)S(1)} %fusion.73), channel_id=1, source_target_pairs={{0,8},{1,9},{2,10},{3,11}} | collective-permute-start | bytes 786440 | tf_op jit(solution)/shard_map/ppermute | solution.py:57
  32.2 12.1 %collective-permute-start.33 = (f32[128,512]{1,0:T(8,128)S(1)}, f32[128,512]{1,0:T(8,128)}, u32[]{:S(2)}, u32[]{:S(2)}) collective-permute-start(f32[128,512]{1,0:T(8,128)S(1)} %broadcast_select_fusion.4), channel_id=1, source_target_pairs={{0,32},{4,36},{8,40},{12,44},{64,96},{68,100},{72,104},{76,108},{1... | collective-permute-start | bytes 786440 | tf_op jit(solution)/shard_map/ppermute | solution.py:67
  42.1 3.6 %collective-permute-start.6 = (f32[128,512]{1,0:T(8,128)S(1)}, f32[128,512]{1,0:T(8,128)S(1)}, u32[]{:S(2)}, u32[]{:S(2)}) collective-permute-start(f32[128,512]{1,0:T(8,128)S(1)} %fusion.70), channel_id=1, source_target_pairs={{4,8},{5,9},{6,10},{7,11}} | collective-permute-start | bytes 786440 | tf_op jit(solution)/shard_map/ppermute | solution.py:57
  42.8 2.9 %collective-permute-start.7 = (f32[128,512]{1,0:T(8,128)S(1)}, f32[128,512]{1,0:T(8,128)S(1)}, u32[]{:S(2)}, u32[]{:S(2)}) collective-permute-start(f32[128,512]{1,0:T(8,128)S(1)} %fusion.70), channel_id=1, source_target_pairs={{4,12},{5,13},{6,14},{7,15}} | collective-permute-start | bytes 786440 | tf_op jit(solution)/shard_map/ppermute | solution.py:57
  43.6 8.3 %collective-permute-start.23 = (f32[128,512]{1,0:T(8,128)S(1)}, f32[128,512]{1,0:T(8,128)S(1)}, u32[]{:S(2)}, u32[]{:S(2)}) collective-permute-start(f32[128,512]{1,0:T(8,128)S(1)} %fusion.70), channel_id=1, source_target_pairs={{4,1},{6,9},{7,13}} | collective-permute-start | bytes 786440 | tf_op jit(solution)/shard_map/ppermute | solution.py:62
  44.4 8.2 %collective-permute-start.34 = (f32[128,512]{1,0:T(8,128)S(1)}, f32[128,512]{1,0:T(8,128)S(1)}, u32[]{:S(2)}, u32[]{:S(2)}) collective-permute-start(f32[128,512]{1,0:T(8,128)S(1)} %broadcast_select_fusion.8), channel_id=1, source_target_pairs={{0,16},{4,20},{8,24},{12,28},{32,48},{36,52},{40,56},{44,60},{64,8... | collective-permute-start | bytes 786440 | tf_op jit(solution)/shard_map/ppermute | solution.py:67
  50.5 6.4 %collective-permute-start.8 = (f32[128,512]{1,0:T(8,128)S(1)}, f32[128,512]{1,0:T(8,128)S(1)}, u32[]{:S(2)}, u32[]{:S(2)}) collective-permute-start(f32[128,512]{1,0:T(8,128)S(1)} %fusion.67), channel_id=1, source_target_pairs={{8,12},{9,13},{10,14},{11,15}} | collective-permute-start | bytes 786440 | tf_op jit(solution)/shard_map/ppermute | solution.py:57
  51.2 15.8 %collective-permute-start.16 = (f32[128,512]{1,0:T(8,128)S(1)}, f32[128,512]{1,0:T(8,128)S(1)}, u32[]{:S(2)}, u32[]{:S(2)}) collective-permute-start(f32[128,512]{1,0:T(8,128)S(1)} %fusion.67), channel_id=1, source_target_pairs={{8,2},{9,6},{11,14}} | collective-permute-start | bytes 786440 | tf_op jit(solution)/shard_map/ppermute | solution.py:62
  51.9 15.8 %collective-permute-start.24 = (f32[128,512]{1,0:T(8,128)S(1)}, f32[128,512]{1,0:T(8,128)S(1)}, u32[]{:S(2)}, u32[]{:S(2)}) collective-permute-start(f32[128,512]{1,0:T(8,128)S(1)} %broadcast_select_fusion.17), channel_id=1, source_target_pairs={{1,129},{5,133},{9,137},{13,141}} | collective-permute-start | bytes 786440 | tf_op jit(solution)/shard_map/ppermute | solution.py:67
  52.7 9.1 %collective-permute-start.35 = (f32[128,512]{1,0:T(8,128)S(1)}, f32[128,512]{1,0:T(8,128)S(1)}, u32[]{:S(2)}, u32[]{:S(2)}) collective-permute-start(f32[128,512]{1,0:T(8,128)S(1)} %broadcast_select_fusion.12), channel_id=1, source_target_pairs={{0,8},{4,12},{8,0},{12,4},{16,24},{20,28},{24,16},{28,20},{32,40},... | collective-permute-start | bytes 786440 | tf_op jit(solution)/shard_map/ppermute | solution.py:71
  61.8 11.1 %collective-permute-start.36 = (f32[256,512]{1,0:T(8,128)S(1)}, f32[256,512]{1,0:T(8,128)S(1)}, u32[]{:S(2)}, u32[]{:S(2)}) collective-permute-start(f32[256,512]{1,0:T(8,128)S(1)} %maximum_select_fusion.8), channel_id=1, source_target_pairs={{0,4},{4,0},{8,12},{12,8},{16,20},{20,16},{24,28},{28,24},{32,36},... | collective-permute-start | bytes 1572872 | tf_op jit(solution)/shard_map/ppermute | solution.py:73
  76.0 67.4 %collective-permute-start.21 = (f32[128,512]{1,0:T(8,128)S(1)}, f32[128,512]{1,0:T(8,128)S(1)}, u32[]{:S(2)}, u32[]{:S(2)}) collective-permute-start(f32[128,512]{1,0:T(8,128)S(1)} %broadcast_select_fusion.14), channel_id=1, source_target_pairs={{2,10},{6,14},{10,2},{14,6},{18,26},{22,30},{26,18},{30,22},{34,42... | collective-permute-start | bytes 786440 | tf_op jit(solution)/shard_map/ppermute | solution.py:71
  76.7 68.4 %collective-permute-start.29 = (f32[256,512]{1,0:T(8,128)S(1)}, f32[256,512]{1,0:T(8,128)S(1)}, u32[]{:S(2)}, u32[]{:S(2)}) collective-permute-start(f32[256,512]{1,0:T(8,128)S(1)} %maximum_select_fusion.7), channel_id=1, source_target_pairs={{1,5},{5,1},{9,13},{13,9},{17,21},{21,17},{25,29},{29,25},{33,37},... | collective-permute-start | bytes 1572872 | tf_op jit(solution)/shard_map/ppermute | solution.py:73
  77.6 66.6 %collective-permute-start.14 = (f32[128,512]{1,0:T(8,128)S(1)}, f32[128,512]{1,0:T(8,128)S(1)}, u32[]{:S(2)}, u32[]{:S(2)}) collective-permute-start(f32[128,512]{1,0:T(8,128)S(1)} %broadcast_select_fusion.15), channel_id=1, source_target_pairs={{3,11},{7,15},{11,3},{15,7},{19,27},{23,31},{27,19},{31,23},{35,43... | collective-permute-start | bytes 786440 | tf_op jit(solution)/shard_map/ppermute | solution.py:71
  150.7 45.4 %collective-permute-start.39 = (f32[128,1024]{1,0:T(8,128)S(1)}, f32[128,1024]{1,0:T(8,128)}, u32[]{:S(2)}, u32[]{:S(2)}) collective-permute-start(f32[128,1024]{1,0:T(8,128)S(1)} %get-tuple-element.6), channel_id=1, source_target_pairs={{0,3},{1,0},{2,1},{3,2},{4,7},{5,4},{6,5},{7,6},{8,11},{9,8},{10,9... | collective-permute-start | bytes 1572872 | tf_op jit(solution)/shard_map/ppermute | solution.py:86
  172.4 26.7 %collective-permute-start.38 = (f32[128,1024]{1,0:T(8,128)S(1)}, f32[128,1024]{1,0:T(8,128)}, u32[]{:S(2)}, u32[]{:S(2)}) collective-permute-start(f32[128,1024]{1,0:T(8,128)S(1)} %get-tuple-element.7), channel_id=1, source_target_pairs={{0,2},{1,3},{2,0},{3,1},{4,6},{5,7},{6,4},{7,5},{8,10},{9,11},{10,... | collective-permute-start | bytes 1572872 | tf_op jit(solution)/shard_map/ppermute | solution.py:86
  184.2 26.4 %collective-permute-start.37 = (f32[128,1024]{1,0:T(8,128)S(1)}, f32[128,1024]{1,0:T(8,128)}, u32[]{:S(2)}, u32[]{:S(2)}) collective-permute-start(f32[128,1024]{1,0:T(8,128)S(1)} %get-tuple-element.5), channel_id=1, source_target_pairs={{0,1},{1,2},{2,3},{3,0},{4,5},{5,6},{6,7},{7,4},{8,9},{9,10},{10,1... | collective-permute-start | bytes 1572872 | tf_op jit(solution)/shard_map/ppermute | solution.py:86
  (20 other events, 108.7 us)

commit v3 on v1

--- a/solution.py
+++ b/solution.py
@@ -36,15 +36,33 @@
     for shift in range(1, n_col):
         pairs = [
             (at(i, j), at(i, (j + shift) % n_col))
-            for i in range(1, steps)
-            for j in range(i)
+            for i in range(2, steps)
+            for j in range(1, i)
         ]
         fetched.append(lax.ppermute(top_block, AXES, pairs))
     fetched = jnp.stack(fetched)
 
-    acc = jnp.zeros((rhs_width, block), jnp.float32)
-    own = jnp.zeros((rhs_width, block), jnp.float32)
-    for k in range(steps):
+    solved = contract(top_rhs, inverses[:block])
+    own = jnp.where(row_at == 0, solved, jnp.zeros_like(solved))
+    pairs = [(at(0, c), at(c, 0)) for c in range(1, n_col)]
+    piece = lax.ppermute(solved, AXES, pairs)
+    piece = jnp.where(row_at == 0, solved, piece)
+    b0 = row_at % 2
+    b1 = (row_at // 2) % 2
+    other = lax.ppermute(piece, AXES, [(at(p, 0), at(p ^ 2, 0)) for p in range(steps)])
+    pair = jnp.where(b1 == 0, jnp.concatenate([piece, other]), jnp.concatenate([other, piece]))
+    theirs = lax.ppermute(pair, AXES, [(at(p, 0), at(p ^ 1, 0)) for p in range(steps)])
+    mine_first = jnp.concatenate([pair[:rhs_width], theirs[:rhs_width], pair[rhs_width:], theirs[rhs_width:]])
+    theirs_first = jnp.concatenate([theirs[:rhs_width], pair[:rhs_width], theirs[rhs_width:], pair[rhs_width:]])
+    first_panel = jnp.where(b0 == 0, mine_first, theirs_first)
+    product = contract(first_panel, top_block)
+    acc = jnp.where(col_at == 0, product[:rhs_width], jnp.zeros_like(solved))
+    for shift in range(1, n_col):
+        chunk = product[shift * rhs_width : (shift + 1) * rhs_width]
+        pairs = [(at(i, 0), at(i, shift)) for i in range(1, steps)]
+        acc = acc + lax.ppermute(chunk, AXES, pairs)
+
+    for k in range(1, steps):
         solved = contract(top_rhs - acc, inverses[k * block : (k + 1) * block])
         own = jnp.where(row_at == k, solved, own)
         if k == steps - 1:

time: 196 us -> 207 us (1.056)
  waiting for transfers between devices: 114 us -> 123 us
  starting transfers between devices: 34.5 us -> 37.6 us
  other arithmetic: 3.76 us -> 5.94 us
    reduce_scatter x1, waiting for transfers between devices: 32.8 us -> 55.1 us  [per_device(): lax.psum_scatter(contract(panel, factor), 'pcol', scatter_dimension=0, ti...]
    ppermute x4, waiting for transfers between devices: 75.7 us -> 62.1 us  [per_device(): arrived = lax.ppermute(piece, 'prow', pairs)]
    ppermute x0 -> x6, starting transfers between devices: none -> 4.75 us  [the longest x3 2.7 us: per_device(): acc = acc + lax.ppermute(chunk, AXES, pairs)]
    ppermute x1, starting transfers between devices: 17 us -> 13.4 us  [per_device(): other = lax.ppermute(piece, 'prow', [(p, p ^ 2) for p in range(n_row)])]
    ppermute x6 -> x3, starting transfers between devices: 4.77 us -> 3.4 us  [per_device(): arrived = arrived + lax.ppermute(solved, AXES, pairs)]
  transfers between devices with their start and end apart: 17 -> 20, of which waited for: 6 -> 6; matrix products, arithmetic and copies ran while one was open for 3% -> 3% of each run, Pallas kernels for 0% -> 0%
where the time goes in v3:
time: 207 us; the launch traced here: 206 us
  waiting for transfers between devices  123 us (59%)
  starting transfers between devices  37.6 us (18%)
  matrix products  21.2 us (10%)
  between operations  13.9 us (7%)
  other arithmetic  5.94 us (3%)
  local copies, waits for them, and re-layouts  4.68 us (2%)
    ppermute x4, waiting for transfers between devices, per_device(): arrived = lax.ppermute(piece, 'prow', pairs)  62.1 us
    reduce_scatter x1, waiting for transfers between devices, per_device(): lax.psum_scatter(contract(panel, factor), 'pcol', scatter_dimension=0, ti...  55.1 us
    dot_general x8, matrix products, contract(): lax.dot_general(left, right, (((1,), (1,)), ((), ())), precision=lax.Prec...  21.2 us
    ppermute x1, starting transfers between devices, per_device(): other = lax.ppermute(piece, 'prow', [(p, p ^ 2) for p in range(n_row)])  13.4 us
    ppermute x4, starting transfers between devices, per_device(): arrived = lax.ppermute(piece, 'prow', pairs)  5.95 us
    ppermute x3, starting transfers between devices, per_device(): fetched.append(lax.ppermute(top_block, AXES, pairs))  4.94 us
    ppermute x1, starting transfers between devices, per_device(): theirs = lax.ppermute(pair, 'prow', [(p, p ^ 1) for p in range(n_row)])  4.34 us
  transfers between devices with their start and end apart: 20, of which 6 were waited for; matrix products, arithmetic and copies ran while one was open for 3% of the time, Pallas kernels for 0%

profile of v3, /device:TPU:7, one launch (start us, length us, event | category | flops | bytes accessed | tf_op | source)
XLA Modules:
  0.0 205.9 jit_solution(4286505426070438385)
XLA Ops:
  6.5 2.6 %fusion.38 = f32[128,512]{1,0:T(8,128)S(1)} fusion(f32[2048,512]{1,0:T(8,128)} %param.5, f32[128,1024]{1,0:T(8,128)} %param.3), kind=kOutput, calls=%fused_computation.44 | convolution fusion | flops 402653184 | bytes 1572864 | tf_op jit(solution)/shard_map/dot_general | solution.py:8
  11.5 1.9 fusion.1
  15.2 1.7 collective-permute-start.10
  16.9 1.6 collective-permute-start.9
  18.5 1.7 collective-permute-start.8
  20.9 1.4 collective-permute-start.3
  24.1 2.4 %fusion.36 = f32[128,512]{1,0:T(8,128)S(1)} fusion(f32[2048,512]{1,0:T(8,128)} %param.5, f32[128,512]{1,0:T(8,128)S(1)} %fusion.44, f32[128,1024]{1,0:T(8,128)S(1)} %copy-done.1), kind=kOutput, calls=%fused_computation.42 | convolution fusion | flops 402718720 | bytes 1835008 | tf_op jit(solution)/shard_map/dot_general | solution.py:8
  26.5 1.4 collective-permute-start.6
  29.3 2.3 %pad_maximum_fusion = f32[4,512,512]{2,1,0:T(8,128)S(1)} fusion(f32[1,512,512]{2,1,0:T(8,128)} %bitcast.3, f32[1,512,512]{2,1,0:T(8,128)} %bitcast.2, f32[1,512,512]{2,1,0:T(8,128)} %bitcast.1, f32[1,512,512]{2,1,0:T(8,128)S(1)} %get-tuple-element.5), kind=kLoop, calls=%fused_computation | loop fusion | flops 3145728 | bytes 8388608 | tf_op jit(solution)/shard_map/stack | solution.py:43
  31.6 1.9 copy-done
  33.5 2.2 %convolution_add_fusion.1 = f32[128,512]{1,0:T(8,128)S(1)} fusion(f32[128,512]{1,0:T(8,128)S(1)} %fusion.44, f32[4,512,512]{2,1,0:T(8,128)S(1)} %pad_maximum_fusion, s32[]{:T(128)S(6)} %select_n.161, f32[128,512]{1,0:T(8,128)} %collective-permute-done.6, f32[128,512]{1,0:T(8,128)} %collective-permute-done.7), kind=kOutput, calls=%fused_computation.4 | convolution fusion | flops 402784256 | bytes 2097156 | tf_op jit(solution)/shard_map/dot_general | solution.py:8
  35.8 2.4 %fusion.33 = f32[128,512]{1,0:T(8,128)S(1)} fusion(f32[2048,512]{1,0:T(8,128)} %param.5, f32[128,512]{1,0:T(8,128)S(1)} %convolution_add_fusion.1, f32[128,1024]{1,0:T(8,128)S(1)} %copy-done.1), kind=kOutput, calls=%fused_computation.39 | convolution fusion | flops 402718720 | bytes 1835008 | tf_op jit(solution)/shard_map/dot_general | solution.py:8
  38.9 2.4 %fusion = f32[128,512]{1,0:T(8,128)S(1)} fusion(f32[128,512]{1,0:T(8,128)S(1)} %convolution_add_fusion.1, f32[128,512]{1,0:T(8,128)S(1)} %collective-permute-done.11, f32[4,512,512]{2,1,0:T(8,128)} %copy-done, s32[]{:T(128)S(6)} %select_n.163, f32[128,1024]{1,0:T(8,128)S(1)} %copy-done.1), kind=kOutput, calls=%fused_computation.3 | convolution fusion | flops 402784256 | bytes 2097156 | tf_op jit(solution)/shard_map/dot_general | solution.py:8
  41.3 2.4 %convolution_select_fusion = f32[128,512]{1,0:T(8,128)S(1)} fusion(f32[128,512]{1,0:T(8,128)S(1)} %fusion, f32[2048,512]{1,0:T(8,128)} %param.5, f32[128,512]{1,0:T(8,128)S(1)} %fusion.33, f32[128,512]{1,0:T(8,128)S(1)} %fusion.36, f32[128,512]{1,0:T(8,128)S(1)} %fusion.38, pred[]{:T(512)S(6)} %eq.44, pred[]{:T(512)S(6)} %eq.43, pred[]{:T(512)S(6)} %eq.42, ...), kind=kOutput, calls=%fused_computation.1 | convolution fusion | flops 402915328 | bytes 2359300 | tf_op jit(solution)/shard_map/dot_general | solution.py:8
  47.3 56.2 %collective-permute-done.14 = f32[128,512]{1,0:T(8,128)} collective-permute-done((f32[128,512]{1,0:T(8,128)S(1)}, f32[128,512]{1,0:T(8,128)}, u32[]{:S(2)}, u32[]{:S(2)}) %collective-permute-start.14) | collective-permute-done | bytes 262176 | tf_op jit(solution)/shard_map/ppermute | solution.py:84
  104.5 2.0 collective-permute-start.15
  106.5 2.6 %collective-permute-done.15 = f32[128,512]{1,0:T(8,128)} collective-permute-done((f32[128,512]{1,0:T(8,128)S(1)}, f32[128,512]{1,0:T(8,128)}, u32[]{:S(2)}, u32[]{:S(2)}) %collective-permute-start.15) | collective-permute-done | bytes 262176 | tf_op jit(solution)/shard_map/ppermute | solution.py:84
  110.5 3.3 %collective-permute-done.16 = f32[128,512]{1,0:T(8,128)S(1)} collective-permute-done((f32[128,512]{1,0:T(8,128)S(1)}, f32[128,512]{1,0:T(8,128)S(1)}, u32[]{:S(2)}, u32[]{:S(2)}) %collective-permute-start.16) | collective-permute-done | bytes 262176 | tf_op jit(solution)/shard_map/ppermute | solution.py:84
  113.8 13.4 %collective-permute-start.17 = (f32[128,512]{1,0:T(8,128)S(1)}, f32[128,512]{1,0:T(8,128)S(1)}, u32[]{:S(2)}, u32[]{:S(2)}) collective-permute-start(f32[128,512]{1,0:T(8,128)S(1)} %broadcast_select_fusion.4), channel_id=1, source_target_pairs={{0,8},{4,12},{8,0},{12,4},{16,24},{20,28},{24,16},{28,20},{32,40},... | collective-permute-start | bytes 786440 | tf_op jit(solution)/shard_map/ppermute | solution.py:90
  127.2 3.8 %collective-permute-done.17 = f32[128,512]{1,0:T(8,128)S(1)} collective-permute-done((f32[128,512]{1,0:T(8,128)S(1)}, f32[128,512]{1,0:T(8,128)S(1)}, u32[]{:S(2)}, u32[]{:S(2)}) %collective-permute-start.17) | collective-permute-done | bytes 262176 | tf_op jit(solution)/shard_map/ppermute | solution.py:90
  131.0 4.3 %collective-permute-start.18 = (f32[256,512]{1,0:T(8,128)S(1)}, f32[256,512]{1,0:T(8,128)S(1)}, u32[]{:S(2)}, u32[]{:S(2)}) collective-permute-start(f32[256,512]{1,0:T(8,128)S(1)} %maximum_select_fusion.5), channel_id=1, source_target_pairs={{0,4},{4,0},{8,12},{12,8},{16,20},{20,16},{24,28},{28,24},{32,36},... | collective-permute-start | bytes 1572872 | tf_op jit(solution)/shard_map/ppermute | solution.py:92
  135.4 1.5 collective-permute-done.18
  137.0 5.0 %fusion.15 = f32[512,1024]{1,0:T(8,128)} fusion(f32[1024,512]{1,0:T(8,128)S(1)} %copy-done.5, f32[128,512]{1,0:T(8,128)S(1)} %get-tuple-element.15, f32[128,512]{1,0:T(8,128)S(1)} %get-tuple-element.13, f32[128,512]{1,0:T(8,128)S(1)} %get-tuple-element.14, f32[128,512]{1,0:T(8,128)S(1)} %get-tuple-element.12, pred[]{:T(512)S(6)} %eq.40), kind=kOutput, calls=%fused_computation.21 | convolution fusion | flops 3223060480 | bytes 5242881 | tf_op jit(solution)/shard_map/dot_general | solution.py:8
  142.0 55.1 %reduce-scatter.2.cloned.1.call-done = f32[128,1024]{1,0:T(8,128)} async-done(((f32[512,1024]{1,0:T(8,128)}), f32[128,1024]{1,0:T(8,128)}) %reduce-scatter.2.cloned.1.call-update) | async-done | bytes 524304 | tf_op jit(solution)/shard_map/reduce_scatter | solution.py:97
  (60 shorter events, 16.6 us)
Async XLA Ops:
  6.5 5.0 %copy-start.3 = (f32[1024,512]{1,0:T(8,128)S(1)}, f32[1024,512]{1,0:T(8,128)}, u32[]{:S(2)}) copy-start(f32[1024,512]{1,0:T(8,128)} %param.4) | copy-start | bytes 6291460
  6.5 190.5 %reduce-scatter.2.cloned.1.call-start = ((), (), s32[]{:S(2)}) async-start(), calls=%async_computation.1 | async-start | bytes 2621440 | tf_op jit(solution)/shard_map/reduce_scatter | solution.py:97
  9.2 0.7 collective-permute-start
  9.9 0.7 collective-permute-start.1
  10.7 0.8 collective-permute-start.2
  13.4 6.8 %copy-start.2 = (f32[512,512]{1,0:T(8,128)}, f32[512,512]{1,0:T(8,128)S(1)}, u32[]{:S(2)}) copy-start(f32[512,512]{1,0:T(8,128)S(1)} %fusion.1) | copy-start | bytes 3145732
  13.4 10.7 %copy-start.1 = (f32[128,1024]{1,0:T(8,128)S(1)}, f32[128,1024]{1,0:T(8,128)}, u32[]{:S(2)}) copy-start(f32[128,1024]{1,0:T(8,128)} %param.3) | copy-start | bytes 1572868
  14.3 6.6 %collective-permute-start.5 = (f32[128,512]{1,0:T(8,128)S(1)}, f32[128,512]{1,0:T(8,128)S(1)}, u32[]{:S(2)}, u32[]{:S(2)}) collective-permute-start(f32[128,512]{1,0:T(8,128)S(1)} %get-tuple-element.8), channel_id=1, source_target_pairs={{4,7},{8,11},{12,15}} | collective-permute-start | bytes 786440 | tf_op jit(solution)/shard_map/ppermute | solution.py:63
  15.2 14.0 %collective-permute-start.10 = (f32[512,512]{1,0:T(8,128)S(1)}, f32[512,512]{1,0:T(8,128)}, u32[]{:S(2)}, u32[]{:S(2)}) collective-permute-start(f32[512,512]{1,0:T(8,128)S(1)} %get-tuple-element.6), channel_id=1, source_target_pairs={{9,8},{13,12},{14,13}} | collective-permute-start | bytes 3145736 | tf_op jit(solution)/shard_map/ppermute | solution.py:42
  16.9 12.4 %collective-permute-start.9 = (f32[512,512]{1,0:T(8,128)S(1)}, f32[512,512]{1,0:T(8,128)}, u32[]{:S(2)}, u32[]{:S(2)}) collective-permute-start(f32[512,512]{1,0:T(8,128)S(1)} %get-tuple-element.6), channel_id=1, source_target_pairs={{9,11},{13,15},{14,12}} | collective-permute-start | bytes 3145736 | tf_op jit(solution)/shard_map/ppermute | solution.py:42
  18.5 10.8 %collective-permute-start.8 = (f32[512,512]{1,0:T(8,128)S(1)}, f32[512,512]{1,0:T(8,128)}, u32[]{:S(2)}, u32[]{:S(2)}) collective-permute-start(f32[512,512]{1,0:T(8,128)S(1)} %get-tuple-element.6), channel_id=1, source_target_pairs={{9,10},{13,14},{14,15}} | collective-permute-start | bytes 3145736 | tf_op jit(solution)/shard_map/ppermute | solution.py:42
  20.2 2.1 %collective-permute-start.4 = (f32[128,512]{1,0:T(8,128)}, f32[128,512]{1,0:T(8,128)S(1)}, u32[]{:S(2)}, u32[]{:S(2)}) collective-permute-start(f32[128,512]{1,0:T(8,128)} %get-tuple-element.9), channel_id=1, source_target_pairs={{4,6},{8,10},{12,14}} | collective-permute-start | bytes 786440 | tf_op jit(solution)/shard_map/ppermute | solution.py:63
  20.9 2.1 %collective-permute-start.3 = (f32[128,512]{1,0:T(8,128)}, f32[128,512]{1,0:T(8,128)}, u32[]{:S(2)}, u32[]{:S(2)}) collective-permute-start(f32[128,512]{1,0:T(8,128)} %get-tuple-element.7), channel_id=1, source_target_pairs={{4,5},{8,9},{12,13}} | collective-permute-start | bytes 786440 | tf_op jit(solution)/shard_map/ppermute | solution.py:63
  26.5 5.1 %collective-permute-start.6 = (f32[128,512]{1,0:T(8,128)S(1)}, f32[128,512]{1,0:T(8,128)}, u32[]{:S(2)}, u32[]{:S(2)}) collective-permute-start(f32[128,512]{1,0:T(8,128)S(1)} %fusion.36), channel_id=1, source_target_pairs={{4,8},{5,9},{6,10},{7,11}} | collective-permute-start | bytes 786440 | tf_op jit(solution)/shard_map/ppermute | solution.py:73
  27.9 3.7 %collective-permute-start.7 = (f32[128,512]{1,0:T(8,128)S(1)}, f32[128,512]{1,0:T(8,128)}, u32[]{:S(2)}, u32[]{:S(2)}) collective-permute-start(f32[128,512]{1,0:T(8,128)S(1)} %fusion.36), channel_id=1, source_target_pairs={{4,12},{5,13},{6,14},{7,15}} | collective-permute-start | bytes 786440 | tf_op jit(solution)/shard_map/ppermute | solution.py:73
  38.2 0.7 collective-permute-start.11
  43.7 93.3 %copy-start.5 = (f32[1024,512]{1,0:T(8,128)S(1)}, f32[1024,512]{1,0:T(8,128)}, u32[]{:S(2)}) copy-start(f32[1024,512]{1,0:T(8,128)} %param.4) | copy-start | bytes 6291460
  43.7 0.8 collective-permute-start.12
  44.6 1.4 collective-permute-start.13
  46.0 57.5 %collective-permute-start.14 = (f32[128,512]{1,0:T(8,128)S(1)}, f32[128,512]{1,0:T(8,128)}, u32[]{:S(2)}, u32[]{:S(2)}) collective-permute-start(f32[128,512]{1,0:T(8,128)S(1)} %broadcast_select_fusion.1), channel_id=1, source_target_pairs={{0,64},{4,68},{8,72},{12,76},{128,192},{132,196},{136,200},{140,20... | collective-permute-start | bytes 786440 | tf_op jit(solution)/shard_map/ppermute | solution.py:84
  104.5 4.6 %collective-permute-start.15 = (f32[128,512]{1,0:T(8,128)S(1)}, f32[128,512]{1,0:T(8,128)}, u32[]{:S(2)}, u32[]{:S(2)}) collective-permute-start(f32[128,512]{1,0:T(8,128)S(1)} %broadcast_select_fusion.2), channel_id=1, source_target_pairs={{0,32},{4,36},{8,40},{12,44},{64,96},{68,100},{72,104},{76,108},{1... | collective-permute-start | bytes 786440 | tf_op jit(solution)/shard_map/ppermute | solution.py:84
  109.2 4.6 %collective-permute-start.16 = (f32[128,512]{1,0:T(8,128)S(1)}, f32[128,512]{1,0:T(8,128)S(1)}, u32[]{:S(2)}, u32[]{:S(2)}) collective-permute-start(f32[128,512]{1,0:T(8,128)S(1)} %broadcast_select_fusion.3), channel_id=1, source_target_pairs={{0,16},{4,20},{8,24},{12,28},{32,48},{36,52},{40,56},{44,60},{64,8... | collective-permute-start | bytes 786440 | tf_op jit(solution)/shard_map/ppermute | solution.py:84
  113.8 17.2 %collective-permute-start.17 = (f32[128,512]{1,0:T(8,128)S(1)}, f32[128,512]{1,0:T(8,128)S(1)}, u32[]{:S(2)}, u32[]{:S(2)}) collective-permute-start(f32[128,512]{1,0:T(8,128)S(1)} %broadcast_select_fusion.4), channel_id=1, source_target_pairs={{0,8},{4,12},{8,0},{12,4},{16,24},{20,28},{24,16},{28,20},{32,40},... | collective-permute-start | bytes 786440 | tf_op jit(solution)/shard_map/ppermute | solution.py:90
  131.0 5.9 %collective-permute-start.18 = (f32[256,512]{1,0:T(8,128)S(1)}, f32[256,512]{1,0:T(8,128)S(1)}, u32[]{:S(2)}, u32[]{:S(2)}) collective-permute-start(f32[256,512]{1,0:T(8,128)S(1)} %maximum_select_fusion.5), channel_id=1, source_target_pairs={{0,4},{4,0},{8,12},{12,8},{16,20},{20,16},{24,28},{28,24},{32,36},... | collective-permute-start | bytes 1572872 | tf_op jit(solution)/shard_map/ppermute | solution.py:92
  (4 other events, 7.0 us)
Sparse Core Ops, SparseCore 0:
  142.1 54.9 reduce-scatter.1

commit v4 on v1

--- a/solution.py
+++ b/solution.py
@@ -56,10 +56,9 @@
         lower = lax.dynamic_index_in_dim(fetched, (col_at - k) % n_col, 0, keepdims=False)
         acc = acc + contract(arrived, lower)
 
-    pairs = [(at(j, c), at(c, j)) for j in range(steps) for c in range(n_col) if j != c]
-    piece = lax.ppermute(own, AXES, pairs)
-    piece = jnp.where(row_at == col_at, own, piece)
+    lower_all = lax.all_gather(factor, "pcol", axis=1, tiled=True)
 
+    piece = own
     span = n_row // 2
     while span >= steps:
         pairs = [(p, p + span) for p in range(n_row) if p % (2 * span) < steps]
@@ -70,15 +69,14 @@
     b0 = row_at % 2
     b1 = (row_at // 2) % 2
     other = lax.ppermute(piece, "prow", [(p, p ^ 2) for p in range(n_row)])
-    pair = jnp.where(b1 == 0, jnp.concatenate([piece, other]), jnp.concatenate([other, piece]))
+    pair = jnp.where(b1 == 0, jnp.concatenate([piece, other], axis=1), jnp.concatenate([other, piece], axis=1))
     theirs = lax.ppermute(pair, "prow", [(p, p ^ 1) for p in range(n_row)])
-    mine_first = jnp.concatenate([pair[:rhs_width], theirs[:rhs_width], pair[rhs_width:], theirs[rhs_width:]])
-    theirs_first = jnp.concatenate([theirs[:rhs_width], pair[:rhs_width], theirs[rhs_width:], pair[rhs_width:]])
+    mine, yours = (pair[:, :block], pair[:, block:]), (theirs[:, :block], theirs[:, block:])
+    mine_first = jnp.concatenate([mine[0], yours[0], mine[1], yours[1]], axis=1)
+    theirs_first = jnp.concatenate([yours[0], mine[0], yours[1], mine[1]], axis=1)
     panel = jnp.where(b0 == 0, mine_first, theirs_first)
 
-    updated = right_side - lax.psum_scatter(
-        contract(panel, factor), "pcol", scatter_dimension=0, tiled=True
-    )
+    updated = right_side - contract(panel, lower_all)
     head_block = jnp.where(row_at < steps, own, updated[:, :block])
     return jnp.concatenate([head_block, updated[:, block:]], axis=1)
 

time: 196 us -> 185 us (0.944)
  waiting for transfers between devices: 114 us -> 104 us
  starting transfers between devices: 34.5 us -> 29 us
  matrix products: 23 us -> 27.8 us
    reduce_scatter x1 -> x0, waiting for transfers between devices: 32.8 us -> none  [per_device(): lax.psum_scatter(contract(panel, factor), 'pcol', scatter_dimension=0, ti...]
    ppermute x4, waiting for transfers between devices: 75.7 us -> 98 us  [per_device(): arrived = lax.ppermute(piece, 'prow', pairs)]
    ppermute x1, starting transfers between devices: 17 us -> 12 us  [per_device(): other = lax.ppermute(piece, 'prow', [(p, p ^ 2) for p in range(n_row)])]
    dot_general x8, matrix products: 23 us -> 27.8 us  [contract(): lax.dot_general(left, right, (((1,), (1,)), ((), ())), precision=lax.Prec...]
  transfers between devices with their start and end apart: 17 -> 16, of which waited for: 6 -> 5; matrix products, arithmetic and copies ran while one was open for 3% -> 11% of each run, Pallas kernels for 0% -> 0%
where the time goes in v4:
time: 185 us; the launch traced here: 183 us
  waiting for transfers between devices  104 us (56%)
  starting transfers between devices  29 us (16%)
  matrix products  27.8 us (15%)
  between operations  13.8 us (7%)
  local copies, waits for them, and re-layouts  5.26 us (3%)
  other arithmetic  2.57 us (1%)
    ppermute x4, waiting for transfers between devices, per_device(): arrived = lax.ppermute(piece, 'prow', pairs)  98 us
    dot_general x8, matrix products, contract(): lax.dot_general(left, right, (((1,), (1,)), ((), ())), precision=lax.Prec...  27.8 us
    ppermute x1, starting transfers between devices, per_device(): other = lax.ppermute(piece, 'prow', [(p, p ^ 2) for p in range(n_row)])  12 us
    ppermute x6, starting transfers between devices, per_device(): arrived = arrived + lax.ppermute(solved, AXES, pairs)  4.76 us
    ppermute x4, starting transfers between devices, per_device(): arrived = lax.ppermute(piece, 'prow', pairs)  4.58 us
    ppermute x3, starting transfers between devices, per_device(): fetched.append(lax.ppermute(top_block, AXES, pairs))  4.12 us
    ppermute x1, waiting for transfers between devices, per_device(): other = lax.ppermute(piece, 'prow', [(p, p ^ 2) for p in range(n_row)])  4.07 us
    unnamed x8, local copies, waits for them, and re-layouts  3.72 us
  transfers between devices with their start and end apart: 16, of which 5 were waited for; matrix products, arithmetic and copies ran while one was open for 11% of the time, Pallas kernels for 0%

profile of v4, /device:TPU:7, one launch (start us, length us, event | category | flops | bytes accessed | tf_op | source)
XLA Modules:
  0.0 182.7 jit_solution(7184356342594075621)
XLA Ops:
  7.3 1.5 slice_bitcast_fusion
  9.5 1.7 collective-permute-start.4
  11.1 1.7 collective-permute-start.5
  12.9 2.4 %fusion.26 = f32[128,512]{1,0:T(8,128)S(1)} fusion(f32[2048,512]{1,0:T(8,128)} %param.5, f32[128,1024]{1,0:T(8,128)S(1)} %copy-done.1), kind=kOutput, calls=%fused_computation.32 | convolution fusion | flops 402653184 | bytes 1572864 | tf_op jit(solution)/shard_map/dot_general | solution.py:8
  17.6 1.4 collective-permute-start.2
  19.0 2.3 %pad_maximum_fusion = f32[4,512,512]{2,1,0:T(8,128)S(1)} fusion(f32[1,512,512]{2,1,0:T(8,128)} %bitcast.3, f32[1,512,512]{2,1,0:T(8,128)} %bitcast.2, f32[1,512,512]{2,1,0:T(8,128)} %bitcast.17, f32[1,512,512]{2,1,0:T(8,128)S(1)} %get-tuple-element.5), kind=kLoop, calls=%fused_computation | loop fusion | flops 3145728 | bytes 8388608 | tf_op jit(solution)/shard_map/stack | solution.py:43
  21.4 1.9 %copy-done = f32[4,512,512]{2,1,0:T(8,128)} copy-done((f32[4,512,512]{2,1,0:T(8,128)}, f32[4,512,512]{2,1,0:T(8,128)S(1)}, u32[]{:S(2)}) %copy-start) | copy-done | bytes 4194328
  23.3 2.1 %fusion.16 = f32[128,512]{1,0:T(8,128)S(1)} fusion(f32[4,512,512]{2,1,0:T(8,128)S(1)} %pad_maximum_fusion, s32[]{:T(128)S(6)} %select_n.128, f32[128,512]{1,0:T(8,128)} %collective-permute-done.2, f32[128,512]{1,0:T(8,128)S(1)} %collective-permute-done, f32[128,512]{1,0:T(8,128)S(1)} %collective-permute-done.1), kind=kOutput, calls=%fused_computation.22 | convolution fusion | flops 402784256 | bytes 2097156 | tf_op jit(solution)/shard_map/dot_general | solution.py:8
  25.4 2.5 %fusion.23 = f32[128,512]{1,0:T(8,128)S(1)} fusion(f32[2048,512]{1,0:T(8,128)} %param.5, f32[128,512]{1,0:T(8,128)S(1)} %fusion.16, f32[128,1024]{1,0:T(8,128)S(1)} %copy-done.1), kind=kOutput, calls=%fused_computation.29 | convolution fusion | flops 402718720 | bytes 1835008 | tf_op jit(solution)/shard_map/dot_general | solution.py:8
  29.4 2.5 %convolution_add_fusion.1 = f32[128,512]{1,0:T(8,128)S(1)} fusion(f32[128,512]{1,0:T(8,128)S(1)} %fusion.16, f32[4,512,512]{2,1,0:T(8,128)} %copy-done, s32[]{:T(128)S(6)} %select_n.130, f32[128,512]{1,0:T(8,128)S(1)} %collective-permute-done.6, f32[128,512]{1,0:T(8,128)S(1)} %collective-permute-done.7), kind=kOutput, calls=%fused_computation.5 | convolution fusion | flops 402784256 | bytes 2097156 | tf_op jit(solution)/shard_map/dot_general | solution.py:8
  31.9 2.4 %fusion.20 = f32[128,512]{1,0:T(8,128)S(1)} fusion(f32[2048,512]{1,0:T(8,128)} %param.5, f32[128,512]{1,0:T(8,128)S(1)} %convolution_add_fusion.1, f32[128,1024]{1,0:T(8,128)S(1)} %copy-done.1), kind=kOutput, calls=%fused_computation.26 | convolution fusion | flops 402718720 | bytes 1835008 | tf_op jit(solution)/shard_map/dot_general | solution.py:8
  35.0 2.4 %fusion = f32[128,512]{1,0:T(8,128)S(1)} fusion(f32[128,512]{1,0:T(8,128)S(1)} %convolution_add_fusion.1, f32[128,512]{1,0:T(8,128)S(1)} %collective-permute-done.8, f32[4,512,512]{2,1,0:T(8,128)} %copy-done, s32[]{:T(128)S(6)} %select_n.132, f32[128,1024]{1,0:T(8,128)S(1)} %copy-done.1), kind=kOutput, calls=%fused_computation.4 | convolution fusion | flops 402784256 | bytes 2097156 | tf_op jit(solution)/shard_map/dot_general | solution.py:8
  37.4 2.4 %convolution_select_fusion = f32[128,512]{1,0:T(8,128)S(1)} fusion(f32[128,512]{1,0:T(8,128)S(1)} %fusion, f32[2048,512]{1,0:T(8,128)} %param.5, f32[128,512]{1,0:T(8,128)S(1)} %fusion.20, f32[128,512]{1,0:T(8,128)S(1)} %fusion.23, f32[128,512]{1,0:T(8,128)S(1)} %fusion.26, pred[]{:T(512)S(6)} %eq.31, pred[]{:T(512)S(6)} %eq.30, pred[]{:T(512)S(6)} %eq.29, ...), kind=kOutput, calls=%fused_computation.2 | convolution fusion | flops 402915328 | bytes 2359300 | tf_op jit(solution)/shard_map/dot_general | solution.py:8
  40.6 1.3 collective-permute-start.10
  41.9 91.5 %collective-permute-done.10 = f32[128,512]{1,0:T(8,128)S(1)} collective-permute-done((f32[128,512]{1,0:T(8,128)S(1)}, f32[128,512]{1,0:T(8,128)S(1)}, u32[]{:S(2)}, u32[]{:S(2)}) %collective-permute-start.10) | collective-permute-done | bytes 262176 | tf_op jit(solution)/shard_map/ppermute | solution.py:65
  133.4 1.3 collective-permute-start.11
  134.8 3.3 %collective-permute-done.11 = f32[128,512]{1,0:T(8,128)S(1)} collective-permute-done((f32[128,512]{1,0:T(8,128)S(1)}, f32[128,512]{1,0:T(8,128)S(1)}, u32[]{:S(2)}, u32[]{:S(2)}) %collective-permute-start.11) | collective-permute-done | bytes 262176 | tf_op jit(solution)/shard_map/ppermute | solution.py:65
  138.1 1.3 collective-permute-start.12
  139.4 3.3 %collective-permute-done.12 = f32[128,512]{1,0:T(8,128)S(1)} collective-permute-done((f32[128,512]{1,0:T(8,128)S(1)}, f32[128,512]{1,0:T(8,128)S(1)}, u32[]{:S(2)}, u32[]{:S(2)}) %collective-permute-start.12) | collective-permute-done | bytes 262176 | tf_op jit(solution)/shard_map/ppermute | solution.py:65
  142.7 12.0 %collective-permute-start.13 = (f32[128,512]{1,0:T(8,128)S(1)}, f32[128,512]{1,0:T(8,128)S(1)}, u32[]{:S(2)}, u32[]{:S(2)}) collective-permute-start(f32[128,512]{1,0:T(8,128)S(1)} %broadcast_select_fusion.3), channel_id=1, source_target_pairs={{0,8},{4,12},{8,0},{12,4},{16,24},{20,28},{24,16},{28,20},{32,40},... | collective-permute-start | bytes 786440 | tf_op jit(solution)/shard_map/ppermute | solution.py:71
  154.7 4.1 %collective-permute-done.13 = f32[128,512]{1,0:T(8,128)S(1)} collective-permute-done((f32[128,512]{1,0:T(8,128)S(1)}, f32[128,512]{1,0:T(8,128)S(1)}, u32[]{:S(2)}, u32[]{:S(2)}) %collective-permute-start.13) | collective-permute-done | bytes 262176 | tf_op jit(solution)/shard_map/ppermute | solution.py:71
  158.9 3.5 %collective-permute-start.14 = (f32[128,1024]{1,0:T(8,128)S(1)}, f32[128,1024]{1,0:T(8,128)S(1)}, u32[]{:S(2)}, u32[]{:S(2)}) collective-permute-start(f32[128,1024]{1,0:T(8,128)S(1)} %maximum_select_fusion.2), channel_id=1, source_target_pairs={{0,4},{4,0},{8,12},{12,8},{16,20},{20,16},{24,28},{28,24},{32,36},... | collective-permute-start | bytes 1572872 | tf_op jit(solution)/shard_map/ppermute | solution.py:73
  162.4 1.5 collective-permute-done.14
  163.9 11.1 %convolution_subtract_fusion = f32[128,1024]{1,0:T(8,128)S(1)} fusion(f32[128,1024]{1,0:T(8,128)S(1)} %copy-done.1, f32[1024,2048]{1,0:T(8,128)} %all-gather.2.cloned.1.call-done, f32[128,512]{1,0:T(8,128)S(1)} %get-tuple-element.12, f32[128,512]{1,0:T(8,128)S(1)} %get-tuple-element.10, f32[128,512]{1,0:T(8,128)S(1)} %get-tuple-element.11, ...), kind=kOutput, calls=%fused_computation.1 | convolution fusion | flops 3223191552 | bytes 10485761 | tf_op jit(solution)/shard_map/dot_general | solution.py:8
  (36 shorter events, 7.7 us)
Async XLA Ops:
  6.5 6.3 %copy-start.1 = (f32[128,1024]{1,0:T(8,128)S(1)}, f32[128,1024]{1,0:T(8,128)}, u32[]{:S(2)}) copy-start(f32[128,1024]{1,0:T(8,128)} %param.3) | copy-start | bytes 1572868
  6.5 157.4 %all-gather.2.cloned.1.call-start = ((), (), s32[]{:S(2)}) async-start(), calls=%async_computation | async-start | bytes 10485760 | tf_op jit(solution)/shard_map/all_gather | solution.py:59
  8.7 7.9 %collective-permute-start.3 = (f32[512,512]{1,0:T(8,128)S(1)}, f32[512,512]{1,0:T(8,128)S(1)}, u32[]{:S(2)}, u32[]{:S(2)}) collective-permute-start(f32[512,512]{1,0:T(8,128)S(1)} %get-tuple-element.6), channel_id=1, source_target_pairs={{4,5},{8,9},{9,10},{12,13},{13,14},{14,15}} | collective-permute-start | bytes 3145736 | tf_op jit(solution)/shard_map/ppermute | solution.py:42
  9.5 9.5 %collective-permute-start.4 = (f32[512,512]{1,0:T(8,128)S(1)}, f32[512,512]{1,0:T(8,128)}, u32[]{:S(2)}, u32[]{:S(2)}) collective-permute-start(f32[512,512]{1,0:T(8,128)S(1)} %get-tuple-element.6), channel_id=1, source_target_pairs={{4,6},{8,10},{9,11},{12,14},{13,15},{14,12}} | collective-permute-start | bytes 3145736 | tf_op jit(solution)/shard_map/ppermute | solution.py:42
  11.1 7.9 %collective-permute-start.5 = (f32[512,512]{1,0:T(8,128)S(1)}, f32[512,512]{1,0:T(8,128)}, u32[]{:S(2)}, u32[]{:S(2)}) collective-permute-start(f32[512,512]{1,0:T(8,128)S(1)} %get-tuple-element.6), channel_id=1, source_target_pairs={{4,7},{8,11},{9,8},{12,15},{13,12},{14,13}} | collective-permute-start | bytes 3145736 | tf_op jit(solution)/shard_map/ppermute | solution.py:42
  15.3 6.1 %collective-permute-start = (f32[128,512]{1,0:T(8,128)S(1)}, f32[128,512]{1,0:T(8,128)S(1)}, u32[]{:S(2)}, u32[]{:S(2)}) collective-permute-start(f32[128,512]{1,0:T(8,128)S(1)} %fusion.26), channel_id=1, source_target_pairs={{0,4},{1,5},{2,6},{3,7}} | collective-permute-start | bytes 786440 | tf_op jit(solution)/shard_map/ppermute | solution.py:55
  16.0 5.4 %collective-permute-start.1 = (f32[128,512]{1,0:T(8,128)S(1)}, f32[128,512]{1,0:T(8,128)S(1)}, u32[]{:S(2)}, u32[]{:S(2)}) collective-permute-start(f32[128,512]{1,0:T(8,128)S(1)} %fusion.26), channel_id=1, source_target_pairs={{0,8},{1,9},{2,10},{3,11}} | collective-permute-start | bytes 786440 | tf_op jit(solution)/shard_map/ppermute | solution.py:55
  16.6 1.0 copy-start.2
  17.6 3.7 %collective-permute-start.2 = (f32[128,512]{1,0:T(8,128)S(1)}, f32[128,512]{1,0:T(8,128)}, u32[]{:S(2)}, u32[]{:S(2)}) collective-permute-start(f32[128,512]{1,0:T(8,128)S(1)} %fusion.26), channel_id=1, source_target_pairs={{0,12},{1,13},{2,14},{3,15}} | collective-permute-start | bytes 786440 | tf_op jit(solution)/shard_map/ppermute | solution.py:55
  21.3 2.0 %copy-start = (f32[4,512,512]{2,1,0:T(8,128)}, f32[4,512,512]{2,1,0:T(8,128)S(1)}, u32[]{:S(2)}) copy-start(f32[4,512,512]{2,1,0:T(8,128)S(1)} %pad_maximum_fusion) | copy-start | bytes 12582916
  28.0 1.4 collective-permute-start.6
  28.7 0.7 collective-permute-start.7
  34.3 0.7 collective-permute-start.8
  39.8 0.7 collective-permute-start.9
  40.6 92.8 %collective-permute-start.10 = (f32[128,512]{1,0:T(8,128)S(1)}, f32[128,512]{1,0:T(8,128)S(1)}, u32[]{:S(2)}, u32[]{:S(2)}) collective-permute-start(f32[128,512]{1,0:T(8,128)S(1)} %broadcast_select_fusion), channel_id=1, source_target_pairs={{0,64},{4,68},{8,72},{12,76},{128,192},{132,196},{136,200},{140,20... | collective-permute-start | bytes 786440 | tf_op jit(solution)/shard_map/ppermute | solution.py:65
  133.4 4.6 %collective-permute-start.11 = (f32[128,512]{1,0:T(8,128)S(1)}, f32[128,512]{1,0:T(8,128)S(1)}, u32[]{:S(2)}, u32[]{:S(2)}) collective-permute-start(f32[128,512]{1,0:T(8,128)S(1)} %broadcast_select_fusion.1), channel_id=1, source_target_pairs={{0,32},{4,36},{8,40},{12,44},{64,96},{68,100},{72,104},{76,108},{1... | collective-permute-start | bytes 786440 | tf_op jit(solution)/shard_map/ppermute | solution.py:65
  138.1 4.6 %collective-permute-start.12 = (f32[128,512]{1,0:T(8,128)S(1)}, f32[128,512]{1,0:T(8,128)S(1)}, u32[]{:S(2)}, u32[]{:S(2)}) collective-permute-start(f32[128,512]{1,0:T(8,128)S(1)} %broadcast_select_fusion.2), channel_id=1, source_target_pairs={{0,16},{4,20},{8,24},{12,28},{32,48},{36,52},{40,56},{44,60},{64,8... | collective-permute-start | bytes 786440 | tf_op jit(solution)/shard_map/ppermute | solution.py:65
  142.7 16.1 %collective-permute-start.13 = (f32[128,512]{1,0:T(8,128)S(1)}, f32[128,512]{1,0:T(8,128)S(1)}, u32[]{:S(2)}, u32[]{:S(2)}) collective-permute-start(f32[128,512]{1,0:T(8,128)S(1)} %broadcast_select_fusion.3), channel_id=1, source_target_pairs={{0,8},{4,12},{8,0},{12,4},{16,24},{20,28},{24,16},{28,20},{32,40},... | collective-permute-start | bytes 786440 | tf_op jit(solution)/shard_map/ppermute | solution.py:71
  158.9 5.0 %collective-permute-start.14 = (f32[128,1024]{1,0:T(8,128)S(1)}, f32[128,1024]{1,0:T(8,128)S(1)}, u32[]{:S(2)}, u32[]{:S(2)}) collective-permute-start(f32[128,1024]{1,0:T(8,128)S(1)} %maximum_select_fusion.2), channel_id=1, source_target_pairs={{0,4},{4,0},{8,12},{12,8},{16,20},{20,16},{24,28},{28,24},{32,36},... | collective-permute-start | bytes 1572872 | tf_op jit(solution)/shard_map/ppermute | solution.py:73
  175.1 0.8 copy-start.3
Sparse Core Ops, SparseCore 0:
  9.2 88.5 all-gather.1

commit v5 on v4

--- a/solution.py
+++ b/solution.py
@@ -56,7 +56,8 @@
         lower = lax.dynamic_index_in_dim(fetched, (col_at - k) % n_col, 0, keepdims=False)
         acc = acc + contract(arrived, lower)
 
-    lower_all = lax.all_gather(factor, "pcol", axis=1, tiled=True)
+    factor_later, _ = lax.optimization_barrier((factor, fetched))
+    lower_all = lax.all_gather(factor_later, "pcol", axis=1, tiled=True)
 
     piece = own
     span = n_row // 2

time: 185 us -> 164 us (0.89)
  waiting for transfers between devices: 104 us -> 92.3 us
  starting transfers between devices: 29 us -> 23.2 us
  local copies, waits for them, and re-layouts: 5.26 us -> 2.34 us
    ppermute x4, waiting for transfers between devices: 98 us -> 85.3 us  [per_device(): arrived = lax.ppermute(piece, 'prow', pairs)]
    unnamed x8 -> x4, local copies, waits for them, and re-layouts: 3.72 us -> 0.79 us
    ppermute x1, starting transfers between devices: 12 us -> 9.24 us  [per_device(): other = lax.ppermute(piece, 'prow', [(p, p ^ 2) for p in range(n_row)])]
    ppermute x3, starting transfers between devices: 4.12 us -> 2.18 us  [per_device(): fetched.append(lax.ppermute(top_block, AXES, pairs))]
  transfers between devices with their start and end apart: 16 -> 16, of which waited for: 5 -> 6; matrix products, arithmetic and copies ran while one was open for 11% -> 10% of each run, Pallas kernels for 0% -> 0%
where the time goes in v5:
time: 164 us; the launch traced here: 162 us
  waiting for transfers between devices  92.3 us (56%)
  matrix products  27.7 us (17%)
  starting transfers between devices  23.2 us (14%)
  between operations  13.9 us (8%)
  other arithmetic  2.69 us (2%)
  local copies, waits for them, and re-layouts  2.34 us (1%)
    ppermute x4, waiting for transfers between devices, per_device(): arrived = lax.ppermute(piece, 'prow', pairs)  85.3 us
    dot_general x8, matrix products, contract(): lax.dot_general(left, right, (((1,), (1,)), ((), ())), precision=lax.Prec...  27.7 us
    ppermute x1, starting transfers between devices, per_device(): other = lax.ppermute(piece, 'prow', [(p, p ^ 2) for p in range(n_row)])  9.24 us
    ppermute x4, starting transfers between devices, per_device(): arrived = lax.ppermute(piece, 'prow', pairs)  4.58 us
    ppermute x1, waiting for transfers between devices, per_device(): other = lax.ppermute(piece, 'prow', [(p, p ^ 2) for p in range(n_row)])  4.4 us
    ppermute x6, starting transfers between devices, per_device(): arrived = arrived + lax.ppermute(solved, AXES, pairs)  4.06 us
  transfers between devices with their start and end apart: 16, of which 6 were waited for; matrix products, arithmetic and copies ran while one was open for 10% of the time, Pallas kernels for 0%

profile of v5, /device:TPU:7, one launch (start us, length us, event | category | flops | bytes accessed | tf_op | source)
XLA Modules:
  0.0 162.1 jit_solution(5844528592411442234)
XLA Ops:
  6.5 1.5 slice_bitcast_fusion
  8.0 0.7 collective-permute-start.3
  8.8 0.7 collective-permute-start.4
  10.3 2.4 %pad_maximum_fusion = f32[4,512,512]{2,1,0:T(8,128)} fusion(f32[1,512,512]{2,1,0:T(8,128)S(1)} %bitcast.19, f32[1,512,512]{2,1,0:T(8,128)S(1)} %bitcast.18, f32[1,512,512]{2,1,0:T(8,128)S(1)} %bitcast.17, f32[1,512,512]{2,1,0:T(8,128)S(1)} %get-tuple-element.7), kind=kLoop, calls=%fused_computation | loop fusion | flops 3145728 | bytes 8388608 | tf_op jit(solution)/shard_map/stack | solution.py:43
  12.7 2.4 %fusion.26 = f32[128,512]{1,0:T(8,128)S(1)} fusion(f32[2048,512]{1,0:T(8,128)} %param.5, f32[128,1024]{1,0:T(8,128)S(1)} %copy-done), kind=kOutput, calls=%fused_computation.32 | convolution fusion | flops 402653184 | bytes 1572864 | tf_op jit(solution)/shard_map/dot_general | solution.py:8
  17.2 2.4 %fusion.16 = f32[128,512]{1,0:T(8,128)S(1)} fusion(f32[4,512,512]{2,1,0:T(8,128)} %pad_maximum_fusion, s32[]{:T(128)S(6)} %select_n.128, f32[128,512]{1,0:T(8,128)S(1)} %collective-permute-done.2, f32[128,512]{1,0:T(8,128)S(1)} %collective-permute-done, f32[128,512]{1,0:T(8,128)S(1)} %collective-permute-done.1), kind=kOutput, calls=%fused_computation.22 | convolution fusion | flops 402784256 | bytes 2097156 | tf_op jit(solution)/shard_map/dot_general | solution.py:8
  19.6 2.4 %fusion.23 = f32[128,512]{1,0:T(8,128)S(1)} fusion(f32[2048,512]{1,0:T(8,128)} %param.5, f32[128,512]{1,0:T(8,128)S(1)} %fusion.16, f32[128,1024]{1,0:T(8,128)S(1)} %copy-done), kind=kOutput, calls=%fused_computation.29 | convolution fusion | flops 402718720 | bytes 1835008 | tf_op jit(solution)/shard_map/dot_general | solution.py:8
  23.4 2.4 %convolution_add_fusion.1 = f32[128,512]{1,0:T(8,128)S(1)} fusion(f32[128,512]{1,0:T(8,128)S(1)} %fusion.16, f32[4,512,512]{2,1,0:T(8,128)} %pad_maximum_fusion, s32[]{:T(128)S(6)} %select_n.130, f32[128,512]{1,0:T(8,128)S(1)} %collective-permute-done.6, f32[128,512]{1,0:T(8,128)S(1)} %collective-permute-done.7), kind=kOutput, calls=%fused_computation.5 | convolution fusion | flops 402784256 | bytes 2097156 | tf_op jit(solution)/shard_map/dot_general | solution.py:8
  25.8 2.4 %fusion.20 = f32[128,512]{1,0:T(8,128)S(1)} fusion(f32[2048,512]{1,0:T(8,128)} %param.5, f32[128,512]{1,0:T(8,128)S(1)} %convolution_add_fusion.1, f32[128,1024]{1,0:T(8,128)S(1)} %copy-done), kind=kOutput, calls=%fused_computation.26 | convolution fusion | flops 402718720 | bytes 1835008 | tf_op jit(solution)/shard_map/dot_general | solution.py:8
  28.9 2.4 %fusion = f32[128,512]{1,0:T(8,128)S(1)} fusion(f32[128,512]{1,0:T(8,128)S(1)} %convolution_add_fusion.1, f32[128,512]{1,0:T(8,128)S(1)} %collective-permute-done.8, f32[4,512,512]{2,1,0:T(8,128)} %pad_maximum_fusion, s32[]{:T(128)S(6)} %select_n.132, f32[128,1024]{1,0:T(8,128)S(1)} %copy-done), kind=kOutput, calls=%fused_computation.4 | convolution fusion | flops 402784256 | bytes 2097156 | tf_op jit(solution)/shard_map/dot_general | solution.py:8
  31.3 2.4 %convolution_select_fusion = f32[128,512]{1,0:T(8,128)S(1)} fusion(f32[128,512]{1,0:T(8,128)S(1)} %fusion, f32[2048,512]{1,0:T(8,128)} %param.5, f32[128,512]{1,0:T(8,128)S(1)} %fusion.20, f32[128,512]{1,0:T(8,128)S(1)} %fusion.23, f32[128,512]{1,0:T(8,128)S(1)} %fusion.26, pred[]{:T(512)S(6)} %eq.31, pred[]{:T(512)S(6)} %eq.30, pred[]{:T(512)S(6)} %eq.29, ...), kind=kOutput, calls=%fused_computation.2 | convolution fusion | flops 402915328 | bytes 2359300 | tf_op jit(solution)/shard_map/dot_general | solution.py:8
  34.5 1.3 collective-permute-start.10
  35.8 77.9 %collective-permute-done.10 = f32[128,512]{1,0:T(8,128)S(1)} collective-permute-done((f32[128,512]{1,0:T(8,128)S(1)}, f32[128,512]{1,0:T(8,128)S(1)}, u32[]{:S(2)}, u32[]{:S(2)}) %collective-permute-start.10) | collective-permute-done | bytes 262176 | tf_op jit(solution)/shard_map/ppermute | solution.py:66
  113.7 1.3 collective-permute-start.11
  115.0 4.2 %collective-permute-done.11 = f32[128,512]{1,0:T(8,128)S(1)} collective-permute-done((f32[128,512]{1,0:T(8,128)S(1)}, f32[128,512]{1,0:T(8,128)S(1)}, u32[]{:S(2)}, u32[]{:S(2)}) %collective-permute-start.11) | collective-permute-done | bytes 262176 | tf_op jit(solution)/shard_map/ppermute | solution.py:66
  119.3 1.3 collective-permute-start.12
  120.6 3.3 %collective-permute-done.12 = f32[128,512]{1,0:T(8,128)S(1)} collective-permute-done((f32[128,512]{1,0:T(8,128)S(1)}, f32[128,512]{1,0:T(8,128)S(1)}, u32[]{:S(2)}, u32[]{:S(2)}) %collective-permute-start.12) | collective-permute-done | bytes 262176 | tf_op jit(solution)/shard_map/ppermute | solution.py:66
  123.9 9.2 %collective-permute-start.13 = (f32[128,512]{1,0:T(8,128)S(1)}, f32[128,512]{1,0:T(8,128)S(1)}, u32[]{:S(2)}, u32[]{:S(2)}) collective-permute-start(f32[128,512]{1,0:T(8,128)S(1)} %broadcast_select_fusion.3), channel_id=1, source_target_pairs={{0,8},{4,12},{8,0},{12,4},{16,24},{20,28},{24,16},{28,20},{32,40},... | collective-permute-start | bytes 786440 | tf_op jit(solution)/shard_map/ppermute | solution.py:72
  133.2 4.4 %collective-permute-done.13 = f32[128,512]{1,0:T(8,128)S(1)} collective-permute-done((f32[128,512]{1,0:T(8,128)S(1)}, f32[128,512]{1,0:T(8,128)S(1)}, u32[]{:S(2)}, u32[]{:S(2)}) %collective-permute-start.13) | collective-permute-done | bytes 262176 | tf_op jit(solution)/shard_map/ppermute | solution.py:72
  137.6 3.1 %collective-permute-start.14 = (f32[128,1024]{1,0:T(8,128)S(1)}, f32[128,1024]{1,0:T(8,128)S(1)}, u32[]{:S(2)}, u32[]{:S(2)}) collective-permute-start(f32[128,1024]{1,0:T(8,128)S(1)} %maximum_select_fusion.2), channel_id=1, source_target_pairs={{0,4},{4,0},{8,12},{12,8},{16,20},{20,16},{24,28},{28,24},{32,36},... | collective-permute-start | bytes 1572872 | tf_op jit(solution)/shard_map/ppermute | solution.py:74
  140.8 1.5 collective-permute-done.14
  142.3 1.0 all-gather.2.cloned.1.call-done
  143.3 11.0 %convolution_subtract_fusion = f32[128,1024]{1,0:T(8,128)S(1)} fusion(f32[128,1024]{1,0:T(8,128)S(1)} %copy-done, f32[1024,2048]{1,0:T(8,128)} %all-gather.2.cloned.1.call-done, f32[128,512]{1,0:T(8,128)S(1)} %get-tuple-element.14, f32[128,512]{1,0:T(8,128)S(1)} %get-tuple-element.12, f32[128,512]{1,0:T(8,128)S(1)} %get-tuple-element.13, ...), kind=kOutput, calls=%fused_computation.1 | convolution fusion | flops 3223191552 | bytes 10485761 | tf_op jit(solution)/shard_map/dot_general | solution.py:8
  154.5 0.8 copy-done.1
  (32 shorter events, 5.9 us)
Async XLA Ops:
  6.5 136.8 %all-gather.2.cloned.1.call-start = ((), (), s32[]{:S(2)}) async-start(), calls=%async_computation | async-start | bytes 10485760 | tf_op jit(solution)/shard_map/all_gather | solution.py:60
  8.0 2.2 %collective-permute-start.3 = (f32[512,512]{1,0:T(8,128)S(1)}, f32[512,512]{1,0:T(8,128)S(1)}, u32[]{:S(2)}, u32[]{:S(2)}) collective-permute-start(f32[512,512]{1,0:T(8,128)S(1)} %get-tuple-element.8), channel_id=1, source_target_pairs={{4,5},{8,9},{9,10},{12,13},{13,14},{14,15}} | collective-permute-start | bytes 3145736 | tf_op jit(solution)/shard_map/ppermute | solution.py:42
  8.8 1.5 collective-permute-start.4
  9.5 0.8 collective-permute-start.5
  10.3 2.5 %copy-start = (f32[128,1024]{1,0:T(8,128)S(1)}, f32[128,1024]{1,0:T(8,128)}, u32[]{:S(2)}) copy-start(f32[128,1024]{1,0:T(8,128)} %param.3) | copy-start | bytes 1572868
  15.1 2.1 %collective-permute-start = (f32[128,512]{1,0:T(8,128)S(1)}, f32[128,512]{1,0:T(8,128)S(1)}, u32[]{:S(2)}, u32[]{:S(2)}) collective-permute-start(f32[128,512]{1,0:T(8,128)S(1)} %fusion.26), channel_id=1, source_target_pairs={{0,4},{1,5},{2,6},{3,7}} | collective-permute-start | bytes 786440 | tf_op jit(solution)/shard_map/ppermute | solution.py:55
  15.8 1.4 collective-permute-start.1
  16.5 0.7 collective-permute-start.2
  22.0 1.4 collective-permute-start.6
  22.7 0.7 collective-permute-start.7
  28.2 0.7 collective-permute-start.8
  33.7 0.7 collective-permute-start.9
  34.5 79.2 %collective-permute-start.10 = (f32[128,512]{1,0:T(8,128)S(1)}, f32[128,512]{1,0:T(8,128)S(1)}, u32[]{:S(2)}, u32[]{:S(2)}) collective-permute-start(f32[128,512]{1,0:T(8,128)S(1)} %broadcast_select_fusion), channel_id=1, source_target_pairs={{0,64},{4,68},{8,72},{12,76},{128,192},{132,196},{136,200},{140,20... | collective-permute-start | bytes 786440 | tf_op jit(solution)/shard_map/ppermute | solution.py:66
  113.7 5.5 %collective-permute-start.11 = (f32[128,512]{1,0:T(8,128)S(1)}, f32[128,512]{1,0:T(8,128)S(1)}, u32[]{:S(2)}, u32[]{:S(2)}) collective-permute-start(f32[128,512]{1,0:T(8,128)S(1)} %broadcast_select_fusion.1), channel_id=1, source_target_pairs={{0,32},{4,36},{8,40},{12,44},{64,96},{68,100},{72,104},{76,108},{1... | collective-permute-start | bytes 786440 | tf_op jit(solution)/shard_map/ppermute | solution.py:66
  119.3 4.6 %collective-permute-start.12 = (f32[128,512]{1,0:T(8,128)S(1)}, f32[128,512]{1,0:T(8,128)S(1)}, u32[]{:S(2)}, u32[]{:S(2)}) collective-permute-start(f32[128,512]{1,0:T(8,128)S(1)} %broadcast_select_fusion.2), channel_id=1, source_target_pairs={{0,16},{4,20},{8,24},{12,28},{32,48},{36,52},{40,56},{44,60},{64,8... | collective-permute-start | bytes 786440 | tf_op jit(solution)/shard_map/ppermute | solution.py:66
  123.9 13.6 %collective-permute-start.13 = (f32[128,512]{1,0:T(8,128)S(1)}, f32[128,512]{1,0:T(8,128)S(1)}, u32[]{:S(2)}, u32[]{:S(2)}) collective-permute-start(f32[128,512]{1,0:T(8,128)S(1)} %broadcast_select_fusion.3), channel_id=1, source_target_pairs={{0,8},{4,12},{8,0},{12,4},{16,24},{20,28},{24,16},{28,20},{32,40},... | collective-permute-start | bytes 786440 | tf_op jit(solution)/shard_map/ppermute | solution.py:72
  137.6 4.7 %collective-permute-start.14 = (f32[128,1024]{1,0:T(8,128)S(1)}, f32[128,1024]{1,0:T(8,128)S(1)}, u32[]{:S(2)}, u32[]{:S(2)}) collective-permute-start(f32[128,1024]{1,0:T(8,128)S(1)} %maximum_select_fusion.2), channel_id=1, source_target_pairs={{0,4},{4,0},{8,12},{12,8},{16,20},{20,16},{24,28},{28,24},{32,36},... | collective-permute-start | bytes 1572872 | tf_op jit(solution)/shard_map/ppermute | solution.py:74
  154.5 0.8 copy-start.1
Sparse Core Ops, SparseCore 0:
  12.8 130.4 all-gather.1

commit v6 on v5

--- a/solution.py
+++ b/solution.py
@@ -4,12 +4,12 @@
 from jax.sharding import PartitionSpec as P
 
 
-def contract(left, right):
+def contract(left, right, precision=lax.Precision.HIGHEST):
     return lax.dot_general(
         left,
         right,
         (((1,), (1,)), ((), ())),
-        precision=lax.Precision.HIGHEST,
+        precision=precision,
         preferred_element_type=jnp.float32,
     )
 
@@ -57,7 +57,8 @@
         acc = acc + contract(arrived, lower)
 
     factor_later, _ = lax.optimization_barrier((factor, fetched))
-    lower_all = lax.all_gather(factor_later, "pcol", axis=1, tiled=True)
+    lower_second = lax.all_gather(factor_later[block:], "pcol", axis=1, tiled=True)
+    lower_first = lax.all_gather(factor_later[:block], "pcol", axis=1, tiled=True)
 
     piece = own
     span = n_row // 2
@@ -77,9 +78,10 @@
     theirs_first = jnp.concatenate([yours[0], mine[0], yours[1], mine[1]], axis=1)
     panel = jnp.where(b0 == 0, mine_first, theirs_first)
 
-    updated = right_side - contract(panel, lower_all)
-    head_block = jnp.where(row_at < steps, own, updated[:, :block])
-    return jnp.concatenate([head_block, updated[:, block:]], axis=1)
+    second = right_side[:, block:] - contract(panel, lower_second, lax.Precision.HIGH)
+    first = right_side[:, :block] - contract(panel, lower_first, lax.Precision.HIGH)
+    head_block = jnp.where(row_at < steps, own, first)
+    return jnp.concatenate([head_block, second], axis=1)
 
 
 def solution(mesh):

time: 164 us -> 177 us (1.079)
  waiting for transfers between devices: 92.3 us -> 106 us
  matrix products: 27.7 us -> 25.5 us
    all_gather x1 -> x2, waiting for transfers between devices: 1.03 us -> 14.7 us  [the longest x1 14.7 us: per_device(): lax.all_gather(factor_later[:block], 'pcol', axis=1, tiled=True)]
    dot_general x8 -> x9, matrix products: 27.7 us -> 25.5 us  [contract(): lax.dot_general(left, right, (((1,), (1,)), ((), ())), precision=precisio...]
  transfers between devices with their start and end apart: 16 -> 17, of which waited for: 6 -> 6; matrix products, arithmetic and copies ran while one was open for 10% -> 12% of each run, Pallas kernels for 0% -> 0%
where the time goes in v6:
time: 177 us; the launch traced here: 175 us
  waiting for transfers between devices  106 us (60%)
  matrix products  25.5 us (14%)
  starting transfers between devices  22.7 us (13%)
  between operations  13.9 us (8%)
  other arithmetic  3.49 us (2%)
  local copies, waits for them, and re-layouts  3.03 us (2%)
    ppermute x4, waiting for transfers between devices, per_device(): arrived = lax.ppermute(piece, 'prow', pairs)  85.3 us
    dot_general x9, matrix products, contract(): lax.dot_general(left, right, (((1,), (1,)), ((), ())), precision=precisio...  25.5 us
    all_gather x1, waiting for transfers between devices, per_device(): lax.all_gather(factor_later[:block], 'pcol', axis=1, tiled=True)  14.7 us
    ppermute x1, starting transfers between devices, per_device(): other = lax.ppermute(piece, 'prow', [(p, p ^ 2) for p in range(n_row)])  8.51 us
    ppermute x4, starting transfers between devices, per_device(): arrived = lax.ppermute(piece, 'prow', pairs)  4.58 us
    ppermute x1, waiting for transfers between devices, per_device(): other = lax.ppermute(piece, 'prow', [(p, p ^ 2) for p in range(n_row)])  4.17 us
    ppermute x6, starting transfers between devices, per_device(): arrived = arrived + lax.ppermute(solved, AXES, pairs)  4.06 us
  transfers between devices with their start and end apart: 17, of which 6 were waited for; matrix products, arithmetic and copies ran while one was open for 12% of the time, Pallas kernels for 0%

profile of v6, /device:TPU:7, one launch (start us, length us, event | category | flops | bytes accessed | tf_op | source)
XLA Modules:
  0.0 175.1 jit_solution(7523769655790140576)
XLA Ops:
  6.5 1.5 slice_bitcast_fusion
  10.3 2.5 %pad_maximum_fusion = f32[4,512,512]{2,1,0:T(8,128)} fusion(f32[1,512,512]{2,1,0:T(8,128)S(1)} %bitcast.20, f32[1,512,512]{2,1,0:T(8,128)S(1)} %bitcast.19, f32[1,512,512]{2,1,0:T(8,128)S(1)} %bitcast.18, f32[1,512,512]{2,1,0:T(8,128)S(1)} %get-tuple-element.9), kind=kLoop, calls=%fused_computation | loop fusion | flops 3145728 | bytes 8388608 | tf_op jit(solution)/shard_map/stack | solution.py:43
  12.7 1.5 fusion.29
  15.0 2.4 %fusion.14 = f32[128,512]{1,0:T(8,128)S(1)} fusion(f32[2048,512]{1,0:T(8,128)} %param.5, f32[128,1024]{1,0:T(8,128)S(1)} %copy-done), kind=kOutput, calls=%fused_computation.21 | convolution fusion | flops 402653184 | bytes 1572864 | tf_op jit(solution)/shard_map/dot_general | solution.py:8
  19.5 2.4 %fusion.4 = f32[128,512]{1,0:T(8,128)S(1)} fusion(f32[4,512,512]{2,1,0:T(8,128)} %pad_maximum_fusion, s32[]{:T(128)S(6)} %select_n.128, f32[128,512]{1,0:T(8,128)S(1)} %collective-permute-done.2, f32[128,512]{1,0:T(8,128)S(1)} %collective-permute-done, f32[128,512]{1,0:T(8,128)S(1)} %collective-permute-done.1), kind=kOutput, calls=%fused_computation.11 | convolution fusion | flops 402784256 | bytes 2097156 | tf_op jit(solution)/shard_map/dot_general | solution.py:8
  21.9 2.4 %fusion.11 = f32[128,512]{1,0:T(8,128)S(1)} fusion(f32[2048,512]{1,0:T(8,128)} %param.5, f32[128,512]{1,0:T(8,128)S(1)} %fusion.4, f32[128,1024]{1,0:T(8,128)S(1)} %copy-done), kind=kOutput, calls=%fused_computation.18 | convolution fusion | flops 402718720 | bytes 1835008 | tf_op jit(solution)/shard_map/dot_general | solution.py:8
  25.7 2.4 %convolution_add_fusion.1 = f32[128,512]{1,0:T(8,128)S(1)} fusion(f32[128,512]{1,0:T(8,128)S(1)} %fusion.4, f32[4,512,512]{2,1,0:T(8,128)} %pad_maximum_fusion, s32[]{:T(128)S(6)} %select_n.130, f32[128,512]{1,0:T(8,128)S(1)} %collective-permute-done.6, f32[128,512]{1,0:T(8,128)S(1)} %collective-permute-done.7), kind=kOutput, calls=%fused_computation.7 | convolution fusion | flops 402784256 | bytes 2097156 | tf_op jit(solution)/shard_map/dot_general | solution.py:8
  28.1 2.4 %fusion.8 = f32[128,512]{1,0:T(8,128)S(1)} fusion(f32[2048,512]{1,0:T(8,128)} %param.5, f32[128,512]{1,0:T(8,128)S(1)} %convolution_add_fusion.1, f32[128,1024]{1,0:T(8,128)S(1)} %copy-done), kind=kOutput, calls=%fused_computation.15 | convolution fusion | flops 402718720 | bytes 1835008 | tf_op jit(solution)/shard_map/dot_general | solution.py:8
  31.2 2.4 %fusion.1 = f32[128,512]{1,0:T(8,128)S(1)} fusion(f32[128,512]{1,0:T(8,128)S(1)} %convolution_add_fusion.1, f32[128,512]{1,0:T(8,128)S(1)} %collective-permute-done.8, f32[4,512,512]{2,1,0:T(8,128)} %pad_maximum_fusion, s32[]{:T(128)S(6)} %select_n.132, f32[128,1024]{1,0:T(8,128)S(1)} %copy-done), kind=kOutput, calls=%fused_computation.6 | convolution fusion | flops 402784256 | bytes 2097156 | tf_op jit(solution)/shard_map/dot_general | solution.py:8
  33.6 2.4 %convolution_select_fusion = f32[128,512]{1,0:T(8,128)S(1)} fusion(f32[128,512]{1,0:T(8,128)S(1)} %fusion.1, f32[2048,512]{1,0:T(8,128)} %param.5, f32[128,512]{1,0:T(8,128)S(1)} %fusion.8, f32[128,512]{1,0:T(8,128)S(1)} %fusion.11, f32[128,512]{1,0:T(8,128)S(1)} %fusion.14, pred[]{:T(512)S(6)} %eq.31, pred[]{:T(512)S(6)} %eq.30, pred[]{:T(512)S(6)} %eq.29, ...), kind=kOutput, calls=%fused_computation.4 | convolution fusion | flops 402915328 | bytes 2359300 | tf_op jit(solution)/shard_map/dot_general | solution.py:8
  36.8 1.3 collective-permute-start.10
  38.1 77.4 %collective-permute-done.10 = f32[128,512]{1,0:T(8,128)S(1)} collective-permute-done((f32[128,512]{1,0:T(8,128)S(1)}, f32[128,512]{1,0:T(8,128)S(1)}, u32[]{:S(2)}, u32[]{:S(2)}) %collective-permute-start.10) | collective-permute-done | bytes 262176 | tf_op jit(solution)/shard_map/ppermute | solution.py:67
  115.6 1.3 collective-permute-start.11
  116.9 4.6 %collective-permute-done.11 = f32[128,512]{1,0:T(8,128)S(1)} collective-permute-done((f32[128,512]{1,0:T(8,128)S(1)}, f32[128,512]{1,0:T(8,128)S(1)}, u32[]{:S(2)}, u32[]{:S(2)}) %collective-permute-start.11) | collective-permute-done | bytes 262176 | tf_op jit(solution)/shard_map/ppermute | solution.py:67
  121.5 1.3 collective-permute-start.12
  122.9 3.3 %collective-permute-done.12 = f32[128,512]{1,0:T(8,128)S(1)} collective-permute-done((f32[128,512]{1,0:T(8,128)S(1)}, f32[128,512]{1,0:T(8,128)S(1)}, u32[]{:S(2)}, u32[]{:S(2)}) %collective-permute-start.12) | collective-permute-done | bytes 262176 | tf_op jit(solution)/shard_map/ppermute | solution.py:67
  126.2 8.5 %collective-permute-start.13 = (f32[128,512]{1,0:T(8,128)S(1)}, f32[128,512]{1,0:T(8,128)S(1)}, u32[]{:S(2)}, u32[]{:S(2)}) collective-permute-start(f32[128,512]{1,0:T(8,128)S(1)} %broadcast_select_fusion.3), channel_id=1, source_target_pairs={{0,8},{4,12},{8,0},{12,4},{16,24},{20,28},{24,16},{28,20},{32,40},... | collective-permute-start | bytes 786440 | tf_op jit(solution)/shard_map/ppermute | solution.py:73
  134.7 4.2 %collective-permute-done.13 = f32[128,512]{1,0:T(8,128)S(1)} collective-permute-done((f32[128,512]{1,0:T(8,128)S(1)}, f32[128,512]{1,0:T(8,128)S(1)}, u32[]{:S(2)}, u32[]{:S(2)}) %collective-permute-start.13) | collective-permute-done | bytes 262176 | tf_op jit(solution)/shard_map/ppermute | solution.py:73
  138.9 3.4 %collective-permute-start.14 = (f32[128,1024]{1,0:T(8,128)S(1)}, f32[128,1024]{1,0:T(8,128)S(1)}, u32[]{:S(2)}, u32[]{:S(2)}) collective-permute-start(f32[128,1024]{1,0:T(8,128)S(1)} %maximum_select_fusion.1), channel_id=1, source_target_pairs={{0,4},{4,0},{8,12},{12,8},{16,20},{20,16},{24,28},{28,24},{32,36},... | collective-permute-start | bytes 1572872 | tf_op jit(solution)/shard_map/ppermute | solution.py:75
  142.3 1.5 collective-permute-done.14
  143.9 4.4 %convolution_subtract_fusion = f32[128,512]{1,0:T(8,128)S(1)} fusion(f32[512,2048]{1,0:T(8,128)} %all-gather.5.cloned.1.call-done, f32[128,1024]{1,0:T(8,128)S(1)} %copy-done, f32[128,512]{1,0:T(8,128)S(1)} %get-tuple-element.14, f32[128,512]{1,0:T(8,128)S(1)} %get-tuple-element.12, f32[128,512]{1,0:T(8,128)S(1)} %get-tuple-element.13, ...), kind=kOutput, calls=%fused_computation.1 | convolution fusion | flops 807206912 | bytes 5767169 | tf_op jit(solution)/shard_map/dot_general | solution.py:8
  148.3 14.7 %all-gather.3.cloned.1.call-done = f32[512,2048]{1,0:T(8,128)} async-done(((f32[512,512]{1,0:T(8,128)}), f32[512,2048]{1,0:T(8,128)}) %all-gather.3.cloned.1.call-update) | async-done | bytes 4194320 | tf_op jit(solution)/shard_map/all_gather | solution.py:61
  163.0 4.4 %fusion = f32[128,512]{1,0:T(8,128)S(1)} fusion(f32[128,512]{1,0:T(8,128)S(1)} %convolution_select_fusion, f32[512,2048]{1,0:T(8,128)} %all-gather.3.cloned.1.call-done, f32[128,1024]{1,0:T(8,128)S(1)} %copy-done, pred[]{:T(512)S(6)} %lt.63, f32[128,512]{1,0:T(8,128)S(1)} %get-tuple-element.14, f32[128,512]{1,0:T(8,128)S(1)} %get-tuple-element.12, ...), kind=kOutput, calls=%fused_computation.3 | convolution fusion | flops 807272448 | bytes 6029314 | tf_op jit(solution)/shard_map/dot_general | solution.py:8
  167.4 0.8 pad_maximum_fusion.1
  (36 shorter events, 8.0 us)
Async XLA Ops:
  6.5 137.3 %all-gather.5.cloned.1.call-start = ((), (), s32[]{:S(2)}) async-start(), calls=%async_computation.1 | async-start | bytes 5242880 | tf_op jit(solution)/shard_map/all_gather | solution.py:60
  8.0 2.2 %collective-permute-start.3 = (f32[512,512]{1,0:T(8,128)S(1)}, f32[512,512]{1,0:T(8,128)S(1)}, u32[]{:S(2)}, u32[]{:S(2)}) collective-permute-start(f32[512,512]{1,0:T(8,128)S(1)} %get-tuple-element.10), channel_id=1, source_target_pairs={{4,5},{8,9},{9,10},{12,13},{13,14},{14,15}} | collective-permute-start | bytes 3145736 | tf_op jit(solution)/shard_map/ppermute | solution.py:42
  8.8 1.5 collective-permute-start.4
  9.5 0.8 collective-permute-start.5
  10.3 2.5 %copy-start.1 = (f32[1024,512]{1,0:T(8,128)S(1)}, f32[1024,512]{1,0:T(8,128)}, u32[]{:S(2)}) copy-start(f32[1024,512]{1,0:T(8,128)} %param.4) | copy-start | bytes 6291460
  12.7 2.3 %copy-start = (f32[128,1024]{1,0:T(8,128)S(1)}, f32[128,1024]{1,0:T(8,128)}, u32[]{:S(2)}) copy-start(f32[128,1024]{1,0:T(8,128)} %param.3) | copy-start | bytes 1572868
  14.2 148.8 %all-gather.3.cloned.1.call-start = ((), (), s32[]{:S(2)}) async-start(), calls=%async_computation | async-start | bytes 5242880 | tf_op jit(solution)/shard_map/all_gather | solution.py:61
  17.4 2.1 %collective-permute-start = (f32[128,512]{1,0:T(8,128)S(1)}, f32[128,512]{1,0:T(8,128)S(1)}, u32[]{:S(2)}, u32[]{:S(2)}) collective-permute-start(f32[128,512]{1,0:T(8,128)S(1)} %fusion.14), channel_id=1, source_target_pairs={{0,4},{1,5},{2,6},{3,7}} | collective-permute-start | bytes 786440 | tf_op jit(solution)/shard_map/ppermute | solution.py:55
  18.1 1.4 collective-permute-start.1
  18.8 0.7 collective-permute-start.2
  24.3 1.4 collective-permute-start.6
  25.0 0.7 collective-permute-start.7
  30.5 0.7 collective-permute-start.8
  36.0 0.7 collective-permute-start.9
  36.8 78.8 %collective-permute-start.10 = (f32[128,512]{1,0:T(8,128)S(1)}, f32[128,512]{1,0:T(8,128)S(1)}, u32[]{:S(2)}, u32[]{:S(2)}) collective-permute-start(f32[128,512]{1,0:T(8,128)S(1)} %broadcast_select_fusion), channel_id=1, source_target_pairs={{0,64},{4,68},{8,72},{12,76},{128,192},{132,196},{136,200},{140,20... | collective-permute-start | bytes 786440 | tf_op jit(solution)/shard_map/ppermute | solution.py:67
  115.6 5.9 %collective-permute-start.11 = (f32[128,512]{1,0:T(8,128)S(1)}, f32[128,512]{1,0:T(8,128)S(1)}, u32[]{:S(2)}, u32[]{:S(2)}) collective-permute-start(f32[128,512]{1,0:T(8,128)S(1)} %broadcast_select_fusion.1), channel_id=1, source_target_pairs={{0,32},{4,36},{8,40},{12,44},{64,96},{68,100},{72,104},{76,108},{1... | collective-permute-start | bytes 786440 | tf_op jit(solution)/shard_map/ppermute | solution.py:67
  121.5 4.6 %collective-permute-start.12 = (f32[128,512]{1,0:T(8,128)S(1)}, f32[128,512]{1,0:T(8,128)S(1)}, u32[]{:S(2)}, u32[]{:S(2)}) collective-permute-start(f32[128,512]{1,0:T(8,128)S(1)} %broadcast_select_fusion.2), channel_id=1, source_target_pairs={{0,16},{4,20},{8,24},{12,28},{32,48},{36,52},{40,56},{44,60},{64,8... | collective-permute-start | bytes 786440 | tf_op jit(solution)/shard_map/ppermute | solution.py:67
  126.2 12.7 %collective-permute-start.13 = (f32[128,512]{1,0:T(8,128)S(1)}, f32[128,512]{1,0:T(8,128)S(1)}, u32[]{:S(2)}, u32[]{:S(2)}) collective-permute-start(f32[128,512]{1,0:T(8,128)S(1)} %broadcast_select_fusion.3), channel_id=1, source_target_pairs={{0,8},{4,12},{8,0},{12,4},{16,24},{20,28},{24,16},{28,20},{32,40},... | collective-permute-start | bytes 786440 | tf_op jit(solution)/shard_map/ppermute | solution.py:73
  138.9 4.9 %collective-permute-start.14 = (f32[128,1024]{1,0:T(8,128)S(1)}, f32[128,1024]{1,0:T(8,128)S(1)}, u32[]{:S(2)}, u32[]{:S(2)}) collective-permute-start(f32[128,1024]{1,0:T(8,128)S(1)} %maximum_select_fusion.1), channel_id=1, source_target_pairs={{0,4},{4,0},{8,12},{12,8},{16,20},{20,16},{24,28},{28,24},{32,36},... | collective-permute-start | bytes 1572872 | tf_op jit(solution)/shard_map/ppermute | solution.py:75
Sparse Core Ops, SparseCore 0:
  14.4 95.5 all-gather.4
  111.8 51.1 all-gather.2

commit v7 on v6

--- a/solution.py
+++ b/solution.py
@@ -4,12 +4,12 @@
 from jax.sharding import PartitionSpec as P
 
 
-def contract(left, right, precision=lax.Precision.HIGHEST):
+def contract(left, right):
     return lax.dot_general(
         left,
         right,
         (((1,), (1,)), ((), ())),
-        precision=precision,
+        precision=lax.Precision.HIGHEST,
         preferred_element_type=jnp.float32,
     )
 
@@ -58,7 +58,22 @@
 
     factor_later, _ = lax.optimization_barrier((factor, fetched))
     lower_second = lax.all_gather(factor_later[block:], "pcol", axis=1, tiled=True)
-    lower_first = lax.all_gather(factor_later[:block], "pcol", axis=1, tiled=True)
+    first_rows = [top_block]
+    for shift in range(1, n_col):
+        pairs = [
+            (at(p, c), at(p, (c + shift) % n_col))
+            for p in range(steps, n_row)
+            for c in range(n_col)
+        ]
+        first_rows.append(lax.ppermute(top_block, AXES, pairs))
+    first_rows = jnp.stack(first_rows)
+    lower_first = jnp.concatenate(
+        [
+            lax.dynamic_index_in_dim(first_rows, (col_at - j) % n_col, 0, keepdims=False)
+            for j in range(n_col)
+        ],
+        axis=1,
+    )
 
     piece = own
     span = n_row // 2
@@ -78,8 +93,8 @@
     theirs_first = jnp.concatenate([yours[0], mine[0], yours[1], mine[1]], axis=1)
     panel = jnp.where(b0 == 0, mine_first, theirs_first)
 
-    second = right_side[:, block:] - contract(panel, lower_second, lax.Precision.HIGH)
-    first = right_side[:, :block] - contract(panel, lower_first, lax.Precision.HIGH)
+    second = right_side[:, block:] - contract(panel, lower_second)
+    first = right_side[:, :block] - contract(panel, lower_first)
     head_block = jnp.where(row_at < steps, own, first)
     return jnp.concatenate([head_block, second], axis=1)
 

time: 177 us -> 170 us (0.960)
  waiting for transfers between devices: 106 us -> 80.9 us
  starting transfers between devices: 22.7 us -> 35.1 us
  matrix products: 25.5 us -> 27.7 us
  local copies, waits for them, and re-layouts: 3.03 us -> 5.15 us
    ppermute x4, waiting for transfers between devices: 85.3 us -> 32.7 us  [per_device(): arrived = lax.ppermute(piece, 'prow', pairs)]
    ppermute x0 -> x3, waiting for transfers between devices: none -> 43.9 us  [per_device(): first_rows.append(lax.ppermute(top_block, AXES, pairs))]
    all_gather x1 -> x0, waiting for transfers between devices: 14.7 us -> none  [per_device(): lax.all_gather(factor_later[:block], 'pcol', axis=1, tiled=True)]
    ppermute x0 -> x3, starting transfers between devices: none -> 9.5 us  [per_device(): first_rows.append(lax.ppermute(top_block, AXES, pairs))]
    ppermute x1, starting transfers between devices: 8.51 us -> 11.6 us  [per_device(): other = lax.ppermute(piece, 'prow', [(p, p ^ 2) for p in range(n_row)])]
    squeeze x0 -> x1, local copies, waits for them, and re-layouts: none -> 2.61 us  [per_device(): lax.dynamic_index_in_dim(first_rows, (col_at - j) % n_col, 0, keepdims=Fa...]
    dot_general x9, matrix products: 25.5 us -> 27.7 us  [contract(): lax.dot_general(left, right, (((1,), (1,)), ((), ())), precision=lax.Prec...]
  transfers between devices with their start and end apart: 17 -> 19, of which waited for: 6 -> 7; matrix products, arithmetic and copies ran while one was open for 12% -> 14% of each run, Pallas kernels for 0% -> 0%
where the time goes in v7:
time: 170 us; the launch traced here: 168 us
  waiting for transfers between devices  80.9 us (48%)
  starting transfers between devices  35.1 us (21%)
  matrix products  27.7 us (16%)
  between operations  13.9 us (8%)
  local copies, waits for them, and re-layouts  5.15 us (3%)
  other arithmetic  4.79 us (3%)
    ppermute x3, waiting for transfers between devices, per_device(): first_rows.append(lax.ppermute(top_block, AXES, pairs))  43.9 us
    ppermute x4, waiting for transfers between devices, per_device(): arrived = lax.ppermute(piece, 'prow', pairs)  32.7 us
    dot_general x9, matrix products, contract(): lax.dot_general(left, right, (((1,), (1,)), ((), ())), precision=lax.Prec...  27.7 us
    ppermute x1, starting transfers between devices, per_device(): other = lax.ppermute(piece, 'prow', [(p, p ^ 2) for p in range(n_row)])  11.6 us
    ppermute x3, starting transfers between devices, per_device(): first_rows.append(lax.ppermute(top_block, AXES, pairs))  9.5 us
    ppermute x4, starting transfers between devices, per_device(): arrived = lax.ppermute(piece, 'prow', pairs)  4.58 us
    ppermute x1, waiting for transfers between devices, per_device(): other = lax.ppermute(piece, 'prow', [(p, p ^ 2) for p in range(n_row)])  4.26 us
    ppermute x6, starting transfers between devices, per_device(): arrived = arrived + lax.ppermute(solved, AXES, pairs)  4.06 us
  transfers between devices with their start and end apart: 19, of which 7 were waited for; matrix products, arithmetic and copies ran while one was open for 14% of the time, Pallas kernels for 0%

profile of v7, /device:TPU:7, one launch (start us, length us, event | category | flops | bytes accessed | tf_op | source)
XLA Modules:
  0.0 167.6 jit_solution(2086917812105582074)
XLA Ops:
  6.5 1.4 fusion.46
  7.9 4.6 %collective-permute-start.17 = (f32[512,512]{1,0:T(8,128)S(1)}, f32[512,512]{1,0:T(8,128)S(1)}, u32[]{:S(2)}, u32[]{:S(2)}) collective-permute-start(f32[512,512]{1,0:T(8,128)S(1)} %get-tuple-element.11), channel_id=1, source_target_pairs={{16,19},{17,16},{18,17},{19,18},{20,23},{21,20},{22,21},{23,22},{2... | collective-permute-start | bytes 3145736 | tf_op jit(solution)/shard_map/ppermute | solution.py:68
  12.6 2.3 %collective-permute-start.16 = (f32[512,512]{1,0:T(8,128)S(1)}, f32[512,512]{1,0:T(8,128)S(1)}, u32[]{:S(2)}, u32[]{:S(2)}) collective-permute-start(f32[512,512]{1,0:T(8,128)S(1)} %get-tuple-element.11), channel_id=1, source_target_pairs={{16,18},{17,19},{18,16},{19,17},{20,22},{21,23},{22,20},{23,21},{2... | collective-permute-start | bytes 3145736 | tf_op jit(solution)/shard_map/ppermute | solution.py:68
  14.8 2.6 %collective-permute-start.15 = (f32[512,512]{1,0:T(8,128)S(1)}, f32[512,512]{1,0:T(8,128)S(1)}, u32[]{:S(2)}, u32[]{:S(2)}) collective-permute-start(f32[512,512]{1,0:T(8,128)S(1)} %get-tuple-element.11), channel_id=1, source_target_pairs={{16,17},{17,18},{18,19},{19,16},{20,21},{21,22},{22,23},{23,20},{2... | collective-permute-start | bytes 3145736 | tf_op jit(solution)/shard_map/ppermute | solution.py:68
  18.9 16.5 %collective-permute-done.17 = f32[512,512]{1,0:T(8,128)S(1)} collective-permute-done((f32[512,512]{1,0:T(8,128)S(1)}, f32[512,512]{1,0:T(8,128)S(1)}, u32[]{:S(2)}, u32[]{:S(2)}) %collective-permute-start.17) | collective-permute-done | bytes 1048608 | tf_op jit(solution)/shard_map/ppermute | solution.py:68
  36.1 3.6 %collective-permute-done.16 = f32[512,512]{1,0:T(8,128)S(1)} collective-permute-done((f32[512,512]{1,0:T(8,128)S(1)}, f32[512,512]{1,0:T(8,128)S(1)}, u32[]{:S(2)}, u32[]{:S(2)}) %collective-permute-start.16) | collective-permute-done | bytes 1048608 | tf_op jit(solution)/shard_map/ppermute | solution.py:68
  39.7 23.8 %collective-permute-done.15 = f32[512,512]{1,0:T(8,128)S(1)} collective-permute-done((f32[512,512]{1,0:T(8,128)S(1)}, f32[512,512]{1,0:T(8,128)S(1)}, u32[]{:S(2)}, u32[]{:S(2)}) %collective-permute-start.15) | collective-permute-done | bytes 1048608 | tf_op jit(solution)/shard_map/ppermute | solution.py:68
  63.5 3.8 %fusion.3 = (f32[4,512,512]{2,1,0:T(8,128)}, f32[4,512,512]{2,1,0:T(8,128)}) fusion(f32[1,512,512]{2,1,0:T(8,128)S(1)} %get-tuple-element.12, f32[1,512,512]{2,1,0:T(8,128)S(1)} %bitcast.28, f32[1,512,512]{2,1,0:T(8,128)S(1)} %bitcast.29, f32[1,512,512]{2,1,0:T(8,128)S(1)} %bitcast.30, f32[1,512,512]{2,1,0:T(8,128)S(1)} %bitcast.31, ...), kind=kLoop, calls=%fused_computation.5 | loop fusion | flops 6291456 | bytes 15728640 | tf_op jit(solution)/shard_map/stack | solution.py:69
  68.4 2.4 %fusion.31 = f32[128,512]{1,0:T(8,128)S(1)} fusion(f32[2048,512]{1,0:T(8,128)} %param.5, f32[128,1024]{1,0:T(8,128)S(1)} %copy-done), kind=kOutput, calls=%fused_computation.38 | convolution fusion | flops 402653184 | bytes 1572864 | tf_op jit(solution)/shard_map/dot_general | solution.py:8
  72.9 2.4 %fusion.21 = f32[128,512]{1,0:T(8,128)S(1)} fusion(f32[4,512,512]{2,1,0:T(8,128)} %get-tuple-element.14, s32[]{:T(128)S(6)} %select_n.144, f32[128,512]{1,0:T(8,128)S(1)} %collective-permute-done.2, f32[128,512]{1,0:T(8,128)S(1)} %collective-permute-done, f32[128,512]{1,0:T(8,128)S(1)} %collective-permute-done.1), kind=kOutput, calls=%fused_computation.24 | convolution fusion | flops 402784256 | bytes 2097156 | tf_op jit(solution)/shard_map/dot_general | solution.py:8
  75.3 2.4 %fusion.28 = f32[128,512]{1,0:T(8,128)S(1)} fusion(f32[2048,512]{1,0:T(8,128)} %param.5, f32[128,512]{1,0:T(8,128)S(1)} %fusion.21, f32[128,1024]{1,0:T(8,128)S(1)} %copy-done), kind=kOutput, calls=%fused_computation.35 | convolution fusion | flops 402718720 | bytes 1835008 | tf_op jit(solution)/shard_map/dot_general | solution.py:8
  79.1 2.4 %convolution_add_fusion.1 = f32[128,512]{1,0:T(8,128)S(1)} fusion(f32[128,512]{1,0:T(8,128)S(1)} %fusion.21, f32[4,512,512]{2,1,0:T(8,128)} %get-tuple-element.14, s32[]{:T(128)S(6)} %select_n.146, f32[128,512]{1,0:T(8,128)S(1)} %collective-permute-done.6, f32[128,512]{1,0:T(8,128)S(1)} %collective-permute-done.7), kind=kOutput, calls=%fused_computation.18 | convolution fusion | flops 402784256 | bytes 2097156 | tf_op jit(solution)/shard_map/dot_general | solution.py:8
  81.6 2.5 %fusion.25 = f32[128,512]{1,0:T(8,128)S(1)} fusion(f32[2048,512]{1,0:T(8,128)} %param.5, f32[128,512]{1,0:T(8,128)S(1)} %convolution_add_fusion.1, f32[128,1024]{1,0:T(8,128)S(1)} %copy-done), kind=kOutput, calls=%fused_computation.32 | convolution fusion | flops 402718720 | bytes 1835008 | tf_op jit(solution)/shard_map/dot_general | solution.py:8
  84.8 2.4 %fusion.12 = f32[128,512]{1,0:T(8,128)S(1)} fusion(f32[128,512]{1,0:T(8,128)S(1)} %convolution_add_fusion.1, f32[128,512]{1,0:T(8,128)S(1)} %collective-permute-done.8, f32[4,512,512]{2,1,0:T(8,128)} %get-tuple-element.14, s32[]{:T(128)S(6)} %select_n.148, f32[128,1024]{1,0:T(8,128)S(1)} %copy-done), kind=kOutput, calls=%fused_computation.17 | convolution fusion | flops 402784256 | bytes 2097156 | tf_op jit(solution)/shard_map/dot_general | solution.py:8
  87.2 2.4 %convolution_select_fusion = f32[128,512]{1,0:T(8,128)S(1)} fusion(f32[128,512]{1,0:T(8,128)S(1)} %fusion.12, f32[2048,512]{1,0:T(8,128)} %param.5, f32[128,512]{1,0:T(8,128)S(1)} %fusion.25, f32[128,512]{1,0:T(8,128)S(1)} %fusion.28, f32[128,512]{1,0:T(8,128)S(1)} %fusion.31, pred[]{:T(512)S(6)} %eq.35, pred[]{:T(512)S(6)} %eq.34, pred[]{:T(512)S(6)} %eq.33, ...), kind=kOutput, calls=%fused_computation.15 | convolution fusion | flops 402915328 | bytes 2359300 | tf_op jit(solution)/shard_map/dot_general | solution.py:8
  91.7 25.9 %collective-permute-done.10 = f32[128,512]{1,0:T(8,128)S(1)} collective-permute-done((f32[128,512]{1,0:T(8,128)S(1)}, f32[128,512]{1,0:T(8,128)S(1)}, u32[]{:S(2)}, u32[]{:S(2)}) %collective-permute-start.10) | collective-permute-done | bytes 262176 | tf_op jit(solution)/shard_map/ppermute | solution.py:82
  118.9 3.6 %collective-permute-done.11 = f32[128,512]{1,0:T(8,128)S(1)} collective-permute-done((f32[128,512]{1,0:T(8,128)S(1)}, f32[128,512]{1,0:T(8,128)S(1)}, u32[]{:S(2)}, u32[]{:S(2)}) %collective-permute-start.11) | collective-permute-done | bytes 262176 | tf_op jit(solution)/shard_map/ppermute | solution.py:82
  123.8 3.3 %collective-permute-done.12 = f32[128,512]{1,0:T(8,128)S(1)} collective-permute-done((f32[128,512]{1,0:T(8,128)S(1)}, f32[128,512]{1,0:T(8,128)S(1)}, u32[]{:S(2)}, u32[]{:S(2)}) %collective-permute-start.12) | collective-permute-done | bytes 262176 | tf_op jit(solution)/shard_map/ppermute | solution.py:82
  127.1 11.6 %collective-permute-start.13 = (f32[128,512]{1,0:T(8,128)S(1)}, f32[128,512]{1,0:T(8,128)S(1)}, u32[]{:S(2)}, u32[]{:S(2)}) collective-permute-start(f32[128,512]{1,0:T(8,128)S(1)} %broadcast_select_fusion.3), channel_id=1, source_target_pairs={{0,8},{4,12},{8,0},{12,4},{16,24},{20,28},{24,16},{28,20},{32,40},... | collective-permute-start | bytes 786440 | tf_op jit(solution)/shard_map/ppermute | solution.py:88
  138.7 4.3 %collective-permute-done.13 = f32[128,512]{1,0:T(8,128)S(1)} collective-permute-done((f32[128,512]{1,0:T(8,128)S(1)}, f32[128,512]{1,0:T(8,128)S(1)}, u32[]{:S(2)}, u32[]{:S(2)}) %collective-permute-start.13) | collective-permute-done | bytes 262176 | tf_op jit(solution)/shard_map/ppermute | solution.py:88
  143.0 3.3 %collective-permute-start.14 = (f32[128,1024]{1,0:T(8,128)S(1)}, f32[128,1024]{1,0:T(8,128)S(1)}, u32[]{:S(2)}, u32[]{:S(2)}) collective-permute-start(f32[128,1024]{1,0:T(8,128)S(1)} %maximum_select_fusion.1), channel_id=1, source_target_pairs={{0,4},{4,0},{8,12},{12,8},{16,20},{20,16},{24,28},{28,24},{32,36},... | collective-permute-start | bytes 1572872 | tf_op jit(solution)/shard_map/ppermute | solution.py:90
  146.3 2.6 %dynamic-slice_bitcast_fusion.3 = (f32[512,512]{1,0:T(8,128)S(1)}, f32[512,512]{1,0:T(8,128)S(1)}, f32[512,512]{1,0:T(8,128)S(1)}, f32[512,512]{1,0:T(8,128)S(1)}) fusion(f32[4,512,512]{2,1,0:T(8,128)} %get-tuple-element.13, s32[]{:T(128)S(6)} %select_n.144, s32[]{:T(128)S(6)} %select_n.176, s32[]{:T(128)S(6)} %select_n.148, s32[]{:T(128)S(6)} %select_n.146), kind=kLoop, calls=%fused_computation.29 | loop fusion | bytes 8388624 | tf_op jit(solution)/shard_map/jit(dynamic_index_in_dim)/squeeze | solution.py:72
  149.0 4.4 %fusion.16 = f32[128,512]{1,0:T(8,128)S(1)} fusion(f32[128,512]{1,0:T(8,128)S(1)} %convolution_select_fusion, f32[512,512]{1,0:T(8,128)S(1)} %get-tuple-element.8, f32[512,512]{1,0:T(8,128)S(1)} %get-tuple-element.9, f32[512,512]{1,0:T(8,128)S(1)} %get-tuple-element.10, f32[512,512]{1,0:T(8,128)S(1)} %get-tuple-element.7, f32[128,1024]{1,0:T(8,128)S(1)} %copy-done, ...), kind=kOutput, calls=%fused_computation.20 | convolution fusion | flops 1615724544 | bytes 6029314 | tf_op jit(solution)/shard_map/dot_general | solution.py:8
  153.4 6.5 %convolution_subtract_fusion = f32[128,512]{1,0:T(8,128)S(1)} fusion(f32[512,2048]{1,0:T(8,128)} %all-gather.2.cloned.1.call-done, f32[128,1024]{1,0:T(8,128)S(1)} %copy-done, f32[128,512]{1,0:T(8,128)S(1)} %get-tuple-element.18, f32[128,512]{1,0:T(8,128)S(1)} %get-tuple-element.16, f32[128,512]{1,0:T(8,128)S(1)} %get-tuple-element.17, ...), kind=kOutput, calls=%fused_computation.14 | convolution fusion | flops 1612513280 | bytes 5767169 | tf_op jit(solution)/shard_map/dot_general | solution.py:8
  (40 shorter events, 13.1 us)
Async XLA Ops:
  6.5 146.8 %all-gather.2.cloned.1.call-start = ((), (), s32[]{:S(2)}) async-start(), calls=%async_computation | async-start | bytes 5242880 | tf_op jit(solution)/shard_map/all_gather | solution.py:60
  7.9 27.5 %collective-permute-start.17 = (f32[512,512]{1,0:T(8,128)S(1)}, f32[512,512]{1,0:T(8,128)S(1)}, u32[]{:S(2)}, u32[]{:S(2)}) collective-permute-start(f32[512,512]{1,0:T(8,128)S(1)} %get-tuple-element.11), channel_id=1, source_target_pairs={{16,19},{17,16},{18,17},{19,18},{20,23},{21,20},{22,21},{23,22},{2... | collective-permute-start | bytes 3145736 | tf_op jit(solution)/shard_map/ppermute | solution.py:68
  12.6 27.1 %collective-permute-start.16 = (f32[512,512]{1,0:T(8,128)S(1)}, f32[512,512]{1,0:T(8,128)S(1)}, u32[]{:S(2)}, u32[]{:S(2)}) collective-permute-start(f32[512,512]{1,0:T(8,128)S(1)} %get-tuple-element.11), channel_id=1, source_target_pairs={{16,18},{17,19},{18,16},{19,17},{20,22},{21,23},{22,20},{23,21},{2... | collective-permute-start | bytes 3145736 | tf_op jit(solution)/shard_map/ppermute | solution.py:68
  14.8 48.7 %collective-permute-start.15 = (f32[512,512]{1,0:T(8,128)S(1)}, f32[512,512]{1,0:T(8,128)S(1)}, u32[]{:S(2)}, u32[]{:S(2)}) collective-permute-start(f32[512,512]{1,0:T(8,128)S(1)} %get-tuple-element.11), channel_id=1, source_target_pairs={{16,17},{17,18},{18,19},{19,16},{20,21},{21,22},{22,23},{23,20},{2... | collective-permute-start | bytes 3145736 | tf_op jit(solution)/shard_map/ppermute | solution.py:68
  17.4 46.1 %collective-permute-start.5 = (f32[512,512]{1,0:T(8,128)S(1)}, f32[512,512]{1,0:T(8,128)S(1)}, u32[]{:S(2)}, u32[]{:S(2)}) collective-permute-start(f32[512,512]{1,0:T(8,128)S(1)} %get-tuple-element.11), channel_id=1, source_target_pairs={{4,7},{8,11},{9,8},{12,15},{13,12},{14,13}} | collective-permute-start | bytes 3145736 | tf_op jit(solution)/shard_map/ppermute | solution.py:42
  18.2 45.3 %collective-permute-start.4 = (f32[512,512]{1,0:T(8,128)S(1)}, f32[512,512]{1,0:T(8,128)S(1)}, u32[]{:S(2)}, u32[]{:S(2)}) collective-permute-start(f32[512,512]{1,0:T(8,128)S(1)} %get-tuple-element.11), channel_id=1, source_target_pairs={{4,6},{8,10},{9,11},{12,14},{13,15},{14,12}} | collective-permute-start | bytes 3145736 | tf_op jit(solution)/shard_map/ppermute | solution.py:42
  35.4 28.1 %collective-permute-start.3 = (f32[512,512]{1,0:T(8,128)S(1)}, f32[512,512]{1,0:T(8,128)S(1)}, u32[]{:S(2)}, u32[]{:S(2)}) collective-permute-start(f32[512,512]{1,0:T(8,128)S(1)} %get-tuple-element.11), channel_id=1, source_target_pairs={{4,5},{8,9},{9,10},{12,13},{13,14},{14,15}} | collective-permute-start | bytes 3145736 | tf_op jit(solution)/shard_map/ppermute | solution.py:42
  63.5 3.8 %copy-start.1 = (f32[1024,512]{1,0:T(8,128)S(1)}, f32[1024,512]{1,0:T(8,128)}, u32[]{:S(2)}) copy-start(f32[1024,512]{1,0:T(8,128)} %param.4) | copy-start | bytes 6291460
  63.5 4.9 %copy-start = (f32[128,1024]{1,0:T(8,128)S(1)}, f32[128,1024]{1,0:T(8,128)}, u32[]{:S(2)}) copy-start(f32[128,1024]{1,0:T(8,128)} %param.3) | copy-start | bytes 1572868
  70.8 2.1 %collective-permute-start.2 = (f32[128,512]{1,0:T(8,128)S(1)}, f32[128,512]{1,0:T(8,128)S(1)}, u32[]{:S(2)}, u32[]{:S(2)}) collective-permute-start(f32[128,512]{1,0:T(8,128)S(1)} %fusion.31), channel_id=1, source_target_pairs={{0,12},{1,13},{2,14},{3,15}} | collective-permute-start | bytes 786440 | tf_op jit(solution)/shard_map/ppermute | solution.py:55
  71.5 1.4 collective-permute-start
  72.2 0.7 collective-permute-start.1
  77.7 1.4 collective-permute-start.6
  78.4 0.7 collective-permute-start.7
  84.0 0.7 collective-permute-start.8
  89.6 0.7 collective-permute-start.9
  90.3 27.2 %collective-permute-start.10 = (f32[128,512]{1,0:T(8,128)S(1)}, f32[128,512]{1,0:T(8,128)S(1)}, u32[]{:S(2)}, u32[]{:S(2)}) collective-permute-start(f32[128,512]{1,0:T(8,128)S(1)} %broadcast_select_fusion), channel_id=1, source_target_pairs={{0,64},{4,68},{8,72},{12,76},{128,192},{132,196},{136,200},{140,20... | collective-permute-start | bytes 786440 | tf_op jit(solution)/shard_map/ppermute | solution.py:82
  117.6 4.9 %collective-permute-start.11 = (f32[128,512]{1,0:T(8,128)S(1)}, f32[128,512]{1,0:T(8,128)S(1)}, u32[]{:S(2)}, u32[]{:S(2)}) collective-permute-start(f32[128,512]{1,0:T(8,128)S(1)} %broadcast_select_fusion.1), channel_id=1, source_target_pairs={{0,32},{4,36},{8,40},{12,44},{64,96},{68,100},{72,104},{76,108},{1... | collective-permute-start | bytes 786440 | tf_op jit(solution)/shard_map/ppermute | solution.py:82
  122.5 4.6 %collective-permute-start.12 = (f32[128,512]{1,0:T(8,128)S(1)}, f32[128,512]{1,0:T(8,128)S(1)}, u32[]{:S(2)}, u32[]{:S(2)}) collective-permute-start(f32[128,512]{1,0:T(8,128)S(1)} %broadcast_select_fusion.2), channel_id=1, source_target_pairs={{0,16},{4,20},{8,24},{12,28},{32,48},{36,52},{40,56},{44,60},{64,8... | collective-permute-start | bytes 786440 | tf_op jit(solution)/shard_map/ppermute | solution.py:82
  127.1 15.8 %collective-permute-start.13 = (f32[128,512]{1,0:T(8,128)S(1)}, f32[128,512]{1,0:T(8,128)S(1)}, u32[]{:S(2)}, u32[]{:S(2)}) collective-permute-start(f32[128,512]{1,0:T(8,128)S(1)} %broadcast_select_fusion.3), channel_id=1, source_target_pairs={{0,8},{4,12},{8,0},{12,4},{16,24},{20,28},{24,16},{28,20},{32,40},... | collective-permute-start | bytes 786440 | tf_op jit(solution)/shard_map/ppermute | solution.py:88
  143.0 5.9 %collective-permute-start.14 = (f32[128,1024]{1,0:T(8,128)S(1)}, f32[128,1024]{1,0:T(8,128)S(1)}, u32[]{:S(2)}, u32[]{:S(2)}) collective-permute-start(f32[128,1024]{1,0:T(8,128)S(1)} %maximum_select_fusion.1), channel_id=1, source_target_pairs={{0,4},{4,0},{8,12},{12,8},{16,20},{20,16},{24,28},{28,24},{32,36},... | collective-permute-start | bytes 1572872 | tf_op jit(solution)/shard_map/ppermute | solution.py:90
Sparse Core Ops, SparseCore 0:
  68.6 50.9 all-gather.1

commit v8 on v4

--- a/solution.py
+++ b/solution.py
@@ -30,17 +30,10 @@
         return p * n_col + c
 
     top_rhs = right_side[:, :block]
-    top_block = factor[:block]
 
-    fetched = [top_block]
-    for shift in range(1, n_col):
-        pairs = [
-            (at(i, j), at(i, (j + shift) % n_col))
-            for i in range(1, steps)
-            for j in range(i)
-        ]
-        fetched.append(lax.ppermute(top_block, AXES, pairs))
-    fetched = jnp.stack(fetched)
+    lower_first = lax.all_gather(factor[:block], "pcol", axis=1, tiled=True)
+    second_rows, _ = lax.optimization_barrier((factor[block:], lower_first))
+    lower_second = lax.all_gather(second_rows, "pcol", axis=1, tiled=True)
 
     acc = jnp.zeros((rhs_width, block), jnp.float32)
     own = jnp.zeros((rhs_width, block), jnp.float32)
@@ -53,10 +46,7 @@
         for i in range(k + 1, steps):
             pairs = [(at(k, c), at(i, c)) for c in range(n_col)]
             arrived = arrived + lax.ppermute(solved, AXES, pairs)
-        lower = lax.dynamic_index_in_dim(fetched, (col_at - k) % n_col, 0, keepdims=False)
-        acc = acc + contract(arrived, lower)
-
-    lower_all = lax.all_gather(factor, "pcol", axis=1, tiled=True)
+        acc = acc + contract(arrived, lower_first[:, k * block : (k + 1) * block])
 
     piece = own
     span = n_row // 2
@@ -76,9 +66,10 @@
     theirs_first = jnp.concatenate([yours[0], mine[0], yours[1], mine[1]], axis=1)
     panel = jnp.where(b0 == 0, mine_first, theirs_first)
 
-    updated = right_side - contract(panel, lower_all)
-    head_block = jnp.where(row_at < steps, own, updated[:, :block])
-    return jnp.concatenate([head_block, updated[:, block:]], axis=1)
+    second = right_side[:, block:] - contract(panel, lower_second)
+    first = right_side[:, :block] - contract(panel, lower_first)
+    head_block = jnp.where(row_at < steps, own, first)
+    return jnp.concatenate([head_block, second], axis=1)
 
 
 def solution(mesh):

time: 185 us -> 165 us (0.89)
  waiting for transfers between devices: 104 us -> 94.3 us
  starting transfers between devices: 29 us -> 20.7 us
  matrix products: 27.8 us -> 29.9 us
  local copies, waits for them, and re-layouts: 5.26 us -> 3.3 us
    ppermute x4, waiting for transfers between devices: 98 us -> 34.7 us  [per_device(): arrived = lax.ppermute(piece, 'prow', pairs)]
    all_gather x1 -> x2, waiting for transfers between devices: 0.02 us -> 53.8 us  [the longest x1 53.8 us: per_device(): lower_first = lax.all_gather(factor[:block], 'pcol', axis=1, tiled=True)]
    ppermute x3 -> x0, starting transfers between devices: 4.12 us -> none  [per_device(): fetched.append(lax.ppermute(top_block, AXES, pairs))]
    unnamed x8 -> x2, local copies, waits for them, and re-layouts: 3.72 us -> 0.01 us
    ppermute x1, starting transfers between devices: 12 us -> 8.61 us  [per_device(): other = lax.ppermute(piece, 'prow', [(p, p ^ 2) for p in range(n_row)])]
    slice x0 -> x1, local copies, waits for them, and re-layouts: none -> 3.23 us  [per_device(): lower_first = lax.all_gather(factor[:block], 'pcol', axis=1, tiled=True)]
    another operation x1 -> x0, other arithmetic: 2.3 us -> none  [per_device(): fetched = jnp.stack(fetched)]
    dot_general x8 -> x9, matrix products: 27.8 us -> 29.9 us  [contract(): lax.dot_general(left, right, (((1,), (1,)), ((), ())), precision=lax.Prec...]
  transfers between devices with their start and end apart: 16 -> 14, of which waited for: 5 -> 6; matrix products, arithmetic and copies ran while one was open for 11% -> 15% of each run, Pallas kernels for 0% -> 0%
where the time goes in v8:
time: 165 us; the launch traced here: 163 us
  waiting for transfers between devices  94.3 us (57%)
  matrix products  29.9 us (18%)
  starting transfers between devices  20.7 us (13%)
  between operations  13.7 us (8%)
  local copies, waits for them, and re-layouts  3.3 us (2%)
    all_gather x1, waiting for transfers between devices, per_device(): lower_first = lax.all_gather(factor[:block], 'pcol', axis=1, tiled=True)  53.8 us
    ppermute x4, waiting for transfers between devices, per_device(): arrived = lax.ppermute(piece, 'prow', pairs)  34.7 us
    dot_general x9, matrix products, contract(): lax.dot_general(left, right, (((1,), (1,)), ((), ())), precision=lax.Prec...  29.9 us
    ppermute x1, starting transfers between devices, per_device(): other = lax.ppermute(piece, 'prow', [(p, p ^ 2) for p in range(n_row)])  8.61 us
    ppermute x4, starting transfers between devices, per_device(): arrived = lax.ppermute(piece, 'prow', pairs)  4.58 us
    ppermute x1, waiting for transfers between devices, per_device(): other = lax.ppermute(piece, 'prow', [(p, p ^ 2) for p in range(n_row)])  4.17 us
    ppermute x6, starting transfers between devices, per_device(): arrived = arrived + lax.ppermute(solved, AXES, pairs)  4.06 us
    ppermute x1, starting transfers between devices, per_device(): theirs = lax.ppermute(pair, 'prow', [(p, p ^ 1) for p in range(n_row)])  3.36 us
  transfers between devices with their start and end apart: 14, of which 6 were waited for; matrix products, arithmetic and copies ran while one was open for 15% of the time, Pallas kernels for 0%

profile of v8, /device:TPU:7, one launch (start us, length us, event | category | flops | bytes accessed | tf_op | source)
XLA Modules:
  0.0 162.9 jit_solution(8277263130826927874)
XLA Ops:
  6.5 3.2 %fusion.23 = (f32[512,512]{1,0:T(8,128)}, f32[512,512]{1,0:T(8,128)}) fusion(f32[1024,512]{1,0:T(8,128)} %param.4), kind=kLoop, calls=%fused_computation.35 | loop fusion | bytes 4194304 | tf_op jit(solution)/shard_map/slice | solution.py:34
  9.8 53.8 %all-gather.3.cloned.1.call-done = f32[512,2048]{1,0:T(8,128)} async-done(((f32[512,512]{1,0:T(8,128)}), f32[512,2048]{1,0:T(8,128)}) %all-gather.3.cloned.1.call-update) | async-done | bytes 4194320 | tf_op jit(solution)/shard_map/all_gather | solution.py:34
  63.7 2.4 %fusion.11 = f32[128,512]{1,0:T(8,128)S(1)} fusion(f32[2048,512]{1,0:T(8,128)} %param.5, f32[128,1024]{1,0:T(8,128)S(1)} %copy-done), kind=kOutput, calls=%fused_computation.17 | convolution fusion | flops 402653184 | bytes 1572864 | tf_op jit(solution)/shard_map/dot_general | solution.py:8
  66.1 0.7 collective-permute-start
  68.2 2.4 %fusion.4 = f32[128,512]{1,0:T(8,128)S(1)} fusion(f32[512,2048]{1,0:T(8,128)} %all-gather.3.cloned.1.call-done, f32[128,512]{1,0:T(8,128)S(1)} %collective-permute-done.2, f32[128,512]{1,0:T(8,128)S(1)} %collective-permute-done, f32[128,512]{1,0:T(8,128)S(1)} %collective-permute-done.1), kind=kOutput, calls=%fused_computation.9 | convolution fusion | flops 402784256 | bytes 2097152 | tf_op jit(solution)/shard_map/dot_general | solution.py:8
  70.5 2.4 %fusion.9 = f32[128,512]{1,0:T(8,128)S(1)} fusion(f32[2048,512]{1,0:T(8,128)} %param.5, f32[128,512]{1,0:T(8,128)S(1)} %fusion.4, f32[128,1024]{1,0:T(8,128)S(1)} %copy-done), kind=kOutput, calls=%fused_computation.15 | convolution fusion | flops 402718720 | bytes 1835008 | tf_op jit(solution)/shard_map/dot_general | solution.py:8
  74.3 2.4 %convolution_add_fusion.1 = f32[128,512]{1,0:T(8,128)S(1)} fusion(f32[128,512]{1,0:T(8,128)S(1)} %fusion.4, f32[512,2048]{1,0:T(8,128)} %all-gather.3.cloned.1.call-done, f32[128,512]{1,0:T(8,128)S(1)} %collective-permute-done.3, f32[128,512]{1,0:T(8,128)S(1)} %collective-permute-done.4), kind=kOutput, calls=%fused_computation.6 | convolution fusion | flops 402784256 | bytes 2097152 | tf_op jit(solution)/shard_map/dot_general | solution.py:8
  76.7 2.5 %fusion.7 = f32[128,512]{1,0:T(8,128)S(1)} fusion(f32[2048,512]{1,0:T(8,128)} %param.5, f32[128,512]{1,0:T(8,128)S(1)} %convolution_add_fusion.1, f32[128,1024]{1,0:T(8,128)S(1)} %copy-done), kind=kOutput, calls=%fused_computation.13 | convolution fusion | flops 402718720 | bytes 1835008 | tf_op jit(solution)/shard_map/dot_general | solution.py:8
  79.2 0.7 collective-permute-start.5
  79.9 2.5 %fusion.1 = f32[128,512]{1,0:T(8,128)S(1)} fusion(f32[128,512]{1,0:T(8,128)S(1)} %convolution_add_fusion.1, f32[128,512]{1,0:T(8,128)S(1)} %collective-permute-done.5, f32[512,2048]{1,0:T(8,128)} %all-gather.3.cloned.1.call-done, f32[128,1024]{1,0:T(8,128)S(1)} %copy-done), kind=kOutput, calls=%fused_computation.5 | convolution fusion | flops 402784256 | bytes 2097152 | tf_op jit(solution)/shard_map/dot_general | solution.py:8
  82.4 2.4 %convolution_select_fusion = f32[128,512]{1,0:T(8,128)S(1)} fusion(f32[128,512]{1,0:T(8,128)S(1)} %fusion.1, f32[2048,512]{1,0:T(8,128)} %param.5, f32[128,512]{1,0:T(8,128)S(1)} %fusion.7, f32[128,512]{1,0:T(8,128)S(1)} %fusion.9, f32[128,512]{1,0:T(8,128)S(1)} %fusion.11, pred[]{:T(512)S(6)} %eq.28, pred[]{:T(512)S(6)} %eq.27, pred[]{:T(512)S(6)} %eq.26, ...), kind=kOutput, calls=%fused_computation.3 | convolution fusion | flops 402915328 | bytes 2359300 | tf_op jit(solution)/shard_map/dot_general | solution.py:8
  85.6 1.3 collective-permute-start.7
  86.9 27.3 %collective-permute-done.7 = f32[128,512]{1,0:T(8,128)S(1)} collective-permute-done((f32[128,512]{1,0:T(8,128)S(1)}, f32[128,512]{1,0:T(8,128)S(1)}, u32[]{:S(2)}, u32[]{:S(2)}) %collective-permute-start.7) | collective-permute-done | bytes 262176 | tf_op jit(solution)/shard_map/ppermute | solution.py:55
  114.2 1.3 collective-permute-start.8
  115.5 4.2 %collective-permute-done.8 = f32[128,512]{1,0:T(8,128)S(1)} collective-permute-done((f32[128,512]{1,0:T(8,128)S(1)}, f32[128,512]{1,0:T(8,128)S(1)}, u32[]{:S(2)}, u32[]{:S(2)}) %collective-permute-start.8) | collective-permute-done | bytes 262176 | tf_op jit(solution)/shard_map/ppermute | solution.py:55
  119.8 1.3 collective-permute-start.9
  121.1 3.3 %collective-permute-done.9 = f32[128,512]{1,0:T(8,128)S(1)} collective-permute-done((f32[128,512]{1,0:T(8,128)S(1)}, f32[128,512]{1,0:T(8,128)S(1)}, u32[]{:S(2)}, u32[]{:S(2)}) %collective-permute-start.9) | collective-permute-done | bytes 262176 | tf_op jit(solution)/shard_map/ppermute | solution.py:55
  124.4 8.6 %collective-permute-start.10 = (f32[128,512]{1,0:T(8,128)S(1)}, f32[128,512]{1,0:T(8,128)S(1)}, u32[]{:S(2)}, u32[]{:S(2)}) collective-permute-start(f32[128,512]{1,0:T(8,128)S(1)} %broadcast_select_fusion.3), channel_id=1, source_target_pairs={{0,8},{4,12},{8,0},{12,4},{16,24},{20,28},{24,16},{28,20},{32,40},... | collective-permute-start | bytes 786440 | tf_op jit(solution)/shard_map/ppermute | solution.py:61
  133.0 4.2 %collective-permute-done.10 = f32[128,512]{1,0:T(8,128)S(1)} collective-permute-done((f32[128,512]{1,0:T(8,128)S(1)}, f32[128,512]{1,0:T(8,128)S(1)}, u32[]{:S(2)}, u32[]{:S(2)}) %collective-permute-start.10) | collective-permute-done | bytes 262176 | tf_op jit(solution)/shard_map/ppermute | solution.py:61
  137.3 3.4 %collective-permute-start.11 = (f32[128,1024]{1,0:T(8,128)S(1)}, f32[128,1024]{1,0:T(8,128)S(1)}, u32[]{:S(2)}, u32[]{:S(2)}) collective-permute-start(f32[128,1024]{1,0:T(8,128)S(1)} %maximum_select_fusion.1), channel_id=1, source_target_pairs={{0,4},{4,0},{8,12},{12,8},{16,20},{20,16},{24,28},{28,24},{32,36},... | collective-permute-start | bytes 1572872 | tf_op jit(solution)/shard_map/ppermute | solution.py:63
  140.6 1.5 collective-permute-done.11
  142.2 6.5 %fusion = f32[128,512]{1,0:T(8,128)S(1)} fusion(f32[128,512]{1,0:T(8,128)S(1)} %convolution_select_fusion, f32[512,2048]{1,0:T(8,128)} %all-gather.3.cloned.1.call-done, f32[128,1024]{1,0:T(8,128)S(1)} %copy-done, pred[]{:T(512)S(6)} %lt.41, f32[128,512]{1,0:T(8,128)S(1)} %get-tuple-element.12, f32[128,512]{1,0:T(8,128)S(1)} %get-tuple-element.10, ...), kind=kOutput, calls=%fused_computation.2 | convolution fusion | flops 1612578816 | bytes 6029314 | tf_op jit(solution)/shard_map/dot_general | solution.py:8
  148.7 6.5 %convolution_subtract_fusion = f32[128,512]{1,0:T(8,128)S(1)} fusion(f32[512,2048]{1,0:T(8,128)} %all-gather.5.cloned.1.call-done, f32[128,1024]{1,0:T(8,128)S(1)} %copy-done, f32[128,512]{1,0:T(8,128)S(1)} %get-tuple-element.12, f32[128,512]{1,0:T(8,128)S(1)} %get-tuple-element.10, f32[128,512]{1,0:T(8,128)S(1)} %get-tuple-element.11, ...), kind=kOutput, calls=%fused_computation | convolution fusion | flops 1612513280 | bytes 5767169 | tf_op jit(solution)/shard_map/dot_general | solution.py:8
  155.2 0.8 pad_maximum_fusion
  (26 shorter events, 3.8 us)
Async XLA Ops:
  6.5 57.2 %copy-start = (f32[128,1024]{1,0:T(8,128)S(1)}, f32[128,1024]{1,0:T(8,128)}, u32[]{:S(2)}) copy-start(f32[128,1024]{1,0:T(8,128)} %param.3) | copy-start | bytes 1572868
  6.5 57.1 %all-gather.3.cloned.1.call-start = ((), (), s32[]{:S(2)}) async-start(), calls=%async_computation | async-start | bytes 5242880 | tf_op jit(solution)/shard_map/all_gather | solution.py:34
  9.8 138.9 %all-gather.5.cloned.1.call-start = ((), (), s32[]{:S(2)}) async-start(), calls=%async_computation.1 | async-start | bytes 5242880 | tf_op jit(solution)/shard_map/all_gather | solution.py:36
  66.1 2.1 %collective-permute-start = (f32[128,512]{1,0:T(8,128)S(1)}, f32[128,512]{1,0:T(8,128)S(1)}, u32[]{:S(2)}, u32[]{:S(2)}) collective-permute-start(f32[128,512]{1,0:T(8,128)S(1)} %fusion.11), channel_id=1, source_target_pairs={{0,4},{1,5},{2,6},{3,7}} | collective-permute-start | bytes 786440 | tf_op jit(solution)/shard_map/ppermute | solution.py:48
  66.8 1.4 collective-permute-start.1
  67.5 0.7 collective-permute-start.2
  72.9 1.4 collective-permute-start.3
  73.6 0.7 collective-permute-start.4
  79.2 0.7 collective-permute-start.5
  84.8 0.7 collective-permute-start.6
  85.6 28.6 %collective-permute-start.7 = (f32[128,512]{1,0:T(8,128)S(1)}, f32[128,512]{1,0:T(8,128)S(1)}, u32[]{:S(2)}, u32[]{:S(2)}) collective-permute-start(f32[128,512]{1,0:T(8,128)S(1)} %broadcast_select_fusion), channel_id=1, source_target_pairs={{0,64},{4,68},{8,72},{12,76},{128,192},{132,196},{136,200},{140,20... | collective-permute-start | bytes 786440 | tf_op jit(solution)/shard_map/ppermute | solution.py:55
  114.2 5.5 %collective-permute-start.8 = (f32[128,512]{1,0:T(8,128)S(1)}, f32[128,512]{1,0:T(8,128)S(1)}, u32[]{:S(2)}, u32[]{:S(2)}) collective-permute-start(f32[128,512]{1,0:T(8,128)S(1)} %broadcast_select_fusion.1), channel_id=1, source_target_pairs={{0,32},{4,36},{8,40},{12,44},{64,96},{68,100},{72,104},{76,108},{1... | collective-permute-start | bytes 786440 | tf_op jit(solution)/shard_map/ppermute | solution.py:55
  119.8 4.6 %collective-permute-start.9 = (f32[128,512]{1,0:T(8,128)S(1)}, f32[128,512]{1,0:T(8,128)S(1)}, u32[]{:S(2)}, u32[]{:S(2)}) collective-permute-start(f32[128,512]{1,0:T(8,128)S(1)} %broadcast_select_fusion.2), channel_id=1, source_target_pairs={{0,16},{4,20},{8,24},{12,28},{32,48},{36,52},{40,56},{44,60},{64,8... | collective-permute-start | bytes 786440 | tf_op jit(solution)/shard_map/ppermute | solution.py:55
  124.4 12.8 %collective-permute-start.10 = (f32[128,512]{1,0:T(8,128)S(1)}, f32[128,512]{1,0:T(8,128)S(1)}, u32[]{:S(2)}, u32[]{:S(2)}) collective-permute-start(f32[128,512]{1,0:T(8,128)S(1)} %broadcast_select_fusion.3), channel_id=1, source_target_pairs={{0,8},{4,12},{8,0},{12,4},{16,24},{20,28},{24,16},{28,20},{32,40},... | collective-permute-start | bytes 786440 | tf_op jit(solution)/shard_map/ppermute | solution.py:61
  137.3 4.9 %collective-permute-start.11 = (f32[128,1024]{1,0:T(8,128)S(1)}, f32[128,1024]{1,0:T(8,128)S(1)}, u32[]{:S(2)}, u32[]{:S(2)}) collective-permute-start(f32[128,1024]{1,0:T(8,128)S(1)} %maximum_select_fusion.1), channel_id=1, source_target_pairs={{0,4},{4,0},{8,12},{12,8},{16,20},{20,16},{24,28},{28,24},{32,36},... | collective-permute-start | bytes 1572872 | tf_op jit(solution)/shard_map/ppermute | solution.py:63
Sparse Core Ops, SparseCore 0:
  9.9 53.6 all-gather.2
  65.5 51.1 all-gather.4

commit v9 on v8

--- a/solution.py
+++ b/solution.py
@@ -35,17 +35,28 @@
     second_rows, _ = lax.optimization_barrier((factor[block:], lower_first))
     lower_second = lax.all_gather(second_rows, "pcol", axis=1, tiled=True)
 
+    first_rhs = top_rhs
+    for i in range(1, steps):
+        pairs = [(at(0, c), at(i, c)) for c in range(n_col)]
+        first_rhs = jnp.where(row_at == i, lax.ppermute(top_rhs, AXES, pairs), first_rhs)
+
     acc = jnp.zeros((rhs_width, block), jnp.float32)
     own = jnp.zeros((rhs_width, block), jnp.float32)
     for k in range(steps):
-        solved = contract(top_rhs - acc, inverses[k * block : (k + 1) * block])
+        if k == 0:
+            solved = contract(first_rhs, inverses[:block])
+        else:
+            solved = contract(top_rhs - acc, inverses[k * block : (k + 1) * block])
         own = jnp.where(row_at == k, solved, own)
         if k == steps - 1:
             break
-        arrived = jnp.zeros_like(solved)
-        for i in range(k + 1, steps):
-            pairs = [(at(k, c), at(i, c)) for c in range(n_col)]
-            arrived = arrived + lax.ppermute(solved, AXES, pairs)
+        if k == 0:
+            arrived = solved
+        else:
+            arrived = jnp.zeros_like(solved)
+            for i in range(k + 1, steps):
+                pairs = [(at(k, c), at(i, c)) for c in range(n_col)]
+                arrived = arrived + lax.ppermute(solved, AXES, pairs)
         acc = acc + contract(arrived, lower_first[:, k * block : (k + 1) * block])
 
     piece = own

time: 165 us -> 167 us (1.012)
  starting transfers between devices: 20.7 us -> 23.5 us
    ppermute x1, starting transfers between devices: 8.61 us -> 11.6 us  [per_device(): other = lax.ppermute(piece, 'prow', [(p, p ^ 2) for p in range(n_row)])]
    ppermute x0 -> x3, starting transfers between devices: none -> 2.03 us  [per_device(): lax.ppermute(top_rhs, AXES, pairs)]
    ppermute x6 -> x3, starting transfers between devices: 4.06 us -> 2.03 us  [per_device(): arrived = arrived + lax.ppermute(solved, AXES, pairs)]
  transfers between devices with their start and end apart: 14 -> 14, of which waited for: 6 -> 6; matrix products, arithmetic and copies ran while one was open for 15% -> 14% of each run, Pallas kernels for 0% -> 0%
where the time goes in v9:
time: 167 us; the launch traced here: 165 us
  waiting for transfers between devices  93.1 us (56%)
  matrix products  29.9 us (18%)
  starting transfers between devices  23.5 us (14%)
  between operations  13.7 us (8%)
  local copies, waits for them, and re-layouts  3.32 us (2%)
    all_gather x1, waiting for transfers between devices, per_device(): lower_first = lax.all_gather(factor[:block], 'pcol', axis=1, tiled=True)  53.8 us
    ppermute x4, waiting for transfers between devices, per_device(): arrived = lax.ppermute(piece, 'prow', pairs)  33.5 us
    dot_general x9, matrix products, contract(): lax.dot_general(left, right, (((1,), (1,)), ((), ())), precision=lax.Prec...  29.9 us
    ppermute x1, starting transfers between devices, per_device(): other = lax.ppermute(piece, 'prow', [(p, p ^ 2) for p in range(n_row)])  11.6 us
    ppermute x4, starting transfers between devices, per_device(): arrived = lax.ppermute(piece, 'prow', pairs)  4.58 us
    ppermute x1, waiting for transfers between devices, per_device(): other = lax.ppermute(piece, 'prow', [(p, p ^ 2) for p in range(n_row)])  4.24 us
  transfers between devices with their start and end apart: 14, of which 6 were waited for; matrix products, arithmetic and copies ran while one was open for 14% of the time, Pallas kernels for 0%

profile of v9, /device:TPU:7, one launch (start us, length us, event | category | flops | bytes accessed | tf_op | source)
XLA Modules:
  0.0 164.6 jit_solution(16373685961116259796)
XLA Ops:
  6.5 3.2 %fusion.27 = (f32[512,512]{1,0:T(8,128)}, f32[512,512]{1,0:T(8,128)}) fusion(f32[1024,512]{1,0:T(8,128)} %param.4), kind=kLoop, calls=%fused_computation.39 | loop fusion | bytes 4194304 | tf_op jit(solution)/shard_map/slice | solution.py:34
  9.8 53.8 %all-gather.3.cloned.1.call-done = f32[512,2048]{1,0:T(8,128)} async-done(((f32[512,512]{1,0:T(8,128)}), f32[512,2048]{1,0:T(8,128)}) %all-gather.3.cloned.1.call-update) | async-done | bytes 4194320 | tf_op jit(solution)/shard_map/all_gather | solution.py:34
  65.1 0.7 collective-permute-start.2
  65.8 2.4 %fusion.11 = f32[128,512]{1,0:T(8,128)S(1)} fusion(f32[2048,512]{1,0:T(8,128)} %param.5, f32[128,512]{1,0:T(8,128)S(1)} %collective-permute-done, f32[128,512]{1,0:T(8,128)S(1)} %collective-permute-done.1, f32[128,512]{1,0:T(8,128)S(1)} %collective-permute-done.2, pred[]{:T(512)S(6)} %eq.30, pred[]{:T(512)S(6)} %eq.29, pred[]{:T(512)S(6)} %eq.28, ...), kind=kOutput, calls=%fused_computation.17 | convolution fusion | flops 402849792 | bytes 2359299 | tf_op jit(solution)/shard_map/dot_general | solution.py:8
  68.2 2.4 %fusion.4 = f32[128,512]{1,0:T(8,128)S(1)} fusion(f32[128,512]{1,0:T(8,128)S(1)} %fusion.11, f32[512,2048]{1,0:T(8,128)} %all-gather.3.cloned.1.call-done), kind=kOutput, calls=%fused_computation.9 | convolution fusion | flops 402653184 | bytes 1572864 | tf_op jit(solution)/shard_map/dot_general | solution.py:8
  70.6 2.4 %fusion.9 = f32[128,512]{1,0:T(8,128)S(1)} fusion(f32[2048,512]{1,0:T(8,128)} %param.5, f32[128,512]{1,0:T(8,128)S(1)} %fusion.4, f32[128,1024]{1,0:T(8,128)S(1)} %copy-done), kind=kOutput, calls=%fused_computation.15 | convolution fusion | flops 402718720 | bytes 1835008 | tf_op jit(solution)/shard_map/dot_general | solution.py:8
  73.0 0.7 collective-permute-start.3
  74.4 2.4 %convolution_add_fusion.1 = f32[128,512]{1,0:T(8,128)S(1)} fusion(f32[128,512]{1,0:T(8,128)S(1)} %fusion.4, f32[512,2048]{1,0:T(8,128)} %all-gather.3.cloned.1.call-done, f32[128,512]{1,0:T(8,128)S(1)} %collective-permute-done.3, f32[128,512]{1,0:T(8,128)S(1)} %collective-permute-done.4), kind=kOutput, calls=%fused_computation.6 | convolution fusion | flops 402784256 | bytes 2097152 | tf_op jit(solution)/shard_map/dot_general | solution.py:8
  76.8 2.5 %fusion.7 = f32[128,512]{1,0:T(8,128)S(1)} fusion(f32[2048,512]{1,0:T(8,128)} %param.5, f32[128,512]{1,0:T(8,128)S(1)} %convolution_add_fusion.1, f32[128,1024]{1,0:T(8,128)S(1)} %copy-done), kind=kOutput, calls=%fused_computation.13 | convolution fusion | flops 402718720 | bytes 1835008 | tf_op jit(solution)/shard_map/dot_general | solution.py:8
  80.0 2.5 %fusion.1 = f32[128,512]{1,0:T(8,128)S(1)} fusion(f32[128,512]{1,0:T(8,128)S(1)} %convolution_add_fusion.1, f32[128,512]{1,0:T(8,128)S(1)} %collective-permute-done.5, f32[512,2048]{1,0:T(8,128)} %all-gather.3.cloned.1.call-done, f32[128,1024]{1,0:T(8,128)S(1)} %copy-done), kind=kOutput, calls=%fused_computation.5 | convolution fusion | flops 402784256 | bytes 2097152 | tf_op jit(solution)/shard_map/dot_general | solution.py:8
  82.5 2.4 %convolution_select_fusion = f32[128,512]{1,0:T(8,128)S(1)} fusion(f32[128,512]{1,0:T(8,128)S(1)} %fusion.1, f32[2048,512]{1,0:T(8,128)} %param.5, f32[128,512]{1,0:T(8,128)S(1)} %fusion.7, f32[128,512]{1,0:T(8,128)S(1)} %fusion.9, f32[128,512]{1,0:T(8,128)S(1)} %fusion.11, pred[]{:T(512)S(6)} %eq.31, pred[]{:T(512)S(6)} %eq.30, pred[]{:T(512)S(6)} %eq.29, ...), kind=kOutput, calls=%fused_computation.3 | convolution fusion | flops 402915328 | bytes 2359300 | tf_op jit(solution)/shard_map/dot_general | solution.py:8
  85.6 1.3 collective-permute-start.7
  86.9 26.5 %collective-permute-done.7 = f32[128,512]{1,0:T(8,128)S(1)} collective-permute-done((f32[128,512]{1,0:T(8,128)S(1)}, f32[128,512]{1,0:T(8,128)S(1)}, u32[]{:S(2)}, u32[]{:S(2)}) %collective-permute-start.7) | collective-permute-done | bytes 262176 | tf_op jit(solution)/shard_map/ppermute | solution.py:66
  113.5 1.3 collective-permute-start.8
  114.8 3.7 %collective-permute-done.8 = f32[128,512]{1,0:T(8,128)S(1)} collective-permute-done((f32[128,512]{1,0:T(8,128)S(1)}, f32[128,512]{1,0:T(8,128)S(1)}, u32[]{:S(2)}, u32[]{:S(2)}) %collective-permute-start.8) | collective-permute-done | bytes 262176 | tf_op jit(solution)/shard_map/ppermute | solution.py:66
  118.6 1.3 collective-permute-start.9
  119.9 3.3 %collective-permute-done.9 = f32[128,512]{1,0:T(8,128)S(1)} collective-permute-done((f32[128,512]{1,0:T(8,128)S(1)}, f32[128,512]{1,0:T(8,128)S(1)}, u32[]{:S(2)}, u32[]{:S(2)}) %collective-permute-start.9) | collective-permute-done | bytes 262176 | tf_op jit(solution)/shard_map/ppermute | solution.py:66
  123.2 11.6 %collective-permute-start.10 = (f32[128,512]{1,0:T(8,128)S(1)}, f32[128,512]{1,0:T(8,128)S(1)}, u32[]{:S(2)}, u32[]{:S(2)}) collective-permute-start(f32[128,512]{1,0:T(8,128)S(1)} %broadcast_select_fusion.3), channel_id=1, source_target_pairs={{0,8},{4,12},{8,0},{12,4},{16,24},{20,28},{24,16},{28,20},{32,40},... | collective-permute-start | bytes 786440 | tf_op jit(solution)/shard_map/ppermute | solution.py:72
  134.7 4.2 %collective-permute-done.10 = f32[128,512]{1,0:T(8,128)S(1)} collective-permute-done((f32[128,512]{1,0:T(8,128)S(1)}, f32[128,512]{1,0:T(8,128)S(1)}, u32[]{:S(2)}, u32[]{:S(2)}) %collective-permute-start.10) | collective-permute-done | bytes 262176 | tf_op jit(solution)/shard_map/ppermute | solution.py:72
  139.0 3.3 %collective-permute-start.11 = (f32[128,1024]{1,0:T(8,128)S(1)}, f32[128,1024]{1,0:T(8,128)S(1)}, u32[]{:S(2)}, u32[]{:S(2)}) collective-permute-start(f32[128,1024]{1,0:T(8,128)S(1)} %maximum_select_fusion.1), channel_id=1, source_target_pairs={{0,4},{4,0},{8,12},{12,8},{16,20},{20,16},{24,28},{28,24},{32,36},... | collective-permute-start | bytes 1572872 | tf_op jit(solution)/shard_map/ppermute | solution.py:74
  142.4 1.5 collective-permute-done.11
  143.9 6.5 %fusion = f32[128,512]{1,0:T(8,128)S(1)} fusion(f32[128,512]{1,0:T(8,128)S(1)} %convolution_select_fusion, f32[512,2048]{1,0:T(8,128)} %all-gather.3.cloned.1.call-done, pred[]{:T(512)S(6)} %lt.41, f32[128,512]{1,0:T(8,128)S(1)} %get-tuple-element.12, f32[128,512]{1,0:T(8,128)S(1)} %get-tuple-element.10, f32[128,512]{1,0:T(8,128)S(1)} %get-tuple-element.11, ...), kind=kOutput, calls=%fused_computation.2 | convolution fusion | flops 1612578816 | bytes 6029314 | tf_op jit(solution)/shard_map/dot_general | solution.py:8
  150.4 6.5 %convolution_subtract_fusion = f32[128,512]{1,0:T(8,128)S(1)} fusion(f32[512,2048]{1,0:T(8,128)} %all-gather.5.cloned.1.call-done, f32[128,1024]{1,0:T(8,128)S(1)} %copy-done, f32[128,512]{1,0:T(8,128)S(1)} %get-tuple-element.12, f32[128,512]{1,0:T(8,128)S(1)} %get-tuple-element.10, f32[128,512]{1,0:T(8,128)S(1)} %get-tuple-element.11, ...), kind=kOutput, calls=%fused_computation | convolution fusion | flops 1612513280 | bytes 5767169 | tf_op jit(solution)/shard_map/dot_general | solution.py:8
  156.9 0.8 pad_maximum_fusion
  (27 shorter events, 3.8 us)
Async XLA Ops:
  6.5 57.2 %copy-start = (f32[128,1024]{1,0:T(8,128)S(1)}, f32[128,1024]{1,0:T(8,128)}, u32[]{:S(2)}) copy-start(f32[128,1024]{1,0:T(8,128)} %param.3) | copy-start | bytes 1572868
  6.5 57.1 %all-gather.3.cloned.1.call-start = ((), (), s32[]{:S(2)}) async-start(), calls=%async_computation | async-start | bytes 5242880 | tf_op jit(solution)/shard_map/all_gather | solution.py:34
  9.8 140.6 %all-gather.5.cloned.1.call-start = ((), (), s32[]{:S(2)}) async-start(), calls=%async_computation.1 | async-start | bytes 5242880 | tf_op jit(solution)/shard_map/all_gather | solution.py:36
  63.7 2.1 %collective-permute-start = (f32[128,512]{1,0:T(8,128)S(1)}, f32[128,512]{1,0:T(8,128)S(1)}, u32[]{:S(2)}, u32[]{:S(2)}) collective-permute-start(f32[128,512]{1,0:T(8,128)S(1)} %slice.46), channel_id=1, source_target_pairs={{0,12},{1,13},{2,14},{3,15}} | collective-permute-start | bytes 786440 | tf_op jit(solution)/shard_map/ppermute | solution.py:41
  64.4 1.4 collective-permute-start.1
  65.1 0.7 collective-permute-start.2
  73.0 1.4 collective-permute-start.3
  73.7 0.7 collective-permute-start.4
  79.3 0.7 collective-permute-start.5
  84.9 0.7 collective-permute-start.6
  85.6 27.8 %collective-permute-start.7 = (f32[128,512]{1,0:T(8,128)S(1)}, f32[128,512]{1,0:T(8,128)S(1)}, u32[]{:S(2)}, u32[]{:S(2)}) collective-permute-start(f32[128,512]{1,0:T(8,128)S(1)} %broadcast_select_fusion), channel_id=1, source_target_pairs={{0,64},{4,68},{8,72},{12,76},{128,192},{132,196},{136,200},{140,20... | collective-permute-start | bytes 786440 | tf_op jit(solution)/shard_map/ppermute | solution.py:66
  113.5 5.0 %collective-permute-start.8 = (f32[128,512]{1,0:T(8,128)S(1)}, f32[128,512]{1,0:T(8,128)S(1)}, u32[]{:S(2)}, u32[]{:S(2)}) collective-permute-start(f32[128,512]{1,0:T(8,128)S(1)} %broadcast_select_fusion.1), channel_id=1, source_target_pairs={{0,32},{4,36},{8,40},{12,44},{64,96},{68,100},{72,104},{76,108},{1... | collective-permute-start | bytes 786440 | tf_op jit(solution)/shard_map/ppermute | solution.py:66
  118.6 4.6 %collective-permute-start.9 = (f32[128,512]{1,0:T(8,128)S(1)}, f32[128,512]{1,0:T(8,128)S(1)}, u32[]{:S(2)}, u32[]{:S(2)}) collective-permute-start(f32[128,512]{1,0:T(8,128)S(1)} %broadcast_select_fusion.2), channel_id=1, source_target_pairs={{0,16},{4,20},{8,24},{12,28},{32,48},{36,52},{40,56},{44,60},{64,8... | collective-permute-start | bytes 786440 | tf_op jit(solution)/shard_map/ppermute | solution.py:66
  123.2 15.8 %collective-permute-start.10 = (f32[128,512]{1,0:T(8,128)S(1)}, f32[128,512]{1,0:T(8,128)S(1)}, u32[]{:S(2)}, u32[]{:S(2)}) collective-permute-start(f32[128,512]{1,0:T(8,128)S(1)} %broadcast_select_fusion.3), channel_id=1, source_target_pairs={{0,8},{4,12},{8,0},{12,4},{16,24},{20,28},{24,16},{28,20},{32,40},... | collective-permute-start | bytes 786440 | tf_op jit(solution)/shard_map/ppermute | solution.py:72
  139.0 4.8 %collective-permute-start.11 = (f32[128,1024]{1,0:T(8,128)S(1)}, f32[128,1024]{1,0:T(8,128)S(1)}, u32[]{:S(2)}, u32[]{:S(2)}) collective-permute-start(f32[128,1024]{1,0:T(8,128)S(1)} %maximum_select_fusion.1), channel_id=1, source_target_pairs={{0,4},{4,0},{8,12},{12,8},{16,20},{20,16},{24,28},{28,24},{32,36},... | collective-permute-start | bytes 1572872 | tf_op jit(solution)/shard_map/ppermute | solution.py:74
Sparse Core Ops, SparseCore 0:
  9.9 53.6 all-gather.2
  65.5 51.1 all-gather.4

commit v10 on v9

--- a/solution.py
+++ b/solution.py
@@ -31,14 +31,15 @@
 
     top_rhs = right_side[:, :block]
 
-    lower_first = lax.all_gather(factor[:block], "pcol", axis=1, tiled=True)
-    second_rows, _ = lax.optimization_barrier((factor[block:], lower_first))
-    lower_second = lax.all_gather(second_rows, "pcol", axis=1, tiled=True)
-
     first_rhs = top_rhs
     for i in range(1, steps):
         pairs = [(at(0, c), at(i, c)) for c in range(n_col)]
         first_rhs = jnp.where(row_at == i, lax.ppermute(top_rhs, AXES, pairs), first_rhs)
+
+    first_rhs, first_rows = lax.optimization_barrier((first_rhs, factor[:block]))
+    lower_first = lax.all_gather(first_rows, "pcol", axis=1, tiled=True)
+    second_rows, _ = lax.optimization_barrier((factor[block:], lower_first))
+    lower_second = lax.all_gather(second_rows, "pcol", axis=1, tiled=True)
 
     acc = jnp.zeros((rhs_width, block), jnp.float32)
     own = jnp.zeros((rhs_width, block), jnp.float32)

time: 167 us -> 159 us (0.952)
  waiting for transfers between devices: 93.1 us -> 87.9 us
  starting transfers between devices: 23.5 us -> 20.1 us
    ppermute x4, waiting for transfers between devices: 33.5 us -> 28.1 us  [per_device(): arrived = lax.ppermute(piece, 'prow', pairs)]
    ppermute x1, starting transfers between devices: 11.6 us -> 8.2 us  [per_device(): other = lax.ppermute(piece, 'prow', [(p, p ^ 2) for p in range(n_row)])]
  transfers between devices with their start and end apart: 14 -> 14, of which waited for: 6 -> 6; matrix products, arithmetic and copies ran while one was open for 14% -> 17% of each run, Pallas kernels for 0% -> 0%
where the time goes in v10:
time: 159 us; the launch traced here: 157 us
  waiting for transfers between devices  87.9 us (55%)
  matrix products  29.9 us (19%)
  starting transfers between devices  20.1 us (13%)
  between operations  13.7 us (9%)
  local copies, waits for them, and re-layouts  4.29 us (3%)
    all_gather x1, waiting for transfers between devices, per_device(): lower_first = lax.all_gather(first_rows, 'pcol', axis=1, tiled=True)  53.8 us
    dot_general x9, matrix products, contract(): lax.dot_general(left, right, (((1,), (1,)), ((), ())), precision=lax.Prec...  29.9 us
    ppermute x4, waiting for transfers between devices, per_device(): arrived = lax.ppermute(piece, 'prow', pairs)  28.1 us
    ppermute x1, starting transfers between devices, per_device(): other = lax.ppermute(piece, 'prow', [(p, p ^ 2) for p in range(n_row)])  8.2 us
    ppermute x4, starting transfers between devices, per_device(): arrived = lax.ppermute(piece, 'prow', pairs)  4.58 us
    ppermute x1, waiting for transfers between devices, per_device(): other = lax.ppermute(piece, 'prow', [(p, p ^ 2) for p in range(n_row)])  4.34 us
    ppermute x1, starting transfers between devices, per_device(): theirs = lax.ppermute(pair, 'prow', [(p, p ^ 1) for p in range(n_row)])  3.19 us
  transfers between devices with their start and end apart: 14, of which 6 were waited for; matrix products, arithmetic and copies ran while one was open for 17% of the time, Pallas kernels for 0%

profile of v10, /device:TPU:7, one launch (start us, length us, event | category | flops | bytes accessed | tf_op | source)
XLA Modules:
  0.0 157.0 jit_solution(7969996735936644664)
XLA Ops:
  6.5 1.0 slice.46
  7.6 0.7 collective-permute-start
  9.6 3.2 %fusion.20 = (f32[512,512]{1,0:T(8,128)}, f32[512,512]{1,0:T(8,128)}) fusion(f32[1024,512]{1,0:T(8,128)} %param.4), kind=kLoop, calls=%fused_computation.33 | loop fusion | bytes 4194304 | tf_op jit(solution)/shard_map/slice | solution.py:39
  13.0 53.8 %all-gather.3.cloned.1.call-done = f32[512,2048]{1,0:T(8,128)} async-done(((f32[512,512]{1,0:T(8,128)}), f32[512,2048]{1,0:T(8,128)}) %all-gather.3.cloned.1.call-update) | async-done | bytes 4194320 | tf_op jit(solution)/shard_map/all_gather | solution.py:40
  66.9 2.4 %fusion.11 = f32[128,512]{1,0:T(8,128)S(1)} fusion(f32[128,512]{1,0:T(8,128)S(1)} %select_select_fusion, f32[2048,512]{1,0:T(8,128)} %param.5), kind=kOutput, calls=%fused_computation.17 | convolution fusion | flops 402653184 | bytes 1572864 | tf_op jit(solution)/shard_map/dot_general | solution.py:8
  69.2 2.4 %fusion.4 = f32[128,512]{1,0:T(8,128)S(1)} fusion(f32[128,512]{1,0:T(8,128)S(1)} %fusion.11, f32[512,2048]{1,0:T(8,128)} %all-gather.3.cloned.1.call-done), kind=kOutput, calls=%fused_computation.9 | convolution fusion | flops 402653184 | bytes 1572864 | tf_op jit(solution)/shard_map/dot_general | solution.py:8
  71.6 2.4 %fusion.9 = f32[128,512]{1,0:T(8,128)S(1)} fusion(f32[2048,512]{1,0:T(8,128)} %param.5, f32[128,512]{1,0:T(8,128)S(1)} %fusion.4, f32[128,1024]{1,0:T(8,128)S(1)} %copy-done), kind=kOutput, calls=%fused_computation.15 | convolution fusion | flops 402718720 | bytes 1835008 | tf_op jit(solution)/shard_map/dot_general | solution.py:8
  75.4 2.4 %convolution_add_fusion.1 = f32[128,512]{1,0:T(8,128)S(1)} fusion(f32[128,512]{1,0:T(8,128)S(1)} %fusion.4, f32[512,2048]{1,0:T(8,128)} %all-gather.3.cloned.1.call-done, f32[128,512]{1,0:T(8,128)S(1)} %collective-permute-done.3, f32[128,512]{1,0:T(8,128)S(1)} %collective-permute-done.4), kind=kOutput, calls=%fused_computation.6 | convolution fusion | flops 402784256 | bytes 2097152 | tf_op jit(solution)/shard_map/dot_general | solution.py:8
  77.8 2.4 %fusion.7 = f32[128,512]{1,0:T(8,128)S(1)} fusion(f32[2048,512]{1,0:T(8,128)} %param.5, f32[128,512]{1,0:T(8,128)S(1)} %convolution_add_fusion.1, f32[128,1024]{1,0:T(8,128)S(1)} %copy-done), kind=kOutput, calls=%fused_computation.13 | convolution fusion | flops 402718720 | bytes 1835008 | tf_op jit(solution)/shard_map/dot_general | solution.py:8
  80.9 2.5 %fusion.1 = f32[128,512]{1,0:T(8,128)S(1)} fusion(f32[128,512]{1,0:T(8,128)S(1)} %convolution_add_fusion.1, f32[128,512]{1,0:T(8,128)S(1)} %collective-permute-done.5, f32[512,2048]{1,0:T(8,128)} %all-gather.3.cloned.1.call-done, f32[128,1024]{1,0:T(8,128)S(1)} %copy-done), kind=kOutput, calls=%fused_computation.5 | convolution fusion | flops 402784256 | bytes 2097152 | tf_op jit(solution)/shard_map/dot_general | solution.py:8
  83.4 2.5 %convolution_select_fusion = f32[128,512]{1,0:T(8,128)S(1)} fusion(f32[128,512]{1,0:T(8,128)S(1)} %fusion.1, f32[2048,512]{1,0:T(8,128)} %param.5, f32[128,512]{1,0:T(8,128)S(1)} %fusion.7, f32[128,512]{1,0:T(8,128)S(1)} %fusion.9, f32[128,512]{1,0:T(8,128)S(1)} %fusion.11, pred[]{:T(512)S(6)} %eq.31, pred[]{:T(512)S(6)} %eq.30, pred[]{:T(512)S(6)} %eq.29, ...), kind=kOutput, calls=%fused_computation.3 | convolution fusion | flops 402915328 | bytes 2359300 | tf_op jit(solution)/shard_map/dot_general | solution.py:8
  86.7 1.3 collective-permute-start.7
  88.0 19.5 %collective-permute-done.7 = f32[128,512]{1,0:T(8,128)S(1)} collective-permute-done((f32[128,512]{1,0:T(8,128)S(1)}, f32[128,512]{1,0:T(8,128)S(1)}, u32[]{:S(2)}, u32[]{:S(2)}) %collective-permute-start.7) | collective-permute-done | bytes 262176 | tf_op jit(solution)/shard_map/ppermute | solution.py:67
  107.6 1.3 collective-permute-start.8
  108.9 5.3 %collective-permute-done.8 = f32[128,512]{1,0:T(8,128)S(1)} collective-permute-done((f32[128,512]{1,0:T(8,128)S(1)}, f32[128,512]{1,0:T(8,128)S(1)}, u32[]{:S(2)}, u32[]{:S(2)}) %collective-permute-start.8) | collective-permute-done | bytes 262176 | tf_op jit(solution)/shard_map/ppermute | solution.py:67
  114.3 1.3 collective-permute-start.9
  115.6 3.3 %collective-permute-done.9 = f32[128,512]{1,0:T(8,128)S(1)} collective-permute-done((f32[128,512]{1,0:T(8,128)S(1)}, f32[128,512]{1,0:T(8,128)S(1)}, u32[]{:S(2)}, u32[]{:S(2)}) %collective-permute-start.9) | collective-permute-done | bytes 262176 | tf_op jit(solution)/shard_map/ppermute | solution.py:67
  118.9 8.2 %collective-permute-start.10 = (f32[128,512]{1,0:T(8,128)S(1)}, f32[128,512]{1,0:T(8,128)S(1)}, u32[]{:S(2)}, u32[]{:S(2)}) collective-permute-start(f32[128,512]{1,0:T(8,128)S(1)} %broadcast_select_fusion.3), channel_id=1, source_target_pairs={{0,8},{4,12},{8,0},{12,4},{16,24},{20,28},{24,16},{28,20},{32,40},... | collective-permute-start | bytes 786440 | tf_op jit(solution)/shard_map/ppermute | solution.py:73
  127.1 4.3 %collective-permute-done.10 = f32[128,512]{1,0:T(8,128)S(1)} collective-permute-done((f32[128,512]{1,0:T(8,128)S(1)}, f32[128,512]{1,0:T(8,128)S(1)}, u32[]{:S(2)}, u32[]{:S(2)}) %collective-permute-start.10) | collective-permute-done | bytes 262176 | tf_op jit(solution)/shard_map/ppermute | solution.py:73
  131.5 3.2 %collective-permute-start.11 = (f32[128,1024]{1,0:T(8,128)S(1)}, f32[128,1024]{1,0:T(8,128)S(1)}, u32[]{:S(2)}, u32[]{:S(2)}) collective-permute-start(f32[128,1024]{1,0:T(8,128)S(1)} %maximum_select_fusion.1), channel_id=1, source_target_pairs={{0,4},{4,0},{8,12},{12,8},{16,20},{20,16},{24,28},{28,24},{32,36},... | collective-permute-start | bytes 1572872 | tf_op jit(solution)/shard_map/ppermute | solution.py:75
  134.7 1.5 collective-permute-done.11
  136.3 6.5 %fusion = f32[128,512]{1,0:T(8,128)S(1)} fusion(f32[128,512]{1,0:T(8,128)S(1)} %convolution_select_fusion, f32[512,2048]{1,0:T(8,128)} %all-gather.3.cloned.1.call-done, pred[]{:T(512)S(6)} %lt.41, f32[128,512]{1,0:T(8,128)S(1)} %get-tuple-element.16, f32[128,512]{1,0:T(8,128)S(1)} %get-tuple-element.14, f32[128,512]{1,0:T(8,128)S(1)} %get-tuple-element.15, ...), kind=kOutput, calls=%fused_computation.2 | convolution fusion | flops 1612578816 | bytes 6029314 | tf_op jit(solution)/shard_map/dot_general | solution.py:8
  142.8 6.5 %convolution_subtract_fusion = f32[128,512]{1,0:T(8,128)S(1)} fusion(f32[512,2048]{1,0:T(8,128)} %all-gather.5.cloned.1.call-done, f32[128,1024]{1,0:T(8,128)S(1)} %copy-done, f32[128,512]{1,0:T(8,128)S(1)} %get-tuple-element.16, f32[128,512]{1,0:T(8,128)S(1)} %get-tuple-element.14, f32[128,512]{1,0:T(8,128)S(1)} %get-tuple-element.15, ...), kind=kOutput, calls=%fused_computation | convolution fusion | flops 1612513280 | bytes 5767169 | tf_op jit(solution)/shard_map/dot_general | solution.py:8
  149.3 0.8 pad_maximum_fusion
  (28 shorter events, 4.5 us)
Async XLA Ops:
  6.5 6.3 %copy-start = (f32[128,1024]{1,0:T(8,128)S(1)}, f32[128,1024]{1,0:T(8,128)}, u32[]{:S(2)}) copy-start(f32[128,1024]{1,0:T(8,128)} %param.3) | copy-start | bytes 1572868
  6.5 60.3 %all-gather.3.cloned.1.call-start = ((), (), s32[]{:S(2)}) async-start(), calls=%async_computation | async-start | bytes 5242880 | tf_op jit(solution)/shard_map/all_gather | solution.py:40
  7.6 5.2 %collective-permute-start = (f32[128,512]{1,0:T(8,128)S(1)}, f32[128,512]{1,0:T(8,128)S(1)}, u32[]{:S(2)}, u32[]{:S(2)}) collective-permute-start(f32[128,512]{1,0:T(8,128)S(1)} %slice.46), channel_id=1, source_target_pairs={{0,12},{1,13},{2,14},{3,15}} | collective-permute-start | bytes 786440 | tf_op jit(solution)/shard_map/ppermute | solution.py:37
  8.3 4.6 %collective-permute-start.1 = (f32[128,512]{1,0:T(8,128)S(1)}, f32[128,512]{1,0:T(8,128)S(1)}, u32[]{:S(2)}, u32[]{:S(2)}) collective-permute-start(f32[128,512]{1,0:T(8,128)S(1)} %slice.46), channel_id=1, source_target_pairs={{0,8},{1,9},{2,10},{3,11}} | collective-permute-start | bytes 786440 | tf_op jit(solution)/shard_map/ppermute | solution.py:37
  8.9 3.9 %collective-permute-start.2 = (f32[128,512]{1,0:T(8,128)S(1)}, f32[128,512]{1,0:T(8,128)S(1)}, u32[]{:S(2)}, u32[]{:S(2)}) collective-permute-start(f32[128,512]{1,0:T(8,128)S(1)} %slice.46), channel_id=1, source_target_pairs={{0,4},{1,5},{2,6},{3,7}} | collective-permute-start | bytes 786440 | tf_op jit(solution)/shard_map/ppermute | solution.py:37
  13.0 129.8 %all-gather.5.cloned.1.call-start = ((), (), s32[]{:S(2)}) async-start(), calls=%async_computation.1 | async-start | bytes 5242880 | tf_op jit(solution)/shard_map/all_gather | solution.py:42
  74.0 1.4 collective-permute-start.3
  74.7 0.7 collective-permute-start.4
  80.2 0.7 collective-permute-start.5
  85.9 0.7 collective-permute-start.6
  86.7 20.9 %collective-permute-start.7 = (f32[128,512]{1,0:T(8,128)S(1)}, f32[128,512]{1,0:T(8,128)S(1)}, u32[]{:S(2)}, u32[]{:S(2)}) collective-permute-start(f32[128,512]{1,0:T(8,128)S(1)} %broadcast_select_fusion), channel_id=1, source_target_pairs={{0,64},{4,68},{8,72},{12,76},{128,192},{132,196},{136,200},{140,20... | collective-permute-start | bytes 786440 | tf_op jit(solution)/shard_map/ppermute | solution.py:67
  107.6 6.7 %collective-permute-start.8 = (f32[128,512]{1,0:T(8,128)S(1)}, f32[128,512]{1,0:T(8,128)S(1)}, u32[]{:S(2)}, u32[]{:S(2)}) collective-permute-start(f32[128,512]{1,0:T(8,128)S(1)} %broadcast_select_fusion.1), channel_id=1, source_target_pairs={{0,32},{4,36},{8,40},{12,44},{64,96},{68,100},{72,104},{76,108},{1... | collective-permute-start | bytes 786440 | tf_op jit(solution)/shard_map/ppermute | solution.py:67
  114.3 4.6 %collective-permute-start.9 = (f32[128,512]{1,0:T(8,128)S(1)}, f32[128,512]{1,0:T(8,128)S(1)}, u32[]{:S(2)}, u32[]{:S(2)}) collective-permute-start(f32[128,512]{1,0:T(8,128)S(1)} %broadcast_select_fusion.2), channel_id=1, source_target_pairs={{0,16},{4,20},{8,24},{12,28},{32,48},{36,52},{40,56},{44,60},{64,8... | collective-permute-start | bytes 786440 | tf_op jit(solution)/shard_map/ppermute | solution.py:67
  118.9 12.5 %collective-permute-start.10 = (f32[128,512]{1,0:T(8,128)S(1)}, f32[128,512]{1,0:T(8,128)S(1)}, u32[]{:S(2)}, u32[]{:S(2)}) collective-permute-start(f32[128,512]{1,0:T(8,128)S(1)} %broadcast_select_fusion.3), channel_id=1, source_target_pairs={{0,8},{4,12},{8,0},{12,4},{16,24},{20,28},{24,16},{28,20},{32,40},... | collective-permute-start | bytes 786440 | tf_op jit(solution)/shard_map/ppermute | solution.py:73
  131.5 4.7 %collective-permute-start.11 = (f32[128,1024]{1,0:T(8,128)S(1)}, f32[128,1024]{1,0:T(8,128)S(1)}, u32[]{:S(2)}, u32[]{:S(2)}) collective-permute-start(f32[128,1024]{1,0:T(8,128)S(1)} %maximum_select_fusion.1), channel_id=1, source_target_pairs={{0,4},{4,0},{8,12},{12,8},{16,20},{20,16},{24,28},{28,24},{32,36},... | collective-permute-start | bytes 1572872 | tf_op jit(solution)/shard_map/ppermute | solution.py:75
Sparse Core Ops, SparseCore 0:
  13.1 53.6 all-gather.2
  68.6 51.1 all-gather.4

commit v11 on v10

--- a/solution.py
+++ b/solution.py
@@ -37,9 +37,9 @@
         first_rhs = jnp.where(row_at == i, lax.ppermute(top_rhs, AXES, pairs), first_rhs)
 
     first_rhs, first_rows = lax.optimization_barrier((first_rhs, factor[:block]))
-    lower_first = lax.all_gather(first_rows, "pcol", axis=1, tiled=True)
+    lower_first = lax.all_to_all(jnp.tile(first_rows, (1, 4)), "pcol", 1, 1, tiled=True)
     second_rows, _ = lax.optimization_barrier((factor[block:], lower_first))
-    lower_second = lax.all_gather(second_rows, "pcol", axis=1, tiled=True)
+    lower_second = lax.all_to_all(jnp.tile(second_rows, (1, 4)), "pcol", 1, 1, tiled=True)
 
     acc = jnp.zeros((rhs_width, block), jnp.float32)
     own = jnp.zeros((rhs_width, block), jnp.float32)

time: 159 us -> 167 us (1.050)
  the two profiles are of different devices: /device:TPU:7 before, /device:TPU:32 now
where the time goes in v11:
time: 167 us; the launch traced here: 166 us
  waiting for transfers between devices  97.2 us (58%)
  matrix products  24.7 us (15%)
  starting transfers between devices  24.4 us (15%)
  local copies, waits for them, and re-layouts  18.5 us (11%)
    all_to_all x1, waiting for transfers between devices, per_device(): lax.all_to_all(jnp.tile(first_rows, (1, 4)), 'pcol', 1, 1, tiled=True)  43.9 us
    dot_general x9, matrix products, contract(): lax.dot_general(left, right, (((1,), (1,)), ((), ())), precision=lax.Prec...  24.7 us
    ppermute x4, waiting for transfers between devices, per_device(): arrived = lax.ppermute(piece, 'prow', pairs)  17.3 us
    all_to_all x1, waiting for transfers between devices, per_device(): lax.all_to_all(jnp.tile(second_rows, (1, 4)), 'pcol', 1, 1, tiled=True)  14.4 us
    ppermute x3, waiting for transfers between devices, per_device(): arrived = arrived + lax.ppermute(solved, AXES, pairs)  6.83 us
    ppermute x1, waiting for transfers between devices, per_device(): other = lax.ppermute(piece, 'prow', [(p, p ^ 2) for p in range(n_row)])  6.76 us
    ppermute x3, starting transfers between devices, per_device(): arrived = arrived + lax.ppermute(solved, AXES, pairs)  6.51 us
    ppermute x3, waiting for transfers between devices, per_device(): lax.ppermute(top_rhs, AXES, pairs)  6.11 us
  transfers between devices with their start and end apart: 14, of which 10 were waited for; matrix products, arithmetic and copies ran while one was open for 7% of the time, Pallas kernels for 0%

profile of v11, /device:TPU:32, one launch (start us, length us, event | category | flops | bytes accessed | tf_op | source)
XLA Modules:
  0.0 166.2 jit_solution(13730389937935826812)
XLA Ops:
  5.5 6.1 %collective-permute-done.1 = f32[128,512]{1,0:T(8,128)S(1)} collective-permute-done((f32[128,512]{1,0:T(8,128)S(1)}, f32[128,512]{1,0:T(8,128)S(1)}, u32[]{:S(2)}, u32[]{:S(2)}) %collective-permute-start.1) | collective-permute-done | bytes 262176 | tf_op jit(solution)/shard_map/ppermute | solution.py:37
  11.7 2.5 %tile.4 = f32[512,4,512]{2,0,1:T(8,128)} broadcast(f32[512,512]{1,0:T(8,128)S(1)} %get-tuple-element.9), dimensions={0,2} | broadcast | bytes 5242880 | tf_op jit(solution)/shard_map/tile | solution.py:40
  14.2 4.8 %all-to-all-start = ((f32[512,4,512]{2,0,1:T(8,128)}), f32[512,4,512]{2,0,1:T(8,128)}, u32[]{:S(2)}, u32[]{:S(2)}) async-start(f32[512,4,512]{2,0,1:T(8,128)} %tile.4), calls=%async_computation | async-start | bytes 8388608 | tf_op jit(solution)/shard_map/all_to_all | solution.py:40
  19.0 2.4 %fusion.11 = f32[128,512]{1,0:T(8,128)S(1)} fusion(f32[128,512]{1,0:T(8,128)S(1)} %select_select_fusion, f32[2048,512]{1,0:T(8,128)} %param.5), kind=kOutput, calls=%fused_computation.17 | convolution fusion | flops 402653184 | bytes 1572864 | tf_op jit(solution)/shard_map/dot_general | solution.py:8
  21.4 43.9 %all-to-all-done = f32[512,4,512]{2,0,1:T(8,128)} async-done(((f32[512,4,512]{2,0,1:T(8,128)}), f32[512,4,512]{2,0,1:T(8,128)}, u32[]{:S(2)}, u32[]{:S(2)}) %all-to-all-start) | async-done | bytes 4194336 | tf_op jit(solution)/shard_map/all_to_all | solution.py:40
  65.4 5.3 %copy.4 = f32[512,4,512]{0,2,1:T(8,128)} copy(f32[512,4,512]{2,0,1:T(8,128)} %all-to-all-done) | data formatting | bytes 8388608 | tf_op jit(solution)/shard_map/all_to_all | solution.py:40
  70.6 1.9 %fusion.4 = f32[128,512]{1,0:T(8,128)S(1)} fusion(f32[128,512]{1,0:T(8,128)S(1)} %fusion.11, f32[512,2048]{0,1:T(8,128)} %bitcast.8), kind=kOutput, calls=%fused_computation.9 | convolution fusion | flops 402653184 | bytes 1572864 | tf_op jit(solution)/shard_map/dot_general | solution.py:8
  72.6 2.4 %fusion.9 = f32[128,512]{1,0:T(8,128)S(1)} fusion(f32[2048,512]{1,0:T(8,128)} %param.5, f32[128,512]{1,0:T(8,128)S(1)} %fusion.4, f32[128,1024]{1,0:T(8,128)S(1)} %copy-done), kind=kOutput, calls=%fused_computation.15 | convolution fusion | flops 402718720 | bytes 1835008 | tf_op jit(solution)/shard_map/dot_general | solution.py:8
  77.0 5.7 %collective-permute-done.3 = f32[128,512]{1,0:T(8,128)S(1)} collective-permute-done((f32[128,512]{1,0:T(8,128)S(1)}, f32[128,512]{1,0:T(8,128)S(1)}, u32[]{:S(2)}, u32[]{:S(2)}) %collective-permute-start.3) | collective-permute-done | bytes 262176 | tf_op jit(solution)/shard_map/ppermute | solution.py:60
  82.7 1.9 %convolution_add_fusion.1 = f32[128,512]{1,0:T(8,128)S(1)} fusion(f32[128,512]{1,0:T(8,128)S(1)} %fusion.4, f32[512,2048]{0,1:T(8,128)} %bitcast.9, f32[128,512]{1,0:T(8,128)S(1)} %collective-permute-done.3, f32[128,512]{1,0:T(8,128)S(1)} %collective-permute-done.4), kind=kOutput, calls=%fused_computation.6 | convolution fusion | flops 402784256 | bytes 2097152 | tf_op jit(solution)/shard_map/dot_general | solution.py:8
  84.6 2.4 %fusion.7 = f32[128,512]{1,0:T(8,128)S(1)} fusion(f32[2048,512]{1,0:T(8,128)} %param.5, f32[128,512]{1,0:T(8,128)S(1)} %convolution_add_fusion.1, f32[128,1024]{1,0:T(8,128)S(1)} %copy-done), kind=kOutput, calls=%fused_computation.13 | convolution fusion | flops 402718720 | bytes 1835008 | tf_op jit(solution)/shard_map/dot_general | solution.py:8
  87.0 4.5 %collective-permute-start.5 = (f32[128,512]{1,0:T(8,128)S(1)}, f32[128,512]{1,0:T(8,128)S(1)}, u32[]{:S(2)}, u32[]{:S(2)}) collective-permute-start(f32[128,512]{1,0:T(8,128)S(1)} %fusion.7), channel_id=1, source_target_pairs={{8,12},{9,13},{10,14},{11,15}} | collective-permute-start | bytes 786440 | tf_op jit(solution)/shard_map/ppermute | solution.py:60
  92.7 1.9 %fusion.1 = f32[128,512]{1,0:T(8,128)S(1)} fusion(f32[128,512]{1,0:T(8,128)S(1)} %convolution_add_fusion.1, f32[128,512]{1,0:T(8,128)S(1)} %collective-permute-done.5, f32[512,2048]{0,1:T(8,128)} %bitcast.10, f32[128,1024]{1,0:T(8,128)S(1)} %copy-done), kind=kOutput, calls=%fused_computation.5 | convolution fusion | flops 402784256 | bytes 2097152 | tf_op jit(solution)/shard_map/dot_general | solution.py:8
  94.7 2.4 %convolution_select_fusion = f32[128,512]{1,0:T(8,128)S(1)} fusion(f32[128,512]{1,0:T(8,128)S(1)} %fusion.1, f32[2048,512]{1,0:T(8,128)} %param.5, f32[128,512]{1,0:T(8,128)S(1)} %fusion.7, f32[128,512]{1,0:T(8,128)S(1)} %fusion.9, f32[128,512]{1,0:T(8,128)S(1)} %fusion.11, pred[]{:T(512)S(6)} %eq.31, pred[]{:T(512)S(6)} %eq.30, pred[]{:T(512)S(6)} %eq.29, ...), kind=kOutput, calls=%fused_computation.3 | convolution fusion | flops 402915328 | bytes 2359300 | tf_op jit(solution)/shard_map/dot_general | solution.py:8
  98.4 2.5 %tile.5 = f32[512,4,512]{2,0,1:T(8,128)} broadcast(f32[512,512]{1,0:T(8,128)S(1)} %get-tuple-element.10), dimensions={0,2} | broadcast | bytes 5242880 | tf_op jit(solution)/shard_map/tile | solution.py:42
  100.9 4.8 %all-to-all-start.1 = ((f32[512,4,512]{2,0,1:T(8,128)}), f32[512,4,512]{2,0,1:T(8,128)}, u32[]{:S(2)}, u32[]{:S(2)}) async-start(f32[512,4,512]{2,0,1:T(8,128)} %tile.5), calls=%async_computation.1 | async-start | bytes 8388608 | tf_op jit(solution)/shard_map/all_to_all | solution.py:42
  107.2 6.3 %collective-permute-done.7 = f32[128,512]{1,0:T(8,128)S(1)} collective-permute-done((f32[128,512]{1,0:T(8,128)S(1)}, f32[128,512]{1,0:T(8,128)S(1)}, u32[]{:S(2)}, u32[]{:S(2)}) %collective-permute-start.7) | collective-permute-done | bytes 262176 | tf_op jit(solution)/shard_map/ppermute | solution.py:67
  114.8 5.7 %collective-permute-done.8 = f32[128,512]{1,0:T(8,128)S(1)} collective-permute-done((f32[128,512]{1,0:T(8,128)S(1)}, f32[128,512]{1,0:T(8,128)S(1)}, u32[]{:S(2)}, u32[]{:S(2)}) %collective-permute-start.8) | collective-permute-done | bytes 262176 | tf_op jit(solution)/shard_map/ppermute | solution.py:67
  122.0 5.2 %collective-permute-done.9 = f32[128,512]{1,0:T(8,128)S(1)} collective-permute-done((f32[128,512]{1,0:T(8,128)S(1)}, f32[128,512]{1,0:T(8,128)S(1)}, u32[]{:S(2)}, u32[]{:S(2)}) %collective-permute-start.9) | collective-permute-done | bytes 262176 | tf_op jit(solution)/shard_map/ppermute | solution.py:67
  127.3 6.8 %collective-permute-done.10 = f32[128,512]{1,0:T(8,128)S(1)} collective-permute-done((f32[128,512]{1,0:T(8,128)S(1)}, f32[128,512]{1,0:T(8,128)S(1)}, u32[]{:S(2)}, u32[]{:S(2)}) %collective-permute-start.10) | collective-permute-done | bytes 262176 | tf_op jit(solution)/shard_map/ppermute | solution.py:73
  136.3 4.6 %fusion = f32[128,512]{1,0:T(8,128)S(1)} fusion(f32[128,512]{1,0:T(8,128)S(1)} %convolution_select_fusion, f32[512,2048]{0,1:T(8,128)} %bitcast.11, pred[]{:T(512)S(6)} %lt.41, f32[128,512]{1,0:T(8,128)S(1)} %get-tuple-element.16, f32[128,512]{1,0:T(8,128)S(1)} %get-tuple-element.14, f32[128,512]{1,0:T(8,128)S(1)} %get-tuple-element.15, ...), kind=kOutput, calls=%fused_computation.2 | convolution fusion | flops 1612578816 | bytes 6029314 | tf_op jit(solution)/shard_map/dot_general | solution.py:8
  141.0 14.4 %all-to-all-done.1 = f32[512,4,512]{2,0,1:T(8,128)} async-done(((f32[512,4,512]{2,0,1:T(8,128)}), f32[512,4,512]{2,0,1:T(8,128)}, u32[]{:S(2)}, u32[]{:S(2)}) %all-to-all-start.1) | async-done | bytes 4194336 | tf_op jit(solution)/shard_map/all_to_all | solution.py:42
  155.4 5.3 %copy.5 = f32[512,4,512]{0,2,1:T(8,128)} copy(f32[512,4,512]{2,0,1:T(8,128)} %all-to-all-done.1) | data formatting | bytes 8388608 | tf_op jit(solution)/shard_map/all_to_all | solution.py:42
  160.7 4.6 %convolution_subtract_fusion = f32[128,512]{1,0:T(8,128)S(1)} fusion(f32[512,2048]{0,1:T(8,128)} %bitcast.12, f32[128,1024]{1,0:T(8,128)S(1)} %copy-done, f32[128,512]{1,0:T(8,128)S(1)} %get-tuple-element.16, f32[128,512]{1,0:T(8,128)S(1)} %get-tuple-element.14, f32[128,512]{1,0:T(8,128)S(1)} %get-tuple-element.15, f32[128,512]{1,0:T(8,128)S(1)} %get-tuple-element.13, ...), kind=kOutput, calls=%fused_computation | convolution fusion | flops 1612513280 | bytes 5767169 | tf_op jit(solution)/shard_map/dot_general | solution.py:8
  (30 shorter events, 17.1 us)
Async XLA Ops:
  0.0 11.6 %copy-start = (f32[128,1024]{1,0:T(8,128)S(1)}, f32[128,1024]{1,0:T(8,128)}, u32[]{:S(2)}) copy-start(f32[128,1024]{1,0:T(8,128)} %param.3) | copy-start | bytes 1572868
  1.0 4.4 %collective-permute-start = (f32[128,512]{1,0:T(8,128)S(1)}, f32[128,512]{1,0:T(8,128)S(1)}, u32[]{:S(2)}, u32[]{:S(2)}) collective-permute-start(f32[128,512]{1,0:T(8,128)S(1)} %slice.46), channel_id=1, source_target_pairs={{0,12},{1,13},{2,14},{3,15}} | collective-permute-start | bytes 786440 | tf_op jit(solution)/shard_map/ppermute | solution.py:37
  1.7 9.8 %collective-permute-start.1 = (f32[128,512]{1,0:T(8,128)S(1)}, f32[128,512]{1,0:T(8,128)S(1)}, u32[]{:S(2)}, u32[]{:S(2)}) collective-permute-start(f32[128,512]{1,0:T(8,128)S(1)} %slice.46), channel_id=1, source_target_pairs={{0,8},{1,9},{2,10},{3,11}} | collective-permute-start | bytes 786440 | tf_op jit(solution)/shard_map/ppermute | solution.py:37
  3.0 8.5 %collective-permute-start.2 = (f32[128,512]{1,0:T(8,128)S(1)}, f32[128,512]{1,0:T(8,128)S(1)}, u32[]{:S(2)}, u32[]{:S(2)}) collective-permute-start(f32[128,512]{1,0:T(8,128)S(1)} %slice.46), channel_id=1, source_target_pairs={{0,4},{1,5},{2,6},{3,7}} | collective-permute-start | bytes 786440 | tf_op jit(solution)/shard_map/ppermute | solution.py:37
  14.2 51.2 %all-to-all-start = ((f32[512,4,512]{2,0,1:T(8,128)}), f32[512,4,512]{2,0,1:T(8,128)}, u32[]{:S(2)}, u32[]{:S(2)}) async-start(f32[512,4,512]{2,0,1:T(8,128)} %tile.4), calls=%async_computation | async-start | bytes 8388608 | tf_op jit(solution)/shard_map/all_to_all | solution.py:40
  75.0 7.7 %collective-permute-start.3 = (f32[128,512]{1,0:T(8,128)S(1)}, f32[128,512]{1,0:T(8,128)S(1)}, u32[]{:S(2)}, u32[]{:S(2)}) collective-permute-start(f32[128,512]{1,0:T(8,128)S(1)} %fusion.9), channel_id=1, source_target_pairs={{4,8},{5,9},{6,10},{7,11}} | collective-permute-start | bytes 786440 | tf_op jit(solution)/shard_map/ppermute | solution.py:60
  76.3 6.4 %collective-permute-start.4 = (f32[128,512]{1,0:T(8,128)S(1)}, f32[128,512]{1,0:T(8,128)S(1)}, u32[]{:S(2)}, u32[]{:S(2)}) collective-permute-start(f32[128,512]{1,0:T(8,128)S(1)} %fusion.9), channel_id=1, source_target_pairs={{4,12},{5,13},{6,14},{7,15}} | collective-permute-start | bytes 786440 | tf_op jit(solution)/shard_map/ppermute | solution.py:60
  87.0 5.7 %collective-permute-start.5 = (f32[128,512]{1,0:T(8,128)S(1)}, f32[128,512]{1,0:T(8,128)S(1)}, u32[]{:S(2)}, u32[]{:S(2)}) collective-permute-start(f32[128,512]{1,0:T(8,128)S(1)} %fusion.7), channel_id=1, source_target_pairs={{8,12},{9,13},{10,14},{11,15}} | collective-permute-start | bytes 786440 | tf_op jit(solution)/shard_map/ppermute | solution.py:60
  97.1 8.7 %collective-permute-start.6 = (f32[128,512]{1,0:T(8,128)S(1)}, f32[128,512]{1,0:T(8,128)S(1)}, u32[]{:S(2)}, u32[]{:S(2)}) collective-permute-start(f32[128,512]{1,0:T(8,128)S(1)} %convolution_select_fusion), channel_id=1, source_target_pairs={{0,128},{4,132},{8,136},{12,140},{1,129},{5,133},{9,137},{13,141},... | collective-permute-start | bytes 786440 | tf_op jit(solution)/shard_map/ppermute | solution.py:67
  100.9 54.5 %all-to-all-start.1 = ((f32[512,4,512]{2,0,1:T(8,128)}), f32[512,4,512]{2,0,1:T(8,128)}, u32[]{:S(2)}, u32[]{:S(2)}) async-start(f32[512,4,512]{2,0,1:T(8,128)} %tile.5), calls=%async_computation.1 | async-start | bytes 8388608 | tf_op jit(solution)/shard_map/all_to_all | solution.py:42
  105.8 7.7 %collective-permute-start.7 = (f32[128,512]{1,0:T(8,128)S(1)}, f32[128,512]{1,0:T(8,128)S(1)}, u32[]{:S(2)}, u32[]{:S(2)}) collective-permute-start(f32[128,512]{1,0:T(8,128)S(1)} %broadcast_select_fusion), channel_id=1, source_target_pairs={{0,64},{4,68},{8,72},{12,76},{128,192},{132,196},{136,200},{140,20... | collective-permute-start | bytes 786440 | tf_op jit(solution)/shard_map/ppermute | solution.py:67
  113.5 7.1 %collective-permute-start.8 = (f32[128,512]{1,0:T(8,128)S(1)}, f32[128,512]{1,0:T(8,128)S(1)}, u32[]{:S(2)}, u32[]{:S(2)}) collective-permute-start(f32[128,512]{1,0:T(8,128)S(1)} %broadcast_select_fusion.1), channel_id=1, source_target_pairs={{0,32},{4,36},{8,40},{12,44},{64,96},{68,100},{72,104},{76,108},{1... | collective-permute-start | bytes 786440 | tf_op jit(solution)/shard_map/ppermute | solution.py:67
  120.6 6.5 %collective-permute-start.9 = (f32[128,512]{1,0:T(8,128)S(1)}, f32[128,512]{1,0:T(8,128)S(1)}, u32[]{:S(2)}, u32[]{:S(2)}) collective-permute-start(f32[128,512]{1,0:T(8,128)S(1)} %broadcast_select_fusion.2), channel_id=1, source_target_pairs={{0,16},{4,20},{8,24},{12,28},{32,48},{36,52},{40,56},{44,60},{64,8... | collective-permute-start | bytes 786440 | tf_op jit(solution)/shard_map/ppermute | solution.py:67
  127.2 6.9 %collective-permute-start.10 = (f32[128,512]{1,0:T(8,128)S(1)}, f32[128,512]{1,0:T(8,128)S(1)}, u32[]{:S(2)}, u32[]{:S(2)}) collective-permute-start(f32[128,512]{1,0:T(8,128)S(1)} %broadcast_select_fusion.3), channel_id=1, source_target_pairs={{0,8},{4,12},{8,0},{12,4},{16,24},{20,28},{24,16},{28,20},{32,40},... | collective-permute-start | bytes 786440 | tf_op jit(solution)/shard_map/ppermute | solution.py:73
  134.1 2.2 %collective-permute-start.11 = (f32[128,1024]{1,0:T(8,128)S(1)}, f32[128,1024]{1,0:T(8,128)S(1)}, u32[]{:S(2)}, u32[]{:S(2)}) collective-permute-start(f32[128,1024]{1,0:T(8,128)S(1)} %maximum_select_fusion.1), channel_id=1, source_target_pairs={{0,4},{4,0},{8,12},{12,8},{16,20},{20,16},{24,28},{28,24},{32,36},... | collective-permute-start | bytes 1572872 | tf_op jit(solution)/shard_map/ppermute | solution.py:75

commit v12 on v10

--- a/solution.py
+++ b/solution.py
@@ -61,13 +61,16 @@
         acc = acc + contract(arrived, lower_first[:, k * block : (k + 1) * block])
 
     piece = own
-    span = n_row // 2
-    while span >= steps:
-        pairs = [(p, p + span) for p in range(n_row) if p % (2 * span) < steps]
-        arrived = lax.ppermute(piece, "prow", pairs)
-        rel = row_at % (2 * span)
-        piece = jnp.where((rel >= span) & (rel < span + steps), arrived, piece)
-        span //= 2
+    fan_z = min(steps, n_row // steps)
+    stride_x = steps * fan_z
+    for stride, fan in ((stride_x, n_row // stride_x), (steps, fan_z)):
+        holders = [p for p in range(n_row) if p % (stride * fan) < steps]
+        received = piece
+        for hop in range(1, fan):
+            pairs = [(p, p + hop * stride) for p in holders]
+            arrived = lax.ppermute(piece, "prow", pairs)
+            received = jnp.where((row_at % (stride * fan)) // stride == hop, arrived, received)
+        piece = jnp.where(row_at % stride < steps, received, piece)
     b0 = row_at % 2
     b1 = (row_at // 2) % 2
     other = lax.ppermute(piece, "prow", [(p, p ^ 2) for p in range(n_row)])

time: 159 us -> 157 us (0.987)
  the two profiles are of different devices: /device:TPU:7 before, /device:TPU:3 now
where the time goes in v12:
time: 157 us
  waiting for transfers between devices  83.2 us (53%)
  matrix products  29.9 us (19%)
  starting transfers between devices  24.2 us (15%)
  between operations  13.8 us (9%)
  local copies, waits for them, and re-layouts  4.28 us (3%)
    all_gather x1, waiting for transfers between devices, per_device(): lower_first = lax.all_gather(first_rows, 'pcol', axis=1, tiled=True)  53.9 us
    dot_general x9, matrix products, contract(): lax.dot_general(left, right, (((1,), (1,)), ((), ())), precision=lax.Prec...  29.9 us
    ppermute x6, waiting for transfers between devices, per_device(): arrived = lax.ppermute(piece, 'prow', pairs)  22.2 us
    ppermute x1, starting transfers between devices, per_device(): other = lax.ppermute(piece, 'prow', [(p, p ^ 2) for p in range(n_row)])  11.6 us
    ppermute x6, starting transfers between devices, per_device(): arrived = lax.ppermute(piece, 'prow', pairs)  6.56 us
    ppermute x1, waiting for transfers between devices, per_device(): other = lax.ppermute(piece, 'prow', [(p, p ^ 2) for p in range(n_row)])  5.59 us
    slice x1, local copies, waits for them, and re-layouts, per_device(): factor[:block]  3.17 us
  transfers between devices with their start and end apart: 16, of which 6 were waited for; matrix products, arithmetic and copies ran while one was open for 17% of the time, Pallas kernels for 0%

profile of v12, /device:TPU:3, one launch (start us, length us, event | category | flops | bytes accessed | tf_op | source)
XLA Modules:
  0.0 156.6 jit_solution(12777950523381630904)
XLA Ops:
  6.5 1.0 slice.46
  9.6 3.2 %fusion.20 = (f32[512,512]{1,0:T(8,128)}, f32[512,512]{1,0:T(8,128)}) fusion(f32[1024,512]{1,0:T(8,128)} %param.4), kind=kLoop, calls=%fused_computation.31 | loop fusion | bytes 4194304 | tf_op jit(solution)/shard_map/slice | solution.py:39
  13.0 53.9 %all-gather.3.cloned.1.call-done = f32[512,2048]{1,0:T(8,128)} async-done(((f32[512,512]{1,0:T(8,128)}), f32[512,2048]{1,0:T(8,128)}) %all-gather.3.cloned.1.call-update) | async-done | bytes 4194320 | tf_op jit(solution)/shard_map/all_gather | solution.py:40
  66.9 2.4 %fusion.11 = f32[128,512]{1,0:T(8,128)S(1)} fusion(f32[128,512]{1,0:T(8,128)S(1)} %select_select_fusion.2, f32[2048,512]{1,0:T(8,128)} %param.5), kind=kOutput, calls=%fused_computation.17 | convolution fusion | flops 402653184 | bytes 1572864 | tf_op jit(solution)/shard_map/dot_general | solution.py:8
  69.3 2.4 %fusion.4 = f32[128,512]{1,0:T(8,128)S(1)} fusion(f32[128,512]{1,0:T(8,128)S(1)} %fusion.11, f32[512,2048]{1,0:T(8,128)} %all-gather.3.cloned.1.call-done), kind=kOutput, calls=%fused_computation.9 | convolution fusion | flops 402653184 | bytes 1572864 | tf_op jit(solution)/shard_map/dot_general | solution.py:8
  71.7 2.4 %fusion.9 = f32[128,512]{1,0:T(8,128)S(1)} fusion(f32[2048,512]{1,0:T(8,128)} %param.5, f32[128,512]{1,0:T(8,128)S(1)} %fusion.4, f32[128,1024]{1,0:T(8,128)S(1)} %copy-done), kind=kOutput, calls=%fused_computation.15 | convolution fusion | flops 402718720 | bytes 1835008 | tf_op jit(solution)/shard_map/dot_general | solution.py:8
  75.5 2.4 %convolution_add_fusion.1 = f32[128,512]{1,0:T(8,128)S(1)} fusion(f32[128,512]{1,0:T(8,128)S(1)} %fusion.4, f32[512,2048]{1,0:T(8,128)} %all-gather.3.cloned.1.call-done, f32[128,512]{1,0:T(8,128)S(1)} %collective-permute-done.3, f32[128,512]{1,0:T(8,128)S(1)} %collective-permute-done.4), kind=kOutput, calls=%fused_computation.6 | convolution fusion | flops 402784256 | bytes 2097152 | tf_op jit(solution)/shard_map/dot_general | solution.py:8
  77.9 2.4 %fusion.7 = f32[128,512]{1,0:T(8,128)S(1)} fusion(f32[2048,512]{1,0:T(8,128)} %param.5, f32[128,512]{1,0:T(8,128)S(1)} %convolution_add_fusion.1, f32[128,1024]{1,0:T(8,128)S(1)} %copy-done), kind=kOutput, calls=%fused_computation.13 | convolution fusion | flops 402718720 | bytes 1835008 | tf_op jit(solution)/shard_map/dot_general | solution.py:8
  81.0 2.5 %fusion.1 = f32[128,512]{1,0:T(8,128)S(1)} fusion(f32[128,512]{1,0:T(8,128)S(1)} %convolution_add_fusion.1, f32[128,512]{1,0:T(8,128)S(1)} %collective-permute-done.5, f32[512,2048]{1,0:T(8,128)} %all-gather.3.cloned.1.call-done, f32[128,1024]{1,0:T(8,128)S(1)} %copy-done), kind=kOutput, calls=%fused_computation.5 | convolution fusion | flops 402784256 | bytes 2097152 | tf_op jit(solution)/shard_map/dot_general | solution.py:8
  83.5 2.5 %convolution_select_fusion = f32[128,512]{1,0:T(8,128)S(1)} fusion(f32[128,512]{1,0:T(8,128)S(1)} %fusion.1, f32[2048,512]{1,0:T(8,128)} %param.5, f32[128,512]{1,0:T(8,128)S(1)} %fusion.7, f32[128,512]{1,0:T(8,128)S(1)} %fusion.9, f32[128,512]{1,0:T(8,128)S(1)} %fusion.11, pred[]{:T(512)S(6)} %eq.53, pred[]{:T(512)S(6)} %eq.52, pred[]{:T(512)S(6)} %eq.51, ...), kind=kOutput, calls=%fused_computation.3 | convolution fusion | flops 402915328 | bytes 2359300 | tf_op jit(solution)/shard_map/dot_general | solution.py:8
  87.3 1.3 collective-permute-start.8
  88.7 16.9 %collective-permute-done.8 = f32[128,512]{1,0:T(8,128)S(1)} collective-permute-done((f32[128,512]{1,0:T(8,128)S(1)}, f32[128,512]{1,0:T(8,128)S(1)}, u32[]{:S(2)}, u32[]{:S(2)}) %collective-permute-start.8) | collective-permute-done | bytes 262176 | tf_op jit(solution)/shard_map/ppermute | solution.py:71
  105.7 1.3 collective-permute-start.10
  107.0 1.3 collective-permute-start.11
  108.4 1.3 collective-permute-start.9
  109.7 2.5 %collective-permute-done.10 = f32[128,512]{1,0:T(8,128)S(1)} collective-permute-done((f32[128,512]{1,0:T(8,128)S(1)}, f32[128,512]{1,0:T(8,128)S(1)}, u32[]{:S(2)}, u32[]{:S(2)}) %collective-permute-start.10) | collective-permute-done | bytes 262176 | tf_op jit(solution)/shard_map/ppermute | solution.py:71
  112.2 2.8 %collective-permute-done.11 = f32[128,512]{1,0:T(8,128)S(1)} collective-permute-done((f32[128,512]{1,0:T(8,128)S(1)}, f32[128,512]{1,0:T(8,128)S(1)}, u32[]{:S(2)}, u32[]{:S(2)}) %collective-permute-start.11) | collective-permute-done | bytes 262176 | tf_op jit(solution)/shard_map/ppermute | solution.py:71
  115.1 11.6 %collective-permute-start.12 = (f32[128,512]{1,0:T(8,128)S(1)}, f32[128,512]{1,0:T(8,128)S(1)}, u32[]{:S(2)}, u32[]{:S(2)}) collective-permute-start(f32[128,512]{1,0:T(8,128)S(1)} %select_select_fusion), channel_id=1, source_target_pairs={{0,8},{4,12},{8,0},{12,4},{16,24},{20,28},{24,16},{28,20},{32,40},... | collective-permute-start | bytes 786440 | tf_op jit(solution)/shard_map/ppermute | solution.py:76
  126.6 5.6 %collective-permute-done.12 = f32[128,512]{1,0:T(8,128)S(1)} collective-permute-done((f32[128,512]{1,0:T(8,128)S(1)}, f32[128,512]{1,0:T(8,128)S(1)}, u32[]{:S(2)}, u32[]{:S(2)}) %collective-permute-start.12) | collective-permute-done | bytes 262176 | tf_op jit(solution)/shard_map/ppermute | solution.py:76
  132.3 2.0 %collective-permute-start.13 = (f32[128,1024]{1,0:T(8,128)S(1)}, f32[128,1024]{1,0:T(8,128)S(1)}, u32[]{:S(2)}, u32[]{:S(2)}) collective-permute-start(f32[128,1024]{1,0:T(8,128)S(1)} %maximum_select_fusion.1), channel_id=1, source_target_pairs={{0,4},{4,0},{8,12},{12,8},{16,20},{20,16},{24,28},{28,24},{32,36},... | collective-permute-start | bytes 1572872 | tf_op jit(solution)/shard_map/ppermute | solution.py:78
  134.3 1.5 collective-permute-done.13
  135.8 6.5 %fusion = f32[128,512]{1,0:T(8,128)S(1)} fusion(f32[128,512]{1,0:T(8,128)S(1)} %convolution_select_fusion, f32[512,2048]{1,0:T(8,128)} %all-gather.3.cloned.1.call-done, pred[]{:T(512)S(6)} %lt.41, f32[128,512]{1,0:T(8,128)S(1)} %get-tuple-element.16, f32[128,512]{1,0:T(8,128)S(1)} %get-tuple-element.14, f32[128,512]{1,0:T(8,128)S(1)} %get-tuple-element.15, ...), kind=kOutput, calls=%fused_computation.2 | convolution fusion | flops 1612578816 | bytes 6029314 | tf_op jit(solution)/shard_map/dot_general | solution.py:8
  142.4 6.5 %convolution_subtract_fusion = f32[128,512]{1,0:T(8,128)S(1)} fusion(f32[512,2048]{1,0:T(8,128)} %all-gather.5.cloned.1.call-done, f32[128,1024]{1,0:T(8,128)S(1)} %copy-done, f32[128,512]{1,0:T(8,128)S(1)} %get-tuple-element.16, f32[128,512]{1,0:T(8,128)S(1)} %get-tuple-element.14, f32[128,512]{1,0:T(8,128)S(1)} %get-tuple-element.15, ...), kind=kOutput, calls=%fused_computation | convolution fusion | flops 1612513280 | bytes 5767169 | tf_op jit(solution)/shard_map/dot_general | solution.py:8
  148.9 0.8 pad_maximum_fusion
  (30 shorter events, 5.9 us)
Async XLA Ops:
  6.5 6.3 %copy-start = (f32[128,1024]{1,0:T(8,128)S(1)}, f32[128,1024]{1,0:T(8,128)}, u32[]{:S(2)}) copy-start(f32[128,1024]{1,0:T(8,128)} %param.3) | copy-start | bytes 1572868
  6.5 60.3 %all-gather.3.cloned.1.call-start = ((), (), s32[]{:S(2)}) async-start(), calls=%async_computation | async-start | bytes 5242880 | tf_op jit(solution)/shard_map/all_gather | solution.py:40
  7.6 5.2 %collective-permute-start = (f32[128,512]{1,0:T(8,128)S(1)}, f32[128,512]{1,0:T(8,128)S(1)}, u32[]{:S(2)}, u32[]{:S(2)}) collective-permute-start(f32[128,512]{1,0:T(8,128)S(1)} %slice.46), channel_id=1, source_target_pairs={{0,12},{1,13},{2,14},{3,15}} | collective-permute-start | bytes 786440 | tf_op jit(solution)/shard_map/ppermute | solution.py:37
  8.3 4.6 %collective-permute-start.1 = (f32[128,512]{1,0:T(8,128)S(1)}, f32[128,512]{1,0:T(8,128)S(1)}, u32[]{:S(2)}, u32[]{:S(2)}) collective-permute-start(f32[128,512]{1,0:T(8,128)S(1)} %slice.46), channel_id=1, source_target_pairs={{0,8},{1,9},{2,10},{3,11}} | collective-permute-start | bytes 786440 | tf_op jit(solution)/shard_map/ppermute | solution.py:37
  8.9 3.9 %collective-permute-start.2 = (f32[128,512]{1,0:T(8,128)S(1)}, f32[128,512]{1,0:T(8,128)S(1)}, u32[]{:S(2)}, u32[]{:S(2)}) collective-permute-start(f32[128,512]{1,0:T(8,128)S(1)} %slice.46), channel_id=1, source_target_pairs={{0,4},{1,5},{2,6},{3,7}} | collective-permute-start | bytes 786440 | tf_op jit(solution)/shard_map/ppermute | solution.py:37
  13.0 129.4 %all-gather.5.cloned.1.call-start = ((), (), s32[]{:S(2)}) async-start(), calls=%async_computation.1 | async-start | bytes 5242880 | tf_op jit(solution)/shard_map/all_gather | solution.py:42
  74.1 1.4 collective-permute-start.3
  74.8 0.7 collective-permute-start.4
  80.3 0.7 collective-permute-start.5
  86.0 2.7 %collective-permute-start.6 = (f32[128,512]{1,0:T(8,128)S(1)}, f32[128,512]{1,0:T(8,128)S(1)}, u32[]{:S(2)}, u32[]{:S(2)}) collective-permute-start(f32[128,512]{1,0:T(8,128)S(1)} %convolution_select_fusion), channel_id=1, source_target_pairs={{0,192},{4,196},{8,200},{12,204},{1,193},{5,197},{9,201},{13,205},... | collective-permute-start | bytes 786440 | tf_op jit(solution)/shard_map/ppermute | solution.py:71
  86.7 2.0 %collective-permute-start.7 = (f32[128,512]{1,0:T(8,128)S(1)}, f32[128,512]{1,0:T(8,128)S(1)}, u32[]{:S(2)}, u32[]{:S(2)}) collective-permute-start(f32[128,512]{1,0:T(8,128)S(1)} %convolution_select_fusion), channel_id=1, source_target_pairs={{0,128},{4,132},{8,136},{12,140},{1,129},{5,133},{9,137},{13,141},... | collective-permute-start | bytes 786440 | tf_op jit(solution)/shard_map/ppermute | solution.py:71
  87.3 18.3 %collective-permute-start.8 = (f32[128,512]{1,0:T(8,128)S(1)}, f32[128,512]{1,0:T(8,128)S(1)}, u32[]{:S(2)}, u32[]{:S(2)}) collective-permute-start(f32[128,512]{1,0:T(8,128)S(1)} %convolution_select_fusion), channel_id=1, source_target_pairs={{0,64},{4,68},{8,72},{12,76},{1,65},{5,69},{9,73},{13,77},{2,66},{... | collective-permute-start | bytes 786440 | tf_op jit(solution)/shard_map/ppermute | solution.py:71
  105.7 6.4 %collective-permute-start.10 = (f32[128,512]{1,0:T(8,128)S(1)}, f32[128,512]{1,0:T(8,128)S(1)}, u32[]{:S(2)}, u32[]{:S(2)}) collective-permute-start(f32[128,512]{1,0:T(8,128)S(1)} %select_select_fusion.1), channel_id=1, source_target_pairs={{0,32},{4,36},{8,40},{12,44},{64,96},{68,100},{72,104},{76,108},{1... | collective-permute-start | bytes 786440 | tf_op jit(solution)/shard_map/ppermute | solution.py:71
  107.0 7.9 %collective-permute-start.11 = (f32[128,512]{1,0:T(8,128)S(1)}, f32[128,512]{1,0:T(8,128)S(1)}, u32[]{:S(2)}, u32[]{:S(2)}) collective-permute-start(f32[128,512]{1,0:T(8,128)S(1)} %select_select_fusion.1), channel_id=1, source_target_pairs={{0,16},{4,20},{8,24},{12,28},{64,80},{68,84},{72,88},{76,92},{128,... | collective-permute-start | bytes 786440 | tf_op jit(solution)/shard_map/ppermute | solution.py:71
  108.4 6.6 %collective-permute-start.9 = (f32[128,512]{1,0:T(8,128)S(1)}, f32[128,512]{1,0:T(8,128)S(1)}, u32[]{:S(2)}, u32[]{:S(2)}) collective-permute-start(f32[128,512]{1,0:T(8,128)S(1)} %select_select_fusion.1), channel_id=1, source_target_pairs={{0,48},{4,52},{8,56},{12,60},{64,112},{68,116},{72,120},{76,124},{... | collective-permute-start | bytes 786440 | tf_op jit(solution)/shard_map/ppermute | solution.py:71
  115.1 17.2 %collective-permute-start.12 = (f32[128,512]{1,0:T(8,128)S(1)}, f32[128,512]{1,0:T(8,128)S(1)}, u32[]{:S(2)}, u32[]{:S(2)}) collective-permute-start(f32[128,512]{1,0:T(8,128)S(1)} %select_select_fusion), channel_id=1, source_target_pairs={{0,8},{4,12},{8,0},{12,4},{16,24},{20,28},{24,16},{28,20},{32,40},... | collective-permute-start | bytes 786440 | tf_op jit(solution)/shard_map/ppermute | solution.py:76
  132.3 3.5 %collective-permute-start.13 = (f32[128,1024]{1,0:T(8,128)S(1)}, f32[128,1024]{1,0:T(8,128)S(1)}, u32[]{:S(2)}, u32[]{:S(2)}) collective-permute-start(f32[128,1024]{1,0:T(8,128)S(1)} %maximum_select_fusion.1), channel_id=1, source_target_pairs={{0,4},{4,0},{8,12},{12,8},{16,20},{20,16},{24,28},{28,24},{32,36},... | collective-permute-start | bytes 1572872 | tf_op jit(solution)/shard_map/ppermute | solution.py:78
Sparse Core Ops, SparseCore 0:
  13.1 53.7 all-gather.2
  68.7 51.1 all-gather.4

commit v13 on v12

--- a/solution.py
+++ b/solution.py
@@ -81,8 +81,28 @@
     theirs_first = jnp.concatenate([yours[0], mine[0], yours[1], mine[1]], axis=1)
     panel = jnp.where(b0 == 0, mine_first, theirs_first)
 
-    second = right_side[:, block:] - contract(panel, lower_second)
-    first = right_side[:, :block] - contract(panel, lower_first)
+    def parts(value):
+        high = lax.reduce_precision(value, exponent_bits=8, mantissa_bits=7)
+        rest = value - high
+        middle = lax.reduce_precision(rest, exponent_bits=8, mantissa_bits=7)
+        low = rest - middle
+        return [part.astype(jnp.bfloat16) for part in (high, middle, low)]
+
+    panel_parts = parts(panel)
+
+    def product(lower):
+        lower_parts = parts(lower)
+        total = None
+        for i, j in ((2, 0), (1, 1), (0, 2), (1, 0), (0, 1), (0, 0)):
+            term = lax.dot_general(
+                panel_parts[i], lower_parts[j], (((1,), (1,)), ((), ())),
+                preferred_element_type=jnp.float32,
+            )
+            total = term if total is None else total + term
+        return total
+
+    second = right_side[:, block:] - product(lower_second)
+    first = right_side[:, :block] - product(lower_first)
     head_block = jnp.where(row_at < steps, own, first)
     return jnp.concatenate([head_block, second], axis=1)
 

time: 157 us -> 157 us (level)
  waiting for transfers between devices: 83.2 us -> 80.6 us
  matrix products: 29.9 us -> 31.9 us
    dot_general x0 -> x12, matrix products: none -> 15.1 us  [product(): lax.dot_general(panel_parts[i], lower_parts[j], (((1,), (1,)), ((), ())),...]
    dot_general x9 -> x7, matrix products: 29.9 us -> 16.7 us  [contract(): lax.dot_general(left, right, (((1,), (1,)), ((), ())), precision=lax.Prec...]
    all_gather x1, waiting for transfers between devices: 53.9 us -> 51.5 us  [per_device(): lower_first = lax.all_gather(first_rows, 'pcol', axis=1, tiled=True)]
  transfers between devices with their start and end apart: 16 -> 16, of which waited for: 6 -> 6; matrix products, arithmetic and copies ran while one was open for 17% -> 15% of each run, Pallas kernels for 0% -> 0%
where the time goes in v13:
time: 157 us
  waiting for transfers between devices  80.6 us (51%)
  matrix products  31.9 us (20%)
  starting transfers between devices  24.7 us (16%)
  between operations  13.9 us (9%)
  local copies, waits for them, and re-layouts  4.58 us (3%)
    all_gather x1, waiting for transfers between devices, per_device(): lower_first = lax.all_gather(first_rows, 'pcol', axis=1, tiled=True)  51.5 us
    ppermute x6, waiting for transfers between devices, per_device(): arrived = lax.ppermute(piece, 'prow', pairs)  22 us
    dot_general x7, matrix products, contract(): lax.dot_general(left, right, (((1,), (1,)), ((), ())), precision=lax.Prec...  16.7 us
    dot_general x12, matrix products, product(): lax.dot_general(panel_parts[i], lower_parts[j], (((1,), (1,)), ((), ())),...  15.1 us
    ppermute x1, starting transfers between devices, per_device(): other = lax.ppermute(piece, 'prow', [(p, p ^ 2) for p in range(n_row)])  12 us
    ppermute x6, starting transfers between devices, per_device(): arrived = lax.ppermute(piece, 'prow', pairs)  6.56 us
    ppermute x1, waiting for transfers between devices, per_device(): other = lax.ppermute(piece, 'prow', [(p, p ^ 2) for p in range(n_row)])  5.61 us
    slice x1, local copies, waits for them, and re-layouts, per_device(): second_rows, _ = lax.optimization_barrier((factor[block:], lower_first))  3.21 us
  transfers between devices with their start and end apart: 16, of which 6 were waited for; matrix products, arithmetic and copies ran while one was open for 15% of the time, Pallas kernels for 0%

profile of v13, /device:TPU:3, one launch (start us, length us, event | category | flops | bytes accessed | tf_op | source)
XLA Modules:
  0.0 156.8 jit_solution(4174176255241743536)
XLA Ops:
  6.5 1.0 slice.46
  9.6 3.2 %fusion.33 = (f32[512,512]{1,0:T(8,128)}, f32[512,512]{1,0:T(8,128)}) fusion(f32[1024,512]{1,0:T(8,128)} %param.4), kind=kLoop, calls=%fused_computation.58 | loop fusion | bytes 4194304 | tf_op jit(solution)/shard_map/slice | solution.py:41
  13.1 2.4 %fusion.22 = f32[128,512]{1,0:T(8,128)S(1)} fusion(f32[128,512]{1,0:T(8,128)S(1)} %select_select_fusion.2, f32[2048,512]{1,0:T(8,128)} %param.5), kind=kOutput, calls=%fused_computation.44 | convolution fusion | flops 402653184 | bytes 1572864 | tf_op jit(solution)/shard_map/dot_general | solution.py:8
  15.4 51.5 %all-gather.3.cloned.1.call-done = f32[512,2048]{1,0:T(8,128)} async-done(((f32[512,512]{1,0:T(8,128)}), f32[512,2048]{1,0:T(8,128)}) %all-gather.3.cloned.1.call-update) | async-done | bytes 4194320 | tf_op jit(solution)/shard_map/all_gather | solution.py:40
  66.9 2.4 %fusion.15 = f32[128,512]{1,0:T(8,128)S(1)} fusion(f32[128,512]{1,0:T(8,128)S(1)} %fusion.22, f32[512,2048]{1,0:T(8,128)} %all-gather.3.cloned.1.call-done), kind=kOutput, calls=%fused_computation.36 | convolution fusion | flops 402653184 | bytes 1572864 | tf_op jit(solution)/shard_map/dot_general | solution.py:8
  69.3 2.4 %fusion.20 = f32[128,512]{1,0:T(8,128)S(1)} fusion(f32[2048,512]{1,0:T(8,128)} %param.5, f32[128,512]{1,0:T(8,128)S(1)} %fusion.15, f32[128,1024]{1,0:T(8,128)S(1)} %copy-done.2), kind=kOutput, calls=%fused_computation.42 | convolution fusion | flops 402718720 | bytes 1835008 | tf_op jit(solution)/shard_map/dot_general | solution.py:8
  73.1 2.4 %convolution_add_fusion.9 = f32[128,512]{1,0:T(8,128)S(1)} fusion(f32[128,512]{1,0:T(8,128)S(1)} %fusion.15, f32[512,2048]{1,0:T(8,128)} %all-gather.3.cloned.1.call-done, f32[128,512]{1,0:T(8,128)S(1)} %collective-permute-done.3, f32[128,512]{1,0:T(8,128)S(1)} %collective-permute-done.4), kind=kOutput, calls=%fused_computation.32 | convolution fusion | flops 402784256 | bytes 2097152 | tf_op jit(solution)/shard_map/dot_general | solution.py:8
  75.5 2.4 %fusion.18 = f32[128,512]{1,0:T(8,128)S(1)} fusion(f32[2048,512]{1,0:T(8,128)} %param.5, f32[128,512]{1,0:T(8,128)S(1)} %convolution_add_fusion.9, f32[128,1024]{1,0:T(8,128)S(1)} %copy-done.2), kind=kOutput, calls=%fused_computation.40 | convolution fusion | flops 402718720 | bytes 1835008 | tf_op jit(solution)/shard_map/dot_general | solution.py:8
  78.6 2.4 %fusion.11 = f32[128,512]{1,0:T(8,128)S(1)} fusion(f32[128,512]{1,0:T(8,128)S(1)} %convolution_add_fusion.9, f32[128,512]{1,0:T(8,128)S(1)} %collective-permute-done.5, f32[512,2048]{1,0:T(8,128)} %all-gather.3.cloned.1.call-done, f32[128,1024]{1,0:T(8,128)S(1)} %copy-done.2), kind=kOutput, calls=%fused_computation.31 | convolution fusion | flops 402784256 | bytes 2097152 | tf_op jit(solution)/shard_map/dot_general | solution.py:8
  81.0 2.4 %convolution_select_fusion = f32[128,512]{1,0:T(8,128)S(1)} fusion(f32[128,512]{1,0:T(8,128)S(1)} %fusion.11, f32[2048,512]{1,0:T(8,128)} %param.5, f32[128,512]{1,0:T(8,128)S(1)} %fusion.18, f32[128,512]{1,0:T(8,128)S(1)} %fusion.20, f32[128,512]{1,0:T(8,128)S(1)} %fusion.22, pred[]{:T(512)S(6)} %eq.53, pred[]{:T(512)S(6)} %eq.52, pred[]{:T(512)S(6)} %eq.51, ...), kind=kOutput, calls=%fused_computation.29 | convolution fusion | flops 402915328 | bytes 2359300 | tf_op jit(solution)/shard_map/dot_general | solution.py:8
  84.8 1.3 collective-permute-start.8
  86.1 16.9 %collective-permute-done.8 = f32[128,512]{1,0:T(8,128)S(1)} collective-permute-done((f32[128,512]{1,0:T(8,128)S(1)}, f32[128,512]{1,0:T(8,128)S(1)}, u32[]{:S(2)}, u32[]{:S(2)}) %collective-permute-start.8) | collective-permute-done | bytes 262176 | tf_op jit(solution)/shard_map/ppermute | solution.py:71
  103.2 1.3 collective-permute-start.10
  104.5 1.3 collective-permute-start.11
  105.8 1.3 collective-permute-start.9
  107.1 2.2 %collective-permute-done.10 = f32[128,512]{1,0:T(8,128)S(1)} collective-permute-done((f32[128,512]{1,0:T(8,128)S(1)}, f32[128,512]{1,0:T(8,128)S(1)}, u32[]{:S(2)}, u32[]{:S(2)}) %collective-permute-start.10) | collective-permute-done | bytes 262176 | tf_op jit(solution)/shard_map/ppermute | solution.py:71
  109.4 2.8 %collective-permute-done.11 = f32[128,512]{1,0:T(8,128)S(1)} collective-permute-done((f32[128,512]{1,0:T(8,128)S(1)}, f32[128,512]{1,0:T(8,128)S(1)}, u32[]{:S(2)}, u32[]{:S(2)}) %collective-permute-start.11) | collective-permute-done | bytes 262176 | tf_op jit(solution)/shard_map/ppermute | solution.py:71
  112.3 12.0 %collective-permute-start.12 = (f32[128,512]{1,0:T(8,128)S(1)}, f32[128,512]{1,0:T(8,128)S(1)}, u32[]{:S(2)}, u32[]{:S(2)}) collective-permute-start(f32[128,512]{1,0:T(8,128)S(1)} %select_select_fusion), channel_id=1, source_target_pairs={{0,8},{4,12},{8,0},{12,4},{16,24},{20,28},{24,16},{28,20},{32,40},... | collective-permute-start | bytes 786440 | tf_op jit(solution)/shard_map/ppermute | solution.py:76
  124.3 5.6 %collective-permute-done.12 = f32[128,512]{1,0:T(8,128)S(1)} collective-permute-done((f32[128,512]{1,0:T(8,128)S(1)}, f32[128,512]{1,0:T(8,128)S(1)}, u32[]{:S(2)}, u32[]{:S(2)}) %collective-permute-start.12) | collective-permute-done | bytes 262176 | tf_op jit(solution)/shard_map/ppermute | solution.py:76
  130.0 2.0 %collective-permute-start.13 = (f32[128,1024]{1,0:T(8,128)S(1)}, f32[128,1024]{1,0:T(8,128)S(1)}, u32[]{:S(2)}, u32[]{:S(2)}) collective-permute-start(f32[128,1024]{1,0:T(8,128)S(1)} %maximum_select_fusion.1), channel_id=1, source_target_pairs={{0,4},{4,0},{8,12},{12,8},{16,20},{20,16},{24,28},{28,24},{32,36},... | collective-permute-start | bytes 1572872 | tf_op jit(solution)/shard_map/ppermute | solution.py:78
  132.0 1.5 collective-permute-done.13
  133.6 3.1 %fusion.4 = f32[128,512]{1,0:T(8,128)S(1)} fusion(bf16[128,2048]{1,0:T(8,128)(2,1)S(1)} %reduce-precision_convert_fusion.5, f32[512,2048]{1,0:T(8,128)} %all-gather.3.cloned.1.call-done), kind=kOutput, calls=%fused_computation.11 | convolution fusion | flops 273678336 | bytes 4980736 | tf_op jit(solution)/shard_map/dot_general | solution.py:97
  141.2 3.2 %fusion.27 = f32[128,512]{1,0:T(8,128)S(1)} fusion(f32[512,2048]{1,0:T(8,128)} %all-gather.5.cloned.1.call-done, f32[128,512]{1,0:T(8,128)S(1)} %get-tuple-element.14, f32[128,512]{1,0:T(8,128)S(1)} %get-tuple-element.16, f32[128,512]{1,0:T(8,128)S(1)} %get-tuple-element.13, f32[128,512]{1,0:T(8,128)S(1)} %get-tuple-element.15, pred[]{:T(512)S(6)} %eq.54), kind=kOutput, calls=%fused_computation.54 | convolution fusion | flops 273678336 | bytes 5505025 | tf_op jit(solution)/shard_map/dot_general | solution.py:97
  144.6 1.0 fusion.2
  (45 shorter events, 15.0 us)
Async XLA Ops:
  6.5 6.3 %copy-start.2 = (f32[128,1024]{1,0:T(8,128)S(1)}, f32[128,1024]{1,0:T(8,128)}, u32[]{:S(2)}) copy-start(f32[128,1024]{1,0:T(8,128)} %param.3) | copy-start | bytes 1572868
  6.5 60.4 %all-gather.3.cloned.1.call-start = ((), (), s32[]{:S(2)}) async-start(), calls=%async_computation | async-start | bytes 5242880 | tf_op jit(solution)/shard_map/all_gather | solution.py:40
  7.6 5.3 %collective-permute-start = (f32[128,512]{1,0:T(8,128)S(1)}, f32[128,512]{1,0:T(8,128)S(1)}, u32[]{:S(2)}, u32[]{:S(2)}) collective-permute-start(f32[128,512]{1,0:T(8,128)S(1)} %slice.46), channel_id=1, source_target_pairs={{0,12},{1,13},{2,14},{3,15}} | collective-permute-start | bytes 786440 | tf_op jit(solution)/shard_map/ppermute | solution.py:37
  8.3 4.6 %collective-permute-start.1 = (f32[128,512]{1,0:T(8,128)S(1)}, f32[128,512]{1,0:T(8,128)S(1)}, u32[]{:S(2)}, u32[]{:S(2)}) collective-permute-start(f32[128,512]{1,0:T(8,128)S(1)} %slice.46), channel_id=1, source_target_pairs={{0,8},{1,9},{2,10},{3,11}} | collective-permute-start | bytes 786440 | tf_op jit(solution)/shard_map/ppermute | solution.py:37
  8.9 3.9 %collective-permute-start.2 = (f32[128,512]{1,0:T(8,128)S(1)}, f32[128,512]{1,0:T(8,128)S(1)}, u32[]{:S(2)}, u32[]{:S(2)}) collective-permute-start(f32[128,512]{1,0:T(8,128)S(1)} %slice.46), channel_id=1, source_target_pairs={{0,4},{1,5},{2,6},{3,7}} | collective-permute-start | bytes 786440 | tf_op jit(solution)/shard_map/ppermute | solution.py:37
  13.0 128.2 %all-gather.5.cloned.1.call-start = ((), (), s32[]{:S(2)}) async-start(), calls=%async_computation.1 | async-start | bytes 5242880 | tf_op jit(solution)/shard_map/all_gather | solution.py:42
  71.7 1.4 collective-permute-start.3
  72.4 0.7 collective-permute-start.4
  77.9 0.7 collective-permute-start.5
  83.4 2.7 %collective-permute-start.6 = (f32[128,512]{1,0:T(8,128)S(1)}, f32[128,512]{1,0:T(8,128)S(1)}, u32[]{:S(2)}, u32[]{:S(2)}) collective-permute-start(f32[128,512]{1,0:T(8,128)S(1)} %convolution_select_fusion), channel_id=1, source_target_pairs={{0,192},{4,196},{8,200},{12,204},{1,193},{5,197},{9,201},{13,205},... | collective-permute-start | bytes 786440 | tf_op jit(solution)/shard_map/ppermute | solution.py:71
  84.1 2.0 %collective-permute-start.7 = (f32[128,512]{1,0:T(8,128)S(1)}, f32[128,512]{1,0:T(8,128)S(1)}, u32[]{:S(2)}, u32[]{:S(2)}) collective-permute-start(f32[128,512]{1,0:T(8,128)S(1)} %convolution_select_fusion), channel_id=1, source_target_pairs={{0,128},{4,132},{8,136},{12,140},{1,129},{5,133},{9,137},{13,141},... | collective-permute-start | bytes 786440 | tf_op jit(solution)/shard_map/ppermute | solution.py:71
  84.8 18.3 %collective-permute-start.8 = (f32[128,512]{1,0:T(8,128)S(1)}, f32[128,512]{1,0:T(8,128)S(1)}, u32[]{:S(2)}, u32[]{:S(2)}) collective-permute-start(f32[128,512]{1,0:T(8,128)S(1)} %convolution_select_fusion), channel_id=1, source_target_pairs={{0,64},{4,68},{8,72},{12,76},{1,65},{5,69},{9,73},{13,77},{2,66},{... | collective-permute-start | bytes 786440 | tf_op jit(solution)/shard_map/ppermute | solution.py:71
  103.2 6.2 %collective-permute-start.10 = (f32[128,512]{1,0:T(8,128)S(1)}, f32[128,512]{1,0:T(8,128)S(1)}, u32[]{:S(2)}, u32[]{:S(2)}) collective-permute-start(f32[128,512]{1,0:T(8,128)S(1)} %select_select_fusion.1), channel_id=1, source_target_pairs={{0,32},{4,36},{8,40},{12,44},{64,96},{68,100},{72,104},{76,108},{1... | collective-permute-start | bytes 786440 | tf_op jit(solution)/shard_map/ppermute | solution.py:71
  104.5 7.7 %collective-permute-start.11 = (f32[128,512]{1,0:T(8,128)S(1)}, f32[128,512]{1,0:T(8,128)S(1)}, u32[]{:S(2)}, u32[]{:S(2)}) collective-permute-start(f32[128,512]{1,0:T(8,128)S(1)} %select_select_fusion.1), channel_id=1, source_target_pairs={{0,16},{4,20},{8,24},{12,28},{64,80},{68,84},{72,88},{76,92},{128,... | collective-permute-start | bytes 786440 | tf_op jit(solution)/shard_map/ppermute | solution.py:71
  105.8 6.4 %collective-permute-start.9 = (f32[128,512]{1,0:T(8,128)S(1)}, f32[128,512]{1,0:T(8,128)S(1)}, u32[]{:S(2)}, u32[]{:S(2)}) collective-permute-start(f32[128,512]{1,0:T(8,128)S(1)} %select_select_fusion.1), channel_id=1, source_target_pairs={{0,48},{4,52},{8,56},{12,60},{64,112},{68,116},{72,120},{76,124},{... | collective-permute-start | bytes 786440 | tf_op jit(solution)/shard_map/ppermute | solution.py:71
  112.3 17.6 %collective-permute-start.12 = (f32[128,512]{1,0:T(8,128)S(1)}, f32[128,512]{1,0:T(8,128)S(1)}, u32[]{:S(2)}, u32[]{:S(2)}) collective-permute-start(f32[128,512]{1,0:T(8,128)S(1)} %select_select_fusion), channel_id=1, source_target_pairs={{0,8},{4,12},{8,0},{12,4},{16,24},{20,28},{24,16},{28,20},{32,40},... | collective-permute-start | bytes 786440 | tf_op jit(solution)/shard_map/ppermute | solution.py:76
  130.0 3.5 %collective-permute-start.13 = (f32[128,1024]{1,0:T(8,128)S(1)}, f32[128,1024]{1,0:T(8,128)S(1)}, u32[]{:S(2)}, u32[]{:S(2)}) collective-permute-start(f32[128,1024]{1,0:T(8,128)S(1)} %maximum_select_fusion.1), channel_id=1, source_target_pairs={{0,4},{4,0},{8,12},{12,8},{16,20},{20,16},{24,28},{28,24},{32,36},... | collective-permute-start | bytes 1572872 | tf_op jit(solution)/shard_map/ppermute | solution.py:78
  132.0 4.8 %copy-start = (f32[512,2048]{1,0:T(8,128)S(1)}, f32[512,2048]{1,0:T(8,128)}, u32[]{:S(2)}) copy-start(f32[512,2048]{1,0:T(8,128)} %all-gather.3.cloned.1.call-done) | copy-start | bytes 12582916
  141.2 3.5 %copy-start.1 = (f32[512,2048]{1,0:T(8,128)S(1)}, f32[512,2048]{1,0:T(8,128)}, u32[]{:S(2)}) copy-start(f32[512,2048]{1,0:T(8,128)} %all-gather.5.cloned.1.call-done) | copy-start | bytes 12582916
Sparse Core Ops, SparseCore 0:
  13.1 53.7 all-gather.2
  73.2 51.1 all-gather.4

commit v14 on v13

--- a/solution.py
+++ b/solution.py
@@ -60,7 +60,14 @@
                 arrived = arrived + lax.ppermute(solved, AXES, pairs)
         acc = acc + contract(arrived, lower_first[:, k * block : (k + 1) * block])
 
-    piece = own
+    def parts(value):
+        high = lax.reduce_precision(value, exponent_bits=8, mantissa_bits=7)
+        rest = value - high
+        middle = lax.reduce_precision(rest, exponent_bits=8, mantissa_bits=7)
+        low = rest - middle
+        return [part.astype(jnp.bfloat16) for part in (high, middle, low)]
+
+    first_parts, piece = lax.optimization_barrier((parts(lower_first), own))
     fan_z = min(steps, n_row // steps)
     stride_x = steps * fan_z
     for stride, fan in ((stride_x, n_row // stride_x), (steps, fan_z)):
@@ -71,6 +78,7 @@
             arrived = lax.ppermute(piece, "prow", pairs)
             received = jnp.where((row_at % (stride * fan)) // stride == hop, arrived, received)
         piece = jnp.where(row_at % stride < steps, received, piece)
+    second_parts, piece = lax.optimization_barrier((parts(lower_second), piece))
     b0 = row_at % 2
     b1 = (row_at // 2) % 2
     other = lax.ppermute(piece, "prow", [(p, p ^ 2) for p in range(n_row)])
@@ -81,17 +89,9 @@
     theirs_first = jnp.concatenate([yours[0], mine[0], yours[1], mine[1]], axis=1)
     panel = jnp.where(b0 == 0, mine_first, theirs_first)
 
-    def parts(value):
-        high = lax.reduce_precision(value, exponent_bits=8, mantissa_bits=7)
-        rest = value - high
-        middle = lax.reduce_precision(rest, exponent_bits=8, mantissa_bits=7)
-        low = rest - middle
-        return [part.astype(jnp.bfloat16) for part in (high, middle, low)]
-
     panel_parts = parts(panel)
 
-    def product(lower):
-        lower_parts = parts(lower)
+    def product(lower_parts):
         total = None
         for i, j in ((2, 0), (1, 1), (0, 2), (1, 0), (0, 1), (0, 0)):
             term = lax.dot_general(
@@ -101,8 +101,8 @@
             total = term if total is None else total + term
         return total
 
-    second = right_side[:, block:] - product(lower_second)
-    first = right_side[:, :block] - product(lower_first)
+    second = right_side[:, block:] - product(second_parts)
+    first = right_side[:, :block] - product(first_parts)
     head_block = jnp.where(row_at < steps, own, first)
     return jnp.concatenate([head_block, second], axis=1)
 

time: 157 us -> 169 us (1.076)
  the two profiles are of different devices: /device:TPU:3 before, /device:TPU:7 now
where the time goes in v14:
time: 169 us; the launch traced here: 168 us
  waiting for transfers between devices  89.6 us (53%)
  matrix products  26.8 us (16%)
  other arithmetic  15.4 us (9%)
  between operations  13.8 us (8%)
  starting transfers between devices  12.7 us (8%)
  local copies, waits for them, and re-layouts  9.64 us (6%)
    all_gather x1, waiting for transfers between devices, per_device(): lower_first = lax.all_gather(first_rows, 'pcol', axis=1, tiled=True)  53.8 us
    ppermute x6, waiting for transfers between devices, per_device(): arrived = lax.ppermute(piece, 'prow', pairs)  25.9 us
    dot_general x7, matrix products, contract(): lax.dot_general(left, right, (((1,), (1,)), ((), ())), precision=lax.Prec...  16.8 us
    convert_element_type x3, other arithmetic, parts(): return [part.astype(jnp.bfloat16) for part in (high, middle, low)]  12 us
    dot_general x12, matrix products, product(): lax.dot_general(panel_parts[i], lower_parts[j], (((1,), (1,)), ((), ())),...  10 us
    ppermute x1, waiting for transfers between devices, per_device(): other = lax.ppermute(piece, 'prow', [(p, p ^ 2) for p in range(n_row)])  8.19 us
    ppermute x6, starting transfers between devices, per_device(): arrived = lax.ppermute(piece, 'prow', pairs)  7.94 us
    unnamed x18, local copies, waits for them, and re-layouts  4.43 us
  transfers between devices with their start and end apart: 16, of which 7 were waited for; matrix products, arithmetic and copies ran while one was open for 16% of the time, Pallas kernels for 0%

profile of v14, /device:TPU:7, one launch (start us, length us, event | category | flops | bytes accessed | tf_op | source)
XLA Modules:
  0.0 168.0 jit_solution(16818166214260549264)
XLA Ops:
  9.6 3.1 %fusion.27 = (f32[512,512]{1,0:T(8,128)}, f32[512,512]{1,0:T(8,128)}) fusion(f32[1024,512]{1,0:T(8,128)} %param.4), kind=kLoop, calls=%fused_computation.56 | loop fusion | bytes 4194304 | tf_op jit(solution)/shard_map/slice | solution.py:39
  12.9 53.8 %all-gather.3.cloned.1.call-done = f32[512,2048]{1,0:T(8,128)} async-done(((f32[512,512]{1,0:T(8,128)}), f32[512,2048]{1,0:T(8,128)}) %all-gather.3.cloned.1.call-update) | async-done | bytes 4194320 | tf_op jit(solution)/shard_map/all_gather | solution.py:40
  66.8 2.4 %fusion.16 = f32[128,512]{1,0:T(8,128)S(1)} fusion(f32[128,512]{1,0:T(8,128)S(1)} %select_select_fusion.2, f32[2048,512]{1,0:T(8,128)} %param.5), kind=kOutput, calls=%fused_computation.42 | convolution fusion | flops 402653184 | bytes 1572864 | tf_op jit(solution)/shard_map/dot_general | solution.py:8
  69.2 2.4 %fusion.9 = f32[128,512]{1,0:T(8,128)S(1)} fusion(f32[128,512]{1,0:T(8,128)S(1)} %fusion.16, f32[512,2048]{1,0:T(8,128)} %all-gather.3.cloned.1.call-done), kind=kOutput, calls=%fused_computation.34 | convolution fusion | flops 402653184 | bytes 1572864 | tf_op jit(solution)/shard_map/dot_general | solution.py:8
  71.5 2.4 %fusion.14 = f32[128,512]{1,0:T(8,128)S(1)} fusion(f32[2048,512]{1,0:T(8,128)} %param.5, f32[128,512]{1,0:T(8,128)S(1)} %fusion.9, f32[128,1024]{1,0:T(8,128)S(1)} %copy-done.5), kind=kOutput, calls=%fused_computation.40 | convolution fusion | flops 402718720 | bytes 1835008 | tf_op jit(solution)/shard_map/dot_general | solution.py:8
  75.3 2.4 %convolution_add_fusion.11 = f32[128,512]{1,0:T(8,128)S(1)} fusion(f32[128,512]{1,0:T(8,128)S(1)} %fusion.9, f32[512,2048]{1,0:T(8,128)} %all-gather.3.cloned.1.call-done, f32[128,512]{1,0:T(8,128)S(1)} %collective-permute-done.3, f32[128,512]{1,0:T(8,128)S(1)} %collective-permute-done.4), kind=kOutput, calls=%fused_computation.30 | convolution fusion | flops 402784256 | bytes 2097152 | tf_op jit(solution)/shard_map/dot_general | solution.py:8
  77.7 2.4 %fusion.12 = f32[128,512]{1,0:T(8,128)S(1)} fusion(f32[2048,512]{1,0:T(8,128)} %param.5, f32[128,512]{1,0:T(8,128)S(1)} %convolution_add_fusion.11, f32[128,1024]{1,0:T(8,128)S(1)} %copy-done.5), kind=kOutput, calls=%fused_computation.38 | convolution fusion | flops 402718720 | bytes 1835008 | tf_op jit(solution)/shard_map/dot_general | solution.py:8
  80.8 5.9 %fusion.1 = (bf16[512,2048]{1,0:T(8,128)(2,1)}, bf16[512,2048]{1,0:T(8,128)(2,1)}, bf16[512,2048]{1,0:T(8,128)(2,1)S(1)}) fusion(f32[512,2048]{1,0:T(8,128)} %all-gather.3.cloned.1.call-done), kind=kLoop, calls=%fused_computation.9 | loop fusion | flops 7340032 | bytes 10485760 | tf_op jit(solution)/shard_map/convert_element_type | solution.py:68
  86.7 2.4 %fusion.5 = f32[128,512]{1,0:T(8,128)S(1)} fusion(f32[128,512]{1,0:T(8,128)S(1)} %convolution_add_fusion.11, f32[128,512]{1,0:T(8,128)S(1)} %collective-permute-done.5, f32[512,2048]{1,0:T(8,128)} %all-gather.3.cloned.1.call-done, f32[128,1024]{1,0:T(8,128)S(1)} %copy-done.5), kind=kOutput, calls=%fused_computation.29 | convolution fusion | flops 402784256 | bytes 2097152 | tf_op jit(solution)/shard_map/dot_general | solution.py:8
  89.1 2.4 %convolution_select_fusion = f32[128,512]{1,0:T(8,128)S(1)} fusion(f32[128,512]{1,0:T(8,128)S(1)} %fusion.5, f32[2048,512]{1,0:T(8,128)} %param.5, f32[128,512]{1,0:T(8,128)S(1)} %fusion.12, f32[128,512]{1,0:T(8,128)S(1)} %fusion.14, f32[128,512]{1,0:T(8,128)S(1)} %fusion.16, pred[]{:T(512)S(6)} %eq.53, pred[]{:T(512)S(6)} %eq.52, pred[]{:T(512)S(6)} %eq.51, ...), kind=kOutput, calls=%fused_computation.27 | convolution fusion | flops 402915328 | bytes 2359300 | tf_op jit(solution)/shard_map/dot_general | solution.py:8
  92.9 1.3 collective-permute-start.6
  95.0 12.6 %collective-permute-done.6 = f32[128,512]{1,0:T(8,128)} collective-permute-done((f32[128,512]{1,0:T(8,128)S(1)}, f32[128,512]{1,0:T(8,128)}, u32[]{:S(2)}, u32[]{:S(2)}) %collective-permute-start.6) | collective-permute-done | bytes 262176 | tf_op jit(solution)/shard_map/ppermute | solution.py:78
  107.6 1.0 select_select_fusion.1
  108.6 1.3 collective-permute-start.11
  109.9 2.0 %collective-permute-start.10 = (f32[128,512]{1,0:T(8,128)S(1)}, f32[128,512]{1,0:T(8,128)}, u32[]{:S(2)}, u32[]{:S(2)}) collective-permute-start(f32[128,512]{1,0:T(8,128)S(1)} %select_select_fusion.1), channel_id=1, source_target_pairs={{0,32},{4,36},{8,40},{12,44},{64,96},{68,100},{72,104},{76,108},{1... | collective-permute-start | bytes 786440 | tf_op jit(solution)/shard_map/ppermute | solution.py:78
  111.9 2.0 %collective-permute-start.9 = (f32[128,512]{1,0:T(8,128)S(1)}, f32[128,512]{1,0:T(8,128)}, u32[]{:S(2)}, u32[]{:S(2)}) collective-permute-start(f32[128,512]{1,0:T(8,128)S(1)} %select_select_fusion.1), channel_id=1, source_target_pairs={{0,48},{4,52},{8,56},{12,60},{64,112},{68,116},{72,120},{76,124},{... | collective-permute-start | bytes 786440 | tf_op jit(solution)/shard_map/ppermute | solution.py:78
  113.9 1.6 collective-permute-done.11
  115.5 2.8 %collective-permute-done.10 = f32[128,512]{1,0:T(8,128)} collective-permute-done((f32[128,512]{1,0:T(8,128)S(1)}, f32[128,512]{1,0:T(8,128)}, u32[]{:S(2)}, u32[]{:S(2)}) %collective-permute-start.10) | collective-permute-done | bytes 262176 | tf_op jit(solution)/shard_map/ppermute | solution.py:78
  118.4 8.9 %collective-permute-done.9 = f32[128,512]{1,0:T(8,128)} collective-permute-done((f32[128,512]{1,0:T(8,128)S(1)}, f32[128,512]{1,0:T(8,128)}, u32[]{:S(2)}, u32[]{:S(2)}) %collective-permute-start.9) | collective-permute-done | bytes 262176 | tf_op jit(solution)/shard_map/ppermute | solution.py:78
  127.4 6.1 %fusion = (bf16[512,2048]{1,0:T(8,128)(2,1)}, bf16[512,2048]{1,0:T(8,128)(2,1)}, bf16[512,2048]{1,0:T(8,128)(2,1)}) fusion(f32[512,2048]{1,0:T(8,128)} %all-gather.5.cloned.1.call-done), kind=kLoop, calls=%fused_computation.8 | loop fusion | flops 7340032 | bytes 10485760 | tf_op jit(solution)/shard_map/convert_element_type | solution.py:68
  133.4 8.2 %collective-permute-done.12 = f32[128,512]{1,0:T(8,128)} collective-permute-done((f32[128,512]{1,0:T(8,128)S(1)}, f32[128,512]{1,0:T(8,128)}, u32[]{:S(2)}, u32[]{:S(2)}) %collective-permute-start.12) | collective-permute-done | bytes 262176 | tf_op jit(solution)/shard_map/ppermute | solution.py:84
  141.6 1.3 maximum_select_fusion.1
  143.6 1.6 collective-permute-done.13
  145.3 1.1 fusion.29
  (59 shorter events, 22.8 us)
Async XLA Ops:
  6.5 60.2 %all-gather.3.cloned.1.call-start = ((), (), s32[]{:S(2)}) async-start(), calls=%async_computation | async-start | bytes 5242880 | tf_op jit(solution)/shard_map/all_gather | solution.py:40
  7.5 5.2 %collective-permute-start.2 = (f32[128,512]{1,0:T(8,128)S(1)}, f32[128,512]{1,0:T(8,128)S(1)}, u32[]{:S(2)}, u32[]{:S(2)}) collective-permute-start(f32[128,512]{1,0:T(8,128)S(1)} %slice.46), channel_id=1, source_target_pairs={{0,4},{1,5},{2,6},{3,7}} | collective-permute-start | bytes 786440 | tf_op jit(solution)/shard_map/ppermute | solution.py:37
  8.2 4.5 %collective-permute-start.1 = (f32[128,512]{1,0:T(8,128)S(1)}, f32[128,512]{1,0:T(8,128)S(1)}, u32[]{:S(2)}, u32[]{:S(2)}) collective-permute-start(f32[128,512]{1,0:T(8,128)S(1)} %slice.46), channel_id=1, source_target_pairs={{0,8},{1,9},{2,10},{3,11}} | collective-permute-start | bytes 786440 | tf_op jit(solution)/shard_map/ppermute | solution.py:37
  8.9 3.9 %collective-permute-start = (f32[128,512]{1,0:T(8,128)S(1)}, f32[128,512]{1,0:T(8,128)S(1)}, u32[]{:S(2)}, u32[]{:S(2)}) collective-permute-start(f32[128,512]{1,0:T(8,128)S(1)} %slice.46), channel_id=1, source_target_pairs={{0,12},{1,13},{2,14},{3,15}} | collective-permute-start | bytes 786440 | tf_op jit(solution)/shard_map/ppermute | solution.py:37
  9.6 3.2 %copy-start.5 = (f32[128,1024]{1,0:T(8,128)S(1)}, f32[128,1024]{1,0:T(8,128)}, u32[]{:S(2)}) copy-start(f32[128,1024]{1,0:T(8,128)} %param.3) | copy-start | bytes 1572868
  12.9 114.5 %all-gather.5.cloned.1.call-start = ((), (), s32[]{:S(2)}) async-start(), calls=%async_computation.1 | async-start | bytes 5242880 | tf_op jit(solution)/shard_map/all_gather | solution.py:42
  73.9 1.4 collective-permute-start.4
  74.6 0.7 collective-permute-start.3
  80.1 6.6 %collective-permute-start.5 = (f32[128,512]{1,0:T(8,128)S(1)}, f32[128,512]{1,0:T(8,128)S(1)}, u32[]{:S(2)}, u32[]{:S(2)}) collective-permute-start(f32[128,512]{1,0:T(8,128)S(1)} %fusion.12), channel_id=1, source_target_pairs={{8,12},{9,13},{10,14},{11,15}} | collective-permute-start | bytes 786440 | tf_op jit(solution)/shard_map/ppermute | solution.py:60
  91.5 2.7 %collective-permute-start.8 = (f32[128,512]{1,0:T(8,128)S(1)}, f32[128,512]{1,0:T(8,128)S(1)}, u32[]{:S(2)}, u32[]{:S(2)}) collective-permute-start(f32[128,512]{1,0:T(8,128)S(1)} %convolution_select_fusion), channel_id=1, source_target_pairs={{0,64},{4,68},{8,72},{12,76},{1,65},{5,69},{9,73},{13,77},{2,66},{... | collective-permute-start | bytes 786440 | tf_op jit(solution)/shard_map/ppermute | solution.py:78
  92.2 2.0 %collective-permute-start.7 = (f32[128,512]{1,0:T(8,128)S(1)}, f32[128,512]{1,0:T(8,128)S(1)}, u32[]{:S(2)}, u32[]{:S(2)}) collective-permute-start(f32[128,512]{1,0:T(8,128)S(1)} %convolution_select_fusion), channel_id=1, source_target_pairs={{0,128},{4,132},{8,136},{12,140},{1,129},{5,133},{9,137},{13,141},... | collective-permute-start | bytes 786440 | tf_op jit(solution)/shard_map/ppermute | solution.py:78
  92.9 14.7 %collective-permute-start.6 = (f32[128,512]{1,0:T(8,128)S(1)}, f32[128,512]{1,0:T(8,128)}, u32[]{:S(2)}, u32[]{:S(2)}) collective-permute-start(f32[128,512]{1,0:T(8,128)S(1)} %convolution_select_fusion), channel_id=1, source_target_pairs={{0,192},{4,196},{8,200},{12,204},{1,193},{5,197},{9,201},{13,205},... | collective-permute-start | bytes 786440 | tf_op jit(solution)/shard_map/ppermute | solution.py:78
  108.6 6.9 %collective-permute-start.11 = (f32[128,512]{1,0:T(8,128)S(1)}, f32[128,512]{1,0:T(8,128)S(1)}, u32[]{:S(2)}, u32[]{:S(2)}) collective-permute-start(f32[128,512]{1,0:T(8,128)S(1)} %select_select_fusion.1), channel_id=1, source_target_pairs={{0,16},{4,20},{8,24},{12,28},{64,80},{68,84},{72,88},{76,92},{128,... | collective-permute-start | bytes 786440 | tf_op jit(solution)/shard_map/ppermute | solution.py:78
  109.9 8.4 %collective-permute-start.10 = (f32[128,512]{1,0:T(8,128)S(1)}, f32[128,512]{1,0:T(8,128)}, u32[]{:S(2)}, u32[]{:S(2)}) collective-permute-start(f32[128,512]{1,0:T(8,128)S(1)} %select_select_fusion.1), channel_id=1, source_target_pairs={{0,32},{4,36},{8,40},{12,44},{64,96},{68,100},{72,104},{76,108},{1... | collective-permute-start | bytes 786440 | tf_op jit(solution)/shard_map/ppermute | solution.py:78
  111.9 15.3 %collective-permute-start.9 = (f32[128,512]{1,0:T(8,128)S(1)}, f32[128,512]{1,0:T(8,128)}, u32[]{:S(2)}, u32[]{:S(2)}) collective-permute-start(f32[128,512]{1,0:T(8,128)S(1)} %select_select_fusion.1), channel_id=1, source_target_pairs={{0,48},{4,52},{8,56},{12,60},{64,112},{68,116},{72,120},{76,124},{... | collective-permute-start | bytes 786440 | tf_op jit(solution)/shard_map/ppermute | solution.py:78
  115.5 2.8 %copy-start.8 = (f32[128,512]{1,0:T(8,128)}, f32[128,512]{1,0:T(8,128)S(1)}, u32[]{:S(2)}) copy-start(f32[128,512]{1,0:T(8,128)S(1)} %collective-permute-done.11) | copy-start | bytes 786436
  127.3 6.1 %copy-start.6 = (f32[128,512]{1,0:T(8,128)}, f32[128,512]{1,0:T(8,128)S(1)}, u32[]{:S(2)}) copy-start(f32[128,512]{1,0:T(8,128)S(1)} %select_select_fusion) | copy-start | bytes 786436
  133.4 8.2 %collective-permute-start.12 = (f32[128,512]{1,0:T(8,128)S(1)}, f32[128,512]{1,0:T(8,128)}, u32[]{:S(2)}, u32[]{:S(2)}) collective-permute-start(f32[128,512]{1,0:T(8,128)S(1)} %select_select_fusion), channel_id=1, source_target_pairs={{0,8},{4,12},{8,0},{12,4},{16,24},{20,28},{24,16},{28,20},{32,40},... | collective-permute-start | bytes 786440 | tf_op jit(solution)/shard_map/ppermute | solution.py:84
  142.9 2.3 %collective-permute-start.13 = (f32[128,1024]{1,0:T(8,128)S(1)}, f32[128,1024]{1,0:T(8,128)}, u32[]{:S(2)}, u32[]{:S(2)}) collective-permute-start(f32[128,1024]{1,0:T(8,128)S(1)} %maximum_select_fusion.1), channel_id=1, source_target_pairs={{0,4},{4,0},{8,12},{12,8},{16,20},{20,16},{24,28},{28,24},{32,36},... | collective-permute-start | bytes 1572872 | tf_op jit(solution)/shard_map/ppermute | solution.py:86
  146.4 1.6 copy-start.4
  148.0 1.6 copy-start
  149.6 1.6 copy-start.1
  152.9 1.6 copy-start.2
  154.5 1.6 copy-start.3
  (1 other events, 0.7 us)
Sparse Core Ops, SparseCore 0:
  13.0 53.6 all-gather.2
  68.5 51.1 all-gather.4

commit v15 on v12

--- a/solution.py
+++ b/solution.py
@@ -49,6 +49,8 @@
         else:
             solved = contract(top_rhs - acc, inverses[k * block : (k + 1) * block])
         own = jnp.where(row_at == k, solved, own)
+        if k == steps - 2:
+            own_early = own
         if k == steps - 1:
             break
         if k == 0:
@@ -60,17 +62,20 @@
                 arrived = arrived + lax.ppermute(solved, AXES, pairs)
         acc = acc + contract(arrived, lower_first[:, k * block : (k + 1) * block])
 
-    piece = own
     fan_z = min(steps, n_row // steps)
     stride_x = steps * fan_z
-    for stride, fan in ((stride_x, n_row // stride_x), (steps, fan_z)):
-        holders = [p for p in range(n_row) if p % (stride * fan) < steps]
-        received = piece
-        for hop in range(1, fan):
-            pairs = [(p, p + hop * stride) for p in holders]
-            arrived = lax.ppermute(piece, "prow", pairs)
-            received = jnp.where((row_at % (stride * fan)) // stride == hop, arrived, received)
-        piece = jnp.where(row_at % stride < steps, received, piece)
+    spread = []
+    for piece, sources in ((own_early, range(steps - 1)), (own, (steps - 1,))):
+        for stride, fan in ((stride_x, n_row // stride_x), (steps, fan_z)):
+            holders = [p for p in range(n_row) if p % (stride * fan) in sources]
+            received = piece
+            for hop in range(1, fan):
+                pairs = [(p, p + hop * stride) for p in holders]
+                arrived = lax.ppermute(piece, "prow", pairs)
+                received = jnp.where((row_at % (stride * fan)) // stride == hop, arrived, received)
+            piece = jnp.where(row_at % stride < steps, received, piece)
+        spread.append(piece)
+    piece = jnp.where(row_at % steps == steps - 1, spread[1], spread[0])
     b0 = row_at % 2
     b1 = (row_at // 2) % 2
     other = lax.ppermute(piece, "prow", [(p, p ^ 2) for p in range(n_row)])

time: 157 us -> 150 us (0.955)
  the two profiles are of different devices: /device:TPU:3 before, /device:TPU:7 now
where the time goes in v15:
time: 150 us; the launch traced here: 147 us
  waiting for transfers between devices  80.2 us (53%)
  matrix products  29.8 us (20%)
  starting transfers between devices  17.9 us (12%)
  between operations  13.9 us (9%)
  local copies, waits for them, and re-layouts  4.28 us (3%)
    all_gather x1, waiting for transfers between devices, per_device(): lower_first = lax.all_gather(first_rows, 'pcol', axis=1, tiled=True)  53.8 us
    dot_general x9, matrix products, contract(): lax.dot_general(left, right, (((1,), (1,)), ((), ())), precision=lax.Prec...  29.8 us
    ppermute x12, waiting for transfers between devices, per_device(): arrived = lax.ppermute(piece, 'prow', pairs)  18.3 us
    ppermute x12, starting transfers between devices, per_device(): arrived = lax.ppermute(piece, 'prow', pairs)  10.6 us
    ppermute x1, waiting for transfers between devices, per_device(): other = lax.ppermute(piece, 'prow', [(p, p ^ 2) for p in range(n_row)])  6.55 us
    slice x1, local copies, waits for them, and re-layouts, per_device(): factor[:block]  3.17 us
  transfers between devices with their start and end apart: 22, of which 5 were waited for; matrix products, arithmetic and copies ran while one was open for 18% of the time, Pallas kernels for 0%

profile of v15, /device:TPU:7, one launch (start us, length us, event | category | flops | bytes accessed | tf_op | source)
XLA Modules:
  0.0 147.4 jit_solution(12491023725893435237)
XLA Ops:
  6.5 1.0 slice.46
  8.9 0.7 collective-permute-start.2
  9.6 3.2 %fusion.20 = (f32[512,512]{1,0:T(8,128)}, f32[512,512]{1,0:T(8,128)}) fusion(f32[1024,512]{1,0:T(8,128)} %param.4), kind=kLoop, calls=%fused_computation.33 | loop fusion | bytes 4194304 | tf_op jit(solution)/shard_map/slice | solution.py:39
  13.0 53.8 %all-gather.3.cloned.1.call-done = f32[512,2048]{1,0:T(8,128)} async-done(((f32[512,512]{1,0:T(8,128)}), f32[512,2048]{1,0:T(8,128)}) %all-gather.3.cloned.1.call-update) | async-done | bytes 4194320 | tf_op jit(solution)/shard_map/all_gather | solution.py:40
  66.8 2.4 %fusion.11 = f32[128,512]{1,0:T(8,128)S(1)} fusion(f32[128,512]{1,0:T(8,128)S(1)} %select_select_fusion.4, f32[2048,512]{1,0:T(8,128)} %param.5), kind=kOutput, calls=%fused_computation.17 | convolution fusion | flops 402653184 | bytes 1572864 | tf_op jit(solution)/shard_map/dot_general | solution.py:8
  69.2 2.4 %fusion.4 = f32[128,512]{1,0:T(8,128)S(1)} fusion(f32[128,512]{1,0:T(8,128)S(1)} %fusion.11, f32[512,2048]{1,0:T(8,128)} %all-gather.3.cloned.1.call-done), kind=kOutput, calls=%fused_computation.9 | convolution fusion | flops 402653184 | bytes 1572864 | tf_op jit(solution)/shard_map/dot_general | solution.py:8
  71.6 2.4 %fusion.9 = f32[128,512]{1,0:T(8,128)S(1)} fusion(f32[2048,512]{1,0:T(8,128)} %param.5, f32[128,512]{1,0:T(8,128)S(1)} %fusion.4, f32[128,1024]{1,0:T(8,128)S(1)} %copy-done), kind=kOutput, calls=%fused_computation.15 | convolution fusion | flops 402718720 | bytes 1835008 | tf_op jit(solution)/shard_map/dot_general | solution.py:8
  75.4 2.4 %convolution_add_fusion.1 = f32[128,512]{1,0:T(8,128)S(1)} fusion(f32[128,512]{1,0:T(8,128)S(1)} %fusion.4, f32[512,2048]{1,0:T(8,128)} %all-gather.3.cloned.1.call-done, f32[128,512]{1,0:T(8,128)S(1)} %collective-permute-done.3, f32[128,512]{1,0:T(8,128)S(1)} %collective-permute-done.4), kind=kOutput, calls=%fused_computation.6 | convolution fusion | flops 402784256 | bytes 2097152 | tf_op jit(solution)/shard_map/dot_general | solution.py:8
  77.8 2.4 %select_select_fusion.3 = (f32[128,512]{1,0:T(8,128)S(1)}, f32[128,512]{1,0:T(8,128)S(1)}) fusion(f32[128,512]{1,0:T(8,128)S(1)} %fusion.9, f32[128,512]{1,0:T(8,128)S(1)} %fusion.11, pred[]{:T(512)S(6)} %eq.71, pred[]{:T(512)S(6)} %eq.70, pred[]{:T(512)S(6)} %eq.69, f32[2048,512]{1,0:T(8,128)} %param.5, f32[128,512]{1,0:T(8,128)S(1)} %convolution_add_fusion.1, ...), kind=kOutput, calls=%fused_computation.24 | convolution fusion | flops 402915328 | bytes 2621443 | tf_op jit(solution)/shard_map/dot_general | solution.py:8
  81.0 1.3 collective-permute-start.12
  83.6 2.5 %fusion.1 = f32[128,512]{1,0:T(8,128)S(1)} fusion(f32[128,512]{1,0:T(8,128)S(1)} %convolution_add_fusion.1, f32[128,512]{1,0:T(8,128)S(1)} %collective-permute-done.5, f32[512,2048]{1,0:T(8,128)} %all-gather.3.cloned.1.call-done, f32[128,1024]{1,0:T(8,128)S(1)} %copy-done), kind=kOutput, calls=%fused_computation.5 | convolution fusion | flops 402784256 | bytes 2097152 | tf_op jit(solution)/shard_map/dot_general | solution.py:8
  86.1 2.4 %convolution_select_fusion = f32[128,512]{1,0:T(8,128)S(1)} fusion(f32[128,512]{1,0:T(8,128)S(1)} %get-tuple-element.17, f32[128,512]{1,0:T(8,128)S(1)} %fusion.1, f32[2048,512]{1,0:T(8,128)} %param.5, pred[]{:T(512)S(6)} %eq.68), kind=kOutput, calls=%fused_computation.3 | convolution fusion | flops 402718720 | bytes 1835009 | tf_op jit(solution)/shard_map/dot_general | solution.py:8
  89.9 5.3 %collective-permute-done.12 = f32[128,512]{1,0:T(8,128)S(1)} collective-permute-done((f32[128,512]{1,0:T(8,128)S(1)}, f32[128,512]{1,0:T(8,128)S(1)}, u32[]{:S(2)}, u32[]{:S(2)}) %collective-permute-start.12) | collective-permute-done | bytes 262176 | tf_op jit(solution)/shard_map/ppermute | solution.py:74
  96.0 1.3 collective-permute-start.15
  97.3 1.3 collective-permute-start.16
  98.7 1.3 collective-permute-start.17
  101.5 12.9 %collective-permute-done.15 = f32[128,512]{1,0:T(8,128)S(1)} collective-permute-done((f32[128,512]{1,0:T(8,128)S(1)}, f32[128,512]{1,0:T(8,128)S(1)}, u32[]{:S(2)}, u32[]{:S(2)}) %collective-permute-start.15) | collective-permute-done | bytes 262176 | tf_op jit(solution)/shard_map/ppermute | solution.py:74
  115.4 2.2 %collective-permute-start.18 = (f32[128,512]{1,0:T(8,128)S(1)}, f32[128,512]{1,0:T(8,128)S(1)}, u32[]{:S(2)}, u32[]{:S(2)}) collective-permute-start(f32[128,512]{1,0:T(8,128)S(1)} %select_select_fusion), channel_id=1, source_target_pairs={{0,8},{4,12},{8,0},{12,4},{16,24},{20,28},{24,16},{28,20},{32,40},... | collective-permute-start | bytes 786440 | tf_op jit(solution)/shard_map/ppermute | solution.py:81
  117.6 6.6 %collective-permute-done.18 = f32[128,512]{1,0:T(8,128)S(1)} collective-permute-done((f32[128,512]{1,0:T(8,128)S(1)}, f32[128,512]{1,0:T(8,128)S(1)}, u32[]{:S(2)}, u32[]{:S(2)}) %collective-permute-start.18) | collective-permute-done | bytes 262176 | tf_op jit(solution)/shard_map/ppermute | solution.py:81
  124.2 1.0 collective-permute-start.19
  125.2 1.5 %collective-permute-done.19 = f32[128,1024]{1,0:T(8,128)S(1)} collective-permute-done((f32[128,1024]{1,0:T(8,128)S(1)}, f32[128,1024]{1,0:T(8,128)S(1)}, u32[]{:S(2)}, u32[]{:S(2)}) %collective-permute-start.19) | collective-permute-done | bytes 524320 | tf_op jit(solution)/shard_map/ppermute | solution.py:83
  126.7 6.5 %fusion = f32[128,512]{1,0:T(8,128)S(1)} fusion(f32[128,512]{1,0:T(8,128)S(1)} %convolution_select_fusion, f32[512,2048]{1,0:T(8,128)} %all-gather.3.cloned.1.call-done, pred[]{:T(512)S(6)} %lt.61, f32[128,512]{1,0:T(8,128)S(1)} %get-tuple-element.16, f32[128,512]{1,0:T(8,128)S(1)} %get-tuple-element.14, f32[128,512]{1,0:T(8,128)S(1)} %get-tuple-element.15, ...), kind=kOutput, calls=%fused_computation.2 | convolution fusion | flops 1612578816 | bytes 6029314 | tf_op jit(solution)/shard_map/dot_general | solution.py:8
  133.3 6.5 %convolution_subtract_fusion = f32[128,512]{1,0:T(8,128)S(1)} fusion(f32[512,2048]{1,0:T(8,128)} %all-gather.5.cloned.1.call-done, f32[128,1024]{1,0:T(8,128)S(1)} %copy-done, f32[128,512]{1,0:T(8,128)S(1)} %get-tuple-element.16, f32[128,512]{1,0:T(8,128)S(1)} %get-tuple-element.14, f32[128,512]{1,0:T(8,128)S(1)} %get-tuple-element.15, ...), kind=kOutput, calls=%fused_computation | convolution fusion | flops 1612513280 | bytes 5767169 | tf_op jit(solution)/shard_map/dot_general | solution.py:8
  139.8 0.8 pad_maximum_fusion
  (43 shorter events, 9.6 us)
Async XLA Ops:
  6.5 6.3 %copy-start = (f32[128,1024]{1,0:T(8,128)S(1)}, f32[128,1024]{1,0:T(8,128)}, u32[]{:S(2)}) copy-start(f32[128,1024]{1,0:T(8,128)} %param.3) | copy-start | bytes 1572868
  6.5 60.3 %all-gather.3.cloned.1.call-start = ((), (), s32[]{:S(2)}) async-start(), calls=%async_computation | async-start | bytes 5242880 | tf_op jit(solution)/shard_map/all_gather | solution.py:40
  7.6 5.2 %collective-permute-start = (f32[128,512]{1,0:T(8,128)S(1)}, f32[128,512]{1,0:T(8,128)S(1)}, u32[]{:S(2)}, u32[]{:S(2)}) collective-permute-start(f32[128,512]{1,0:T(8,128)S(1)} %slice.46), channel_id=1, source_target_pairs={{0,12},{1,13},{2,14},{3,15}} | collective-permute-start | bytes 786440 | tf_op jit(solution)/shard_map/ppermute | solution.py:37
  8.3 4.6 %collective-permute-start.1 = (f32[128,512]{1,0:T(8,128)S(1)}, f32[128,512]{1,0:T(8,128)S(1)}, u32[]{:S(2)}, u32[]{:S(2)}) collective-permute-start(f32[128,512]{1,0:T(8,128)S(1)} %slice.46), channel_id=1, source_target_pairs={{0,8},{1,9},{2,10},{3,11}} | collective-permute-start | bytes 786440 | tf_op jit(solution)/shard_map/ppermute | solution.py:37
  8.9 3.9 %collective-permute-start.2 = (f32[128,512]{1,0:T(8,128)S(1)}, f32[128,512]{1,0:T(8,128)S(1)}, u32[]{:S(2)}, u32[]{:S(2)}) collective-permute-start(f32[128,512]{1,0:T(8,128)S(1)} %slice.46), channel_id=1, source_target_pairs={{0,4},{1,5},{2,6},{3,7}} | collective-permute-start | bytes 786440 | tf_op jit(solution)/shard_map/ppermute | solution.py:37
  13.0 120.3 %all-gather.5.cloned.1.call-start = ((), (), s32[]{:S(2)}) async-start(), calls=%async_computation.1 | async-start | bytes 5242880 | tf_op jit(solution)/shard_map/all_gather | solution.py:42
  74.0 1.4 collective-permute-start.3
  74.7 0.7 collective-permute-start.4
  80.2 3.4 %collective-permute-start.5 = (f32[128,512]{1,0:T(8,128)S(1)}, f32[128,512]{1,0:T(8,128)S(1)}, u32[]{:S(2)}, u32[]{:S(2)}) collective-permute-start(f32[128,512]{1,0:T(8,128)S(1)} %get-tuple-element.18), channel_id=1, source_target_pairs={{8,12},{9,13},{10,14},{11,15}} | collective-permute-start | bytes 786440 | tf_op jit(solution)/shard_map/ppermute | solution.py:62
  81.0 14.3 %collective-permute-start.12 = (f32[128,512]{1,0:T(8,128)S(1)}, f32[128,512]{1,0:T(8,128)S(1)}, u32[]{:S(2)}, u32[]{:S(2)}) collective-permute-start(f32[128,512]{1,0:T(8,128)S(1)} %get-tuple-element.17), channel_id=1, source_target_pairs={{0,192},{4,196},{8,200},{1,193},{5,197},{9,201},{2,194},{6,198},{1... | collective-permute-start | bytes 786440 | tf_op jit(solution)/shard_map/ppermute | solution.py:74
  82.3 13.6 %collective-permute-start.13 = (f32[128,512]{1,0:T(8,128)S(1)}, f32[128,512]{1,0:T(8,128)S(1)}, u32[]{:S(2)}, u32[]{:S(2)}) collective-permute-start(f32[128,512]{1,0:T(8,128)S(1)} %get-tuple-element.17), channel_id=1, source_target_pairs={{0,128},{4,132},{8,136},{1,129},{5,133},{9,137},{2,130},{6,134},{1... | collective-permute-start | bytes 786440 | tf_op jit(solution)/shard_map/ppermute | solution.py:74
  82.9 13.0 %collective-permute-start.14 = (f32[128,512]{1,0:T(8,128)S(1)}, f32[128,512]{1,0:T(8,128)S(1)}, u32[]{:S(2)}, u32[]{:S(2)}) collective-permute-start(f32[128,512]{1,0:T(8,128)S(1)} %get-tuple-element.17), channel_id=1, source_target_pairs={{0,64},{4,68},{8,72},{1,65},{5,69},{9,73},{2,66},{6,70},{10,74},{3... | collective-permute-start | bytes 786440 | tf_op jit(solution)/shard_map/ppermute | solution.py:74
  88.5 10.1 %collective-permute-start.6 = (f32[128,512]{1,0:T(8,128)S(1)}, f32[128,512]{1,0:T(8,128)S(1)}, u32[]{:S(2)}, u32[]{:S(2)}) collective-permute-start(f32[128,512]{1,0:T(8,128)S(1)} %convolution_select_fusion), channel_id=1, source_target_pairs={{12,204},{13,205},{14,206},{15,207}} | collective-permute-start | bytes 786440 | tf_op jit(solution)/shard_map/ppermute | solution.py:74
  89.2 10.8 %collective-permute-start.7 = (f32[128,512]{1,0:T(8,128)S(1)}, f32[128,512]{1,0:T(8,128)S(1)}, u32[]{:S(2)}, u32[]{:S(2)}) collective-permute-start(f32[128,512]{1,0:T(8,128)S(1)} %convolution_select_fusion), channel_id=1, source_target_pairs={{12,140},{13,141},{14,142},{15,143}} | collective-permute-start | bytes 786440 | tf_op jit(solution)/shard_map/ppermute | solution.py:74
  95.2 4.8 %collective-permute-start.8 = (f32[128,512]{1,0:T(8,128)S(1)}, f32[128,512]{1,0:T(8,128)S(1)}, u32[]{:S(2)}, u32[]{:S(2)}) collective-permute-start(f32[128,512]{1,0:T(8,128)S(1)} %convolution_select_fusion), channel_id=1, source_target_pairs={{12,76},{13,77},{14,78},{15,79}} | collective-permute-start | bytes 786440 | tf_op jit(solution)/shard_map/ppermute | solution.py:74
  96.0 18.4 %collective-permute-start.15 = (f32[128,512]{1,0:T(8,128)S(1)}, f32[128,512]{1,0:T(8,128)S(1)}, u32[]{:S(2)}, u32[]{:S(2)}) collective-permute-start(f32[128,512]{1,0:T(8,128)S(1)} %select_select_fusion.1), channel_id=1, source_target_pairs={{0,48},{4,52},{8,56},{64,112},{68,116},{72,120},{128,176},{132,180... | collective-permute-start | bytes 786440 | tf_op jit(solution)/shard_map/ppermute | solution.py:74
  97.3 17.8 %collective-permute-start.16 = (f32[128,512]{1,0:T(8,128)S(1)}, f32[128,512]{1,0:T(8,128)S(1)}, u32[]{:S(2)}, u32[]{:S(2)}) collective-permute-start(f32[128,512]{1,0:T(8,128)S(1)} %select_select_fusion.1), channel_id=1, source_target_pairs={{0,32},{4,36},{8,40},{64,96},{68,100},{72,104},{128,160},{132,164}... | collective-permute-start | bytes 786440 | tf_op jit(solution)/shard_map/ppermute | solution.py:74
  98.7 16.5 %collective-permute-start.17 = (f32[128,512]{1,0:T(8,128)S(1)}, f32[128,512]{1,0:T(8,128)S(1)}, u32[]{:S(2)}, u32[]{:S(2)}) collective-permute-start(f32[128,512]{1,0:T(8,128)S(1)} %select_select_fusion.1), channel_id=1, source_target_pairs={{0,16},{4,20},{8,24},{64,80},{68,84},{72,88},{128,144},{132,148},{... | collective-permute-start | bytes 786440 | tf_op jit(solution)/shard_map/ppermute | solution.py:74
  100.1 15.0 %collective-permute-start.10 = (f32[128,512]{1,0:T(8,128)S(1)}, f32[128,512]{1,0:T(8,128)S(1)}, u32[]{:S(2)}, u32[]{:S(2)}) collective-permute-start(f32[128,512]{1,0:T(8,128)S(1)} %select_select_fusion.2), channel_id=1, source_target_pairs={{12,44},{76,108},{140,172},{204,236},{13,45},{77,109},{141,173},{2... | collective-permute-start | bytes 786440 | tf_op jit(solution)/shard_map/ppermute | solution.py:74
  100.8 14.4 %collective-permute-start.11 = (f32[128,512]{1,0:T(8,128)S(1)}, f32[128,512]{1,0:T(8,128)S(1)}, u32[]{:S(2)}, u32[]{:S(2)}) collective-permute-start(f32[128,512]{1,0:T(8,128)S(1)} %select_select_fusion.2), channel_id=1, source_target_pairs={{12,28},{76,92},{140,156},{204,220},{13,29},{77,93},{141,157},{205... | collective-permute-start | bytes 786440 | tf_op jit(solution)/shard_map/ppermute | solution.py:74
  114.4 0.8 collective-permute-start.9
  115.4 8.7 %collective-permute-start.18 = (f32[128,512]{1,0:T(8,128)S(1)}, f32[128,512]{1,0:T(8,128)S(1)}, u32[]{:S(2)}, u32[]{:S(2)}) collective-permute-start(f32[128,512]{1,0:T(8,128)S(1)} %select_select_fusion), channel_id=1, source_target_pairs={{0,8},{4,12},{8,0},{12,4},{16,24},{20,28},{24,16},{28,20},{32,40},... | collective-permute-start | bytes 786440 | tf_op jit(solution)/shard_map/ppermute | solution.py:81
  124.2 2.5 %collective-permute-start.19 = (f32[128,1024]{1,0:T(8,128)S(1)}, f32[128,1024]{1,0:T(8,128)S(1)}, u32[]{:S(2)}, u32[]{:S(2)}) collective-permute-start(f32[128,1024]{1,0:T(8,128)S(1)} %maximum_select_fusion.1), channel_id=1, source_target_pairs={{0,4},{4,0},{8,12},{12,8},{16,20},{20,16},{24,28},{28,24},{32,36},... | collective-permute-start | bytes 1572872 | tf_op jit(solution)/shard_map/ppermute | solution.py:83
Sparse Core Ops, SparseCore 0:
  13.1 53.6 all-gather.2
  68.6 51.1 all-gather.4

commit v16 on v15

--- a/solution.py
+++ b/solution.py
@@ -75,7 +75,7 @@
                 received = jnp.where((row_at % (stride * fan)) // stride == hop, arrived, received)
             piece = jnp.where(row_at % stride < steps, received, piece)
         spread.append(piece)
-    piece = jnp.where(row_at % steps == steps - 1, spread[1], spread[0])
+    piece = spread[0]
     b0 = row_at % 2
     b1 = (row_at // 2) % 2
     other = lax.ppermute(piece, "prow", [(p, p ^ 2) for p in range(n_row)])
@@ -85,9 +85,18 @@
     mine_first = jnp.concatenate([mine[0], yours[0], mine[1], yours[1]], axis=1)
     theirs_first = jnp.concatenate([yours[0], mine[0], yours[1], mine[1]], axis=1)
     panel = jnp.where(b0 == 0, mine_first, theirs_first)
+    last = jnp.where(row_at % steps == steps - 1, spread[1], jnp.zeros_like(spread[1]))
+    for mask in range(1, steps):
+        pairs = [(p, p ^ mask) for p in range(n_row) if p % steps == steps - 1]
+        last = last + lax.ppermute(spread[1], "prow", pairs)
+    last_cols = slice((steps - 1) * block, steps * block)
 
-    second = right_side[:, block:] - contract(panel, lower_second)
-    first = right_side[:, :block] - contract(panel, lower_first)
+    second = right_side[:, block:] - (
+        contract(panel, lower_second) + contract(last, lower_second[:, last_cols])
+    )
+    first = right_side[:, :block] - (
+        contract(panel, lower_first) + contract(last, lower_first[:, last_cols])
+    )
     head_block = jnp.where(row_at < steps, own, first)
     return jnp.concatenate([head_block, second], axis=1)
 

time: 150 us -> 156 us (1.040)
  the two profiles are of different devices: /device:TPU:7 before, /device:TPU:4 now
where the time goes in v16:
time: 156 us; the launch traced here: 155 us
  waiting for transfers between devices  80.1 us (51%)
  matrix products  31.3 us (20%)
  starting transfers between devices  24 us (15%)
  between operations  14 us (9%)
  local copies, waits for them, and re-layouts  4.26 us (3%)
    all_gather x1, waiting for transfers between devices, per_device(): lower_first = lax.all_gather(first_rows, 'pcol', axis=1, tiled=True)  53.9 us
    dot_general x11, matrix products, contract(): lax.dot_general(left, right, (((1,), (1,)), ((), ())), precision=lax.Prec...  31.3 us
    ppermute x12, starting transfers between devices, per_device(): arrived = lax.ppermute(piece, 'prow', pairs)  16.7 us
    ppermute x12, waiting for transfers between devices, per_device(): arrived = lax.ppermute(piece, 'prow', pairs)  15.9 us
    ppermute x1, waiting for transfers between devices, per_device(): other = lax.ppermute(piece, 'prow', [(p, p ^ 2) for p in range(n_row)])  6.04 us
    ppermute x3, waiting for transfers between devices, per_device(): last = last + lax.ppermute(spread[1], 'prow', pairs)  4.2 us
    slice x1, local copies, waits for them, and re-layouts, per_device(): second_rows, _ = lax.optimization_barrier((factor[block:], lower_first))  3.15 us
  transfers between devices with their start and end apart: 25, of which 7 were waited for; matrix products, arithmetic and copies ran while one was open for 17% of the time, Pallas kernels for 0%

profile of v16, /device:TPU:4, one launch (start us, length us, event | category | flops | bytes accessed | tf_op | source)
XLA Modules:
  0.0 155.1 jit_solution(11421569683290515868)
XLA Ops:
  9.6 3.1 %fusion.26 = (f32[512,512]{1,0:T(8,128)}, f32[512,512]{1,0:T(8,128)}) fusion(f32[1024,512]{1,0:T(8,128)} %param.4), kind=kLoop, calls=%fused_computation.41 | loop fusion | bytes 4194304 | tf_op jit(solution)/shard_map/slice | solution.py:41
  13.0 53.9 %all-gather.3.cloned.1.call-done = f32[512,2048]{1,0:T(8,128)} async-done(((f32[512,512]{1,0:T(8,128)}), f32[512,2048]{1,0:T(8,128)}) %all-gather.3.cloned.1.call-update) | async-done | bytes 4194320 | tf_op jit(solution)/shard_map/all_gather | solution.py:40
  66.9 2.4 %fusion.17 = f32[128,512]{1,0:T(8,128)S(1)} fusion(f32[128,512]{1,0:T(8,128)S(1)} %select_select_fusion.5, f32[2048,512]{1,0:T(8,128)} %param.5), kind=kOutput, calls=%fused_computation.23 | convolution fusion | flops 402653184 | bytes 1572864 | tf_op jit(solution)/shard_map/dot_general | solution.py:8
  69.3 2.4 %fusion.10 = f32[128,512]{1,0:T(8,128)S(1)} fusion(f32[128,512]{1,0:T(8,128)S(1)} %fusion.17, f32[512,2048]{1,0:T(8,128)} %all-gather.3.cloned.1.call-done), kind=kOutput, calls=%fused_computation.15 | convolution fusion | flops 402653184 | bytes 1572864 | tf_op jit(solution)/shard_map/dot_general | solution.py:8
  71.7 2.4 %fusion.15 = f32[128,512]{1,0:T(8,128)S(1)} fusion(f32[2048,512]{1,0:T(8,128)} %param.5, f32[128,512]{1,0:T(8,128)S(1)} %fusion.10, f32[128,1024]{1,0:T(8,128)S(1)} %copy-done.1), kind=kOutput, calls=%fused_computation.21 | convolution fusion | flops 402718720 | bytes 1835008 | tf_op jit(solution)/shard_map/dot_general | solution.py:8
  75.5 2.4 %convolution_add_fusion.3 = f32[128,512]{1,0:T(8,128)S(1)} fusion(f32[128,512]{1,0:T(8,128)S(1)} %fusion.10, f32[512,2048]{1,0:T(8,128)} %all-gather.3.cloned.1.call-done, f32[128,512]{1,0:T(8,128)S(1)} %collective-permute-done.3, f32[128,512]{1,0:T(8,128)S(1)} %collective-permute-done.4), kind=kOutput, calls=%fused_computation.8 | convolution fusion | flops 402784256 | bytes 2097152 | tf_op jit(solution)/shard_map/dot_general | solution.py:8
  77.9 2.4 %select_select_fusion.4 = (f32[128,512]{1,0:T(8,128)S(1)}, f32[128,512]{1,0:T(8,128)S(1)}) fusion(f32[128,512]{1,0:T(8,128)S(1)} %fusion.15, f32[128,512]{1,0:T(8,128)S(1)} %fusion.17, pred[]{:T(512)S(6)} %eq.71, pred[]{:T(512)S(6)} %eq.70, pred[]{:T(512)S(6)} %eq.69, f32[2048,512]{1,0:T(8,128)} %param.5, f32[128,512]{1,0:T(8,128)S(1)} %convolution_add_fusion.3, ...), kind=kOutput, calls=%fused_computation.32 | convolution fusion | flops 402915328 | bytes 2621443 | tf_op jit(solution)/shard_map/dot_general | solution.py:8
  81.6 1.3 collective-permute-start.7
  83.6 2.5 %fusion.3 = f32[128,512]{1,0:T(8,128)S(1)} fusion(f32[128,512]{1,0:T(8,128)S(1)} %convolution_add_fusion.3, f32[128,512]{1,0:T(8,128)S(1)} %collective-permute-done.5, f32[512,2048]{1,0:T(8,128)} %all-gather.3.cloned.1.call-done, f32[128,1024]{1,0:T(8,128)S(1)} %copy-done.1), kind=kOutput, calls=%fused_computation.7 | convolution fusion | flops 402784256 | bytes 2097152 | tf_op jit(solution)/shard_map/dot_general | solution.py:8
  86.1 2.4 %convolution_select_fusion = f32[128,512]{1,0:T(8,128)S(1)} fusion(f32[128,512]{1,0:T(8,128)S(1)} %get-tuple-element.17, f32[128,512]{1,0:T(8,128)S(1)} %fusion.3, f32[2048,512]{1,0:T(8,128)} %param.5, pred[]{:T(512)S(6)} %eq.68), kind=kOutput, calls=%fused_computation.5 | convolution fusion | flops 402718720 | bytes 1835009 | tf_op jit(solution)/shard_map/dot_general | solution.py:8
  90.0 1.4 collective-permute-start.16
  91.8 6.6 %collective-permute-start.10 = (f32[128,512]{1,0:T(8,128)S(1)}, f32[128,512]{1,0:T(8,128)S(1)}, u32[]{:S(2)}, u32[]{:S(2)}) collective-permute-start(f32[128,512]{1,0:T(8,128)S(1)} %select_select_fusion.3), channel_id=1, source_target_pairs={{0,32},{4,36},{8,40},{64,96},{68,100},{72,104},{128,160},{132,164}... | collective-permute-start | bytes 786440 | tf_op jit(solution)/shard_map/ppermute | solution.py:74
  98.5 1.3 collective-permute-start.11
  99.8 1.3 collective-permute-start.9
  102.7 2.5 %collective-permute-done.10 = f32[128,512]{1,0:T(8,128)S(1)} collective-permute-done((f32[128,512]{1,0:T(8,128)S(1)}, f32[128,512]{1,0:T(8,128)S(1)}, u32[]{:S(2)}, u32[]{:S(2)}) %collective-permute-start.10) | collective-permute-done | bytes 262176 | tf_op jit(solution)/shard_map/ppermute | solution.py:74
  105.9 4.8 %collective-permute-done.11 = f32[128,512]{1,0:T(8,128)S(1)} collective-permute-done((f32[128,512]{1,0:T(8,128)S(1)}, f32[128,512]{1,0:T(8,128)S(1)}, u32[]{:S(2)}, u32[]{:S(2)}) %collective-permute-start.11) | collective-permute-done | bytes 262176 | tf_op jit(solution)/shard_map/ppermute | solution.py:74
  110.6 8.2 %collective-permute-done.9 = f32[128,512]{1,0:T(8,128)S(1)} collective-permute-done((f32[128,512]{1,0:T(8,128)S(1)}, f32[128,512]{1,0:T(8,128)S(1)}, u32[]{:S(2)}, u32[]{:S(2)}) %collective-permute-start.9) | collective-permute-done | bytes 262176 | tf_op jit(solution)/shard_map/ppermute | solution.py:74
  120.9 1.3 collective-permute-start.22
  122.2 6.0 %collective-permute-done.12 = f32[128,512]{1,0:T(8,128)S(1)} collective-permute-done((f32[128,512]{1,0:T(8,128)S(1)}, f32[128,512]{1,0:T(8,128)S(1)}, u32[]{:S(2)}, u32[]{:S(2)}) %collective-permute-start.12) | collective-permute-done | bytes 262176 | tf_op jit(solution)/shard_map/ppermute | solution.py:81
  128.6 4.2 %collective-permute-done.22 = f32[128,512]{1,0:T(8,128)S(1)} collective-permute-done((f32[128,512]{1,0:T(8,128)S(1)}, f32[128,512]{1,0:T(8,128)S(1)}, u32[]{:S(2)}, u32[]{:S(2)}) %collective-permute-start.22) | collective-permute-done | bytes 262176 | tf_op jit(solution)/shard_map/ppermute | solution.py:91
  132.9 1.2 fusion.6
  134.2 4.4 %fusion.2 = f32[128,512]{1,0:T(8,128)S(1)} fusion(f32[128,512]{1,0:T(8,128)S(1)} %convolution_select_fusion, f32[128,512]{1,0:T(8,128)S(1)} %fusion.6, f32[512,2048]{1,0:T(8,128)S(1)} %copy-done, pred[]{:T(512)S(6)} %lt.61, f32[128,512]{1,0:T(8,128)S(1)} %get-tuple-element.16, f32[128,512]{1,0:T(8,128)S(1)} %get-tuple-element.14, ...), kind=kOutput, calls=%fused_computation.4 | convolution fusion | flops 1612644352 | bytes 6291458 | tf_op jit(solution)/shard_map/dot_general | solution.py:8
  138.6 2.4 %fusion.4 = f32[128,512]{1,0:T(8,128)S(1)} fusion(f32[128,512]{1,0:T(8,128)S(1)} %add_add_fusion, f32[512,2048]{1,0:T(8,128)} %all-gather.5.cloned.1.call-done), kind=kOutput, calls=%fused_computation.9 | convolution fusion | flops 402653184 | bytes 1572864 | tf_op jit(solution)/shard_map/dot_general | solution.py:8
  141.0 6.5 %fusion = f32[128,512]{1,0:T(8,128)S(1)} fusion(f32[128,512]{1,0:T(8,128)S(1)} %fusion.4, f32[512,2048]{1,0:T(8,128)} %all-gather.5.cloned.1.call-done, f32[128,1024]{1,0:T(8,128)S(1)} %copy-done.1, f32[128,512]{1,0:T(8,128)S(1)} %get-tuple-element.16, f32[128,512]{1,0:T(8,128)S(1)} %get-tuple-element.14, f32[128,512]{1,0:T(8,128)S(1)} %get-tuple-element.15, ...), kind=kOutput, calls=%fused_computation.1 | convolution fusion | flops 1612578816 | bytes 6029313 | tf_op jit(solution)/shard_map/dot_general | solution.py:8
  (55 shorter events, 13.9 us)
Async XLA Ops:
  6.5 60.3 %all-gather.3.cloned.1.call-start = ((), (), s32[]{:S(2)}) async-start(), calls=%async_computation | async-start | bytes 5242880 | tf_op jit(solution)/shard_map/all_gather | solution.py:40
  7.6 5.2 %collective-permute-start = (f32[128,512]{1,0:T(8,128)S(1)}, f32[128,512]{1,0:T(8,128)S(1)}, u32[]{:S(2)}, u32[]{:S(2)}) collective-permute-start(f32[128,512]{1,0:T(8,128)S(1)} %slice.52), channel_id=1, source_target_pairs={{0,12},{1,13},{2,14},{3,15}} | collective-permute-start | bytes 786440 | tf_op jit(solution)/shard_map/ppermute | solution.py:37
  8.3 4.5 %collective-permute-start.1 = (f32[128,512]{1,0:T(8,128)S(1)}, f32[128,512]{1,0:T(8,128)S(1)}, u32[]{:S(2)}, u32[]{:S(2)}) collective-permute-start(f32[128,512]{1,0:T(8,128)S(1)} %slice.52), channel_id=1, source_target_pairs={{0,8},{1,9},{2,10},{3,11}} | collective-permute-start | bytes 786440 | tf_op jit(solution)/shard_map/ppermute | solution.py:37
  8.9 3.9 %collective-permute-start.2 = (f32[128,512]{1,0:T(8,128)S(1)}, f32[128,512]{1,0:T(8,128)S(1)}, u32[]{:S(2)}, u32[]{:S(2)}) collective-permute-start(f32[128,512]{1,0:T(8,128)S(1)} %slice.52), channel_id=1, source_target_pairs={{0,4},{1,5},{2,6},{3,7}} | collective-permute-start | bytes 786440 | tf_op jit(solution)/shard_map/ppermute | solution.py:37
  12.9 125.6 %all-gather.5.cloned.1.call-start = ((), (), s32[]{:S(2)}) async-start(), calls=%async_computation.1 | async-start | bytes 5242880 | tf_op jit(solution)/shard_map/all_gather | solution.py:42
  74.1 1.4 collective-permute-start.3
  80.3 3.4 %collective-permute-start.5 = (f32[128,512]{1,0:T(8,128)S(1)}, f32[128,512]{1,0:T(8,128)S(1)}, u32[]{:S(2)}, u32[]{:S(2)}) collective-permute-start(f32[128,512]{1,0:T(8,128)S(1)} %get-tuple-element.18), channel_id=1, source_target_pairs={{8,12},{9,13},{10,14},{11,15}} | collective-permute-start | bytes 786440 | tf_op jit(solution)/shard_map/ppermute | solution.py:62
  81.0 9.0 %collective-permute-start.6 = (f32[128,512]{1,0:T(8,128)S(1)}, f32[128,512]{1,0:T(8,128)S(1)}, u32[]{:S(2)}, u32[]{:S(2)}) collective-permute-start(f32[128,512]{1,0:T(8,128)S(1)} %get-tuple-element.17), channel_id=1, source_target_pairs={{0,192},{4,196},{8,200},{1,193},{5,197},{9,201},{2,194},{6,198},{1... | collective-permute-start | bytes 786440 | tf_op jit(solution)/shard_map/ppermute | solution.py:74
  81.6 10.1 %collective-permute-start.7 = (f32[128,512]{1,0:T(8,128)S(1)}, f32[128,512]{1,0:T(8,128)S(1)}, u32[]{:S(2)}, u32[]{:S(2)}) collective-permute-start(f32[128,512]{1,0:T(8,128)S(1)} %get-tuple-element.17), channel_id=1, source_target_pairs={{0,128},{4,132},{8,136},{1,129},{5,133},{9,137},{2,130},{6,134},{1... | collective-permute-start | bytes 786440 | tf_op jit(solution)/shard_map/ppermute | solution.py:74
  82.9 8.8 %collective-permute-start.8 = (f32[128,512]{1,0:T(8,128)S(1)}, f32[128,512]{1,0:T(8,128)S(1)}, u32[]{:S(2)}, u32[]{:S(2)}) collective-permute-start(f32[128,512]{1,0:T(8,128)S(1)} %get-tuple-element.17), channel_id=1, source_target_pairs={{0,64},{4,68},{8,72},{1,65},{5,69},{9,73},{2,66},{6,70},{10,74},{3... | collective-permute-start | bytes 786440 | tf_op jit(solution)/shard_map/ppermute | solution.py:74
  88.5 11.3 %collective-permute-start.14 = (f32[128,512]{1,0:T(8,128)S(1)}, f32[128,512]{1,0:T(8,128)S(1)}, u32[]{:S(2)}, u32[]{:S(2)}) collective-permute-start(f32[128,512]{1,0:T(8,128)S(1)} %convolution_select_fusion), channel_id=1, source_target_pairs={{12,204},{13,205},{14,206},{15,207}} | collective-permute-start | bytes 786440 | tf_op jit(solution)/shard_map/ppermute | solution.py:74
  89.3 11.9 %collective-permute-start.15 = (f32[128,512]{1,0:T(8,128)S(1)}, f32[128,512]{1,0:T(8,128)S(1)}, u32[]{:S(2)}, u32[]{:S(2)}) collective-permute-start(f32[128,512]{1,0:T(8,128)S(1)} %convolution_select_fusion), channel_id=1, source_target_pairs={{12,140},{13,141},{14,142},{15,143}} | collective-permute-start | bytes 786440 | tf_op jit(solution)/shard_map/ppermute | solution.py:74
  90.0 11.2 %collective-permute-start.16 = (f32[128,512]{1,0:T(8,128)S(1)}, f32[128,512]{1,0:T(8,128)}, u32[]{:S(2)}, u32[]{:S(2)}) collective-permute-start(f32[128,512]{1,0:T(8,128)S(1)} %convolution_select_fusion), channel_id=1, source_target_pairs={{12,76},{13,77},{14,78},{15,79}} | collective-permute-start | bytes 786440 | tf_op jit(solution)/shard_map/ppermute | solution.py:74
  91.8 13.4 %collective-permute-start.10 = (f32[128,512]{1,0:T(8,128)S(1)}, f32[128,512]{1,0:T(8,128)S(1)}, u32[]{:S(2)}, u32[]{:S(2)}) collective-permute-start(f32[128,512]{1,0:T(8,128)S(1)} %select_select_fusion.3), channel_id=1, source_target_pairs={{0,32},{4,36},{8,40},{64,96},{68,100},{72,104},{128,160},{132,164}... | collective-permute-start | bytes 786440 | tf_op jit(solution)/shard_map/ppermute | solution.py:74
  98.5 12.1 %collective-permute-start.11 = (f32[128,512]{1,0:T(8,128)S(1)}, f32[128,512]{1,0:T(8,128)S(1)}, u32[]{:S(2)}, u32[]{:S(2)}) collective-permute-start(f32[128,512]{1,0:T(8,128)S(1)} %select_select_fusion.3), channel_id=1, source_target_pairs={{0,16},{4,20},{8,24},{64,80},{68,84},{72,88},{128,144},{132,148},{... | collective-permute-start | bytes 786440 | tf_op jit(solution)/shard_map/ppermute | solution.py:74
  99.8 19.0 %collective-permute-start.9 = (f32[128,512]{1,0:T(8,128)S(1)}, f32[128,512]{1,0:T(8,128)S(1)}, u32[]{:S(2)}, u32[]{:S(2)}) collective-permute-start(f32[128,512]{1,0:T(8,128)S(1)} %select_select_fusion.3), channel_id=1, source_target_pairs={{0,48},{4,52},{8,56},{64,112},{68,116},{72,120},{128,176},{132,180... | collective-permute-start | bytes 786440 | tf_op jit(solution)/shard_map/ppermute | solution.py:74
  101.3 17.8 %collective-permute-start.17 = (f32[128,512]{1,0:T(8,128)S(1)}, f32[128,512]{1,0:T(8,128)S(1)}, u32[]{:S(2)}, u32[]{:S(2)}) collective-permute-start(f32[128,512]{1,0:T(8,128)S(1)} %select_select_fusion.1), channel_id=1, source_target_pairs={{12,60},{76,124},{140,188},{204,252},{13,61},{77,125},{141,189},{2... | collective-permute-start | bytes 786440 | tf_op jit(solution)/shard_map/ppermute | solution.py:74
  102.0 17.1 %collective-permute-start.18 = (f32[128,512]{1,0:T(8,128)S(1)}, f32[128,512]{1,0:T(8,128)S(1)}, u32[]{:S(2)}, u32[]{:S(2)}) collective-permute-start(f32[128,512]{1,0:T(8,128)S(1)} %select_select_fusion.1), channel_id=1, source_target_pairs={{12,44},{76,108},{140,172},{204,236},{13,45},{77,109},{141,173},{2... | collective-permute-start | bytes 786440 | tf_op jit(solution)/shard_map/ppermute | solution.py:74
  105.2 13.9 %collective-permute-start.19 = (f32[128,512]{1,0:T(8,128)S(1)}, f32[128,512]{1,0:T(8,128)S(1)}, u32[]{:S(2)}, u32[]{:S(2)}) collective-permute-start(f32[128,512]{1,0:T(8,128)S(1)} %select_select_fusion.1), channel_id=1, source_target_pairs={{12,28},{76,92},{140,156},{204,220},{13,29},{77,93},{141,157},{205... | collective-permute-start | bytes 786440 | tf_op jit(solution)/shard_map/ppermute | solution.py:74
  118.9 9.3 %collective-permute-start.12 = (f32[128,512]{1,0:T(8,128)S(1)}, f32[128,512]{1,0:T(8,128)S(1)}, u32[]{:S(2)}, u32[]{:S(2)}) collective-permute-start(f32[128,512]{1,0:T(8,128)S(1)} %select_select_fusion.2), channel_id=1, source_target_pairs={{0,8},{4,12},{8,0},{12,4},{16,24},{20,28},{24,16},{28,20},{32,40},... | collective-permute-start | bytes 786440 | tf_op jit(solution)/shard_map/ppermute | solution.py:81
  119.2 9.4 %collective-permute-start.20 = (f32[128,512]{1,0:T(8,128)S(1)}, f32[128,512]{1,0:T(8,128)S(1)}, u32[]{:S(2)}, u32[]{:S(2)}) collective-permute-start(f32[128,512]{1,0:T(8,128)S(1)} %select_select_fusion), channel_id=1, source_target_pairs={{12,8},{28,24},{44,40},{60,56},{76,72},{92,88},{108,104},{124,120}... | collective-permute-start | bytes 786440 | tf_op jit(solution)/shard_map/ppermute | solution.py:91
  120.1 8.5 %collective-permute-start.21 = (f32[128,512]{1,0:T(8,128)S(1)}, f32[128,512]{1,0:T(8,128)S(1)}, u32[]{:S(2)}, u32[]{:S(2)}) collective-permute-start(f32[128,512]{1,0:T(8,128)S(1)} %select_select_fusion), channel_id=1, source_target_pairs={{12,4},{28,20},{44,36},{60,52},{76,68},{92,84},{108,100},{124,116}... | collective-permute-start | bytes 786440 | tf_op jit(solution)/shard_map/ppermute | solution.py:91
  120.9 11.9 %collective-permute-start.22 = (f32[128,512]{1,0:T(8,128)S(1)}, f32[128,512]{1,0:T(8,128)S(1)}, u32[]{:S(2)}, u32[]{:S(2)}) collective-permute-start(f32[128,512]{1,0:T(8,128)S(1)} %select_select_fusion), channel_id=1, source_target_pairs={{12,0},{28,16},{44,32},{60,48},{76,64},{92,80},{108,96},{124,112},... | collective-permute-start | bytes 786440 | tf_op jit(solution)/shard_map/ppermute | solution.py:91
  128.3 5.8 %collective-permute-start.13 = (f32[128,1024]{1,0:T(8,128)S(1)}, f32[128,1024]{1,0:T(8,128)S(1)}, u32[]{:S(2)}, u32[]{:S(2)}) collective-permute-start(f32[128,1024]{1,0:T(8,128)S(1)} %maximum_select_fusion.1), channel_id=1, source_target_pairs={{0,4},{4,0},{8,12},{12,8},{16,20},{20,16},{24,28},{28,24},{32,36},... | collective-permute-start | bytes 1572872 | tf_op jit(solution)/shard_map/ppermute | solution.py:83
  (3 other events, 20.8 us)
Sparse Core Ops, SparseCore 0:
  13.1 53.7 all-gather.2
  68.7 51.1 all-gather.4

commit v17 on v15

--- a/solution.py
+++ b/solution.py
@@ -69,7 +69,7 @@
         for stride, fan in ((stride_x, n_row // stride_x), (steps, fan_z)):
             holders = [p for p in range(n_row) if p % (stride * fan) in sources]
             received = piece
-            for hop in range(1, fan):
+            for hop in sorted(range(1, fan), key=lambda h: -min(h, fan - h)):
                 pairs = [(p, p + hop * stride) for p in holders]
                 arrived = lax.ppermute(piece, "prow", pairs)
                 received = jnp.where((row_at % (stride * fan)) // stride == hop, arrived, received)

time: 150 us -> 149 us (level)
  no operation moved by 1% of the time
where the time goes in v17:
time: 149 us; the launch traced here: 147 us
  waiting for transfers between devices  80.2 us (54%)
  matrix products  29.8 us (20%)
  starting transfers between devices  17.6 us (12%)
  between operations  13.9 us (9%)
  local copies, waits for them, and re-layouts  4.28 us (3%)
    all_gather x1, waiting for transfers between devices, per_device(): lower_first = lax.all_gather(first_rows, 'pcol', axis=1, tiled=True)  53.8 us
    dot_general x9, matrix products, contract(): lax.dot_general(left, right, (((1,), (1,)), ((), ())), precision=lax.Prec...  29.8 us
    ppermute x12, waiting for transfers between devices, per_device(): arrived = lax.ppermute(piece, 'prow', pairs)  18.3 us
    ppermute x12, starting transfers between devices, per_device(): arrived = lax.ppermute(piece, 'prow', pairs)  10.6 us
    ppermute x1, waiting for transfers between devices, per_device(): other = lax.ppermute(piece, 'prow', [(p, p ^ 2) for p in range(n_row)])  6.55 us
    slice x1, local copies, waits for them, and re-layouts, per_device(): factor[:block]  3.17 us
  transfers between devices with their start and end apart: 22, of which 5 were waited for; matrix products, arithmetic and copies ran while one was open for 18% of the time, Pallas kernels for 0%

profile of v17, /device:TPU:7, one launch (start us, length us, event | category | flops | bytes accessed | tf_op | source)
XLA Modules:
  0.0 147.2 jit_solution(318537297239091147)
XLA Ops:
  6.5 1.0 slice.46
  9.6 3.2 %fusion.20 = (f32[512,512]{1,0:T(8,128)}, f32[512,512]{1,0:T(8,128)}) fusion(f32[1024,512]{1,0:T(8,128)} %param.4), kind=kLoop, calls=%fused_computation.33 | loop fusion | bytes 4194304 | tf_op jit(solution)/shard_map/slice | solution.py:39
  13.0 53.8 %all-gather.3.cloned.1.call-done = f32[512,2048]{1,0:T(8,128)} async-done(((f32[512,512]{1,0:T(8,128)}), f32[512,2048]{1,0:T(8,128)}) %all-gather.3.cloned.1.call-update) | async-done | bytes 4194320 | tf_op jit(solution)/shard_map/all_gather | solution.py:40
  66.8 2.4 %fusion.11 = f32[128,512]{1,0:T(8,128)S(1)} fusion(f32[128,512]{1,0:T(8,128)S(1)} %select_select_fusion.4, f32[2048,512]{1,0:T(8,128)} %param.5), kind=kOutput, calls=%fused_computation.17 | convolution fusion | flops 402653184 | bytes 1572864 | tf_op jit(solution)/shard_map/dot_general | solution.py:8
  69.2 2.4 %fusion.4 = f32[128,512]{1,0:T(8,128)S(1)} fusion(f32[128,512]{1,0:T(8,128)S(1)} %fusion.11, f32[512,2048]{1,0:T(8,128)} %all-gather.3.cloned.1.call-done), kind=kOutput, calls=%fused_computation.9 | convolution fusion | flops 402653184 | bytes 1572864 | tf_op jit(solution)/shard_map/dot_general | solution.py:8
  71.6 2.4 %fusion.9 = f32[128,512]{1,0:T(8,128)S(1)} fusion(f32[2048,512]{1,0:T(8,128)} %param.5, f32[128,512]{1,0:T(8,128)S(1)} %fusion.4, f32[128,1024]{1,0:T(8,128)S(1)} %copy-done), kind=kOutput, calls=%fused_computation.15 | convolution fusion | flops 402718720 | bytes 1835008 | tf_op jit(solution)/shard_map/dot_general | solution.py:8
  74.0 0.7 collective-permute-start.3
  75.4 2.4 %convolution_add_fusion.1 = f32[128,512]{1,0:T(8,128)S(1)} fusion(f32[128,512]{1,0:T(8,128)S(1)} %fusion.4, f32[512,2048]{1,0:T(8,128)} %all-gather.3.cloned.1.call-done, f32[128,512]{1,0:T(8,128)S(1)} %collective-permute-done.3, f32[128,512]{1,0:T(8,128)S(1)} %collective-permute-done.4), kind=kOutput, calls=%fused_computation.6 | convolution fusion | flops 402784256 | bytes 2097152 | tf_op jit(solution)/shard_map/dot_general | solution.py:8
  77.8 2.4 %select_select_fusion.3 = (f32[128,512]{1,0:T(8,128)S(1)}, f32[128,512]{1,0:T(8,128)S(1)}) fusion(f32[128,512]{1,0:T(8,128)S(1)} %fusion.9, f32[128,512]{1,0:T(8,128)S(1)} %fusion.11, pred[]{:T(512)S(6)} %eq.71, pred[]{:T(512)S(6)} %eq.70, pred[]{:T(512)S(6)} %eq.69, f32[2048,512]{1,0:T(8,128)} %param.5, f32[128,512]{1,0:T(8,128)S(1)} %convolution_add_fusion.1, ...), kind=kOutput, calls=%fused_computation.24 | convolution fusion | flops 402915328 | bytes 2621443 | tf_op jit(solution)/shard_map/dot_general | solution.py:8
  81.0 1.3 collective-permute-start.12
  83.6 2.5 %fusion.1 = f32[128,512]{1,0:T(8,128)S(1)} fusion(f32[128,512]{1,0:T(8,128)S(1)} %convolution_add_fusion.1, f32[128,512]{1,0:T(8,128)S(1)} %collective-permute-done.5, f32[512,2048]{1,0:T(8,128)} %all-gather.3.cloned.1.call-done, f32[128,1024]{1,0:T(8,128)S(1)} %copy-done), kind=kOutput, calls=%fused_computation.5 | convolution fusion | flops 402784256 | bytes 2097152 | tf_op jit(solution)/shard_map/dot_general | solution.py:8
  86.1 2.4 %convolution_select_fusion = f32[128,512]{1,0:T(8,128)S(1)} fusion(f32[128,512]{1,0:T(8,128)S(1)} %get-tuple-element.17, f32[128,512]{1,0:T(8,128)S(1)} %fusion.1, f32[2048,512]{1,0:T(8,128)} %param.5, pred[]{:T(512)S(6)} %eq.68), kind=kOutput, calls=%fused_computation.3 | convolution fusion | flops 402718720 | bytes 1835009 | tf_op jit(solution)/shard_map/dot_general | solution.py:8
  89.9 5.3 %collective-permute-done.12 = f32[128,512]{1,0:T(8,128)S(1)} collective-permute-done((f32[128,512]{1,0:T(8,128)S(1)}, f32[128,512]{1,0:T(8,128)S(1)}, u32[]{:S(2)}, u32[]{:S(2)}) %collective-permute-start.12) | collective-permute-done | bytes 262176 | tf_op jit(solution)/shard_map/ppermute | solution.py:74
  96.0 1.3 collective-permute-start.15
  97.3 1.3 collective-permute-start.16
  98.7 1.3 collective-permute-start.17
  101.5 12.9 %collective-permute-done.15 = f32[128,512]{1,0:T(8,128)S(1)} collective-permute-done((f32[128,512]{1,0:T(8,128)S(1)}, f32[128,512]{1,0:T(8,128)S(1)}, u32[]{:S(2)}, u32[]{:S(2)}) %collective-permute-start.15) | collective-permute-done | bytes 262176 | tf_op jit(solution)/shard_map/ppermute | solution.py:74
  115.4 1.9 %collective-permute-start.18 = (f32[128,512]{1,0:T(8,128)S(1)}, f32[128,512]{1,0:T(8,128)S(1)}, u32[]{:S(2)}, u32[]{:S(2)}) collective-permute-start(f32[128,512]{1,0:T(8,128)S(1)} %select_select_fusion), channel_id=1, source_target_pairs={{0,8},{4,12},{8,0},{12,4},{16,24},{20,28},{24,16},{28,20},{32,40},... | collective-permute-start | bytes 786440 | tf_op jit(solution)/shard_map/ppermute | solution.py:81
  117.3 6.5 %collective-permute-done.18 = f32[128,512]{1,0:T(8,128)S(1)} collective-permute-done((f32[128,512]{1,0:T(8,128)S(1)}, f32[128,512]{1,0:T(8,128)S(1)}, u32[]{:S(2)}, u32[]{:S(2)}) %collective-permute-start.18) | collective-permute-done | bytes 262176 | tf_op jit(solution)/shard_map/ppermute | solution.py:81
  123.9 1.0 collective-permute-start.19
  124.9 1.5 %collective-permute-done.19 = f32[128,1024]{1,0:T(8,128)S(1)} collective-permute-done((f32[128,1024]{1,0:T(8,128)S(1)}, f32[128,1024]{1,0:T(8,128)S(1)}, u32[]{:S(2)}, u32[]{:S(2)}) %collective-permute-start.19) | collective-permute-done | bytes 524320 | tf_op jit(solution)/shard_map/ppermute | solution.py:83
  126.5 6.5 %fusion = f32[128,512]{1,0:T(8,128)S(1)} fusion(f32[128,512]{1,0:T(8,128)S(1)} %convolution_select_fusion, f32[512,2048]{1,0:T(8,128)} %all-gather.3.cloned.1.call-done, pred[]{:T(512)S(6)} %lt.61, f32[128,512]{1,0:T(8,128)S(1)} %get-tuple-element.16, f32[128,512]{1,0:T(8,128)S(1)} %get-tuple-element.14, f32[128,512]{1,0:T(8,128)S(1)} %get-tuple-element.15, ...), kind=kOutput, calls=%fused_computation.2 | convolution fusion | flops 1612578816 | bytes 6029314 | tf_op jit(solution)/shard_map/dot_general | solution.py:8
  133.0 6.5 %convolution_subtract_fusion = f32[128,512]{1,0:T(8,128)S(1)} fusion(f32[512,2048]{1,0:T(8,128)} %all-gather.5.cloned.1.call-done, f32[128,1024]{1,0:T(8,128)S(1)} %copy-done, f32[128,512]{1,0:T(8,128)S(1)} %get-tuple-element.16, f32[128,512]{1,0:T(8,128)S(1)} %get-tuple-element.14, f32[128,512]{1,0:T(8,128)S(1)} %get-tuple-element.15, ...), kind=kOutput, calls=%fused_computation | convolution fusion | flops 1612513280 | bytes 5767169 | tf_op jit(solution)/shard_map/dot_general | solution.py:8
  139.5 0.8 pad_maximum_fusion
  (43 shorter events, 9.6 us)
Async XLA Ops:
  6.5 6.3 %copy-start = (f32[128,1024]{1,0:T(8,128)S(1)}, f32[128,1024]{1,0:T(8,128)}, u32[]{:S(2)}) copy-start(f32[128,1024]{1,0:T(8,128)} %param.3) | copy-start | bytes 1572868
  6.5 60.3 %all-gather.3.cloned.1.call-start = ((), (), s32[]{:S(2)}) async-start(), calls=%async_computation | async-start | bytes 5242880 | tf_op jit(solution)/shard_map/all_gather | solution.py:40
  7.6 5.2 %collective-permute-start = (f32[128,512]{1,0:T(8,128)S(1)}, f32[128,512]{1,0:T(8,128)S(1)}, u32[]{:S(2)}, u32[]{:S(2)}) collective-permute-start(f32[128,512]{1,0:T(8,128)S(1)} %slice.46), channel_id=1, source_target_pairs={{0,12},{1,13},{2,14},{3,15}} | collective-permute-start | bytes 786440 | tf_op jit(solution)/shard_map/ppermute | solution.py:37
  8.3 4.6 %collective-permute-start.1 = (f32[128,512]{1,0:T(8,128)S(1)}, f32[128,512]{1,0:T(8,128)S(1)}, u32[]{:S(2)}, u32[]{:S(2)}) collective-permute-start(f32[128,512]{1,0:T(8,128)S(1)} %slice.46), channel_id=1, source_target_pairs={{0,8},{1,9},{2,10},{3,11}} | collective-permute-start | bytes 786440 | tf_op jit(solution)/shard_map/ppermute | solution.py:37
  8.9 3.9 %collective-permute-start.2 = (f32[128,512]{1,0:T(8,128)S(1)}, f32[128,512]{1,0:T(8,128)S(1)}, u32[]{:S(2)}, u32[]{:S(2)}) collective-permute-start(f32[128,512]{1,0:T(8,128)S(1)} %slice.46), channel_id=1, source_target_pairs={{0,4},{1,5},{2,6},{3,7}} | collective-permute-start | bytes 786440 | tf_op jit(solution)/shard_map/ppermute | solution.py:37
  13.0 120.0 %all-gather.5.cloned.1.call-start = ((), (), s32[]{:S(2)}) async-start(), calls=%async_computation.1 | async-start | bytes 5242880 | tf_op jit(solution)/shard_map/all_gather | solution.py:42
  74.0 1.4 collective-permute-start.3
  74.7 0.7 collective-permute-start.4
  80.2 3.4 %collective-permute-start.5 = (f32[128,512]{1,0:T(8,128)S(1)}, f32[128,512]{1,0:T(8,128)S(1)}, u32[]{:S(2)}, u32[]{:S(2)}) collective-permute-start(f32[128,512]{1,0:T(8,128)S(1)} %get-tuple-element.18), channel_id=1, source_target_pairs={{8,12},{9,13},{10,14},{11,15}} | collective-permute-start | bytes 786440 | tf_op jit(solution)/shard_map/ppermute | solution.py:62
  81.0 14.3 %collective-permute-start.12 = (f32[128,512]{1,0:T(8,128)S(1)}, f32[128,512]{1,0:T(8,128)S(1)}, u32[]{:S(2)}, u32[]{:S(2)}) collective-permute-start(f32[128,512]{1,0:T(8,128)S(1)} %get-tuple-element.17), channel_id=1, source_target_pairs={{0,192},{4,196},{8,200},{1,193},{5,197},{9,201},{2,194},{6,198},{1... | collective-permute-start | bytes 786440 | tf_op jit(solution)/shard_map/ppermute | solution.py:74
  82.3 13.6 %collective-permute-start.13 = (f32[128,512]{1,0:T(8,128)S(1)}, f32[128,512]{1,0:T(8,128)S(1)}, u32[]{:S(2)}, u32[]{:S(2)}) collective-permute-start(f32[128,512]{1,0:T(8,128)S(1)} %get-tuple-element.17), channel_id=1, source_target_pairs={{0,64},{4,68},{8,72},{1,65},{5,69},{9,73},{2,66},{6,70},{10,74},{3... | collective-permute-start | bytes 786440 | tf_op jit(solution)/shard_map/ppermute | solution.py:74
  82.9 13.0 %collective-permute-start.14 = (f32[128,512]{1,0:T(8,128)S(1)}, f32[128,512]{1,0:T(8,128)S(1)}, u32[]{:S(2)}, u32[]{:S(2)}) collective-permute-start(f32[128,512]{1,0:T(8,128)S(1)} %get-tuple-element.17), channel_id=1, source_target_pairs={{0,128},{4,132},{8,136},{1,129},{5,133},{9,137},{2,130},{6,134},{1... | collective-permute-start | bytes 786440 | tf_op jit(solution)/shard_map/ppermute | solution.py:74
  88.5 10.1 %collective-permute-start.6 = (f32[128,512]{1,0:T(8,128)S(1)}, f32[128,512]{1,0:T(8,128)S(1)}, u32[]{:S(2)}, u32[]{:S(2)}) collective-permute-start(f32[128,512]{1,0:T(8,128)S(1)} %convolution_select_fusion), channel_id=1, source_target_pairs={{12,204},{13,205},{14,206},{15,207}} | collective-permute-start | bytes 786440 | tf_op jit(solution)/shard_map/ppermute | solution.py:74
  89.2 10.8 %collective-permute-start.7 = (f32[128,512]{1,0:T(8,128)S(1)}, f32[128,512]{1,0:T(8,128)S(1)}, u32[]{:S(2)}, u32[]{:S(2)}) collective-permute-start(f32[128,512]{1,0:T(8,128)S(1)} %convolution_select_fusion), channel_id=1, source_target_pairs={{12,76},{13,77},{14,78},{15,79}} | collective-permute-start | bytes 786440 | tf_op jit(solution)/shard_map/ppermute | solution.py:74
  95.2 4.8 %collective-permute-start.8 = (f32[128,512]{1,0:T(8,128)S(1)}, f32[128,512]{1,0:T(8,128)S(1)}, u32[]{:S(2)}, u32[]{:S(2)}) collective-permute-start(f32[128,512]{1,0:T(8,128)S(1)} %convolution_select_fusion), channel_id=1, source_target_pairs={{12,140},{13,141},{14,142},{15,143}} | collective-permute-start | bytes 786440 | tf_op jit(solution)/shard_map/ppermute | solution.py:74
  96.0 18.4 %collective-permute-start.15 = (f32[128,512]{1,0:T(8,128)S(1)}, f32[128,512]{1,0:T(8,128)S(1)}, u32[]{:S(2)}, u32[]{:S(2)}) collective-permute-start(f32[128,512]{1,0:T(8,128)S(1)} %select_select_fusion.1), channel_id=1, source_target_pairs={{0,48},{4,52},{8,56},{64,112},{68,116},{72,120},{128,176},{132,180... | collective-permute-start | bytes 786440 | tf_op jit(solution)/shard_map/ppermute | solution.py:74
  97.3 17.8 %collective-permute-start.16 = (f32[128,512]{1,0:T(8,128)S(1)}, f32[128,512]{1,0:T(8,128)S(1)}, u32[]{:S(2)}, u32[]{:S(2)}) collective-permute-start(f32[128,512]{1,0:T(8,128)S(1)} %select_select_fusion.1), channel_id=1, source_target_pairs={{0,16},{4,20},{8,24},{64,80},{68,84},{72,88},{128,144},{132,148},{... | collective-permute-start | bytes 786440 | tf_op jit(solution)/shard_map/ppermute | solution.py:74
  98.7 16.5 %collective-permute-start.17 = (f32[128,512]{1,0:T(8,128)S(1)}, f32[128,512]{1,0:T(8,128)S(1)}, u32[]{:S(2)}, u32[]{:S(2)}) collective-permute-start(f32[128,512]{1,0:T(8,128)S(1)} %select_select_fusion.1), channel_id=1, source_target_pairs={{0,32},{4,36},{8,40},{64,96},{68,100},{72,104},{128,160},{132,164}... | collective-permute-start | bytes 786440 | tf_op jit(solution)/shard_map/ppermute | solution.py:74
  100.1 15.0 %collective-permute-start.10 = (f32[128,512]{1,0:T(8,128)S(1)}, f32[128,512]{1,0:T(8,128)S(1)}, u32[]{:S(2)}, u32[]{:S(2)}) collective-permute-start(f32[128,512]{1,0:T(8,128)S(1)} %select_select_fusion.2), channel_id=1, source_target_pairs={{12,28},{76,92},{140,156},{204,220},{13,29},{77,93},{141,157},{205... | collective-permute-start | bytes 786440 | tf_op jit(solution)/shard_map/ppermute | solution.py:74
  100.8 14.4 %collective-permute-start.11 = (f32[128,512]{1,0:T(8,128)S(1)}, f32[128,512]{1,0:T(8,128)S(1)}, u32[]{:S(2)}, u32[]{:S(2)}) collective-permute-start(f32[128,512]{1,0:T(8,128)S(1)} %select_select_fusion.2), channel_id=1, source_target_pairs={{12,44},{76,108},{140,172},{204,236},{13,45},{77,109},{141,173},{2... | collective-permute-start | bytes 786440 | tf_op jit(solution)/shard_map/ppermute | solution.py:74
  114.4 0.8 collective-permute-start.9
  115.4 8.5 %collective-permute-start.18 = (f32[128,512]{1,0:T(8,128)S(1)}, f32[128,512]{1,0:T(8,128)S(1)}, u32[]{:S(2)}, u32[]{:S(2)}) collective-permute-start(f32[128,512]{1,0:T(8,128)S(1)} %select_select_fusion), channel_id=1, source_target_pairs={{0,8},{4,12},{8,0},{12,4},{16,24},{20,28},{24,16},{28,20},{32,40},... | collective-permute-start | bytes 786440 | tf_op jit(solution)/shard_map/ppermute | solution.py:81
  123.9 2.5 %collective-permute-start.19 = (f32[128,1024]{1,0:T(8,128)S(1)}, f32[128,1024]{1,0:T(8,128)S(1)}, u32[]{:S(2)}, u32[]{:S(2)}) collective-permute-start(f32[128,1024]{1,0:T(8,128)S(1)} %maximum_select_fusion.1), channel_id=1, source_target_pairs={{0,4},{4,0},{8,12},{12,8},{16,20},{20,16},{24,28},{28,24},{32,36},... | collective-permute-start | bytes 1572872 | tf_op jit(solution)/shard_map/ppermute | solution.py:83
Sparse Core Ops, SparseCore 0:
  13.1 53.6 all-gather.2
  68.6 51.1 all-gather.4

commit v18 on v15

--- a/solution.py
+++ b/solution.py
@@ -75,16 +75,20 @@
                 received = jnp.where((row_at % (stride * fan)) // stride == hop, arrived, received)
             piece = jnp.where(row_at % stride < steps, received, piece)
         spread.append(piece)
-    piece = jnp.where(row_at % steps == steps - 1, spread[1], spread[0])
+    piece = spread[0]
     b0 = row_at % 2
     b1 = (row_at // 2) % 2
     other = lax.ppermute(piece, "prow", [(p, p ^ 2) for p in range(n_row)])
     pair = jnp.where(b1 == 0, jnp.concatenate([piece, other], axis=1), jnp.concatenate([other, piece], axis=1))
     theirs = lax.ppermute(pair, "prow", [(p, p ^ 1) for p in range(n_row)])
     mine, yours = (pair[:, :block], pair[:, block:]), (theirs[:, :block], theirs[:, block:])
-    mine_first = jnp.concatenate([mine[0], yours[0], mine[1], yours[1]], axis=1)
-    theirs_first = jnp.concatenate([yours[0], mine[0], yours[1], mine[1]], axis=1)
-    panel = jnp.where(b0 == 0, mine_first, theirs_first)
+    mine_first = jnp.concatenate([mine[0], yours[0], mine[1]], axis=1)
+    theirs_first = jnp.concatenate([yours[0], mine[0], yours[1]], axis=1)
+    last = jnp.where(row_at % steps == steps - 1, spread[1], jnp.zeros_like(spread[1]))
+    for mask in range(1, steps):
+        pairs = [(p, p ^ mask) for p in range(n_row) if p % steps == steps - 1]
+        last = last + lax.ppermute(spread[1], "prow", pairs)
+    panel = jnp.concatenate([jnp.where(b0 == 0, mine_first, theirs_first), last], axis=1)
 
     second = right_side[:, block:] - contract(panel, lower_second)
     first = right_side[:, :block] - contract(panel, lower_first)

time: 150 us -> 155 us (1.033)
  the two profiles are of different devices: /device:TPU:7 before, /device:TPU:2 now
where the time goes in v18:
time: 155 us; the launch traced here: 154 us
  waiting for transfers between devices  86.5 us (56%)
  matrix products  27.8 us (18%)
  starting transfers between devices  19.7 us (13%)
  between operations  14 us (9%)
  local copies, waits for them, and re-layouts  4.26 us (3%)
    all_gather x1, waiting for transfers between devices, per_device(): lower_first = lax.all_gather(first_rows, 'pcol', axis=1, tiled=True)  53.9 us
    dot_general x9, matrix products, contract(): lax.dot_general(left, right, (((1,), (1,)), ((), ())), precision=lax.Prec...  27.8 us
    ppermute x12, waiting for transfers between devices, per_device(): arrived = lax.ppermute(piece, 'prow', pairs)  16.4 us
    ppermute x3, waiting for transfers between devices, per_device(): last = last + lax.ppermute(spread[1], 'prow', pairs)  11.7 us
    ppermute x12, starting transfers between devices, per_device(): arrived = lax.ppermute(piece, 'prow', pairs)  10.6 us
    ppermute x1, waiting for transfers between devices, per_device(): other = lax.ppermute(piece, 'prow', [(p, p ^ 2) for p in range(n_row)])  4.48 us
    slice x1, local copies, waits for them, and re-layouts, per_device(): factor[:block]  3.14 us
  transfers between devices with their start and end apart: 25, of which 5 were waited for; matrix products, arithmetic and copies ran while one was open for 16% of the time, Pallas kernels for 0%

profile of v18, /device:TPU:2, one launch (start us, length us, event | category | flops | bytes accessed | tf_op | source)
XLA Modules:
  0.0 153.9 jit_solution(234869240694827521)
XLA Ops:
  6.5 1.0 slice.46
  7.6 0.7 collective-permute-start
  9.6 3.1 %fusion.20 = (f32[512,512]{1,0:T(8,128)}, f32[512,512]{1,0:T(8,128)}) fusion(f32[1024,512]{1,0:T(8,128)} %param.4), kind=kLoop, calls=%fused_computation.36 | loop fusion | bytes 4194304 | tf_op jit(solution)/shard_map/slice | solution.py:39
  13.0 53.9 %all-gather.3.cloned.1.call-done = f32[512,2048]{1,0:T(8,128)} async-done(((f32[512,512]{1,0:T(8,128)}), f32[512,2048]{1,0:T(8,128)}) %all-gather.3.cloned.1.call-update) | async-done | bytes 4194320 | tf_op jit(solution)/shard_map/all_gather | solution.py:40
  66.9 2.4 %fusion.11 = f32[128,512]{1,0:T(8,128)S(1)} fusion(f32[128,512]{1,0:T(8,128)S(1)} %select_select_fusion.5, f32[2048,512]{1,0:T(8,128)} %param.5), kind=kOutput, calls=%fused_computation.17 | convolution fusion | flops 402653184 | bytes 1572864 | tf_op jit(solution)/shard_map/dot_general | solution.py:8
  69.3 2.4 %fusion.4 = f32[128,512]{1,0:T(8,128)S(1)} fusion(f32[128,512]{1,0:T(8,128)S(1)} %fusion.11, f32[512,2048]{1,0:T(8,128)} %all-gather.3.cloned.1.call-done), kind=kOutput, calls=%fused_computation.9 | convolution fusion | flops 402653184 | bytes 1572864 | tf_op jit(solution)/shard_map/dot_general | solution.py:8
  71.7 2.4 %fusion.9 = f32[128,512]{1,0:T(8,128)S(1)} fusion(f32[2048,512]{1,0:T(8,128)} %param.5, f32[128,512]{1,0:T(8,128)S(1)} %fusion.4, f32[128,1024]{1,0:T(8,128)S(1)} %copy-done.1), kind=kOutput, calls=%fused_computation.15 | convolution fusion | flops 402718720 | bytes 1835008 | tf_op jit(solution)/shard_map/dot_general | solution.py:8
  75.5 2.4 %convolution_add_fusion.1 = f32[128,512]{1,0:T(8,128)S(1)} fusion(f32[128,512]{1,0:T(8,128)S(1)} %fusion.4, f32[512,2048]{1,0:T(8,128)} %all-gather.3.cloned.1.call-done, f32[128,512]{1,0:T(8,128)S(1)} %collective-permute-done.3, f32[128,512]{1,0:T(8,128)S(1)} %collective-permute-done.4), kind=kOutput, calls=%fused_computation.6 | convolution fusion | flops 402784256 | bytes 2097152 | tf_op jit(solution)/shard_map/dot_general | solution.py:8
  77.9 2.4 %select_select_fusion.4 = (f32[128,512]{1,0:T(8,128)S(1)}, f32[128,512]{1,0:T(8,128)S(1)}) fusion(f32[128,512]{1,0:T(8,128)S(1)} %fusion.9, f32[128,512]{1,0:T(8,128)S(1)} %fusion.11, pred[]{:T(512)S(6)} %eq.71, pred[]{:T(512)S(6)} %eq.70, pred[]{:T(512)S(6)} %eq.69, f32[2048,512]{1,0:T(8,128)} %param.5, f32[128,512]{1,0:T(8,128)S(1)} %convolution_add_fusion.1, ...), kind=kOutput, calls=%fused_computation.27 | convolution fusion | flops 402915328 | bytes 2621443 | tf_op jit(solution)/shard_map/dot_general | solution.py:8
  81.7 1.3 collective-permute-start.8
  83.7 11.4 %collective-permute-done.8 = f32[128,512]{1,0:T(8,128)S(1)} collective-permute-done((f32[128,512]{1,0:T(8,128)S(1)}, f32[128,512]{1,0:T(8,128)S(1)}, u32[]{:S(2)}, u32[]{:S(2)}) %collective-permute-start.8) | collective-permute-done | bytes 262176 | tf_op jit(solution)/shard_map/ppermute | solution.py:74
  95.2 1.3 collective-permute-start.10
  96.5 1.3 collective-permute-start.11
  97.8 1.3 collective-permute-start.9
  99.1 2.4 %fusion.1 = f32[128,512]{1,0:T(8,128)S(1)} fusion(f32[128,512]{1,0:T(8,128)S(1)} %convolution_add_fusion.1, f32[128,512]{1,0:T(8,128)S(1)} %collective-permute-done.5, f32[512,2048]{1,0:T(8,128)} %all-gather.3.cloned.1.call-done, f32[128,1024]{1,0:T(8,128)S(1)} %copy-done.1), kind=kOutput, calls=%fused_computation.5 | convolution fusion | flops 402784256 | bytes 2097152 | tf_op jit(solution)/shard_map/dot_general | solution.py:8
  101.5 2.4 %convolution_select_fusion = f32[128,512]{1,0:T(8,128)S(1)} fusion(f32[128,512]{1,0:T(8,128)S(1)} %get-tuple-element.17, f32[128,512]{1,0:T(8,128)S(1)} %fusion.1, f32[2048,512]{1,0:T(8,128)} %param.5, pred[]{:T(512)S(6)} %eq.68), kind=kOutput, calls=%fused_computation.3 | convolution fusion | flops 402718720 | bytes 1835009 | tf_op jit(solution)/shard_map/dot_general | solution.py:8
  106.1 5.0 %collective-permute-done.9 = f32[128,512]{1,0:T(8,128)S(1)} collective-permute-done((f32[128,512]{1,0:T(8,128)S(1)}, f32[128,512]{1,0:T(8,128)S(1)}, u32[]{:S(2)}, u32[]{:S(2)}) %collective-permute-start.9) | collective-permute-done | bytes 262176 | tf_op jit(solution)/shard_map/ppermute | solution.py:74
  111.2 2.1 %collective-permute-start.12 = (f32[128,512]{1,0:T(8,128)S(1)}, f32[128,512]{1,0:T(8,128)S(1)}, u32[]{:S(2)}, u32[]{:S(2)}) collective-permute-start(f32[128,512]{1,0:T(8,128)S(1)} %select_select_fusion.2), channel_id=1, source_target_pairs={{0,8},{4,12},{8,0},{12,4},{16,24},{20,28},{24,16},{28,20},{32,40},... | collective-permute-start | bytes 786440 | tf_op jit(solution)/shard_map/ppermute | solution.py:81
  115.4 4.5 %collective-permute-done.12 = f32[128,512]{1,0:T(8,128)S(1)} collective-permute-done((f32[128,512]{1,0:T(8,128)S(1)}, f32[128,512]{1,0:T(8,128)S(1)}, u32[]{:S(2)}, u32[]{:S(2)}) %collective-permute-start.12) | collective-permute-done | bytes 262176 | tf_op jit(solution)/shard_map/ppermute | solution.py:81
  121.6 1.5 collective-permute-start.22
  123.2 11.7 %collective-permute-done.22 = f32[128,512]{1,0:T(8,128)S(1)} collective-permute-done((f32[128,512]{1,0:T(8,128)S(1)}, f32[128,512]{1,0:T(8,128)S(1)}, u32[]{:S(2)}, u32[]{:S(2)}) %collective-permute-start.22) | collective-permute-done | bytes 262176 | tf_op jit(solution)/shard_map/ppermute | solution.py:90
  135.1 4.5 %fusion = f32[128,512]{1,0:T(8,128)S(1)} fusion(f32[128,512]{1,0:T(8,128)S(1)} %convolution_select_fusion, f32[512,2048]{1,0:T(8,128)S(1)} %copy-done, f32[128,512]{1,0:T(8,128)S(1)} %add_add_fusion, f32[128,1536]{1,0:T(8,128)S(1)} %maximum_select_fusion, pred[]{:T(512)S(6)} %lt.61, f32[128,1024]{1,0:T(8,128)S(1)} %copy-done.1), kind=kOutput, calls=%fused_computation.2 | convolution fusion | flops 1611005952 | bytes 6029313 | tf_op jit(solution)/shard_map/dot_general | solution.py:8
  139.6 6.6 %convolution_subtract_fusion = f32[128,512]{1,0:T(8,128)S(1)} fusion(f32[512,2048]{1,0:T(8,128)} %all-gather.5.cloned.1.call-done, f32[128,512]{1,0:T(8,128)S(1)} %add_add_fusion, f32[128,1536]{1,0:T(8,128)S(1)} %maximum_select_fusion, f32[128,1024]{1,0:T(8,128)S(1)} %copy-done.1), kind=kOutput, calls=%fused_computation | convolution fusion | flops 1610940416 | bytes 5767168 | tf_op jit(solution)/shard_map/dot_general | solution.py:8
  146.2 0.8 pad_maximum_fusion.3
  (54 shorter events, 11.2 us)
Async XLA Ops:
  6.5 60.3 %all-gather.3.cloned.1.call-start = ((), (), s32[]{:S(2)}) async-start(), calls=%async_computation | async-start | bytes 5242880 | tf_op jit(solution)/shard_map/all_gather | solution.py:40
  7.6 5.2 %collective-permute-start = (f32[128,512]{1,0:T(8,128)S(1)}, f32[128,512]{1,0:T(8,128)S(1)}, u32[]{:S(2)}, u32[]{:S(2)}) collective-permute-start(f32[128,512]{1,0:T(8,128)S(1)} %slice.46), channel_id=1, source_target_pairs={{0,12},{1,13},{2,14},{3,15}} | collective-permute-start | bytes 786440 | tf_op jit(solution)/shard_map/ppermute | solution.py:37
  8.3 4.5 %collective-permute-start.1 = (f32[128,512]{1,0:T(8,128)S(1)}, f32[128,512]{1,0:T(8,128)S(1)}, u32[]{:S(2)}, u32[]{:S(2)}) collective-permute-start(f32[128,512]{1,0:T(8,128)S(1)} %slice.46), channel_id=1, source_target_pairs={{0,8},{1,9},{2,10},{3,11}} | collective-permute-start | bytes 786440 | tf_op jit(solution)/shard_map/ppermute | solution.py:37
  8.9 3.8 %collective-permute-start.2 = (f32[128,512]{1,0:T(8,128)S(1)}, f32[128,512]{1,0:T(8,128)S(1)}, u32[]{:S(2)}, u32[]{:S(2)}) collective-permute-start(f32[128,512]{1,0:T(8,128)S(1)} %slice.46), channel_id=1, source_target_pairs={{0,4},{1,5},{2,6},{3,7}} | collective-permute-start | bytes 786440 | tf_op jit(solution)/shard_map/ppermute | solution.py:37
  12.9 126.7 %all-gather.5.cloned.1.call-start = ((), (), s32[]{:S(2)}) async-start(), calls=%async_computation.1 | async-start | bytes 5242880 | tf_op jit(solution)/shard_map/all_gather | solution.py:42
  74.1 1.4 collective-permute-start.3
  80.3 3.4 %collective-permute-start.6 = (f32[128,512]{1,0:T(8,128)S(1)}, f32[128,512]{1,0:T(8,128)S(1)}, u32[]{:S(2)}, u32[]{:S(2)}) collective-permute-start(f32[128,512]{1,0:T(8,128)S(1)} %get-tuple-element.17), channel_id=1, source_target_pairs={{0,192},{4,196},{8,200},{1,193},{5,197},{9,201},{2,194},{6,198},{1... | collective-permute-start | bytes 786440 | tf_op jit(solution)/shard_map/ppermute | solution.py:74
  81.0 2.7 %collective-permute-start.7 = (f32[128,512]{1,0:T(8,128)S(1)}, f32[128,512]{1,0:T(8,128)S(1)}, u32[]{:S(2)}, u32[]{:S(2)}) collective-permute-start(f32[128,512]{1,0:T(8,128)S(1)} %get-tuple-element.17), channel_id=1, source_target_pairs={{0,128},{4,132},{8,136},{1,129},{5,133},{9,137},{2,130},{6,134},{1... | collective-permute-start | bytes 786440 | tf_op jit(solution)/shard_map/ppermute | solution.py:74
  81.7 13.4 %collective-permute-start.8 = (f32[128,512]{1,0:T(8,128)S(1)}, f32[128,512]{1,0:T(8,128)S(1)}, u32[]{:S(2)}, u32[]{:S(2)}) collective-permute-start(f32[128,512]{1,0:T(8,128)S(1)} %get-tuple-element.17), channel_id=1, source_target_pairs={{0,64},{4,68},{8,72},{1,65},{5,69},{9,73},{2,66},{6,70},{10,74},{3... | collective-permute-start | bytes 786440 | tf_op jit(solution)/shard_map/ppermute | solution.py:74
  83.0 16.2 %collective-permute-start.5 = (f32[128,512]{1,0:T(8,128)S(1)}, f32[128,512]{1,0:T(8,128)S(1)}, u32[]{:S(2)}, u32[]{:S(2)}) collective-permute-start(f32[128,512]{1,0:T(8,128)S(1)} %get-tuple-element.18), channel_id=1, source_target_pairs={{8,12},{9,13},{10,14},{11,15}} | collective-permute-start | bytes 786440 | tf_op jit(solution)/shard_map/ppermute | solution.py:62
  95.2 10.1 %collective-permute-start.10 = (f32[128,512]{1,0:T(8,128)S(1)}, f32[128,512]{1,0:T(8,128)S(1)}, u32[]{:S(2)}, u32[]{:S(2)}) collective-permute-start(f32[128,512]{1,0:T(8,128)S(1)} %select_select_fusion.3), channel_id=1, source_target_pairs={{0,32},{4,36},{8,40},{64,96},{68,100},{72,104},{128,160},{132,164}... | collective-permute-start | bytes 786440 | tf_op jit(solution)/shard_map/ppermute | solution.py:74
  96.5 9.6 %collective-permute-start.11 = (f32[128,512]{1,0:T(8,128)S(1)}, f32[128,512]{1,0:T(8,128)S(1)}, u32[]{:S(2)}, u32[]{:S(2)}) collective-permute-start(f32[128,512]{1,0:T(8,128)S(1)} %select_select_fusion.3), channel_id=1, source_target_pairs={{0,16},{4,20},{8,24},{64,80},{68,84},{72,88},{128,144},{132,148},{... | collective-permute-start | bytes 786440 | tf_op jit(solution)/shard_map/ppermute | solution.py:74
  97.8 13.3 %collective-permute-start.9 = (f32[128,512]{1,0:T(8,128)S(1)}, f32[128,512]{1,0:T(8,128)S(1)}, u32[]{:S(2)}, u32[]{:S(2)}) collective-permute-start(f32[128,512]{1,0:T(8,128)S(1)} %select_select_fusion.3), channel_id=1, source_target_pairs={{0,48},{4,52},{8,56},{64,112},{68,116},{72,120},{128,176},{132,180... | collective-permute-start | bytes 786440 | tf_op jit(solution)/shard_map/ppermute | solution.py:74
  104.0 9.3 %collective-permute-start.14 = (f32[128,512]{1,0:T(8,128)S(1)}, f32[128,512]{1,0:T(8,128)S(1)}, u32[]{:S(2)}, u32[]{:S(2)}) collective-permute-start(f32[128,512]{1,0:T(8,128)S(1)} %convolution_select_fusion), channel_id=1, source_target_pairs={{12,204},{13,205},{14,206},{15,207}} | collective-permute-start | bytes 786440 | tf_op jit(solution)/shard_map/ppermute | solution.py:74
  104.6 8.6 %collective-permute-start.15 = (f32[128,512]{1,0:T(8,128)S(1)}, f32[128,512]{1,0:T(8,128)S(1)}, u32[]{:S(2)}, u32[]{:S(2)}) collective-permute-start(f32[128,512]{1,0:T(8,128)S(1)} %convolution_select_fusion), channel_id=1, source_target_pairs={{12,140},{13,141},{14,142},{15,143}} | collective-permute-start | bytes 786440 | tf_op jit(solution)/shard_map/ppermute | solution.py:74
  105.3 7.9 %collective-permute-start.16 = (f32[128,512]{1,0:T(8,128)S(1)}, f32[128,512]{1,0:T(8,128)S(1)}, u32[]{:S(2)}, u32[]{:S(2)}) collective-permute-start(f32[128,512]{1,0:T(8,128)S(1)} %convolution_select_fusion), channel_id=1, source_target_pairs={{12,76},{13,77},{14,78},{15,79}} | collective-permute-start | bytes 786440 | tf_op jit(solution)/shard_map/ppermute | solution.py:74
  111.2 8.7 %collective-permute-start.12 = (f32[128,512]{1,0:T(8,128)S(1)}, f32[128,512]{1,0:T(8,128)S(1)}, u32[]{:S(2)}, u32[]{:S(2)}) collective-permute-start(f32[128,512]{1,0:T(8,128)S(1)} %select_select_fusion.2), channel_id=1, source_target_pairs={{0,8},{4,12},{8,0},{12,4},{16,24},{20,28},{24,16},{28,20},{32,40},... | collective-permute-start | bytes 786440 | tf_op jit(solution)/shard_map/ppermute | solution.py:81
  113.4 6.7 %collective-permute-start.17 = (f32[128,512]{1,0:T(8,128)S(1)}, f32[128,512]{1,0:T(8,128)S(1)}, u32[]{:S(2)}, u32[]{:S(2)}) collective-permute-start(f32[128,512]{1,0:T(8,128)S(1)} %select_select_fusion.1), channel_id=1, source_target_pairs={{12,60},{76,124},{140,188},{204,252},{13,61},{77,125},{141,189},{2... | collective-permute-start | bytes 786440 | tf_op jit(solution)/shard_map/ppermute | solution.py:74
  114.0 6.0 %collective-permute-start.18 = (f32[128,512]{1,0:T(8,128)S(1)}, f32[128,512]{1,0:T(8,128)S(1)}, u32[]{:S(2)}, u32[]{:S(2)}) collective-permute-start(f32[128,512]{1,0:T(8,128)S(1)} %select_select_fusion.1), channel_id=1, source_target_pairs={{12,44},{76,108},{140,172},{204,236},{13,45},{77,109},{141,173},{2... | collective-permute-start | bytes 786440 | tf_op jit(solution)/shard_map/ppermute | solution.py:74
  114.7 5.4 %collective-permute-start.19 = (f32[128,512]{1,0:T(8,128)S(1)}, f32[128,512]{1,0:T(8,128)S(1)}, u32[]{:S(2)}, u32[]{:S(2)}) collective-permute-start(f32[128,512]{1,0:T(8,128)S(1)} %select_select_fusion.1), channel_id=1, source_target_pairs={{12,28},{76,92},{140,156},{204,220},{13,29},{77,93},{141,157},{205... | collective-permute-start | bytes 786440 | tf_op jit(solution)/shard_map/ppermute | solution.py:74
  120.0 14.9 %collective-permute-start.13 = (f32[128,1024]{1,0:T(8,128)S(1)}, f32[128,1024]{1,0:T(8,128)S(1)}, u32[]{:S(2)}, u32[]{:S(2)}) collective-permute-start(f32[128,1024]{1,0:T(8,128)S(1)} %maximum_select_fusion.1), channel_id=1, source_target_pairs={{0,4},{4,0},{8,12},{12,8},{16,20},{20,16},{24,28},{28,24},{32,36},... | collective-permute-start | bytes 1572872 | tf_op jit(solution)/shard_map/ppermute | solution.py:83
  120.2 2.9 %collective-permute-start.20 = (f32[128,512]{1,0:T(8,128)S(1)}, f32[128,512]{1,0:T(8,128)S(1)}, u32[]{:S(2)}, u32[]{:S(2)}) collective-permute-start(f32[128,512]{1,0:T(8,128)S(1)} %select_select_fusion), channel_id=1, source_target_pairs={{12,8},{28,24},{44,40},{60,56},{76,72},{92,88},{108,104},{124,120}... | collective-permute-start | bytes 786440 | tf_op jit(solution)/shard_map/ppermute | solution.py:90
  120.9 2.3 %collective-permute-start.21 = (f32[128,512]{1,0:T(8,128)S(1)}, f32[128,512]{1,0:T(8,128)S(1)}, u32[]{:S(2)}, u32[]{:S(2)}) collective-permute-start(f32[128,512]{1,0:T(8,128)S(1)} %select_select_fusion), channel_id=1, source_target_pairs={{12,4},{28,20},{44,36},{60,52},{76,68},{92,84},{108,100},{124,116}... | collective-permute-start | bytes 786440 | tf_op jit(solution)/shard_map/ppermute | solution.py:90
  121.6 13.2 %collective-permute-start.22 = (f32[128,512]{1,0:T(8,128)S(1)}, f32[128,512]{1,0:T(8,128)S(1)}, u32[]{:S(2)}, u32[]{:S(2)}) collective-permute-start(f32[128,512]{1,0:T(8,128)S(1)} %select_select_fusion), channel_id=1, source_target_pairs={{12,0},{28,16},{44,32},{60,48},{76,64},{92,80},{108,96},{124,112},... | collective-permute-start | bytes 786440 | tf_op jit(solution)/shard_map/ppermute | solution.py:90
  (3 other events, 18.9 us)
Sparse Core Ops, SparseCore 0:
  13.1 53.7 all-gather.2
  68.7 51.1 all-gather.4

commit v19 on v15

--- a/solution.py
+++ b/solution.py
@@ -49,6 +49,8 @@
         else:
             solved = contract(top_rhs - acc, inverses[k * block : (k + 1) * block])
         own = jnp.where(row_at == k, solved, own)
+        if k == steps - 3:
+            own_first = own
         if k == steps - 2:
             own_early = own
         if k == steps - 1:
@@ -65,7 +67,7 @@
     fan_z = min(steps, n_row // steps)
     stride_x = steps * fan_z
     spread = []
-    for piece, sources in ((own_early, range(steps - 1)), (own, (steps - 1,))):
+    for piece, sources in ((own_first, range(steps - 2)), (own_early, (steps - 2,)), (own, (steps - 1,))):
         for stride, fan in ((stride_x, n_row // stride_x), (steps, fan_z)):
             holders = [p for p in range(n_row) if p % (stride * fan) in sources]
             received = piece
@@ -75,7 +77,7 @@
                 received = jnp.where((row_at % (stride * fan)) // stride == hop, arrived, received)
             piece = jnp.where(row_at % stride < steps, received, piece)
         spread.append(piece)
-    piece = jnp.where(row_at % steps == steps - 1, spread[1], spread[0])
+    piece = jnp.where(row_at % steps == steps - 1, spread[2], jnp.where(row_at % steps == steps - 2, spread[1], spread[0]))
     b0 = row_at % 2
     b1 = (row_at // 2) % 2
     other = lax.ppermute(piece, "prow", [(p, p ^ 2) for p in range(n_row)])

time: 150 us -> 157 us (1.047)
  the two profiles are of different devices: /device:TPU:7 before, /device:TPU:99 now
where the time goes in v19:
time: 157 us; the launch traced here: 156 us
  waiting for transfers between devices  82.5 us (53%)
  matrix products  29.7 us (19%)
  starting transfers between devices  22.9 us (15%)
  between operations  14 us (9%)
  local copies, waits for them, and re-layouts  4.24 us (3%)
  other arithmetic  2.58 us (2%)
    all_gather x1, waiting for transfers between devices, per_device(): lower_first = lax.all_gather(first_rows, 'pcol', axis=1, tiled=True)  52.8 us
    dot_general x9, matrix products, contract(): lax.dot_general(left, right, (((1,), (1,)), ((), ())), precision=lax.Prec...  29.7 us
    ppermute x18, waiting for transfers between devices, per_device(): arrived = lax.ppermute(piece, 'prow', pairs)  23 us
    ppermute x18, starting transfers between devices, per_device(): arrived = lax.ppermute(piece, 'prow', pairs)  13.5 us
    ppermute x1, starting transfers between devices, per_device(): theirs = lax.ppermute(pair, 'prow', [(p, p ^ 1) for p in range(n_row)])  5.22 us
    ppermute x1, waiting for transfers between devices, per_device(): other = lax.ppermute(piece, 'prow', [(p, p ^ 2) for p in range(n_row)])  5.18 us
  transfers between devices with their start and end apart: 28, of which 4 were waited for; matrix products, arithmetic and copies ran while one was open for 18% of the time, Pallas kernels for 0%

profile of v19, /device:TPU:99, one launch (start us, length us, event | category | flops | bytes accessed | tf_op | source)
XLA Modules:
  0.0 155.9 jit_solution(12260615094049779931)
XLA Ops:
  6.5 1.0 slice.46
  9.6 3.1 %fusion.20 = (f32[512,512]{1,0:T(8,128)}, f32[512,512]{1,0:T(8,128)}) fusion(f32[1024,512]{1,0:T(8,128)} %param.4), kind=kLoop, calls=%fused_computation.35 | loop fusion | bytes 4194304 | tf_op jit(solution)/shard_map/slice | solution.py:39
  13.0 52.8 %all-gather.3.cloned.1.call-done = f32[512,2048]{1,0:T(8,128)} async-done(((f32[512,512]{1,0:T(8,128)}), f32[512,2048]{1,0:T(8,128)}) %all-gather.3.cloned.1.call-update) | async-done | bytes 4194320 | tf_op jit(solution)/shard_map/all_gather | solution.py:40
  65.8 2.4 %fusion.11 = f32[128,512]{1,0:T(8,128)S(1)} fusion(f32[128,512]{1,0:T(8,128)S(1)} %select_select_fusion.5, f32[2048,512]{1,0:T(8,128)} %param.5), kind=kOutput, calls=%fused_computation.17 | convolution fusion | flops 402653184 | bytes 1572864 | tf_op jit(solution)/shard_map/dot_general | solution.py:8
  68.2 2.4 %fusion.4 = f32[128,512]{1,0:T(8,128)S(1)} fusion(f32[128,512]{1,0:T(8,128)S(1)} %fusion.11, f32[512,2048]{1,0:T(8,128)} %all-gather.3.cloned.1.call-done), kind=kOutput, calls=%fused_computation.9 | convolution fusion | flops 402653184 | bytes 1572864 | tf_op jit(solution)/shard_map/dot_general | solution.py:8
  70.5 2.4 %fusion.9 = f32[128,512]{1,0:T(8,128)S(1)} fusion(f32[2048,512]{1,0:T(8,128)} %param.5, f32[128,512]{1,0:T(8,128)S(1)} %fusion.4, f32[128,1024]{1,0:T(8,128)S(1)} %copy-done), kind=kOutput, calls=%fused_computation.15 | convolution fusion | flops 402718720 | bytes 1835008 | tf_op jit(solution)/shard_map/dot_general | solution.py:8
  73.6 0.7 collective-permute-start.4
  74.3 2.4 %convolution_add_fusion.1 = f32[128,512]{1,0:T(8,128)S(1)} fusion(f32[128,512]{1,0:T(8,128)S(1)} %fusion.4, f32[512,2048]{1,0:T(8,128)} %all-gather.3.cloned.1.call-done, f32[128,512]{1,0:T(8,128)S(1)} %collective-permute-done.3, f32[128,512]{1,0:T(8,128)S(1)} %collective-permute-done.4), kind=kOutput, calls=%fused_computation.6 | convolution fusion | flops 402784256 | bytes 2097152 | tf_op jit(solution)/shard_map/dot_general | solution.py:8
  76.7 2.4 %broadcast_select_fusion = (f32[128,512]{1,0:T(8,128)S(1)}, f32[128,512]{1,0:T(8,128)S(1)}, f32[128,512]{1,0:T(8,128)S(1)}) fusion(pred[]{:T(512)S(6)} %eq.87, f32[128,512]{1,0:T(8,128)S(1)} %fusion.9, f32[128,512]{1,0:T(8,128)S(1)} %fusion.11, pred[]{:T(512)S(6)} %eq.89, pred[]{:T(512)S(6)} %eq.88, f32[2048,512]{1,0:T(8,128)} %param.5, ...), kind=kOutput, calls=%fused_computation.30 | convolution fusion | flops 402915328 | bytes 2883587 | tf_op jit(solution)/shard_map/dot_general | solution.py:8
  81.9 0.7 collective-permute-start.18
  83.3 2.4 %fusion.1 = f32[128,512]{1,0:T(8,128)S(1)} fusion(f32[128,512]{1,0:T(8,128)S(1)} %convolution_add_fusion.1, f32[128,512]{1,0:T(8,128)S(1)} %collective-permute-done.5, f32[512,2048]{1,0:T(8,128)} %all-gather.3.cloned.1.call-done, f32[128,1024]{1,0:T(8,128)S(1)} %copy-done), kind=kOutput, calls=%fused_computation.5 | convolution fusion | flops 402784256 | bytes 2097152 | tf_op jit(solution)/shard_map/dot_general | solution.py:8
  86.4 2.4 %convolution_select_fusion = f32[128,512]{1,0:T(8,128)S(1)} fusion(f32[128,512]{1,0:T(8,128)S(1)} %get-tuple-element.11, f32[128,512]{1,0:T(8,128)S(1)} %fusion.1, f32[2048,512]{1,0:T(8,128)} %param.5, pred[]{:T(512)S(6)} %eq.86), kind=kOutput, calls=%fused_computation.3 | convolution fusion | flops 402718720 | bytes 1835009 | tf_op jit(solution)/shard_map/dot_general | solution.py:8
  89.5 0.7 collective-permute-start.7
  91.7 0.7 collective-permute-start.16
  96.1 1.3 collective-permute-start.11
  97.4 1.4 collective-permute-start.9
  98.8 22.9 %collective-permute-done.11 = f32[128,512]{1,0:T(8,128)} collective-permute-done((f32[128,512]{1,0:T(8,128)S(1)}, f32[128,512]{1,0:T(8,128)}, u32[]{:S(2)}, u32[]{:S(2)}) %collective-permute-start.11) | collective-permute-done | bytes 262176 | tf_op jit(solution)/shard_map/ppermute | solution.py:76
  121.7 1.3 select_select_fusion
  123.2 5.2 %collective-permute-done.24 = f32[128,512]{1,0:T(8,128)S(1)} collective-permute-done((f32[128,512]{1,0:T(8,128)S(1)}, f32[128,512]{1,0:T(8,128)S(1)}, u32[]{:S(2)}, u32[]{:S(2)}) %collective-permute-start.24) | collective-permute-done | bytes 262176 | tf_op jit(solution)/shard_map/ppermute | solution.py:83
  128.4 5.2 %collective-permute-start.25 = (f32[128,1024]{1,0:T(8,128)S(1)}, f32[128,1024]{1,0:T(8,128)S(1)}, u32[]{:S(2)}, u32[]{:S(2)}) collective-permute-start(f32[128,1024]{1,0:T(8,128)S(1)} %maximum_select_fusion.1), channel_id=1, source_target_pairs={{0,4},{4,0},{8,12},{12,8},{16,20},{20,16},{24,28},{28,24},{32,36},... | collective-permute-start | bytes 1572872 | tf_op jit(solution)/shard_map/ppermute | solution.py:85
  133.7 1.5 collective-permute-done.25
  135.2 6.5 %fusion = f32[128,512]{1,0:T(8,128)S(1)} fusion(f32[128,512]{1,0:T(8,128)S(1)} %convolution_select_fusion, f32[512,2048]{1,0:T(8,128)} %all-gather.3.cloned.1.call-done, pred[]{:T(512)S(6)} %lt.81, f32[128,512]{1,0:T(8,128)S(1)} %get-tuple-element.18, f32[128,512]{1,0:T(8,128)S(1)} %get-tuple-element.16, f32[128,512]{1,0:T(8,128)S(1)} %get-tuple-element.17, ...), kind=kOutput, calls=%fused_computation.2 | convolution fusion | flops 1612578816 | bytes 6029314 | tf_op jit(solution)/shard_map/dot_general | solution.py:8
  141.7 6.5 %convolution_subtract_fusion = f32[128,512]{1,0:T(8,128)S(1)} fusion(f32[512,2048]{1,0:T(8,128)} %all-gather.5.cloned.1.call-done, f32[128,1024]{1,0:T(8,128)S(1)} %copy-done, f32[128,512]{1,0:T(8,128)S(1)} %get-tuple-element.18, f32[128,512]{1,0:T(8,128)S(1)} %get-tuple-element.16, f32[128,512]{1,0:T(8,128)S(1)} %get-tuple-element.17, ...), kind=kOutput, calls=%fused_computation | convolution fusion | flops 1612513280 | bytes 5767169 | tf_op jit(solution)/shard_map/dot_general | solution.py:8
  148.2 0.8 pad_maximum_fusion
  (58 shorter events, 12.9 us)
Async XLA Ops:
  6.5 59.2 %all-gather.3.cloned.1.call-start = ((), (), s32[]{:S(2)}) async-start(), calls=%async_computation | async-start | bytes 5242880 | tf_op jit(solution)/shard_map/all_gather | solution.py:40
  7.6 5.2 %collective-permute-start = (f32[128,512]{1,0:T(8,128)S(1)}, f32[128,512]{1,0:T(8,128)S(1)}, u32[]{:S(2)}, u32[]{:S(2)}) collective-permute-start(f32[128,512]{1,0:T(8,128)S(1)} %slice.46), channel_id=1, source_target_pairs={{0,12},{1,13},{2,14},{3,15}} | collective-permute-start | bytes 786440 | tf_op jit(solution)/shard_map/ppermute | solution.py:37
  8.3 4.5 %collective-permute-start.1 = (f32[128,512]{1,0:T(8,128)S(1)}, f32[128,512]{1,0:T(8,128)S(1)}, u32[]{:S(2)}, u32[]{:S(2)}) collective-permute-start(f32[128,512]{1,0:T(8,128)S(1)} %slice.46), channel_id=1, source_target_pairs={{0,8},{1,9},{2,10},{3,11}} | collective-permute-start | bytes 786440 | tf_op jit(solution)/shard_map/ppermute | solution.py:37
  8.9 3.8 %collective-permute-start.2 = (f32[128,512]{1,0:T(8,128)S(1)}, f32[128,512]{1,0:T(8,128)S(1)}, u32[]{:S(2)}, u32[]{:S(2)}) collective-permute-start(f32[128,512]{1,0:T(8,128)S(1)} %slice.46), channel_id=1, source_target_pairs={{0,4},{1,5},{2,6},{3,7}} | collective-permute-start | bytes 786440 | tf_op jit(solution)/shard_map/ppermute | solution.py:37
  12.9 128.8 %all-gather.5.cloned.1.call-start = ((), (), s32[]{:S(2)}) async-start(), calls=%async_computation.1 | async-start | bytes 5242880 | tf_op jit(solution)/shard_map/all_gather | solution.py:42
  79.9 5.8 %collective-permute-start.12 = (f32[128,512]{1,0:T(8,128)S(1)}, f32[128,512]{1,0:T(8,128)S(1)}, u32[]{:S(2)}, u32[]{:S(2)}) collective-permute-start(f32[128,512]{1,0:T(8,128)S(1)} %get-tuple-element.11), channel_id=1, source_target_pairs={{8,200},{9,201},{10,202},{11,203}} | collective-permute-start | bytes 786440 | tf_op jit(solution)/shard_map/ppermute | solution.py:76
  80.6 8.2 %collective-permute-start.13 = (f32[128,512]{1,0:T(8,128)S(1)}, f32[128,512]{1,0:T(8,128)S(1)}, u32[]{:S(2)}, u32[]{:S(2)}) collective-permute-start(f32[128,512]{1,0:T(8,128)S(1)} %get-tuple-element.11), channel_id=1, source_target_pairs={{8,136},{9,137},{10,138},{11,139}} | collective-permute-start | bytes 786440 | tf_op jit(solution)/shard_map/ppermute | solution.py:76
  81.2 8.3 %collective-permute-start.14 = (f32[128,512]{1,0:T(8,128)S(1)}, f32[128,512]{1,0:T(8,128)S(1)}, u32[]{:S(2)}, u32[]{:S(2)}) collective-permute-start(f32[128,512]{1,0:T(8,128)S(1)} %get-tuple-element.11), channel_id=1, source_target_pairs={{8,72},{9,73},{10,74},{11,75}} | collective-permute-start | bytes 786440 | tf_op jit(solution)/shard_map/ppermute | solution.py:76
  81.9 8.4 %collective-permute-start.18 = (f32[128,512]{1,0:T(8,128)S(1)}, f32[128,512]{1,0:T(8,128)S(1)}, u32[]{:S(2)}, u32[]{:S(2)}) collective-permute-start(f32[128,512]{1,0:T(8,128)S(1)} %get-tuple-element.12), channel_id=1, source_target_pairs={{0,192},{4,196},{1,193},{5,197},{2,194},{6,198},{3,195},{7,199}} | collective-permute-start | bytes 786440 | tf_op jit(solution)/shard_map/ppermute | solution.py:76
  82.6 8.4 %collective-permute-start.19 = (f32[128,512]{1,0:T(8,128)S(1)}, f32[128,512]{1,0:T(8,128)S(1)}, u32[]{:S(2)}, u32[]{:S(2)}) collective-permute-start(f32[128,512]{1,0:T(8,128)S(1)} %get-tuple-element.12), channel_id=1, source_target_pairs={{0,128},{4,132},{1,129},{5,133},{2,130},{6,134},{3,131},{7,135}} | collective-permute-start | bytes 786440 | tf_op jit(solution)/shard_map/ppermute | solution.py:76
  85.7 6.0 %collective-permute-start.20 = (f32[128,512]{1,0:T(8,128)S(1)}, f32[128,512]{1,0:T(8,128)S(1)}, u32[]{:S(2)}, u32[]{:S(2)}) collective-permute-start(f32[128,512]{1,0:T(8,128)S(1)} %get-tuple-element.12), channel_id=1, source_target_pairs={{0,64},{4,68},{1,65},{5,69},{2,66},{6,70},{3,67},{7,71}} | collective-permute-start | bytes 786440 | tf_op jit(solution)/shard_map/ppermute | solution.py:76
  88.8 3.7 %collective-permute-start.6 = (f32[128,512]{1,0:T(8,128)S(1)}, f32[128,512]{1,0:T(8,128)S(1)}, u32[]{:S(2)}, u32[]{:S(2)}) collective-permute-start(f32[128,512]{1,0:T(8,128)S(1)} %convolution_select_fusion), channel_id=1, source_target_pairs={{12,204},{13,205},{14,206},{15,207}} | collective-permute-start | bytes 786440 | tf_op jit(solution)/shard_map/ppermute | solution.py:76
  89.5 3.7 %collective-permute-start.7 = (f32[128,512]{1,0:T(8,128)S(1)}, f32[128,512]{1,0:T(8,128)S(1)}, u32[]{:S(2)}, u32[]{:S(2)}) collective-permute-start(f32[128,512]{1,0:T(8,128)S(1)} %convolution_select_fusion), channel_id=1, source_target_pairs={{12,140},{13,141},{14,142},{15,143}} | collective-permute-start | bytes 786440 | tf_op jit(solution)/shard_map/ppermute | solution.py:76
  90.3 3.6 %collective-permute-start.8 = (f32[128,512]{1,0:T(8,128)S(1)}, f32[128,512]{1,0:T(8,128)S(1)}, u32[]{:S(2)}, u32[]{:S(2)}) collective-permute-start(f32[128,512]{1,0:T(8,128)S(1)} %convolution_select_fusion), channel_id=1, source_target_pairs={{12,76},{13,77},{14,78},{15,79}} | collective-permute-start | bytes 786440 | tf_op jit(solution)/shard_map/ppermute | solution.py:76
  91.0 3.7 %collective-permute-start.15 = (f32[128,512]{1,0:T(8,128)S(1)}, f32[128,512]{1,0:T(8,128)S(1)}, u32[]{:S(2)}, u32[]{:S(2)}) collective-permute-start(f32[128,512]{1,0:T(8,128)S(1)} %select_select_fusion.2), channel_id=1, source_target_pairs={{8,56},{72,120},{136,184},{200,248},{9,57},{73,121},{137,185},{201... | collective-permute-start | bytes 786440 | tf_op jit(solution)/shard_map/ppermute | solution.py:76
  91.7 3.7 %collective-permute-start.16 = (f32[128,512]{1,0:T(8,128)S(1)}, f32[128,512]{1,0:T(8,128)S(1)}, u32[]{:S(2)}, u32[]{:S(2)}) collective-permute-start(f32[128,512]{1,0:T(8,128)S(1)} %select_select_fusion.2), channel_id=1, source_target_pairs={{8,40},{72,104},{136,168},{200,232},{9,41},{73,105},{137,169},{201... | collective-permute-start | bytes 786440 | tf_op jit(solution)/shard_map/ppermute | solution.py:76
  92.5 3.6 %collective-permute-start.17 = (f32[128,512]{1,0:T(8,128)S(1)}, f32[128,512]{1,0:T(8,128)S(1)}, u32[]{:S(2)}, u32[]{:S(2)}) collective-permute-start(f32[128,512]{1,0:T(8,128)S(1)} %select_select_fusion.2), channel_id=1, source_target_pairs={{8,24},{72,88},{136,152},{200,216},{9,25},{73,89},{137,153},{201,2... | collective-permute-start | bytes 786440 | tf_op jit(solution)/shard_map/ppermute | solution.py:76
  93.2 4.2 %collective-permute-start.21 = (f32[128,512]{1,0:T(8,128)S(1)}, f32[128,512]{1,0:T(8,128)S(1)}, u32[]{:S(2)}, u32[]{:S(2)}) collective-permute-start(f32[128,512]{1,0:T(8,128)S(1)} %select_select_fusion.1), channel_id=1, source_target_pairs={{0,48},{4,52},{64,112},{68,116},{128,176},{132,180},{192,240},{196... | collective-permute-start | bytes 786440 | tf_op jit(solution)/shard_map/ppermute | solution.py:76
  93.9 4.9 %collective-permute-start.22 = (f32[128,512]{1,0:T(8,128)S(1)}, f32[128,512]{1,0:T(8,128)S(1)}, u32[]{:S(2)}, u32[]{:S(2)}) collective-permute-start(f32[128,512]{1,0:T(8,128)S(1)} %select_select_fusion.1), channel_id=1, source_target_pairs={{0,32},{4,36},{64,96},{68,100},{128,160},{132,164},{192,224},{196,... | collective-permute-start | bytes 786440 | tf_op jit(solution)/shard_map/ppermute | solution.py:76
  94.7 4.1 %collective-permute-start.23 = (f32[128,512]{1,0:T(8,128)S(1)}, f32[128,512]{1,0:T(8,128)S(1)}, u32[]{:S(2)}, u32[]{:S(2)}) collective-permute-start(f32[128,512]{1,0:T(8,128)S(1)} %select_select_fusion.1), channel_id=1, source_target_pairs={{0,16},{4,20},{64,80},{68,84},{128,144},{132,148},{192,208},{196,2... | collective-permute-start | bytes 786440 | tf_op jit(solution)/shard_map/ppermute | solution.py:76
  96.1 25.6 %collective-permute-start.11 = (f32[128,512]{1,0:T(8,128)S(1)}, f32[128,512]{1,0:T(8,128)}, u32[]{:S(2)}, u32[]{:S(2)}) collective-permute-start(f32[128,512]{1,0:T(8,128)S(1)} %select_select_fusion.3), channel_id=1, source_target_pairs={{12,28},{76,92},{140,156},{204,220},{13,29},{77,93},{141,157},{205... | collective-permute-start | bytes 786440 | tf_op jit(solution)/shard_map/ppermute | solution.py:76
  97.4 24.3 %collective-permute-start.9 = (f32[128,512]{1,0:T(8,128)S(1)}, f32[128,512]{1,0:T(8,128)}, u32[]{:S(2)}, u32[]{:S(2)}) collective-permute-start(f32[128,512]{1,0:T(8,128)S(1)} %select_select_fusion.3), channel_id=1, source_target_pairs={{12,60},{76,124},{140,188},{204,252},{13,61},{77,125},{141,189},{2... | collective-permute-start | bytes 786440 | tf_op jit(solution)/shard_map/ppermute | solution.py:76
  123.0 5.3 %collective-permute-start.24 = (f32[128,512]{1,0:T(8,128)S(1)}, f32[128,512]{1,0:T(8,128)S(1)}, u32[]{:S(2)}, u32[]{:S(2)}) collective-permute-start(f32[128,512]{1,0:T(8,128)S(1)} %select_select_fusion), channel_id=1, source_target_pairs={{0,8},{4,12},{8,0},{12,4},{16,24},{20,28},{24,16},{28,20},{32,40},... | collective-permute-start | bytes 786440 | tf_op jit(solution)/shard_map/ppermute | solution.py:83
  128.4 6.8 %collective-permute-start.25 = (f32[128,1024]{1,0:T(8,128)S(1)}, f32[128,1024]{1,0:T(8,128)S(1)}, u32[]{:S(2)}, u32[]{:S(2)}) collective-permute-start(f32[128,1024]{1,0:T(8,128)S(1)} %maximum_select_fusion.1), channel_id=1, source_target_pairs={{0,4},{4,0},{8,12},{12,8},{16,20},{20,16},{24,28},{28,24},{32,36},... | collective-permute-start | bytes 1572872 | tf_op jit(solution)/shard_map/ppermute | solution.py:85
  (6 other events, 38.1 us)
Sparse Core Ops, SparseCore 0:
  13.0 52.6 all-gather.2
  67.5 51.1 all-gather.4
